TPU v7x, 32 devices: a whole 2x2x4 slice. The times are simulated.
32 devices in a mesh: var: 8 (over z, y), samp: 4 (over x, core).
Axes of the slice: x: 2, y: 2, z: 4, core: 2. Of those that a mesh axis runs over, the one named last changes fastest.
Arguments:
- dosages: bfloat16 [8192, 6144], P('samp', 'var'), may hold values from 0 to 2
- observed: int32 [8192, 6144], P('samp', 'var'), may hold values 0 or 1
Outputs:
- ld_scores: float32 [6144], P(('var', 'samp'))
All inputs are finite; a program needn't handle non-finite values. No bound on the sum of `observed` on one device may be relied on, other than what follows from the above.
Results may differ from a plain program's by a relative error of at most 0.00055.
Values may be sent and summed in bfloat16 or wider, within the bound.
No kernel may reach another device: no remote copies, remote signals or barrier semaphores. Data moves between devices by JAX's collectives and lax.ppermute only.
A program may use at most 192 MiB of HBM per device.

v0:
```python
import jax
import jax.numpy as jnp
from jax import lax
from jax.sharding import PartitionSpec as P

BAND = 3


def from_behind(value, axis, steps):
    count = lax.axis_size(axis)
    leading, last = (max(0, -steps), min(count, count - steps))
    return lax.ppermute(value, axis, [(source, source + steps) for source in range(leading, last)])


def adjusted_r2(gram_part, samples):
    correl = gram_part / samples
    squared = correl * correl
    return squared - (1.0 - squared) / (samples - 2)


def local(dosages, observed):
    values = dosages.astype(jnp.float32)
    present = observed.astype(jnp.float32)
    seen_count, first_sum, second_sum = lax.psum(
        (jnp.sum(present, 0), jnp.sum(present * values, 0), jnp.sum(present * values * values, 0)),
        "samp",
    )
    seen_count = jnp.maximum(seen_count, 1.0)
    column_mean = first_sum / seen_count
    spread = second_sum / seen_count - column_mean * column_mean
    standard = ((values - column_mean) * lax.rsqrt(spread + 1e-05) * present).astype(jnp.bfloat16)
    samples = standard.shape[0] * lax.axis_size("samp")
    block_width = standard.shape[1]
    position = lax.axis_index("var")
    chain_len = lax.axis_size("var")
    rows_here = block_width // lax.axis_size("samp")
    partners = [standard]
    for offset in range(1, BAND + 1):
        partners.append(from_behind(standard, "var", -offset))
    band_cat = jnp.concatenate(partners, 1)
    gram_part = lax.psum_scatter(
        lax.dot_general(
            standard, band_cat, (((0,), (0,)), ((), ())), preferred_element_type=jnp.float32
        ).astype(jnp.bfloat16),
        "samp",
        scatter_dimension=0,
        tiled=True,
    ).astype(jnp.float32)
    adjusted = adjusted_r2(gram_part, samples).reshape(rows_here, BAND + 1, block_width)
    in_range = (position + jnp.arange(BAND + 1, dtype=jnp.int32) < chain_len).astype(jnp.float32)
    adjusted = adjusted * in_range[None, :, None]
    ld_total = jnp.sum(adjusted, (1, 2))
    col_sums = jnp.sum(adjusted[:, 1:, :], 0)
    shares = lax.psum_scatter(col_sums, "samp", scatter_dimension=1, tiled=True)
    for offset in range(1, BAND + 1):
        ld_total = ld_total + from_behind(shares[offset - 1], "var", offset)
    return ld_total / block_width


def solution(mesh):
    placed = (P("samp", "var"), P("samp", "var"))
    return jax.shard_map(
        local, mesh=mesh, in_specs=placed, out_specs=P(("var", "samp")), check_vma=False
    )
```

profile of v0, /device:TPU:14, one launch (start us, length us, event | category | flops | bytes accessed | tf_op | source)
XLA Modules:
  0.0 415.2 jit_solution(641120508770835503)
XLA Ops:
  6.5 0.0 copy-start
  6.5 0.0 reduce-scatter.5.cloned.1.call-start
  6.5 5.4 %fusion.12 = (f32[768]{0:T(1024)S(1)}, f32[768]{0:T(1024)S(1)}, f32[768]{0:T(1024)S(1)}) fusion(bf16[2048,768]{1,0:T(8,128)(2,1)} %param.2, s32[2048,768]{1,0:T(8,128)} %param.3), kind=kLoop, calls=%fused_computation.16 | loop fusion | flops 11007744 | bytes 9446400 | tf_op jit(solution)/shard_map/reduce_sum | solution.py:25
  12.0 10.2 %all-reduce = (f32[768]{0:T(1024)S(1)}, f32[768]{0:T(1024)S(1)}, f32[768]{0:T(1024)S(1)}) all-reduce(f32[768]{0:T(1024)S(1)} %get-tuple-element.6, f32[768]{0:T(1024)S(1)} %get-tuple-element.7, f32[768]{0:T(1024)S(1)} %get-tuple-element.5), channel_id=1, replica_groups=mesh['var'=8,'samp'=4] {'samp'}, use_global_device_ids=true, to_apply=%region_5.0 | all-reduce | flops 2304 | bytes 18432 | tf_op jit(solution)/shard_map/psum | solution.py:24
  22.2 0.0 copy-done
  22.2 3.9 fusion.10
  26.1 0.0 copy-start.1
  26.1 2.4 collective-permute-start
  28.5 2.3 collective-permute-start.1
  30.8 0.0 copy-done.1
  30.8 1.9 collective-permute-start.2
  32.8 67.1 %collective-permute-done = bf16[2048,768]{1,0:T(8,128)(2,1)S(1)} collective-permute-done((bf16[2048,768]{1,0:T(8,128)(2,1)S(1)}, bf16[2048,768]{1,0:T(8,128)(2,1)S(1)}, u32[]{:S(2)}, u32[]{:S(2)}) %collective-permute-start) | collective-permute-done | bytes 3145760 | tf_op jit(solution)/shard_map/ppermute | solution.py:12
  99.9 1.5 collective-permute-done.1
  101.4 0.0 copy-start.2
  101.4 1.7 copy-done.2
  103.1 131.2 %collective-permute-done.2 = bf16[2048,768]{1,0:T(8,128)(2,1)} collective-permute-done((bf16[2048,768]{1,0:T(8,128)(2,1)S(1)}, bf16[2048,768]{1,0:T(8,128)(2,1)}, u32[]{:S(2)}, u32[]{:S(2)}) %collective-permute-start.2) | collective-permute-done | bytes 3145760 | tf_op jit(solution)/shard_map/ppermute | solution.py:12
  234.3 17.6 %fusion.13 = bf16[768,3072]{1,0:T(8,128)(2,1)} fusion(bf16[2048,768]{1,0:T(8,128)(2,1)} %copy-done.1, bf16[2048,768]{1,0:T(8,128)(2,1)} %collective-permute-done.2, bf16[2048,768]{1,0:T(8,128)(2,1)} %copy-done.2, bf16[2048,768]{1,0:T(8,128)(2,1)S(1)} %collective-permute-done), kind=kOutput, calls=%fused_computation.17 | convolution fusion | flops 9716367360 | bytes 17301504 | tf_op jit(solution)/shard_map/dot_general | solution.py:42
  251.9 0.0 reduce-scatter.5.cloned.1.call-update
  252.0 0.2 reduce-scatter.7.cloned.1.call-start
  252.2 0.1 slice.17
  252.3 0.1 mul.48
  252.4 112.2 %reduce-scatter.5.cloned.1.call-done = bf16[192,3072]{1,0:T(8,128)(2,1)} async-done(((bf16[768,3072]{1,0:T(8,128)(2,1)}), bf16[192,3072]{1,0:T(8,128)(2,1)}) %reduce-scatter.5.cloned.1.call-update) | async-done | bytes 1179664 | tf_op jit(solution)/shard_map/reduce_scatter | solution.py:41
  364.6 2.0 multiply_reduce_fusion
  366.5 2.2 reshape.12
  368.8 2.5 fusion.16
  371.3 0.9 copy.3
  372.2 0.0 reduce-scatter.7.cloned.1.call-update
  372.2 21.0 %reduce-scatter.7.cloned.1.call-done = f32[192,3]{1,0:T(8,128)} async-done(((f32[768,3]{1,0:T(8,128)}), f32[192,3]{1,0:T(8,128)}) %reduce-scatter.7.cloned.1.call-update) | async-done | bytes 2320
  393.2 1.1 fusion.18
  394.4 0.1 copy.5
  394.5 3.4 collective-permute-start.3
  397.9 0.1 copy.6
  397.9 3.4 collective-permute-start.4
  401.3 0.1 copy.7
  401.4 2.2 collective-permute-start.5
  403.6 0.0 collective-permute-done.3
  403.6 0.0 collective-permute-done.4
  403.6 4.1 collective-permute-done.5
  407.8 0.6 add_multiply_fusion
  (3 shorter events, 0.0 us)
Async XLA Ops:
  6.5 15.6 %copy-start = (bf16[2048,768]{1,0:T(8,128)(2,1)S(1)}, bf16[2048,768]{1,0:T(8,128)(2,1)}, u32[]{:S(2)}) copy-start(bf16[2048,768]{1,0:T(8,128)(2,1)} %param.2) | copy-start | bytes 9437188
  6.5 358.0 %reduce-scatter.5.cloned.1.call-start = ((), (), s32[]{:S(2)}) async-start(), calls=%async_computation.2 | async-start | bytes 5898240 | tf_op jit(solution)/shard_map/reduce_scatter | solution.py:41
  26.1 4.7 %copy-start.1 = (bf16[2048,768]{1,0:T(8,128)(2,1)}, bf16[2048,768]{1,0:T(8,128)(2,1)S(1)}, u32[]{:S(2)}) copy-start(bf16[2048,768]{1,0:T(8,128)(2,1)S(1)} %fusion.10) | copy-start | bytes 9437188
  26.1 73.8 %collective-permute-start = (bf16[2048,768]{1,0:T(8,128)(2,1)S(1)}, bf16[2048,768]{1,0:T(8,128)(2,1)S(1)}, u32[]{:S(2)}, u32[]{:S(2)}) collective-permute-start(bf16[2048,768]{1,0:T(8,128)(2,1)S(1)} %fusion.10), channel_id=1, source_target_pairs={{4,0},{8,4},{12,8},{16,12},{20,16},{24,20},{28,24},{5,1},{9,5},{13... | collective-permute-start | bytes 9437192 | tf_op jit(solution)/shard_map/ppermute | solution.py:12
  28.5 72.9 %collective-permute-start.1 = (bf16[2048,768]{1,0:T(8,128)(2,1)S(1)}, bf16[2048,768]{1,0:T(8,128)(2,1)S(1)}, u32[]{:S(2)}, u32[]{:S(2)}) collective-permute-start(bf16[2048,768]{1,0:T(8,128)(2,1)S(1)} %fusion.10), channel_id=1, source_target_pairs={{8,0},{12,4},{16,8},{20,12},{24,16},{28,20},{9,1},{13,5},{17,9},{2... | collective-permute-start | bytes 9437192 | tf_op jit(solution)/shard_map/ppermute | solution.py:12
  30.8 203.5 %collective-permute-start.2 = (bf16[2048,768]{1,0:T(8,128)(2,1)S(1)}, bf16[2048,768]{1,0:T(8,128)(2,1)}, u32[]{:S(2)}, u32[]{:S(2)}) collective-permute-start(bf16[2048,768]{1,0:T(8,128)(2,1)S(1)} %fusion.10), channel_id=1, source_target_pairs={{12,0},{16,4},{20,8},{24,12},{28,16},{13,1},{17,5},{21,9},{25,13},... | collective-permute-start | bytes 9437192 | tf_op jit(solution)/shard_map/ppermute | solution.py:12
  101.4 1.8 copy-start.2
  252.0 141.3 %reduce-scatter.7.cloned.1.call-start = ((), (), s32[]{:S(2)}) async-start(), calls=%async_computation.3 | async-start | bytes 491520
  394.5 9.2 %collective-permute-start.3 = (f32[192]{0:T(256)S(1)}, f32[192]{0:T(256)S(1)}, u32[]{:S(2)}, u32[]{:S(2)}) collective-permute-start(f32[192]{0:T(256)S(1)} %bitcast.8), channel_id=1, source_target_pairs={{0,4},{4,8},{8,12},{12,16},{16,20},{20,24},{24,28},{1,5},{5,9},{9,... | collective-permute-start | bytes 2312 | tf_op jit(solution)/shard_map/ppermute | solution.py:12
  397.9 5.7 %collective-permute-start.4 = (f32[192]{0:T(256)S(1)}, f32[192]{0:T(256)S(1)}, u32[]{:S(2)}, u32[]{:S(2)}) collective-permute-start(f32[192]{0:T(256)S(1)} %bitcast.9), channel_id=1, source_target_pairs={{0,8},{4,12},{8,16},{12,20},{16,24},{20,28},{1,9},{5,13},{9,17},{1... | collective-permute-start | bytes 2312 | tf_op jit(solution)/shard_map/ppermute | solution.py:12
  401.4 6.4 %collective-permute-start.5 = (f32[192]{0:T(256)S(1)}, f32[192]{0:T(256)S(1)}, u32[]{:S(2)}, u32[]{:S(2)}) collective-permute-start(f32[192]{0:T(256)S(1)} %bitcast.10), channel_id=1, source_target_pairs={{0,12},{4,16},{8,20},{12,24},{16,28},{1,13},{5,17},{9,21},{13,25},... | collective-permute-start | bytes 2312 | tf_op jit(solution)/shard_map/ppermute | solution.py:12
Sparse Core Ops, SparseCore 0:
  252.1 112.4 reduce-scatter.4
  372.4 20.8 reduce-scatter.6
where the time goes:
time: 417 us; the launch traced here: 415 us
  waiting for transfers between devices  337 us (81%)
  matrix products  17.6 us (4%)
  starting transfers between devices  15.8 us (4%)
  other arithmetic  14.4 us (3%)
  between operations  13.5 us (3%)
  blocking collectives  10.2 us (2%)
  local copies, waits for them, and re-layouts  6.46 us (2%)
    ppermute x6, waiting for transfers between devices, from_behind(): lax.ppermute(value, axis, [(source, source + steps) for source in range(l...  204 us
    reduce_scatter x1, waiting for transfers between devices, local(): lax.psum_scatter(lax.dot_general(standard, band_cat, (((0,), (0,)), ((),...  112 us
    unnamed x3, waiting for transfers between devices  21 us
    dot_general x1, matrix products, local(): lax.dot_general(standard, band_cat, (((0,), (0,)), ((), ())), preferred_e...  17.6 us
    ppermute x6, starting transfers between devices, from_behind(): lax.ppermute(value, axis, [(source, source + steps) for source in range(l...  15.6 us
    psum x1, blocking collectives, local(): lax.psum((jnp.sum(present, 0), jnp.sum(present * values, 0), jnp.sum(pres...  10.2 us
  transfers between devices with their start and end apart: 8, of which 6 were waited for; matrix products, arithmetic and copies ran while one was open for 0% of the time, Pallas kernels for 0%

commit v1 on v0

v1 whole, which is shorter than its diff:
```python
import jax
import jax.numpy as jnp
from jax import lax
from jax.sharding import PartitionSpec as P

BAND = 3
PARTNER_STEP = {1: 1, 2: 2, 3: -3}


def from_behind(value, axis, steps):
    count = lax.axis_size(axis)
    leading, last = (max(0, -steps), min(count, count - steps))
    return lax.ppermute(value, axis, [(source, source + steps) for source in range(leading, last)])


def adjusted_r2(gram_part, samples):
    correl = gram_part / samples
    squared = correl * correl
    return squared - (1.0 - squared) / (samples - 2)


def gram_of(left, right):
    return lax.dot_general(left, right, (((0,), (0,)), ((), ())), preferred_element_type=jnp.float32)


def reduce_to_owner(part, owner, n_samp):
    pairs_core = [(s, s ^ 1) for s in range(n_samp) if (s & 1) != (owner & 1)]
    summed = part + lax.ppermute(part.astype(jnp.bfloat16), "samp", pairs_core).astype(jnp.float32)
    pairs_chip = [(owner ^ 2, owner)]
    return summed + lax.ppermute(summed.astype(jnp.bfloat16), "samp", pairs_chip).astype(jnp.float32)


def local(dosages, observed):
    values = dosages.astype(jnp.float32)
    present = observed.astype(jnp.float32)
    seen_count, first_sum, second_sum = lax.psum(
        (jnp.sum(present, 0), jnp.sum(present * values, 0), jnp.sum(present * values * values, 0)),
        "samp",
    )
    seen_count = jnp.maximum(seen_count, 1.0)
    column_mean = first_sum / seen_count
    spread = second_sum / seen_count - column_mean * column_mean
    standard = ((values - column_mean) * lax.rsqrt(spread + 1e-05) * present).astype(jnp.bfloat16)
    n_samp = lax.axis_size("samp")
    n_var = lax.axis_size("var")
    samples = standard.shape[0] * n_samp
    block_width = standard.shape[1]
    position = lax.axis_index("var")
    me = lax.axis_index("samp")

    owned = [reduce_to_owner(gram_of(standard, standard), 0, n_samp)]
    for offset in range(1, BAND + 1):
        step = PARTNER_STEP[offset]
        partner = from_behind(standard, "var", -step)
        owned.append(reduce_to_owner(gram_of(standard, partner), offset, n_samp))
    gram = lax.dynamic_index_in_dim(jnp.stack(owned), me, 0, keepdims=False)

    steps = jnp.array([0] + [PARTNER_STEP[d] for d in range(1, BAND + 1)], jnp.int32)
    target = position + steps[me]
    in_range = ((target >= 0) & (target < n_var)).astype(jnp.float32)
    adjusted = adjusted_r2(gram, samples) * in_range
    row_sums = jnp.sum(adjusted, 1)
    col_sums = jnp.sum(adjusted, 0) * (me > 0).astype(jnp.float32)
    pairs = []
    for var_idx in range(n_var):
        for offset in range(1, BAND + 1):
            dest = var_idx + PARTNER_STEP[offset]
            if 0 <= dest < n_var:
                pairs.append((var_idx * n_samp + offset, dest * n_samp + offset))
    moved = lax.ppermute(col_sums, ("var", "samp"), pairs)
    total = lax.psum_scatter(row_sums + moved, "samp", scatter_dimension=0, tiled=True)
    return total / block_width


def solution(mesh):
    placed = (P("samp", "var"), P("samp", "var"))
    return jax.shard_map(
        local, mesh=mesh, in_specs=placed, out_specs=P(("var", "samp")), check_vma=False
    )
```

time: 417 us -> 228 us (0.55)
  waiting for transfers between devices: 337 us -> 142 us
  between operations: 13.5 us -> 1.61 us
  starting transfers between devices: 15.8 us -> 27.5 us
  other arithmetic: 14.4 us -> 25.1 us
  blocking collectives: 10.2 us -> 15.9 us
  local copies, waits for them, and re-layouts: 6.46 us -> 1.22 us
  matrix products: 17.6 us -> 12.7 us
    reduce_scatter x1 -> x0, waiting for transfers between devices: 112 us -> none  [local(): lax.psum_scatter(lax.dot_general(standard, band_cat, (((0,), (0,)), ((),...]
    ppermute x6 -> x3, waiting for transfers between devices: 204 us -> 125 us  [from_behind(): lax.ppermute(value, axis, [(source, source + steps) for source in range(l...]
    unnamed x3 -> x0, waiting for transfers between devices: 21 us -> none
    ppermute x0 -> x9, starting transfers between devices: none -> 18.1 us  [the longest x4 8.88 us: reduce_to_owner(): lax.ppermute(part.astype(jnp.bfloat16), 'samp', pairs_core)]
    ppermute x0 -> x9, waiting for transfers between devices: none -> 16.8 us  [the longest x4 14.4 us: reduce_to_owner(): lax.ppermute(summed.astype(jnp.bfloat16), 'samp', pairs_chip)]
    another operation x0 -> x4, other arithmetic: none -> 6.69 us  [local(): gram = lax.dynamic_index_in_dim(jnp.stack(owned), me, 0, keepdims=False)]
    convert_element_type x1 -> x4, other arithmetic: 0.01 us -> 6.38 us  [reduce_to_owner(): summed.astype(jnp.bfloat16)]
    ppermute x6 -> x3, starting transfers between devices: 15.6 us -> 9.41 us  [from_behind(): lax.ppermute(value, axis, [(source, source + steps) for source in range(l...]
  transfers between devices with their start and end apart: 8 -> 12, of which waited for: 6 -> 4; matrix products, arithmetic and copies ran while one was open for 0% -> 11% of each run, Pallas kernels for 0% -> 0%
where the time goes in v1:
time: 228 us; the launch traced here: 226 us
  waiting for transfers between devices  142 us (62%)
  starting transfers between devices  27.5 us (12%)
  other arithmetic  25.1 us (11%)
  blocking collectives  15.9 us (7%)
  matrix products  12.7 us (6%)
    ppermute x3, waiting for transfers between devices, from_behind(): lax.ppermute(value, axis, [(source, source + steps) for source in range(l...  125 us
    ppermute x4, waiting for transfers between devices, reduce_to_owner(): lax.ppermute(summed.astype(jnp.bfloat16), 'samp', pairs_chip)  14.4 us
    dot_general x4, matrix products, gram_of(): lax.dot_general(left, right, (((0,), (0,)), ((), ())), preferred_element_...  12.7 us
    psum x1, blocking collectives, local(): lax.psum((jnp.sum(present, 0), jnp.sum(present * values, 0), jnp.sum(pres...  10.2 us
    ppermute x3, starting transfers between devices, from_behind(): lax.ppermute(value, axis, [(source, source + steps) for source in range(l...  9.41 us
    ppermute x4, starting transfers between devices, reduce_to_owner(): lax.ppermute(part.astype(jnp.bfloat16), 'samp', pairs_core)  8.88 us
    ppermute x4, starting transfers between devices, reduce_to_owner(): lax.ppermute(summed.astype(jnp.bfloat16), 'samp', pairs_chip)  7.25 us
    another operation x4, other arithmetic, local(): gram = lax.dynamic_index_in_dim(jnp.stack(owned), me, 0, keepdims=False)  6.69 us
  transfers between devices with their start and end apart: 12, of which 4 were waited for; matrix products, arithmetic and copies ran while one was open for 11% of the time, Pallas kernels for 0%

profile of v1, /device:TPU:14, one launch (start us, length us, event | category | flops | bytes accessed | tf_op | source)
XLA Modules:
  0.0 226.1 jit_solution(10486559457021077171)
XLA Ops:
  0.0 5.3 %fusion.4 = (f32[768]{0:T(1024)S(1)}, f32[768]{0:T(1024)S(1)}, f32[768]{0:T(1024)S(1)}) fusion(bf16[2048,768]{1,0:T(8,128)(2,1)} %param.3, s32[2048,768]{1,0:T(8,128)} %param.4), kind=kLoop, calls=%fused_computation.12 | loop fusion | flops 11007744 | bytes 9446400 | tf_op jit(solution)/shard_map/reduce_sum | solution.py:37
  5.3 10.2 %all-reduce.1 = (f32[768]{0:T(1024)S(1)}, f32[768]{0:T(1024)S(1)}, f32[768]{0:T(1024)S(1)}) all-reduce(f32[768]{0:T(1024)S(1)} %get-tuple-element.6, f32[768]{0:T(1024)S(1)} %get-tuple-element.7, f32[768]{0:T(1024)S(1)} %get-tuple-element.5), channel_id=1, replica_groups=mesh['var'=8,'samp'=4] {'samp'}, use_global_device_ids=true, to_apply=%region_5.0 | all-reduce | flops 2304 | bytes 18432 | tf_op jit(solution)/shard_map/psum | solution.py:36
  15.5 4.9 %fusion.2 = bf16[2048,768]{1,0:T(8,128)(2,1)S(1)} fusion(bf16[2048,768]{1,0:T(8,128)(2,1)} %param.3, s32[2048,768]{1,0:T(8,128)} %param.4, f32[768]{0:T(1024)S(1)} %get-tuple-element.14, f32[768]{0:T(1024)S(1)} %get-tuple-element.13), kind=kLoop, calls=%fused_computation.9 | loop fusion | flops 9437184 | bytes 12589056 | tf_op jit(solution)/shard_map/convert_element_type | solution.py:43
  20.4 4.4 %collective-permute-start.8 = (bf16[2048,768]{1,0:T(8,128)(2,1)S(1)}, bf16[2048,768]{1,0:T(8,128)(2,1)S(1)}, u32[]{:S(2)}, u32[]{:S(2)}) collective-permute-start(bf16[2048,768]{1,0:T(8,128)(2,1)S(1)} %fusion.2), channel_id=1, source_target_pairs={{0,12},{4,16},{8,20},{12,24},{16,28},{1,13},{5,17},{9,21},{13,25},... | collective-permute-start | bytes 9437192 | tf_op jit(solution)/shard_map/ppermute | solution.py:13
  24.8 2.6 %collective-permute-start.5 = (bf16[2048,768]{1,0:T(8,128)(2,1)S(1)}, bf16[2048,768]{1,0:T(8,128)(2,1)S(1)}, u32[]{:S(2)}, u32[]{:S(2)}) collective-permute-start(bf16[2048,768]{1,0:T(8,128)(2,1)S(1)} %fusion.2), channel_id=1, source_target_pairs={{8,0},{12,4},{16,8},{20,12},{24,16},{28,20},{9,1},{13,5},{17,9},{2... | collective-permute-start | bytes 9437192 | tf_op jit(solution)/shard_map/ppermute | solution.py:13
  27.4 2.4 %collective-permute-start.2 = (bf16[2048,768]{1,0:T(8,128)(2,1)S(1)}, bf16[2048,768]{1,0:T(8,128)(2,1)S(1)}, u32[]{:S(2)}, u32[]{:S(2)}) collective-permute-start(bf16[2048,768]{1,0:T(8,128)(2,1)S(1)} %fusion.2), channel_id=1, source_target_pairs={{4,0},{8,4},{12,8},{16,12},{20,16},{24,20},{28,24},{5,1},{9,5},{13... | collective-permute-start | bytes 9437192 | tf_op jit(solution)/shard_map/ppermute | solution.py:13
  29.8 2.7 %fusion.19 = (bf16[768,768]{1,0:T(8,128)(2,1)S(1)}, f32[768,768]{1,0:T(8,128)S(1)}) fusion(bf16[2048,768]{1,0:T(8,128)(2,1)S(1)} %fusion.2), kind=kOutput, calls=%fused_computation.40 | convolution fusion | flops 2416508928 | bytes 6684672 | tf_op jit(solution)/shard_map/dot_general | solution.py:23
  32.5 1.3 collective-permute-start
  33.8 125.2 %collective-permute-done.8 = bf16[2048,768]{1,0:T(8,128)(2,1)S(1)} collective-permute-done((bf16[2048,768]{1,0:T(8,128)(2,1)S(1)}, bf16[2048,768]{1,0:T(8,128)(2,1)S(1)}, u32[]{:S(2)}, u32[]{:S(2)}) %collective-permute-start.8) | collective-permute-done | bytes 3145760 | tf_op jit(solution)/shard_map/ppermute | solution.py:13
  159.0 2.7 %fusion.16 = (bf16[768,768]{1,0:T(8,128)(2,1)S(1)}, f32[768,768]{1,0:T(8,128)S(1)}) fusion(bf16[2048,768]{1,0:T(8,128)(2,1)S(1)} %fusion.2, bf16[2048,768]{1,0:T(8,128)(2,1)S(1)} %collective-permute-done.8), kind=kOutput, calls=%fused_computation.37 | convolution fusion | flops 2416508928 | bytes 9830400 | tf_op jit(solution)/shard_map/dot_general | solution.py:23
  161.7 2.2 collective-permute-start.9
  163.9 0.0 collective-permute-done.5
  163.9 2.7 %fusion.17 = (bf16[768,768]{1,0:T(8,128)(2,1)S(1)}, f32[768,768]{1,0:T(8,128)S(1)}) fusion(bf16[2048,768]{1,0:T(8,128)(2,1)S(1)} %fusion.2, bf16[2048,768]{1,0:T(8,128)(2,1)S(1)} %collective-permute-done.5), kind=kOutput, calls=%fused_computation.38 | convolution fusion | flops 2416508928 | bytes 9830400 | tf_op jit(solution)/shard_map/dot_general | solution.py:23
  166.7 1.3 collective-permute-start.6
  168.0 0.0 collective-permute-done.2
  168.0 4.6 %fusion.18 = (bf16[768,768]{1,0:T(8,128)(2,1)}, f32[768,768]{1,0:T(8,128)}) fusion(bf16[2048,768]{1,0:T(8,128)(2,1)S(1)} %fusion.2, bf16[2048,768]{1,0:T(8,128)(2,1)S(1)} %collective-permute-done.2), kind=kOutput, calls=%fused_computation.39 | convolution fusion | flops 2416508928 | bytes 9830400 | tf_op jit(solution)/shard_map/dot_general | solution.py:23
  172.6 4.1 %collective-permute-start.3 = (bf16[768,768]{1,0:T(8,128)(2,1)}, bf16[768,768]{1,0:T(8,128)(2,1)}, u32[]{:S(2)}, u32[]{:S(2)}) collective-permute-start(bf16[768,768]{1,0:T(8,128)(2,1)} %get-tuple-element.19), channel_id=1, source_target_pairs={{0,1},{2,3},{4,5},{6,7},{8,9},{10,11},{12,13},{14,15},{16,17},{18,... | collective-permute-start | bytes 3538952 | tf_op jit(solution)/shard_map/ppermute | solution.py:28
  176.7 0.0 collective-permute-done
  176.7 1.3 fusion.11
  178.0 3.4 %collective-permute-start.1 = (bf16[768,768]{1,0:T(8,128)(2,1)}, bf16[768,768]{1,0:T(8,128)(2,1)}, u32[]{:S(2)}, u32[]{:S(2)}) collective-permute-start(bf16[768,768]{1,0:T(8,128)(2,1)} %fusion.11), channel_id=1, source_target_pairs={{2,0},{6,4},{10,8},{14,12},{18,16},{22,20},{26,24},{30,28}} | collective-permute-start | bytes 3538952 | tf_op jit(solution)/shard_map/ppermute | solution.py:30
  181.5 0.0 collective-permute-done.9
  181.5 0.0 copy-done
  181.5 1.4 fusion.14
  182.9 1.7 collective-permute-start.10
  184.6 0.0 collective-permute-done.6
  184.6 0.0 copy-done.2
  184.6 1.4 fusion.13
  186.0 0.0 copy-done.7
  186.0 1.3 collective-permute-start.7
  187.3 0.6 dynamic_slice.8
  188.6 0.0 collective-permute-done.3
  188.6 2.2 fusion.12
  190.8 0.9 collective-permute-start.4
  191.7 4.1 %collective-permute-done.1 = bf16[768,768]{1,0:T(8,128)(2,1)} collective-permute-done((bf16[768,768]{1,0:T(8,128)(2,1)}, bf16[768,768]{1,0:T(8,128)(2,1)}, u32[]{:S(2)}, u32[]{:S(2)}) %collective-permute-start.1) | collective-permute-done | bytes 1179680 | tf_op jit(solution)/shard_map/ppermute | solution.py:30
  195.7 1.6 add_bitcast_fusion.3
  197.3 0.0 collective-permute-done.10
  197.4 1.8 add_bitcast_fusion
  199.2 10.4 %collective-permute-done.7 = bf16[768,768]{1,0:T(8,128)(2,1)} collective-permute-done((bf16[768,768]{1,0:T(8,128)(2,1)}, bf16[768,768]{1,0:T(8,128)(2,1)}, u32[]{:S(2)}, u32[]{:S(2)}) %collective-permute-start.7) | collective-permute-done | bytes 1179680 | tf_op jit(solution)/shard_map/ppermute | solution.py:30
  209.6 1.7 add_bitcast_fusion.1
  211.2 0.0 collective-permute-done.4
  211.3 1.7 add_bitcast_fusion.2
  212.9 0.0 copy-start.9
  212.9 1.2 fusion.15
  214.2 1.9 collective-permute-start.11
  216.1 0.6 dynamic-slice
  217.3 2.3 %collective-permute-done.11 = f32[768]{0:T(1024)S(1)} collective-permute-done((f32[768]{0:T(1024)S(1)}, f32[768]{0:T(1024)S(1)}, u32[]{:S(2)}, u32[]{:S(2)}) %collective-permute-start.11) | collective-permute-done | bytes 3104 | tf_op jit(solution)/shard_map/ppermute | solution.py:70
  219.7 5.7 %all-reduce = f32[768]{0:T(1024)S(1)} all-reduce(f32[768]{0:T(1024)S(1)} %add.61), channel_id=2, replica_groups=mesh['var'=8,'samp'=4] {'samp'}, use_global_device_ids=true, to_apply=%region_8.9.clone | all-reduce | flops 768 | bytes 6144
  225.4 0.6 dynamic-slice_multiply_fusion
  (21 shorter events, 0.1 us)
Async XLA Ops:
  20.4 138.6 %collective-permute-start.8 = (bf16[2048,768]{1,0:T(8,128)(2,1)S(1)}, bf16[2048,768]{1,0:T(8,128)(2,1)S(1)}, u32[]{:S(2)}, u32[]{:S(2)}) collective-permute-start(bf16[2048,768]{1,0:T(8,128)(2,1)S(1)} %fusion.2), channel_id=1, source_target_pairs={{0,12},{4,16},{8,20},{12,24},{16,28},{1,13},{5,17},{9,21},{13,25},... | collective-permute-start | bytes 9437192 | tf_op jit(solution)/shard_map/ppermute | solution.py:13
  24.8 139.1 %collective-permute-start.5 = (bf16[2048,768]{1,0:T(8,128)(2,1)S(1)}, bf16[2048,768]{1,0:T(8,128)(2,1)S(1)}, u32[]{:S(2)}, u32[]{:S(2)}) collective-permute-start(bf16[2048,768]{1,0:T(8,128)(2,1)S(1)} %fusion.2), channel_id=1, source_target_pairs={{8,0},{12,4},{16,8},{20,12},{24,16},{28,20},{9,1},{13,5},{17,9},{2... | collective-permute-start | bytes 9437192 | tf_op jit(solution)/shard_map/ppermute | solution.py:13
  27.4 140.6 %collective-permute-start.2 = (bf16[2048,768]{1,0:T(8,128)(2,1)S(1)}, bf16[2048,768]{1,0:T(8,128)(2,1)S(1)}, u32[]{:S(2)}, u32[]{:S(2)}) collective-permute-start(bf16[2048,768]{1,0:T(8,128)(2,1)S(1)} %fusion.2), channel_id=1, source_target_pairs={{4,0},{8,4},{12,8},{16,12},{20,16},{24,20},{28,24},{5,1},{9,5},{13... | collective-permute-start | bytes 9437192 | tf_op jit(solution)/shard_map/ppermute | solution.py:13
  32.5 144.2 %collective-permute-start = (bf16[768,768]{1,0:T(8,128)(2,1)S(1)}, bf16[768,768]{1,0:T(8,128)(2,1)S(1)}, u32[]{:S(2)}, u32[]{:S(2)}) collective-permute-start(bf16[768,768]{1,0:T(8,128)(2,1)S(1)} %get-tuple-element.21), channel_id=1, source_target_pairs={{1,0},{3,2},{5,4},{7,6},{9,8},{11,10},{13,12},{15,14},{17,16},{19,... | collective-permute-start | bytes 3538952 | tf_op jit(solution)/shard_map/ppermute | solution.py:28
  161.7 19.7 %copy-start = (f32[768,768]{1,0:T(8,128)}, f32[768,768]{1,0:T(8,128)S(1)}, u32[]{:S(2)}) copy-start(f32[768,768]{1,0:T(8,128)S(1)} %get-tuple-element.16) | copy-start | bytes 7077892
  161.7 19.7 %collective-permute-start.9 = (bf16[768,768]{1,0:T(8,128)(2,1)S(1)}, bf16[768,768]{1,0:T(8,128)(2,1)S(1)}, u32[]{:S(2)}, u32[]{:S(2)}) collective-permute-start(bf16[768,768]{1,0:T(8,128)(2,1)S(1)} %get-tuple-element.15), channel_id=1, source_target_pairs={{0,1},{2,3},{4,5},{6,7},{8,9},{10,11},{12,13},{14,15},{16,17},{18,... | collective-permute-start | bytes 3538952 | tf_op jit(solution)/shard_map/ppermute | solution.py:28
  166.7 17.9 %copy-start.2 = (f32[768,768]{1,0:T(8,128)}, f32[768,768]{1,0:T(8,128)S(1)}, u32[]{:S(2)}) copy-start(f32[768,768]{1,0:T(8,128)S(1)} %get-tuple-element.18) | copy-start | bytes 7077892
  166.7 17.9 %collective-permute-start.6 = (bf16[768,768]{1,0:T(8,128)(2,1)S(1)}, bf16[768,768]{1,0:T(8,128)(2,1)S(1)}, u32[]{:S(2)}, u32[]{:S(2)}) collective-permute-start(bf16[768,768]{1,0:T(8,128)(2,1)S(1)} %get-tuple-element.17), channel_id=1, source_target_pairs={{1,0},{3,2},{5,4},{7,6},{9,8},{11,10},{13,12},{15,14},{17,16},{19,... | collective-permute-start | bytes 3538952 | tf_op jit(solution)/shard_map/ppermute | solution.py:28
  172.6 16.0 %collective-permute-start.3 = (bf16[768,768]{1,0:T(8,128)(2,1)}, bf16[768,768]{1,0:T(8,128)(2,1)}, u32[]{:S(2)}, u32[]{:S(2)}) collective-permute-start(bf16[768,768]{1,0:T(8,128)(2,1)} %get-tuple-element.19), channel_id=1, source_target_pairs={{0,1},{2,3},{4,5},{6,7},{8,9},{10,11},{12,13},{14,15},{16,17},{18,... | collective-permute-start | bytes 3538952 | tf_op jit(solution)/shard_map/ppermute | solution.py:28
  178.0 17.7 %collective-permute-start.1 = (bf16[768,768]{1,0:T(8,128)(2,1)}, bf16[768,768]{1,0:T(8,128)(2,1)}, u32[]{:S(2)}, u32[]{:S(2)}) collective-permute-start(bf16[768,768]{1,0:T(8,128)(2,1)} %fusion.11), channel_id=1, source_target_pairs={{2,0},{6,4},{10,8},{14,12},{18,16},{22,20},{26,24},{30,28}} | collective-permute-start | bytes 3538952 | tf_op jit(solution)/shard_map/ppermute | solution.py:30
  181.5 1.4 copy-start.5
  182.9 14.5 %collective-permute-start.10 = (bf16[768,768]{1,0:T(8,128)(2,1)}, bf16[768,768]{1,0:T(8,128)(2,1)}, u32[]{:S(2)}, u32[]{:S(2)}) collective-permute-start(bf16[768,768]{1,0:T(8,128)(2,1)} %fusion.14), channel_id=1, source_target_pairs={{1,3},{5,7},{9,11},{13,15},{17,19},{21,23},{25,27},{29,31}} | collective-permute-start | bytes 3538952 | tf_op jit(solution)/shard_map/ppermute | solution.py:30
  184.6 1.4 copy-start.7
  184.6 2.7 %copy-start.10 = (s32[4]{0:T(128)S(1)}, s32[4]{0:T(128)}, u32[]{:S(2)}) copy-start(s32[4]{0:T(128)} %constant.37.clone) | copy-start | bytes 52
  186.0 23.6 %collective-permute-start.7 = (bf16[768,768]{1,0:T(8,128)(2,1)}, bf16[768,768]{1,0:T(8,128)(2,1)}, u32[]{:S(2)}, u32[]{:S(2)}) collective-permute-start(bf16[768,768]{1,0:T(8,128)(2,1)} %fusion.13), channel_id=1, source_target_pairs={{0,2},{4,6},{8,10},{12,14},{16,18},{20,22},{24,26},{28,30}} | collective-permute-start | bytes 3538952 | tf_op jit(solution)/shard_map/ppermute | solution.py:30
  190.8 6.6 %copy-start.1 = (f32[768,768]{1,0:T(8,128)S(1)}, f32[768,768]{1,0:T(8,128)}, u32[]{:S(2)}) copy-start(f32[768,768]{1,0:T(8,128)} %copy-done) | copy-start | bytes 7077892
  190.8 6.6 %copy-start.6 = (bf16[768,768]{1,0:T(8,128)(2,1)S(1)}, bf16[768,768]{1,0:T(8,128)(2,1)}, u32[]{:S(2)}) copy-start(bf16[768,768]{1,0:T(8,128)(2,1)} %copy-done.5) | copy-start | bytes 3538948
  190.8 20.4 %collective-permute-start.4 = (bf16[768,768]{1,0:T(8,128)(2,1)S(1)}, bf16[768,768]{1,0:T(8,128)(2,1)S(1)}, u32[]{:S(2)}, u32[]{:S(2)}) collective-permute-start(bf16[768,768]{1,0:T(8,128)(2,1)S(1)} %fusion.12), channel_id=1, source_target_pairs={{3,1},{7,5},{11,9},{15,13},{19,17},{23,21},{27,25},{31,29}} | collective-permute-start | bytes 3538952 | tf_op jit(solution)/shard_map/ppermute | solution.py:30
  197.3 12.3 %copy-start.3 = (f32[768,768]{1,0:T(8,128)S(1)}, f32[768,768]{1,0:T(8,128)}, u32[]{:S(2)}) copy-start(f32[768,768]{1,0:T(8,128)} %copy-done.2) | copy-start | bytes 7077892
  197.3 12.2 %copy-start.8 = (bf16[768,768]{1,0:T(8,128)(2,1)S(1)}, bf16[768,768]{1,0:T(8,128)(2,1)}, u32[]{:S(2)}) copy-start(bf16[768,768]{1,0:T(8,128)(2,1)} %copy-done.7) | copy-start | bytes 3538948
  199.2 12.1 %copy-start.4 = (f32[768,768]{1,0:T(8,128)S(1)}, f32[768,768]{1,0:T(8,128)}, u32[]{:S(2)}) copy-start(f32[768,768]{1,0:T(8,128)} %get-tuple-element.20) | copy-start | bytes 7077892
  212.9 3.2 %copy-start.9 = (u32[32]{0:T(128)S(1)}, u32[32]{0:T(128)}, u32[]{:S(2)}) copy-start(u32[32]{0:T(128)} %constant.40) | copy-start | bytes 388
  214.2 5.5 %collective-permute-start.11 = (f32[768]{0:T(1024)S(1)}, f32[768]{0:T(1024)S(1)}, u32[]{:S(2)}, u32[]{:S(2)}) collective-permute-start(f32[768]{0:T(1024)S(1)} %broadcast_multiply_fusion), channel_id=1, source_target_pairs={{1,5},{2,10},{5,9},{6,14},{9,13},{10,18},{13,17},{14,22},{15,3},{1... | collective-permute-start | bytes 9224 | tf_op jit(solution)/shard_map/ppermute | solution.py:70

commit v2 on v1

--- a/solution.py
+++ b/solution.py
@@ -5,6 +5,7 @@
 
 BAND = 3
 PARTNER_STEP = {1: 1, 2: 2, 3: -3}
+PROCESS_ORDER = (2, 3, 1)
 
 
 def from_behind(value, axis, steps):
@@ -31,6 +32,8 @@
 
 
 def local(dosages, observed):
+    coded = jnp.where(observed != 0, dosages, jnp.asarray(-1, dosages.dtype))
+    raw = {offset: from_behind(coded, "var", -PARTNER_STEP[offset]) for offset in range(1, BAND + 1)}
     values = dosages.astype(jnp.float32)
     present = observed.astype(jnp.float32)
     seen_count, first_sum, second_sum = lax.psum(
@@ -40,7 +43,9 @@
     seen_count = jnp.maximum(seen_count, 1.0)
     column_mean = first_sum / seen_count
     spread = second_sum / seen_count - column_mean * column_mean
-    standard = ((values - column_mean) * lax.rsqrt(spread + 1e-05) * present).astype(jnp.bfloat16)
+    inverse_sd = lax.rsqrt(spread + 1e-05)
+    standard = ((values - column_mean) * inverse_sd * present).astype(jnp.bfloat16)
+    scales = jnp.stack([column_mean, inverse_sd])
     n_samp = lax.axis_size("samp")
     n_var = lax.axis_size("var")
     samples = standard.shape[0] * n_samp
@@ -48,12 +53,17 @@
     position = lax.axis_index("var")
     me = lax.axis_index("samp")
 
-    owned = [reduce_to_owner(gram_of(standard, standard), 0, n_samp)]
-    for offset in range(1, BAND + 1):
-        step = PARTNER_STEP[offset]
-        partner = from_behind(standard, "var", -step)
-        owned.append(reduce_to_owner(gram_of(standard, partner), offset, n_samp))
-    gram = lax.dynamic_index_in_dim(jnp.stack(owned), me, 0, keepdims=False)
+    owned = {0: reduce_to_owner(gram_of(standard, standard), 0, n_samp)}
+    done = owned[0]
+    for offset in PROCESS_ORDER:
+        partner_scales = from_behind(scales, "var", -PARTNER_STEP[offset])
+        coded_partner, partner_scales, done = lax.optimization_barrier((raw[offset], partner_scales, done))
+        partner_values = coded_partner.astype(jnp.float32)
+        partner_present = (partner_values >= 0).astype(jnp.float32)
+        partner = ((partner_values - partner_scales[0]) * partner_scales[1] * partner_present).astype(jnp.bfloat16)
+        owned[offset] = reduce_to_owner(gram_of(standard, partner), offset, n_samp)
+        done = owned[offset]
+    gram = lax.dynamic_index_in_dim(jnp.stack([owned[d] for d in range(BAND + 1)]), me, 0, keepdims=False)
 
     steps = jnp.array([0] + [PARTNER_STEP[d] for d in range(1, BAND + 1)], jnp.int32)
     target = position + steps[me]

time: 228 us -> 269 us (1.18)
  blocking collectives: 15.9 us -> 53.8 us
  starting transfers between devices: 27.5 us -> 45.7 us
  waiting for transfers between devices: 142 us -> 125 us
    unnamed x1, blocking collectives: 5.74 us -> 42.8 us
    ppermute x3 -> x6, waiting for transfers between devices: 125 us -> 95.4 us  [from_behind(): lax.ppermute(value, axis, [(source, source + steps) for source in range(l...]
    ppermute x4, waiting for transfers between devices: 0.01 us -> 11.6 us  [reduce_to_owner(): lax.ppermute(part.astype(jnp.bfloat16), 'samp', pairs_core)]
    ppermute x4, starting transfers between devices: 8.88 us -> 18.3 us  [reduce_to_owner(): lax.ppermute(part.astype(jnp.bfloat16), 'samp', pairs_core)]
    ppermute x3 -> x6, starting transfers between devices: 9.41 us -> 18.5 us  [from_behind(): lax.ppermute(value, axis, [(source, source + steps) for source in range(l...]
    select_n x0 -> x1, other arithmetic: none -> 6.32 us  [local(): coded = jnp.where(observed != 0, dosages, jnp.asarray(-1, dosages.dtype))]
    add x0 -> x3, other arithmetic: none -> 5.17 us  [reduce_to_owner(): summed + lax.ppermute(summed.astype(jnp.bfloat16), 'samp', pairs_chip).as...]
    another operation x4 -> x2, other arithmetic: 6.69 us -> 1.75 us  [the longest x1 1.74 us: local(): jnp.stack([owned[d] for d in range(BAND + 1)])]
  transfers between devices with their start and end apart: 12 -> 15, of which waited for: 4 -> 10; matrix products, arithmetic and copies ran while one was open for 11% -> 9% of each run, Pallas kernels for 0% -> 0%
where the time goes in v2:
time: 269 us; the launch traced here: 266 us
  waiting for transfers between devices  125 us (46%)
  blocking collectives  53.8 us (20%)
  starting transfers between devices  45.7 us (17%)
  other arithmetic  23.2 us (9%)
  matrix products  13.5 us (5%)
  local copies, waits for them, and re-layouts  2.93 us (1%)
    ppermute x6, waiting for transfers between devices, from_behind(): lax.ppermute(value, axis, [(source, source + steps) for source in range(l...  95.4 us
    unnamed x1, blocking collectives  42.8 us
    ppermute x6, starting transfers between devices, from_behind(): lax.ppermute(value, axis, [(source, source + steps) for source in range(l...  18.5 us
    ppermute x4, starting transfers between devices, reduce_to_owner(): lax.ppermute(part.astype(jnp.bfloat16), 'samp', pairs_core)  18.3 us
    ppermute x4, waiting for transfers between devices, reduce_to_owner(): lax.ppermute(summed.astype(jnp.bfloat16), 'samp', pairs_chip)  16.1 us
    dot_general x4, matrix products, gram_of(): lax.dot_general(left, right, (((0,), (0,)), ((), ())), preferred_element_...  13.5 us
    ppermute x4, waiting for transfers between devices, reduce_to_owner(): lax.ppermute(part.astype(jnp.bfloat16), 'samp', pairs_core)  11.6 us
    psum x1, blocking collectives, local(): lax.psum((jnp.sum(present, 0), jnp.sum(present * values, 0), jnp.sum(pres...  10.9 us
  transfers between devices with their start and end apart: 15, of which 10 were waited for; matrix products, arithmetic and copies ran while one was open for 9% of the time, Pallas kernels for 0%

profile of v2, /device:TPU:14, one launch (start us, length us, event | category | flops | bytes accessed | tf_op | source)
XLA Modules:
  0.0 266.1 jit_solution(3116740928439516735)
XLA Ops:
  0.0 6.3 %compare_select_fusion = bf16[2048,768]{1,0:T(8,128)(2,1)} fusion(bf16[2048,768]{1,0:T(8,128)(2,1)} %param.3, s32[2048,768]{1,0:T(8,128)} %param.4), kind=kLoop, calls=%fused_computation.27 | loop fusion | flops 3145728 | bytes 12582912 | tf_op jit(solution)/shard_map/jit(_where)/select_n | solution.py:35
  6.3 2.5 collective-permute-start.6
  8.8 2.1 fusion.13
  10.9 10.9 %all-reduce.1 = (f32[768]{0:T(1024)S(1)}, f32[768]{0:T(1024)S(1)}, f32[768]{0:T(1024)S(1)}) all-reduce(f32[768]{0:T(1024)S(1)} %get-tuple-element.18, f32[768]{0:T(1024)S(1)} %get-tuple-element.19, f32[768]{0:T(1024)S(1)} %get-tuple-element.17), channel_id=1, replica_groups=mesh['var'=8,'samp'=4] {'samp'}, use_global_device_ids=true, to_apply=%region_5.6 | all-reduce | flops 2304 | bytes 18432 | tf_op jit(solution)/shard_map/psum | solution.py:39
  21.8 3.9 %fusion.11 = bf16[2048,768]{1,0:T(8,128)(2,1)S(1)} fusion(bf16[2048,768]{1,0:T(8,128)(2,1)S(1)} %copy-done.1, s32[2048,768]{1,0:T(8,128)} %param.4, f32[768]{0:T(1024)S(1)} %get-tuple-element.32, f32[768]{0:T(1024)S(1)} %get-tuple-element.31), kind=kLoop, calls=%fused_computation.24 | loop fusion | flops 9437184 | bytes 12589056 | tf_op jit(solution)/shard_map/convert_element_type | solution.py:47
  25.8 2.7 %fusion.43 = (bf16[768,768]{1,0:T(8,128)(2,1)S(1)}, f32[768,768]{1,0:T(8,128)S(1)}) fusion(bf16[2048,768]{1,0:T(8,128)(2,1)S(1)} %fusion.11), kind=kOutput, calls=%fused_computation.75 | convolution fusion | flops 2416508928 | bytes 6684672 | tf_op jit(solution)/shard_map/dot_general | solution.py:24
  28.5 1.3 collective-permute-start
  29.8 3.4 %collective-permute-done = bf16[768,768]{1,0:T(8,128)(2,1)S(1)} collective-permute-done((bf16[768,768]{1,0:T(8,128)(2,1)S(1)}, bf16[768,768]{1,0:T(8,128)(2,1)S(1)}, u32[]{:S(2)}, u32[]{:S(2)}) %collective-permute-start) | collective-permute-done | bytes 1179680 | tf_op jit(solution)/shard_map/ppermute | solution.py:29
  33.2 0.3 fusion.35
  33.5 3.0 %collective-permute-start.1 = (bf16[768,768]{1,0:T(8,128)(2,1)S(1)}, bf16[768,768]{1,0:T(8,128)(2,1)S(1)}, u32[]{:S(2)}, u32[]{:S(2)}) collective-permute-start(bf16[768,768]{1,0:T(8,128)(2,1)S(1)} %fusion.35), channel_id=1, source_target_pairs={{2,0},{6,4},{10,8},{14,12},{18,16},{22,20},{26,24},{30,28}} | collective-permute-start | bytes 3538952 | tf_op jit(solution)/shard_map/ppermute | solution.py:31
  36.5 5.3 %collective-permute-start.4 = (bf16[2048,768]{1,0:T(8,128)(2,1)}, bf16[2048,768]{1,0:T(8,128)(2,1)S(1)}, u32[]{:S(2)}, u32[]{:S(2)}) collective-permute-start(bf16[2048,768]{1,0:T(8,128)(2,1)} %compare_select_fusion), channel_id=1, source_target_pairs={{0,12},{4,16},{8,20},{12,24},{16,28},{1,13},{5,17},{9,21},{13,25},... | collective-permute-start | bytes 9437192 | tf_op jit(solution)/shard_map/ppermute | solution.py:14
  41.8 1.9 collective-permute-start.7
  43.8 6.3 %collective-permute-done.1 = bf16[768,768]{1,0:T(8,128)(2,1)S(1)} collective-permute-done((bf16[768,768]{1,0:T(8,128)(2,1)S(1)}, bf16[768,768]{1,0:T(8,128)(2,1)S(1)}, u32[]{:S(2)}, u32[]{:S(2)}) %collective-permute-start.1) | collective-permute-done | bytes 1179680 | tf_op jit(solution)/shard_map/ppermute | solution.py:31
  50.1 1.7 convert_add_fusion.5
  51.8 26.7 %collective-permute-done.7 = f32[2,768]{1,0:T(2,128)S(1)} collective-permute-done((f32[2,768]{1,0:T(2,128)S(1)}, f32[2,768]{1,0:T(2,128)S(1)}, u32[]{:S(2)}, u32[]{:S(2)}) %collective-permute-start.7) | collective-permute-done | bytes 6176 | tf_op jit(solution)/shard_map/ppermute | solution.py:14
  78.6 4.8 %fusion.44 = (bf16[768,768]{1,0:T(8,128)(2,1)S(1)}, f32[768,768]{1,0:T(8,128)S(1)}) fusion(bf16[2048,768]{1,0:T(8,128)(2,1)S(1)} %fusion.11, bf16[2048,768]{1,0:T(8,128)(2,1)} %collective-permute-done.6, f32[768]{0:T(1024)S(1)} %get-tuple-element.27, f32[768]{0:T(1024)S(1)} %get-tuple-element.26), kind=kOutput, calls=%fused_computation.76 | convolution fusion | flops 2425946112 | bytes 9836544 | tf_op jit(solution)/shard_map/dot_general | solution.py:24
  83.4 1.3 collective-permute-start.8
  84.7 3.4 %collective-permute-done.8 = bf16[768,768]{1,0:T(8,128)(2,1)S(1)} collective-permute-done((bf16[768,768]{1,0:T(8,128)(2,1)S(1)}, bf16[768,768]{1,0:T(8,128)(2,1)S(1)}, u32[]{:S(2)}, u32[]{:S(2)}) %collective-permute-start.8) | collective-permute-done | bytes 1179680 | tf_op jit(solution)/shard_map/ppermute | solution.py:29
  88.2 0.3 fusion.36
  88.5 1.5 collective-permute-start.9
  89.9 2.4 collective-permute-start.5
  92.4 4.4 %collective-permute-start.2 = (bf16[2048,768]{1,0:T(8,128)(2,1)}, bf16[2048,768]{1,0:T(8,128)(2,1)S(1)}, u32[]{:S(2)}, u32[]{:S(2)}) collective-permute-start(bf16[2048,768]{1,0:T(8,128)(2,1)} %compare_select_fusion), channel_id=1, source_target_pairs={{4,0},{8,4},{12,8},{16,12},{20,16},{24,20},{28,24},{5,1},{9,5},{13... | collective-permute-start | bytes 9437192 | tf_op jit(solution)/shard_map/ppermute | solution.py:14
  96.8 9.8 %collective-permute-done.9 = bf16[768,768]{1,0:T(8,128)(2,1)S(1)} collective-permute-done((bf16[768,768]{1,0:T(8,128)(2,1)S(1)}, bf16[768,768]{1,0:T(8,128)(2,1)S(1)}, u32[]{:S(2)}, u32[]{:S(2)}) %collective-permute-start.9) | collective-permute-done | bytes 1179680 | tf_op jit(solution)/shard_map/ppermute | solution.py:31
  106.6 1.8 convert_add_fusion.3
  108.3 65.8 %collective-permute-done.5 = f32[2,768]{1,0:T(2,128)S(1)} collective-permute-done((f32[2,768]{1,0:T(2,128)S(1)}, f32[2,768]{1,0:T(2,128)S(1)}, u32[]{:S(2)}, u32[]{:S(2)}) %collective-permute-start.5) | collective-permute-done | bytes 6176 | tf_op jit(solution)/shard_map/ppermute | solution.py:14
  174.2 3.0 %fusion.45 = (bf16[768,768]{1,0:T(8,128)(2,1)S(1)}, f32[768,768]{1,0:T(8,128)S(1)}) fusion(bf16[2048,768]{1,0:T(8,128)(2,1)S(1)} %fusion.11, bf16[2048,768]{1,0:T(8,128)(2,1)S(1)} %collective-permute-done.4, f32[768]{0:T(1024)S(1)} %get-tuple-element.25, f32[768]{0:T(1024)S(1)} %get-tuple-element.24), kind=kOutput, calls=%fused_computation.77 | convolution fusion | flops 2425946112 | bytes 9836544 | tf_op jit(solution)/shard_map/dot_general | solution.py:24
  177.2 2.0 collective-permute-start.10
  179.1 2.4 collective-permute-done.10
  181.5 0.3 fusion.37
  181.8 0.7 collective-permute-start.11
  182.5 1.9 collective-permute-start.3
  184.5 1.7 convert_add_fusion.1
  186.2 2.8 %collective-permute-done.3 = f32[2,768]{1,0:T(2,128)S(1)} collective-permute-done((f32[2,768]{1,0:T(2,128)S(1)}, f32[2,768]{1,0:T(2,128)S(1)}, u32[]{:S(2)}, u32[]{:S(2)}) %collective-permute-start.3) | collective-permute-done | bytes 6176 | tf_op jit(solution)/shard_map/ppermute | solution.py:14
  189.0 2.9 %fusion.46 = (bf16[768,768]{1,0:T(8,128)(2,1)S(1)}, f32[768,768]{1,0:T(8,128)S(1)}) fusion(bf16[2048,768]{1,0:T(8,128)(2,1)S(1)} %fusion.11, bf16[2048,768]{1,0:T(8,128)(2,1)S(1)} %collective-permute-done.2, f32[768]{0:T(1024)S(1)} %get-tuple-element.23, f32[768]{0:T(1024)S(1)} %get-tuple-element.22), kind=kOutput, calls=%fused_computation.78 | convolution fusion | flops 2425946112 | bytes 9836544 | tf_op jit(solution)/shard_map/dot_general | solution.py:24
  192.0 13.8 %collective-permute-start.12 = (bf16[768,768]{1,0:T(8,128)(2,1)S(1)}, bf16[768,768]{1,0:T(8,128)(2,1)S(1)}, u32[]{:S(2)}, u32[]{:S(2)}) collective-permute-start(bf16[768,768]{1,0:T(8,128)(2,1)S(1)} %get-tuple-element.39), channel_id=1, source_target_pairs={{0,1},{2,3},{4,5},{6,7},{8,9},{10,11},{12,13},{14,15},{16,17},{18,... | collective-permute-start | bytes 3538952 | tf_op jit(solution)/shard_map/ppermute | solution.py:29
  205.8 2.4 collective-permute-done.12
  208.2 1.3 fusion.38
  209.4 1.8 collective-permute-start.13
  211.2 0.6 dynamic_slice.8
  212.5 1.7 add_bitcast_fusion
  214.5 0.7 copy-done.3
  215.2 0.7 copy-done.4
  215.9 1.2 fusion.42
  217.1 1.9 collective-permute-start.14
  219.1 0.6 dynamic-slice
  220.3 2.3 collective-permute-done.14
  222.6 42.8 %all-reduce = f32[768]{0:T(1024)S(1)} all-reduce(f32[768]{0:T(1024)S(1)} %add.61), channel_id=2, replica_groups=mesh['var'=8,'samp'=4] {'samp'}, use_global_device_ids=true, to_apply=%region_8.9.clone | all-reduce | flops 768 | bytes 6144
  265.5 0.6 dynamic-slice_multiply_fusion
  (26 shorter events, 0.4 us)
Async XLA Ops:
  0.0 8.8 %copy-start.1 = (bf16[2048,768]{1,0:T(8,128)(2,1)S(1)}, bf16[2048,768]{1,0:T(8,128)(2,1)}, u32[]{:S(2)}) copy-start(bf16[2048,768]{1,0:T(8,128)(2,1)} %param.3) | copy-start | bytes 9437188
  0.0 8.8 %copy-start = (s32[2048,768]{1,0:T(8,128)S(1)}, s32[2048,768]{1,0:T(8,128)}, u32[]{:S(2)}) copy-start(s32[2048,768]{1,0:T(8,128)} %param.4) | copy-start | bytes 18874372
  6.3 72.2 %collective-permute-start.6 = (bf16[2048,768]{1,0:T(8,128)(2,1)}, bf16[2048,768]{1,0:T(8,128)(2,1)}, u32[]{:S(2)}, u32[]{:S(2)}) collective-permute-start(bf16[2048,768]{1,0:T(8,128)(2,1)} %compare_select_fusion), channel_id=1, source_target_pairs={{8,0},{12,4},{16,8},{20,12},{24,16},{28,20},{9,1},{13,5},{17,9},{2... | collective-permute-start | bytes 9437192 | tf_op jit(solution)/shard_map/ppermute | solution.py:14
  28.5 4.7 %collective-permute-start = (bf16[768,768]{1,0:T(8,128)(2,1)S(1)}, bf16[768,768]{1,0:T(8,128)(2,1)S(1)}, u32[]{:S(2)}, u32[]{:S(2)}) collective-permute-start(bf16[768,768]{1,0:T(8,128)(2,1)S(1)} %get-tuple-element.33), channel_id=1, source_target_pairs={{1,0},{3,2},{5,4},{7,6},{9,8},{11,10},{13,12},{15,14},{17,16},{19,... | collective-permute-start | bytes 3538952 | tf_op jit(solution)/shard_map/ppermute | solution.py:29
  33.5 16.6 %collective-permute-start.1 = (bf16[768,768]{1,0:T(8,128)(2,1)S(1)}, bf16[768,768]{1,0:T(8,128)(2,1)S(1)}, u32[]{:S(2)}, u32[]{:S(2)}) collective-permute-start(bf16[768,768]{1,0:T(8,128)(2,1)S(1)} %fusion.35), channel_id=1, source_target_pairs={{2,0},{6,4},{10,8},{14,12},{18,16},{22,20},{26,24},{30,28}} | collective-permute-start | bytes 3538952 | tf_op jit(solution)/shard_map/ppermute | solution.py:31
  36.5 137.7 %collective-permute-start.4 = (bf16[2048,768]{1,0:T(8,128)(2,1)}, bf16[2048,768]{1,0:T(8,128)(2,1)S(1)}, u32[]{:S(2)}, u32[]{:S(2)}) collective-permute-start(bf16[2048,768]{1,0:T(8,128)(2,1)} %compare_select_fusion), channel_id=1, source_target_pairs={{0,12},{4,16},{8,20},{12,24},{16,28},{1,13},{5,17},{9,21},{13,25},... | collective-permute-start | bytes 9437192 | tf_op jit(solution)/shard_map/ppermute | solution.py:14
  41.8 36.7 %collective-permute-start.7 = (f32[2,768]{1,0:T(2,128)S(1)}, f32[2,768]{1,0:T(2,128)S(1)}, u32[]{:S(2)}, u32[]{:S(2)}) collective-permute-start(f32[2,768]{1,0:T(2,128)S(1)} %pad_maximum_fusion), channel_id=1, source_target_pairs={{8,0},{12,4},{16,8},{20,12},{24,16},{28,20},{9,1},{13,5},{17,9},{2... | collective-permute-start | bytes 18440 | tf_op jit(solution)/shard_map/ppermute | solution.py:14
  83.4 4.7 %collective-permute-start.8 = (bf16[768,768]{1,0:T(8,128)(2,1)S(1)}, bf16[768,768]{1,0:T(8,128)(2,1)S(1)}, u32[]{:S(2)}, u32[]{:S(2)}) collective-permute-start(bf16[768,768]{1,0:T(8,128)(2,1)S(1)} %get-tuple-element.35), channel_id=1, source_target_pairs={{1,0},{3,2},{5,4},{7,6},{9,8},{11,10},{13,12},{15,14},{17,16},{19,... | collective-permute-start | bytes 3538952 | tf_op jit(solution)/shard_map/ppermute | solution.py:29
  88.5 18.1 %collective-permute-start.9 = (bf16[768,768]{1,0:T(8,128)(2,1)S(1)}, bf16[768,768]{1,0:T(8,128)(2,1)S(1)}, u32[]{:S(2)}, u32[]{:S(2)}) collective-permute-start(bf16[768,768]{1,0:T(8,128)(2,1)S(1)} %fusion.36), channel_id=1, source_target_pairs={{0,2},{4,6},{8,10},{12,14},{16,18},{20,22},{24,26},{28,30}} | collective-permute-start | bytes 3538952 | tf_op jit(solution)/shard_map/ppermute | solution.py:31
  89.9 84.2 %collective-permute-start.5 = (f32[2,768]{1,0:T(2,128)S(1)}, f32[2,768]{1,0:T(2,128)S(1)}, u32[]{:S(2)}, u32[]{:S(2)}) collective-permute-start(f32[2,768]{1,0:T(2,128)S(1)} %pad_maximum_fusion), channel_id=1, source_target_pairs={{0,12},{4,16},{8,20},{12,24},{16,28},{1,13},{5,17},{9,21},{13,25},... | collective-permute-start | bytes 18440 | tf_op jit(solution)/shard_map/ppermute | solution.py:14
  92.4 96.6 %collective-permute-start.2 = (bf16[2048,768]{1,0:T(8,128)(2,1)}, bf16[2048,768]{1,0:T(8,128)(2,1)S(1)}, u32[]{:S(2)}, u32[]{:S(2)}) collective-permute-start(bf16[2048,768]{1,0:T(8,128)(2,1)} %compare_select_fusion), channel_id=1, source_target_pairs={{4,0},{8,4},{12,8},{16,12},{20,16},{24,20},{28,24},{5,1},{9,5},{13... | collective-permute-start | bytes 9437192 | tf_op jit(solution)/shard_map/ppermute | solution.py:14
  177.2 4.3 %collective-permute-start.10 = (bf16[768,768]{1,0:T(8,128)(2,1)S(1)}, bf16[768,768]{1,0:T(8,128)(2,1)S(1)}, u32[]{:S(2)}, u32[]{:S(2)}) collective-permute-start(bf16[768,768]{1,0:T(8,128)(2,1)S(1)} %get-tuple-element.37), channel_id=1, source_target_pairs={{0,1},{2,3},{4,5},{6,7},{8,9},{10,11},{12,13},{14,15},{16,17},{18,... | collective-permute-start | bytes 3538952 | tf_op jit(solution)/shard_map/ppermute | solution.py:29
  181.8 2.7 %collective-permute-start.11 = (bf16[768,768]{1,0:T(8,128)(2,1)S(1)}, bf16[768,768]{1,0:T(8,128)(2,1)S(1)}, u32[]{:S(2)}, u32[]{:S(2)}) collective-permute-start(bf16[768,768]{1,0:T(8,128)(2,1)S(1)} %fusion.37), channel_id=1, source_target_pairs={{1,3},{5,7},{9,11},{13,15},{17,19},{21,23},{25,27},{29,31}} | collective-permute-start | bytes 3538952 | tf_op jit(solution)/shard_map/ppermute | solution.py:31
  182.5 6.4 %collective-permute-start.3 = (f32[2,768]{1,0:T(2,128)S(1)}, f32[2,768]{1,0:T(2,128)S(1)}, u32[]{:S(2)}, u32[]{:S(2)}) collective-permute-start(f32[2,768]{1,0:T(2,128)S(1)} %pad_maximum_fusion), channel_id=1, source_target_pairs={{4,0},{8,4},{12,8},{16,12},{20,16},{24,20},{28,24},{5,1},{9,5},{13... | collective-permute-start | bytes 18440 | tf_op jit(solution)/shard_map/ppermute | solution.py:14
  192.0 16.2 %collective-permute-start.12 = (bf16[768,768]{1,0:T(8,128)(2,1)S(1)}, bf16[768,768]{1,0:T(8,128)(2,1)S(1)}, u32[]{:S(2)}, u32[]{:S(2)}) collective-permute-start(bf16[768,768]{1,0:T(8,128)(2,1)S(1)} %get-tuple-element.39), channel_id=1, source_target_pairs={{0,1},{2,3},{4,5},{6,7},{8,9},{10,11},{12,13},{14,15},{16,17},{18,... | collective-permute-start | bytes 3538952 | tf_op jit(solution)/shard_map/ppermute | solution.py:29
  208.2 3.0 %copy-start.6 = (s32[4]{0:T(128)S(1)}, s32[4]{0:T(128)}, u32[]{:S(2)}) copy-start(s32[4]{0:T(128)} %constant.44.clone) | copy-start | bytes 52
  209.4 3.1 %collective-permute-start.13 = (bf16[768,768]{1,0:T(8,128)(2,1)}, bf16[768,768]{1,0:T(8,128)(2,1)}, u32[]{:S(2)}, u32[]{:S(2)}) collective-permute-start(bf16[768,768]{1,0:T(8,128)(2,1)} %fusion.38), channel_id=1, source_target_pairs={{3,1},{7,5},{11,9},{15,13},{19,17},{23,21},{27,25},{31,29}} | collective-permute-start | bytes 3538952 | tf_op jit(solution)/shard_map/ppermute | solution.py:31
  212.4 2.0 copy-start.2
  212.4 2.7 %copy-start.3 = (f32[768,768]{1,0:T(8,128)S(1)}, f32[768,768]{1,0:T(8,128)}, u32[]{:S(2)}) copy-start(f32[768,768]{1,0:T(8,128)} %convert_add_fusion.3) | copy-start | bytes 7077892
  212.5 3.4 %copy-start.4 = (f32[768,768]{1,0:T(8,128)S(1)}, f32[768,768]{1,0:T(8,128)}, u32[]{:S(2)}) copy-start(f32[768,768]{1,0:T(8,128)} %convert_add_fusion.1) | copy-start | bytes 7077892
  215.9 3.2 %copy-start.5 = (u32[32]{0:T(128)S(1)}, u32[32]{0:T(128)}, u32[]{:S(2)}) copy-start(u32[32]{0:T(128)} %constant.47) | copy-start | bytes 388
  217.1 5.5 %collective-permute-start.14 = (f32[768]{0:T(1024)S(1)}, f32[768]{0:T(1024)S(1)}, u32[]{:S(2)}, u32[]{:S(2)}) collective-permute-start(f32[768]{0:T(1024)S(1)} %broadcast_multiply_fusion), channel_id=1, source_target_pairs={{1,5},{2,10},{5,9},{6,14},{9,13},{10,18},{13,17},{14,22},{15,3},{1... | collective-permute-start | bytes 9224 | tf_op jit(solution)/shard_map/ppermute | solution.py:80

commit v3 on v2

--- a/solution.py
+++ b/solution.py
@@ -36,33 +36,33 @@
     raw = {offset: from_behind(coded, "var", -PARTNER_STEP[offset]) for offset in range(1, BAND + 1)}
     values = dosages.astype(jnp.float32)
     present = observed.astype(jnp.float32)
-    seen_count, first_sum, second_sum = lax.psum(
-        (jnp.sum(present, 0), jnp.sum(present * values, 0), jnp.sum(present * values * values, 0)),
-        "samp",
-    )
-    seen_count = jnp.maximum(seen_count, 1.0)
-    column_mean = first_sum / seen_count
-    spread = second_sum / seen_count - column_mean * column_mean
-    inverse_sd = lax.rsqrt(spread + 1e-05)
-    standard = ((values - column_mean) * inverse_sd * present).astype(jnp.bfloat16)
-    scales = jnp.stack([column_mean, inverse_sd])
     n_samp = lax.axis_size("samp")
     n_var = lax.axis_size("var")
+    position = lax.axis_index("var")
+    me = lax.axis_index("samp")
+    partial = jnp.stack([jnp.sum(present, 0), jnp.sum(present * values, 0), jnp.sum(present * values * values, 0)])
+    slots = jnp.zeros((n_var,) + partial.shape, jnp.float32)
+    stats = lax.psum(lax.dynamic_update_index_in_dim(slots, partial, position, 0), ("var", "samp"))
+    seen_count = jnp.maximum(stats[:, 0], 1.0)
+    column_mean = stats[:, 1] / seen_count
+    spread = stats[:, 2] / seen_count - column_mean * column_mean
+    inverse_sd = lax.rsqrt(spread + 1e-05)
+    own_mean = lax.dynamic_index_in_dim(column_mean, position, 0, keepdims=False)
+    own_sd = lax.dynamic_index_in_dim(inverse_sd, position, 0, keepdims=False)
+    standard = ((values - own_mean) * own_sd * present).astype(jnp.bfloat16)
     samples = standard.shape[0] * n_samp
     block_width = standard.shape[1]
-    position = lax.axis_index("var")
-    me = lax.axis_index("samp")
 
     owned = {0: reduce_to_owner(gram_of(standard, standard), 0, n_samp)}
-    done = owned[0]
-    for offset in PROCESS_ORDER:
-        partner_scales = from_behind(scales, "var", -PARTNER_STEP[offset])
-        coded_partner, partner_scales, done = lax.optimization_barrier((raw[offset], partner_scales, done))
+    arrived, owned[0] = lax.optimization_barrier(([raw[d] for d in PROCESS_ORDER], owned[0]))
+    for offset, coded_partner in zip(PROCESS_ORDER, arrived):
+        source = jnp.clip(position + PARTNER_STEP[offset], 0, n_var - 1)
+        partner_mean = lax.dynamic_index_in_dim(column_mean, source, 0, keepdims=False)
+        partner_sd = lax.dynamic_index_in_dim(inverse_sd, source, 0, keepdims=False)
         partner_values = coded_partner.astype(jnp.float32)
         partner_present = (partner_values >= 0).astype(jnp.float32)
-        partner = ((partner_values - partner_scales[0]) * partner_scales[1] * partner_present).astype(jnp.bfloat16)
+        partner = ((partner_values - partner_mean) * partner_sd * partner_present).astype(jnp.bfloat16)
         owned[offset] = reduce_to_owner(gram_of(standard, partner), offset, n_samp)
-        done = owned[offset]
     gram = lax.dynamic_index_in_dim(jnp.stack([owned[d] for d in range(BAND + 1)]), me, 0, keepdims=False)
 
     steps = jnp.array([0] + [PARTNER_STEP[d] for d in range(1, BAND + 1)], jnp.int32)

time: 269 us -> 373 us (1.39)
  waiting for transfers between devices: 125 us -> 269 us
  blocking collectives: 53.8 us -> 9.09 us
  starting transfers between devices: 45.7 us -> 28.8 us
  between operations: 1.6 us -> 15.1 us
  other arithmetic: 23.2 us -> 29 us
    psum x0 -> x1, waiting for transfers between devices: none -> 232 us  [local(): lax.psum(lax.dynamic_update_index_in_dim(slots, partial, position, 0), ('...]
    ppermute x6 -> x3, waiting for transfers between devices: 95.4 us -> 0.01 us  [from_behind(): lax.ppermute(value, axis, [(source, source + steps) for source in range(l...]
    unnamed x1, blocking collectives: 42.8 us -> 9.09 us
    ppermute x4, waiting for transfers between devices: 16.1 us -> 32.1 us  [reduce_to_owner(): lax.ppermute(summed.astype(jnp.bfloat16), 'samp', pairs_chip)]
    ppermute x4, starting transfers between devices: 18.3 us -> 7.3 us  [reduce_to_owner(): lax.ppermute(part.astype(jnp.bfloat16), 'samp', pairs_core)]
    psum x1 -> x0, blocking collectives: 10.9 us -> none  [local(): lax.psum((jnp.sum(present, 0), jnp.sum(present * values, 0), jnp.sum(pres...]
    ppermute x4, waiting for transfers between devices: 11.6 us -> 3.45 us  [reduce_to_owner(): lax.ppermute(part.astype(jnp.bfloat16), 'samp', pairs_core)]
    ppermute x6 -> x3, starting transfers between devices: 18.5 us -> 10.9 us  [from_behind(): lax.ppermute(value, axis, [(source, source + steps) for source in range(l...]
  transfers between devices with their start and end apart: 15 -> 13, of which waited for: 10 -> 5; matrix products, arithmetic and copies ran while one was open for 9% -> 9% of each run, Pallas kernels for 0% -> 0%
where the time goes in v3:
time: 373 us; the launch traced here: 371 us
  waiting for transfers between devices  269 us (72%)
  other arithmetic  29 us (8%)
  starting transfers between devices  28.8 us (8%)
  matrix products  17.2 us (5%)
  between operations  15.1 us (4%)
  blocking collectives  9.09 us (2%)
    psum x1, waiting for transfers between devices, local(): lax.psum(lax.dynamic_update_index_in_dim(slots, partial, position, 0), ('...  232 us
    ppermute x4, waiting for transfers between devices, reduce_to_owner(): lax.ppermute(summed.astype(jnp.bfloat16), 'samp', pairs_chip)  32.1 us
    dot_general x4, matrix products, gram_of(): lax.dot_general(left, right, (((0,), (0,)), ((), ())), preferred_element_...  17.2 us
    ppermute x3, starting transfers between devices, from_behind(): lax.ppermute(value, axis, [(source, source + steps) for source in range(l...  10.9 us
    unnamed x1, blocking collectives  9.09 us
    ppermute x4, starting transfers between devices, reduce_to_owner(): lax.ppermute(summed.astype(jnp.bfloat16), 'samp', pairs_chip)  8.17 us
  transfers between devices with their start and end apart: 13, of which 5 were waited for; matrix products, arithmetic and copies ran while one was open for 9% of the time, Pallas kernels for 0%

profile of v3, /device:TPU:14, one launch (start us, length us, event | category | flops | bytes accessed | tf_op | source)
XLA Modules:
  0.0 370.6 jit_solution(16671350342384689641)
XLA Ops:
  6.5 5.4 %fusion.13 = (f32[768]{0:T(1024)S(1)}, f32[768]{0:T(1024)S(1)}, f32[768]{0:T(1024)S(1)}) fusion(bf16[2048,768]{1,0:T(8,128)(2,1)} %param.3, s32[2048,768]{1,0:T(8,128)} %param.4), kind=kLoop, calls=%fused_computation.28 | loop fusion | flops 11007744 | bytes 9446400 | tf_op jit(solution)/shard_map/reduce_sum | solution.py:43
  12.1 0.6 copy-done.10
  12.7 0.0 all-reduce.3.cloned.1.call-update
  12.7 5.3 %compare_select_fusion = bf16[2048,768]{1,0:T(8,128)(2,1)} fusion(bf16[2048,768]{1,0:T(8,128)(2,1)S(1)} %copy-done, s32[2048,768]{1,0:T(8,128)} %param.4), kind=kLoop, calls=%fused_computation.27 | loop fusion | flops 3145728 | bytes 12582912 | tf_op jit(solution)/shard_map/jit(_where)/select_n | solution.py:35
  18.0 2.3 collective-permute-start
  20.3 6.1 %collective-permute-start.1 = (bf16[2048,768]{1,0:T(8,128)(2,1)}, bf16[2048,768]{1,0:T(8,128)(2,1)}, u32[]{:S(2)}, u32[]{:S(2)}) collective-permute-start(bf16[2048,768]{1,0:T(8,128)(2,1)} %compare_select_fusion), channel_id=1, source_target_pairs={{0,12},{4,16},{8,20},{12,24},{16,28},{1,13},{5,17},{9,21},{13,25},... | collective-permute-start | bytes 9437192 | tf_op jit(solution)/shard_map/ppermute | solution.py:14
  26.4 2.4 collective-permute-start.2
  28.9 232.0 %all-reduce.3.cloned.1.call-done = f32[8,3,768]{2,1,0:T(4,128)} async-done(((f32[8,3,768]{2,1,0:T(4,128)}), f32[8,3,768]{2,1,0:T(4,128)}) %all-reduce.3.cloned.1.call-update) | async-done | bytes 73744 | tf_op jit(solution)/shard_map/psum | solution.py:45
  260.9 1.1 add_rsqrt_fusion
  262.1 0.1 fusion.43
  262.1 3.9 %fusion.12 = bf16[2048,768]{1,0:T(8,128)(2,1)S(1)} fusion(bf16[2048,768]{1,0:T(8,128)(2,1)S(1)} %copy-done, s32[2048,768]{1,0:T(8,128)} %param.4, f32[768]{0:T(1024)S(1)} %get-tuple-element.37, f32[768]{0:T(1024)S(1)} %get-tuple-element.21), kind=kLoop, calls=%fused_computation.25 | loop fusion | flops 9437184 | bytes 12589056 | tf_op jit(solution)/shard_map/convert_element_type | solution.py:52
  266.1 2.7 fusion.53
  268.8 1.3 collective-permute-start.3
  270.1 3.4 collective-permute-done.3
  273.5 0.3 fusion.35
  273.8 3.4 collective-permute-start.4
  277.3 13.6 %collective-permute-done.4 = bf16[768,768]{1,0:T(8,128)(2,1)S(1)} collective-permute-done((bf16[768,768]{1,0:T(8,128)(2,1)S(1)}, bf16[768,768]{1,0:T(8,128)(2,1)S(1)}, u32[]{:S(2)}, u32[]{:S(2)}) %collective-permute-start.4) | collective-permute-done | bytes 1179680 | tf_op jit(solution)/shard_map/ppermute | solution.py:31
  290.9 1.7 convert_add_fusion.3
  292.6 0.0 collective-permute-done
  292.6 0.0 collective-permute-done.1
  292.6 0.0 collective-permute-done.2
  292.6 4.8 %fusion.56 = (bf16[768,768]{1,0:T(8,128)(2,1)S(1)}, f32[768,768]{1,0:T(8,128)S(1)}) fusion(bf16[2048,768]{1,0:T(8,128)(2,1)S(1)} %fusion.12, bf16[2048,768]{1,0:T(8,128)(2,1)} %collective-permute-done.2, f32[768]{0:T(1024)S(1)} %get-tuple-element.39, f32[768]{0:T(1024)S(1)} %get-tuple-element.18), kind=kOutput, calls=%fused_computation.92 | convolution fusion | flops 2425946112 | bytes 9836544 | tf_op jit(solution)/shard_map/dot_general | solution.py:24
  297.4 1.5 collective-permute-start.5
  299.0 4.8 %fusion.55 = (bf16[768,768]{1,0:T(8,128)(2,1)S(1)}, f32[768,768]{1,0:T(8,128)S(1)}) fusion(bf16[2048,768]{1,0:T(8,128)(2,1)S(1)} %fusion.12, bf16[2048,768]{1,0:T(8,128)(2,1)} %collective-permute-done, f32[768]{0:T(1024)S(1)} %get-tuple-element.38, f32[768]{0:T(1024)S(1)} %get-tuple-element.20), kind=kOutput, calls=%fused_computation.91 | convolution fusion | flops 2425946112 | bytes 9836544 | tf_op jit(solution)/shard_map/dot_general | solution.py:24
  303.8 1.3 collective-permute-start.7
  305.1 4.8 %fusion.54 = (bf16[768,768]{1,0:T(8,128)(2,1)S(1)}, f32[768,768]{1,0:T(8,128)S(1)}) fusion(bf16[2048,768]{1,0:T(8,128)(2,1)S(1)} %fusion.12, bf16[2048,768]{1,0:T(8,128)(2,1)} %collective-permute-done.1, f32[768]{0:T(1024)S(1)} %get-tuple-element.36, f32[768]{0:T(1024)S(1)} %get-tuple-element.19), kind=kOutput, calls=%fused_computation.90 | convolution fusion | flops 2425946112 | bytes 9836544 | tf_op jit(solution)/shard_map/dot_general | solution.py:24
  310.0 3.2 collective-permute-start.9
  313.1 0.0 collective-permute-done.5
  313.2 1.3 fusion.36
  314.4 1.7 collective-permute-start.6
  316.1 1.4 fusion.37
  317.6 1.3 collective-permute-start.8
  318.8 0.0 collective-permute-done.9
  318.9 0.0 copy-start.12
  318.9 1.5 fusion.38
  320.3 1.8 collective-permute-start.10
  322.1 0.6 dynamic_slice.41
  323.4 1.7 add_bitcast_fusion.2
  325.2 18.5 %collective-permute-done.8 = bf16[768,768]{1,0:T(8,128)(2,1)} collective-permute-done((bf16[768,768]{1,0:T(8,128)(2,1)}, bf16[768,768]{1,0:T(8,128)(2,1)}, u32[]{:S(2)}, u32[]{:S(2)}) %collective-permute-start.8) | collective-permute-done | bytes 1179680 | tf_op jit(solution)/shard_map/ppermute | solution.py:31
  343.6 1.7 add_bitcast_fusion.1
  345.3 1.8 add_bitcast_fusion
  347.1 0.2 copy-done.5
  347.3 1.2 fusion.52
  348.5 2.5 collective-permute-start.11
  351.0 0.6 dynamic-slice.8
  352.3 1.8 collective-permute-done.11
  354.0 9.1 %all-reduce = f32[768]{0:T(1024)S(1)} all-reduce(f32[768]{0:T(1024)S(1)} %add.83), channel_id=2, replica_groups=mesh['var'=8,'samp'=4] {'samp'}, use_global_device_ids=true, to_apply=%region_6.7.clone | all-reduce | flops 768 | bytes 6144
  363.1 0.6 dynamic-slice_multiply_fusion
  (34 shorter events, 0.1 us)
Async XLA Ops:
  6.5 254.4 %all-reduce.3.cloned.1.call-start = ((), (), s32[]{:S(2)}) async-start(), calls=%async_computation | async-start | bytes 196608 | tf_op jit(solution)/shard_map/psum | solution.py:45
  6.5 6.2 %copy-start = (bf16[2048,768]{1,0:T(8,128)(2,1)S(1)}, bf16[2048,768]{1,0:T(8,128)(2,1)}, u32[]{:S(2)}) copy-start(bf16[2048,768]{1,0:T(8,128)(2,1)} %param.3) | copy-start | bytes 9437188
  12.0 0.6 copy-start.10
  18.0 274.7 %collective-permute-start = (bf16[2048,768]{1,0:T(8,128)(2,1)}, bf16[2048,768]{1,0:T(8,128)(2,1)}, u32[]{:S(2)}, u32[]{:S(2)}) collective-permute-start(bf16[2048,768]{1,0:T(8,128)(2,1)} %compare_select_fusion), channel_id=1, source_target_pairs={{8,0},{12,4},{16,8},{20,12},{24,16},{28,20},{9,1},{13,5},{17,9},{2... | collective-permute-start | bytes 9437192 | tf_op jit(solution)/shard_map/ppermute | solution.py:14
  20.3 272.3 %collective-permute-start.1 = (bf16[2048,768]{1,0:T(8,128)(2,1)}, bf16[2048,768]{1,0:T(8,128)(2,1)}, u32[]{:S(2)}, u32[]{:S(2)}) collective-permute-start(bf16[2048,768]{1,0:T(8,128)(2,1)} %compare_select_fusion), channel_id=1, source_target_pairs={{0,12},{4,16},{8,20},{12,24},{16,28},{1,13},{5,17},{9,21},{13,25},... | collective-permute-start | bytes 9437192 | tf_op jit(solution)/shard_map/ppermute | solution.py:14
  26.4 266.2 %collective-permute-start.2 = (bf16[2048,768]{1,0:T(8,128)(2,1)}, bf16[2048,768]{1,0:T(8,128)(2,1)}, u32[]{:S(2)}, u32[]{:S(2)}) collective-permute-start(bf16[2048,768]{1,0:T(8,128)(2,1)} %compare_select_fusion), channel_id=1, source_target_pairs={{4,0},{8,4},{12,8},{16,12},{20,16},{24,20},{28,24},{5,1},{9,5},{13... | collective-permute-start | bytes 9437192 | tf_op jit(solution)/shard_map/ppermute | solution.py:14
  268.8 4.7 %collective-permute-start.3 = (bf16[768,768]{1,0:T(8,128)(2,1)S(1)}, bf16[768,768]{1,0:T(8,128)(2,1)S(1)}, u32[]{:S(2)}, u32[]{:S(2)}) collective-permute-start(bf16[768,768]{1,0:T(8,128)(2,1)S(1)} %get-tuple-element.28), channel_id=1, source_target_pairs={{1,0},{3,2},{5,4},{7,6},{9,8},{11,10},{13,12},{15,14},{17,16},{19,... | collective-permute-start | bytes 3538952 | tf_op jit(solution)/shard_map/ppermute | solution.py:29
  273.8 17.1 %collective-permute-start.4 = (bf16[768,768]{1,0:T(8,128)(2,1)S(1)}, bf16[768,768]{1,0:T(8,128)(2,1)S(1)}, u32[]{:S(2)}, u32[]{:S(2)}) collective-permute-start(bf16[768,768]{1,0:T(8,128)(2,1)S(1)} %fusion.35), channel_id=1, source_target_pairs={{2,0},{6,4},{10,8},{14,12},{18,16},{22,20},{26,24},{30,28}} | collective-permute-start | bytes 3538952 | tf_op jit(solution)/shard_map/ppermute | solution.py:31
  297.4 15.7 %collective-permute-start.5 = (bf16[768,768]{1,0:T(8,128)(2,1)S(1)}, bf16[768,768]{1,0:T(8,128)(2,1)S(1)}, u32[]{:S(2)}, u32[]{:S(2)}) collective-permute-start(bf16[768,768]{1,0:T(8,128)(2,1)S(1)} %get-tuple-element.34), channel_id=1, source_target_pairs={{0,1},{2,3},{4,5},{6,7},{8,9},{10,11},{12,13},{14,15},{16,17},{18,... | collective-permute-start | bytes 3538952 | tf_op jit(solution)/shard_map/ppermute | solution.py:29
  303.8 12.3 %copy-start.1 = (f32[768,768]{1,0:T(8,128)}, f32[768,768]{1,0:T(8,128)S(1)}, u32[]{:S(2)}) copy-start(f32[768,768]{1,0:T(8,128)S(1)} %get-tuple-element.33) | copy-start | bytes 7077892
  303.8 12.3 %collective-permute-start.7 = (bf16[768,768]{1,0:T(8,128)(2,1)S(1)}, bf16[768,768]{1,0:T(8,128)(2,1)S(1)}, u32[]{:S(2)}, u32[]{:S(2)}) collective-permute-start(bf16[768,768]{1,0:T(8,128)(2,1)S(1)} %get-tuple-element.32), channel_id=1, source_target_pairs={{1,0},{3,2},{5,4},{7,6},{9,8},{11,10},{13,12},{15,14},{17,16},{19,... | collective-permute-start | bytes 3538952 | tf_op jit(solution)/shard_map/ppermute | solution.py:29
  310.0 8.9 %copy-start.3 = (f32[768,768]{1,0:T(8,128)}, f32[768,768]{1,0:T(8,128)S(1)}, u32[]{:S(2)}) copy-start(f32[768,768]{1,0:T(8,128)S(1)} %get-tuple-element.31) | copy-start | bytes 7077892
  310.0 8.9 %collective-permute-start.9 = (bf16[768,768]{1,0:T(8,128)(2,1)S(1)}, bf16[768,768]{1,0:T(8,128)(2,1)S(1)}, u32[]{:S(2)}, u32[]{:S(2)}) collective-permute-start(bf16[768,768]{1,0:T(8,128)(2,1)S(1)} %get-tuple-element.30), channel_id=1, source_target_pairs={{0,1},{2,3},{4,5},{6,7},{8,9},{10,11},{12,13},{14,15},{16,17},{18,... | collective-permute-start | bytes 3538952 | tf_op jit(solution)/shard_map/ppermute | solution.py:29
  314.4 8.9 %collective-permute-start.6 = (bf16[768,768]{1,0:T(8,128)(2,1)}, bf16[768,768]{1,0:T(8,128)(2,1)}, u32[]{:S(2)}, u32[]{:S(2)}) collective-permute-start(bf16[768,768]{1,0:T(8,128)(2,1)} %fusion.36), channel_id=1, source_target_pairs={{3,1},{7,5},{11,9},{15,13},{19,17},{23,21},{27,25},{31,29}} | collective-permute-start | bytes 3538952 | tf_op jit(solution)/shard_map/ppermute | solution.py:31
  316.1 1.4 copy-start.6
  317.6 26.1 %collective-permute-start.8 = (bf16[768,768]{1,0:T(8,128)(2,1)}, bf16[768,768]{1,0:T(8,128)(2,1)}, u32[]{:S(2)}, u32[]{:S(2)}) collective-permute-start(bf16[768,768]{1,0:T(8,128)(2,1)} %fusion.37), channel_id=1, source_target_pairs={{0,2},{4,6},{8,10},{12,14},{16,18},{20,22},{24,26},{28,30}} | collective-permute-start | bytes 3538952 | tf_op jit(solution)/shard_map/ppermute | solution.py:31
  318.9 1.5 copy-start.8
  318.9 3.2 copy-start.12
  320.3 25.0 %collective-permute-start.10 = (bf16[768,768]{1,0:T(8,128)(2,1)}, bf16[768,768]{1,0:T(8,128)(2,1)}, u32[]{:S(2)}, u32[]{:S(2)}) collective-permute-start(bf16[768,768]{1,0:T(8,128)(2,1)} %fusion.38), channel_id=1, source_target_pairs={{1,3},{5,7},{9,11},{13,15},{17,19},{21,23},{25,27},{29,31}} | collective-permute-start | bytes 3538952 | tf_op jit(solution)/shard_map/ppermute | solution.py:31
  323.4 20.3 %copy-start.2 = (f32[768,768]{1,0:T(8,128)S(1)}, f32[768,768]{1,0:T(8,128)}, u32[]{:S(2)}) copy-start(f32[768,768]{1,0:T(8,128)} %copy-done.1) | copy-start | bytes 7077892
  323.4 20.3 %copy-start.7 = (bf16[768,768]{1,0:T(8,128)(2,1)S(1)}, bf16[768,768]{1,0:T(8,128)(2,1)}, u32[]{:S(2)}) copy-start(bf16[768,768]{1,0:T(8,128)(2,1)} %copy-done.6) | copy-start | bytes 3538948
  325.1 20.2 %copy-start.4 = (f32[768,768]{1,0:T(8,128)S(1)}, f32[768,768]{1,0:T(8,128)}, u32[]{:S(2)}) copy-start(f32[768,768]{1,0:T(8,128)} %copy-done.3) | copy-start | bytes 7077892
  325.1 20.2 %copy-start.9 = (bf16[768,768]{1,0:T(8,128)(2,1)S(1)}, bf16[768,768]{1,0:T(8,128)(2,1)}, u32[]{:S(2)}) copy-start(bf16[768,768]{1,0:T(8,128)(2,1)} %copy-done.8) | copy-start | bytes 3538948
  345.3 2.0 copy-start.5
  347.3 3.7 %copy-start.11 = (u32[32]{0:T(128)S(1)}, u32[32]{0:T(128)}, u32[]{:S(2)}) copy-start(u32[32]{0:T(128)} %constant.89) | copy-start | bytes 388
  348.5 5.5 %collective-permute-start.11 = (f32[768]{0:T(1024)S(1)}, f32[768]{0:T(1024)S(1)}, u32[]{:S(2)}, u32[]{:S(2)}) collective-permute-start(f32[768]{0:T(1024)S(1)} %broadcast_multiply_fusion), channel_id=1, source_target_pairs={{1,5},{2,10},{5,9},{6,14},{9,13},{10,18},{13,17},{14,22},{15,3},{1... | collective-permute-start | bytes 9224 | tf_op jit(solution)/shard_map/ppermute | solution.py:80
Sparse Core Ops, SparseCore 0:
  12.9 247.9 all-reduce.2

commit v4 on v3

--- a/solution.py
+++ b/solution.py
@@ -41,8 +41,7 @@
     position = lax.axis_index("var")
     me = lax.axis_index("samp")
     partial = jnp.stack([jnp.sum(present, 0), jnp.sum(present * values, 0), jnp.sum(present * values * values, 0)])
-    slots = jnp.zeros((n_var,) + partial.shape, jnp.float32)
-    stats = lax.psum(lax.dynamic_update_index_in_dim(slots, partial, position, 0), ("var", "samp"))
+    stats = lax.all_gather(lax.psum(partial, "samp"), "var")
     seen_count = jnp.maximum(stats[:, 0], 1.0)
     column_mean = stats[:, 1] / seen_count
     spread = stats[:, 2] / seen_count - column_mean * column_mean

time: 373 us -> 278 us (0.75)
  waiting for transfers between devices: 269 us -> 36.2 us
  blocking collectives: 9.09 us -> 161 us
  between operations: 15.1 us -> 1.68 us
    psum x1 -> x0, waiting for transfers between devices: 232 us -> none  [local(): lax.psum(lax.dynamic_update_index_in_dim(slots, partial, position, 0), ('...]
    all_gather x0 -> x1, blocking collectives: none -> 138 us  [local(): stats = lax.all_gather(lax.psum(partial, 'samp'), 'var')]
    psum x0 -> x1, blocking collectives: none -> 10.9 us  [local(): stats = lax.all_gather(lax.psum(partial, 'samp'), 'var')]
    unnamed x1, blocking collectives: 9.09 us -> 12.9 us
  transfers between devices with their start and end apart: 13 -> 12, of which waited for: 5 -> 4; matrix products, arithmetic and copies ran while one was open for 9% -> 11% of each run, Pallas kernels for 0% -> 0%
where the time goes in v4:
time: 278 us; the launch traced here: 273 us
  blocking collectives  161 us (58%)
  waiting for transfers between devices  36.2 us (13%)
  starting transfers between devices  29.8 us (11%)
  other arithmetic  25.6 us (9%)
  matrix products  17.1 us (6%)
    all_gather x1, blocking collectives, local(): stats = lax.all_gather(lax.psum(partial, 'samp'), 'var')  138 us
    ppermute x4, waiting for transfers between devices, reduce_to_owner(): lax.ppermute(summed.astype(jnp.bfloat16), 'samp', pairs_chip)  32.1 us
    dot_general x4, matrix products, gram_of(): lax.dot_general(left, right, (((0,), (0,)), ((), ())), preferred_element_...  17.1 us
    unnamed x1, blocking collectives  12.9 us
    ppermute x3, starting transfers between devices, from_behind(): lax.ppermute(value, axis, [(source, source + steps) for source in range(l...  11 us
    psum x1, blocking collectives, local(): stats = lax.all_gather(lax.psum(partial, 'samp'), 'var')  10.9 us
    ppermute x4, starting transfers between devices, reduce_to_owner(): lax.ppermute(part.astype(jnp.bfloat16), 'samp', pairs_core)  7.32 us
    ppermute x4, starting transfers between devices, reduce_to_owner(): lax.ppermute(summed.astype(jnp.bfloat16), 'samp', pairs_chip)  7.25 us
  transfers between devices with their start and end apart: 12, of which 4 were waited for; matrix products, arithmetic and copies ran while one was open for 11% of the time, Pallas kernels for 0%

profile of v4, /device:TPU:14, one launch (start us, length us, event | category | flops | bytes accessed | tf_op | source)
XLA Modules:
  0.0 273.3 jit_solution(14759568148351379736)
XLA Ops:
  0.0 6.3 %compare_select_fusion = bf16[2048,768]{1,0:T(8,128)(2,1)} fusion(bf16[2048,768]{1,0:T(8,128)(2,1)} %param.3, s32[2048,768]{1,0:T(8,128)} %param.4), kind=kLoop, calls=%fused_computation.27 | loop fusion | flops 3145728 | bytes 12582912 | tf_op jit(solution)/shard_map/jit(_where)/select_n | solution.py:35
  6.4 2.5 collective-permute-start
  8.8 6.1 %collective-permute-start.1 = (bf16[2048,768]{1,0:T(8,128)(2,1)}, bf16[2048,768]{1,0:T(8,128)(2,1)}, u32[]{:S(2)}, u32[]{:S(2)}) collective-permute-start(bf16[2048,768]{1,0:T(8,128)(2,1)} %compare_select_fusion), channel_id=1, source_target_pairs={{0,12},{4,16},{8,20},{12,24},{16,28},{1,13},{5,17},{9,21},{13,25},... | collective-permute-start | bytes 9437192 | tf_op jit(solution)/shard_map/ppermute | solution.py:14
  15.0 2.4 collective-permute-start.2
  17.4 2.1 fusion.13
  19.5 10.9 %psum.7 = f32[1,3,768]{2,1,0:T(4,128)S(1)} all-reduce(f32[1,3,768]{2,1,0:T(4,128)S(1)} %maximum_bitcast_fusion), channel_id=1, replica_groups=mesh['var'=8,'samp'=4] {'samp'}, use_global_device_ids=true, to_apply=%region_3.4 | all-reduce | flops 2304 | bytes 18432 | tf_op jit(solution)/shard_map/psum | solution.py:44
  30.5 137.6 %all_gather.7 = f32[8,3,768]{2,1,0:T(4,128)S(1)} all-gather(f32[1,3,768]{2,1,0:T(4,128)S(1)} %psum.7), channel_id=1, replica_groups=mesh['var'=8,'samp'=4] {'var'}, dimensions={0}, use_global_device_ids=true | all-gather | bytes 82944 | tf_op jit(solution)/shard_map/all_gather | solution.py:44
  168.1 0.1 add_rsqrt_fusion
  168.2 0.1 dynamic-slice_reduce_fusion.2
  168.3 3.9 %fusion.12 = bf16[2048,768]{1,0:T(8,128)(2,1)S(1)} fusion(bf16[2048,768]{1,0:T(8,128)(2,1)S(1)} %copy-done.1, s32[2048,768]{1,0:T(8,128)} %param.4, f32[768]{0:T(1024)S(1)} %get-tuple-element.24, f32[768]{0:T(1024)S(1)} %get-tuple-element.36), kind=kLoop, calls=%fused_computation.25 | loop fusion | flops 9437184 | bytes 12589056 | tf_op jit(solution)/shard_map/convert_element_type | solution.py:51
  172.2 2.7 fusion.44
  174.9 1.3 collective-permute-start.3
  176.2 3.4 %collective-permute-done.3 = bf16[768,768]{1,0:T(8,128)(2,1)S(1)} collective-permute-done((bf16[768,768]{1,0:T(8,128)(2,1)S(1)}, bf16[768,768]{1,0:T(8,128)(2,1)S(1)}, u32[]{:S(2)}, u32[]{:S(2)}) %collective-permute-start.3) | collective-permute-done | bytes 1179680 | tf_op jit(solution)/shard_map/ppermute | solution.py:29
  179.7 0.3 fusion.35
  179.9 2.5 collective-permute-start.4
  182.5 13.6 %collective-permute-done.4 = bf16[768,768]{1,0:T(8,128)(2,1)S(1)} collective-permute-done((bf16[768,768]{1,0:T(8,128)(2,1)S(1)}, bf16[768,768]{1,0:T(8,128)(2,1)S(1)}, u32[]{:S(2)}, u32[]{:S(2)}) %collective-permute-start.4) | collective-permute-done | bytes 1179680 | tf_op jit(solution)/shard_map/ppermute | solution.py:31
  196.1 1.7 convert_add_fusion.3
  197.8 0.0 collective-permute-done
  197.8 0.0 collective-permute-done.1
  197.8 0.0 collective-permute-done.2
  197.8 4.8 %fusion.47 = (bf16[768,768]{1,0:T(8,128)(2,1)S(1)}, f32[768,768]{1,0:T(8,128)S(1)}) fusion(bf16[2048,768]{1,0:T(8,128)(2,1)S(1)} %fusion.12, bf16[2048,768]{1,0:T(8,128)(2,1)} %collective-permute-done.2, f32[768]{0:T(1024)S(1)} %get-tuple-element.22, f32[768]{0:T(1024)S(1)} %get-tuple-element.39), kind=kOutput, calls=%fused_computation.83 | convolution fusion | flops 2425946112 | bytes 9836544 | tf_op jit(solution)/shard_map/dot_general | solution.py:24
  202.6 1.5 collective-permute-start.5
  204.1 4.8 %fusion.46 = (bf16[768,768]{1,0:T(8,128)(2,1)S(1)}, f32[768,768]{1,0:T(8,128)S(1)}) fusion(bf16[2048,768]{1,0:T(8,128)(2,1)S(1)} %fusion.12, bf16[2048,768]{1,0:T(8,128)(2,1)} %collective-permute-done, f32[768]{0:T(1024)S(1)} %get-tuple-element.23, f32[768]{0:T(1024)S(1)} %get-tuple-element.37), kind=kOutput, calls=%fused_computation.82 | convolution fusion | flops 2425946112 | bytes 9836544 | tf_op jit(solution)/shard_map/dot_general | solution.py:24
  209.0 1.3 collective-permute-start.7
  210.3 4.8 %fusion.45 = (bf16[768,768]{1,0:T(8,128)(2,1)S(1)}, f32[768,768]{1,0:T(8,128)S(1)}) fusion(bf16[2048,768]{1,0:T(8,128)(2,1)S(1)} %fusion.12, bf16[2048,768]{1,0:T(8,128)(2,1)} %collective-permute-done.1, f32[768]{0:T(1024)S(1)} %get-tuple-element.25, f32[768]{0:T(1024)S(1)} %get-tuple-element.38), kind=kOutput, calls=%fused_computation.81 | convolution fusion | flops 2425946112 | bytes 9836544 | tf_op jit(solution)/shard_map/dot_general | solution.py:24
  215.1 3.2 %collective-permute-start.9 = (bf16[768,768]{1,0:T(8,128)(2,1)S(1)}, bf16[768,768]{1,0:T(8,128)(2,1)S(1)}, u32[]{:S(2)}, u32[]{:S(2)}) collective-permute-start(bf16[768,768]{1,0:T(8,128)(2,1)S(1)} %get-tuple-element.30), channel_id=1, source_target_pairs={{0,1},{2,3},{4,5},{6,7},{8,9},{10,11},{12,13},{14,15},{16,17},{18,... | collective-permute-start | bytes 3538952 | tf_op jit(solution)/shard_map/ppermute | solution.py:29
  218.3 0.0 collective-permute-done.5
  218.3 1.3 fusion.36
  219.6 1.7 collective-permute-start.6
  221.3 1.4 fusion.37
  222.7 1.3 collective-permute-start.8
  224.0 0.0 collective-permute-done.9
  224.1 0.0 copy-start.12
  224.1 1.5 fusion.38
  225.5 1.8 collective-permute-start.10
  227.3 0.6 dynamic_slice.41
  228.6 1.7 add_bitcast_fusion.2
  230.3 18.5 %collective-permute-done.8 = bf16[768,768]{1,0:T(8,128)(2,1)} collective-permute-done((bf16[768,768]{1,0:T(8,128)(2,1)}, bf16[768,768]{1,0:T(8,128)(2,1)}, u32[]{:S(2)}, u32[]{:S(2)}) %collective-permute-start.8) | collective-permute-done | bytes 1179680 | tf_op jit(solution)/shard_map/ppermute | solution.py:31
  248.8 1.7 add_bitcast_fusion.1
  250.5 0.0 collective-permute-done.10
  250.5 1.8 add_bitcast_fusion
  252.3 0.2 copy-done.6
  252.5 1.2 fusion.43
  253.7 4.2 %collective-permute-start.11 = (f32[768]{0:T(1024)S(1)}, f32[768]{0:T(1024)S(1)}, u32[]{:S(2)}, u32[]{:S(2)}) collective-permute-start(f32[768]{0:T(1024)S(1)} %broadcast_multiply_fusion), channel_id=1, source_target_pairs={{1,5},{2,10},{5,9},{6,14},{9,13},{10,18},{13,17},{14,22},{15,3},{1... | collective-permute-start | bytes 9224 | tf_op jit(solution)/shard_map/ppermute | solution.py:79
  257.9 0.6 dynamic-slice.8
  259.1 0.6 collective-permute-done.11
  259.8 12.9 %all-reduce = f32[768]{0:T(1024)S(1)} all-reduce(f32[768]{0:T(1024)S(1)} %add.81), channel_id=2, replica_groups=mesh['var'=8,'samp'=4] {'samp'}, use_global_device_ids=true, to_apply=%region_6.7.clone | all-reduce | flops 768 | bytes 6144
  272.7 0.6 dynamic-slice_multiply_fusion
  (32 shorter events, 0.1 us)
Async XLA Ops:
  0.0 17.4 %copy-start.1 = (bf16[2048,768]{1,0:T(8,128)(2,1)S(1)}, bf16[2048,768]{1,0:T(8,128)(2,1)}, u32[]{:S(2)}) copy-start(bf16[2048,768]{1,0:T(8,128)(2,1)} %param.3) | copy-start | bytes 9437188
  0.0 17.4 %copy-start = (s32[2048,768]{1,0:T(8,128)S(1)}, s32[2048,768]{1,0:T(8,128)}, u32[]{:S(2)}) copy-start(s32[2048,768]{1,0:T(8,128)} %param.4) | copy-start | bytes 18874372
  6.4 191.5 %collective-permute-start = (bf16[2048,768]{1,0:T(8,128)(2,1)}, bf16[2048,768]{1,0:T(8,128)(2,1)}, u32[]{:S(2)}, u32[]{:S(2)}) collective-permute-start(bf16[2048,768]{1,0:T(8,128)(2,1)} %compare_select_fusion), channel_id=1, source_target_pairs={{8,0},{12,4},{16,8},{20,12},{24,16},{28,20},{9,1},{13,5},{17,9},{2... | collective-permute-start | bytes 9437192 | tf_op jit(solution)/shard_map/ppermute | solution.py:14
  8.8 189.0 %collective-permute-start.1 = (bf16[2048,768]{1,0:T(8,128)(2,1)}, bf16[2048,768]{1,0:T(8,128)(2,1)}, u32[]{:S(2)}, u32[]{:S(2)}) collective-permute-start(bf16[2048,768]{1,0:T(8,128)(2,1)} %compare_select_fusion), channel_id=1, source_target_pairs={{0,12},{4,16},{8,20},{12,24},{16,28},{1,13},{5,17},{9,21},{13,25},... | collective-permute-start | bytes 9437192 | tf_op jit(solution)/shard_map/ppermute | solution.py:14
  15.0 182.9 %collective-permute-start.2 = (bf16[2048,768]{1,0:T(8,128)(2,1)}, bf16[2048,768]{1,0:T(8,128)(2,1)}, u32[]{:S(2)}, u32[]{:S(2)}) collective-permute-start(bf16[2048,768]{1,0:T(8,128)(2,1)} %compare_select_fusion), channel_id=1, source_target_pairs={{4,0},{8,4},{12,8},{16,12},{20,16},{24,20},{28,24},{5,1},{9,5},{13... | collective-permute-start | bytes 9437192 | tf_op jit(solution)/shard_map/ppermute | solution.py:14
  174.9 4.7 %collective-permute-start.3 = (bf16[768,768]{1,0:T(8,128)(2,1)S(1)}, bf16[768,768]{1,0:T(8,128)(2,1)S(1)}, u32[]{:S(2)}, u32[]{:S(2)}) collective-permute-start(bf16[768,768]{1,0:T(8,128)(2,1)S(1)} %get-tuple-element.28), channel_id=1, source_target_pairs={{1,0},{3,2},{5,4},{7,6},{9,8},{11,10},{13,12},{15,14},{17,16},{19,... | collective-permute-start | bytes 3538952 | tf_op jit(solution)/shard_map/ppermute | solution.py:29
  179.9 16.2 %collective-permute-start.4 = (bf16[768,768]{1,0:T(8,128)(2,1)S(1)}, bf16[768,768]{1,0:T(8,128)(2,1)S(1)}, u32[]{:S(2)}, u32[]{:S(2)}) collective-permute-start(bf16[768,768]{1,0:T(8,128)(2,1)S(1)} %fusion.35), channel_id=1, source_target_pairs={{2,0},{6,4},{10,8},{14,12},{18,16},{22,20},{26,24},{30,28}} | collective-permute-start | bytes 3538952 | tf_op jit(solution)/shard_map/ppermute | solution.py:31
  202.6 15.7 %collective-permute-start.5 = (bf16[768,768]{1,0:T(8,128)(2,1)S(1)}, bf16[768,768]{1,0:T(8,128)(2,1)S(1)}, u32[]{:S(2)}, u32[]{:S(2)}) collective-permute-start(bf16[768,768]{1,0:T(8,128)(2,1)S(1)} %get-tuple-element.34), channel_id=1, source_target_pairs={{0,1},{2,3},{4,5},{6,7},{8,9},{10,11},{12,13},{14,15},{16,17},{18,... | collective-permute-start | bytes 3538952 | tf_op jit(solution)/shard_map/ppermute | solution.py:29
  209.0 12.4 %copy-start.2 = (f32[768,768]{1,0:T(8,128)}, f32[768,768]{1,0:T(8,128)S(1)}, u32[]{:S(2)}) copy-start(f32[768,768]{1,0:T(8,128)S(1)} %get-tuple-element.33) | copy-start | bytes 7077892
  209.0 12.3 %collective-permute-start.7 = (bf16[768,768]{1,0:T(8,128)(2,1)S(1)}, bf16[768,768]{1,0:T(8,128)(2,1)S(1)}, u32[]{:S(2)}, u32[]{:S(2)}) collective-permute-start(bf16[768,768]{1,0:T(8,128)(2,1)S(1)} %get-tuple-element.32), channel_id=1, source_target_pairs={{1,0},{3,2},{5,4},{7,6},{9,8},{11,10},{13,12},{15,14},{17,16},{19,... | collective-permute-start | bytes 3538952 | tf_op jit(solution)/shard_map/ppermute | solution.py:29
  215.1 8.9 %copy-start.4 = (f32[768,768]{1,0:T(8,128)}, f32[768,768]{1,0:T(8,128)S(1)}, u32[]{:S(2)}) copy-start(f32[768,768]{1,0:T(8,128)S(1)} %get-tuple-element.31) | copy-start | bytes 7077892
  215.1 8.9 %collective-permute-start.9 = (bf16[768,768]{1,0:T(8,128)(2,1)S(1)}, bf16[768,768]{1,0:T(8,128)(2,1)S(1)}, u32[]{:S(2)}, u32[]{:S(2)}) collective-permute-start(bf16[768,768]{1,0:T(8,128)(2,1)S(1)} %get-tuple-element.30), channel_id=1, source_target_pairs={{0,1},{2,3},{4,5},{6,7},{8,9},{10,11},{12,13},{14,15},{16,17},{18,... | collective-permute-start | bytes 3538952 | tf_op jit(solution)/shard_map/ppermute | solution.py:29
  219.6 8.9 %collective-permute-start.6 = (bf16[768,768]{1,0:T(8,128)(2,1)}, bf16[768,768]{1,0:T(8,128)(2,1)}, u32[]{:S(2)}, u32[]{:S(2)}) collective-permute-start(bf16[768,768]{1,0:T(8,128)(2,1)} %fusion.36), channel_id=1, source_target_pairs={{3,1},{7,5},{11,9},{15,13},{19,17},{23,21},{27,25},{31,29}} | collective-permute-start | bytes 3538952 | tf_op jit(solution)/shard_map/ppermute | solution.py:31
  221.3 1.4 copy-start.7
  222.7 26.1 %collective-permute-start.8 = (bf16[768,768]{1,0:T(8,128)(2,1)}, bf16[768,768]{1,0:T(8,128)(2,1)}, u32[]{:S(2)}, u32[]{:S(2)}) collective-permute-start(bf16[768,768]{1,0:T(8,128)(2,1)} %fusion.37), channel_id=1, source_target_pairs={{0,2},{4,6},{8,10},{12,14},{16,18},{20,22},{24,26},{28,30}} | collective-permute-start | bytes 3538952 | tf_op jit(solution)/shard_map/ppermute | solution.py:31
  224.0 1.5 copy-start.9
  224.1 3.2 %copy-start.12 = (s32[4]{0:T(128)S(1)}, s32[4]{0:T(128)}, u32[]{:S(2)}) copy-start(s32[4]{0:T(128)} %constant.77.clone) | copy-start | bytes 52
  225.5 24.9 %collective-permute-start.10 = (bf16[768,768]{1,0:T(8,128)(2,1)}, bf16[768,768]{1,0:T(8,128)(2,1)}, u32[]{:S(2)}, u32[]{:S(2)}) collective-permute-start(bf16[768,768]{1,0:T(8,128)(2,1)} %fusion.38), channel_id=1, source_target_pairs={{1,3},{5,7},{9,11},{13,15},{17,19},{21,23},{25,27},{29,31}} | collective-permute-start | bytes 3538952 | tf_op jit(solution)/shard_map/ppermute | solution.py:31
  228.5 20.2 %copy-start.3 = (f32[768,768]{1,0:T(8,128)S(1)}, f32[768,768]{1,0:T(8,128)}, u32[]{:S(2)}) copy-start(f32[768,768]{1,0:T(8,128)} %copy-done.2) | copy-start | bytes 7077892
  228.6 20.2 %copy-start.8 = (bf16[768,768]{1,0:T(8,128)(2,1)S(1)}, bf16[768,768]{1,0:T(8,128)(2,1)}, u32[]{:S(2)}) copy-start(bf16[768,768]{1,0:T(8,128)(2,1)} %copy-done.7) | copy-start | bytes 3538948
  230.3 20.2 %copy-start.5 = (f32[768,768]{1,0:T(8,128)S(1)}, f32[768,768]{1,0:T(8,128)}, u32[]{:S(2)}) copy-start(f32[768,768]{1,0:T(8,128)} %copy-done.4) | copy-start | bytes 7077892
  230.3 20.2 %copy-start.10 = (bf16[768,768]{1,0:T(8,128)(2,1)S(1)}, bf16[768,768]{1,0:T(8,128)(2,1)}, u32[]{:S(2)}) copy-start(bf16[768,768]{1,0:T(8,128)(2,1)} %copy-done.9) | copy-start | bytes 3538948
  250.5 2.0 copy-start.6
  252.5 5.4 %copy-start.11 = (u32[32]{0:T(128)S(1)}, u32[32]{0:T(128)}, u32[]{:S(2)}) copy-start(u32[32]{0:T(128)} %constant.84) | copy-start | bytes 388
  253.7 6.1 %collective-permute-start.11 = (f32[768]{0:T(1024)S(1)}, f32[768]{0:T(1024)S(1)}, u32[]{:S(2)}, u32[]{:S(2)}) collective-permute-start(f32[768]{0:T(1024)S(1)} %broadcast_multiply_fusion), channel_id=1, source_target_pairs={{1,5},{2,10},{5,9},{6,14},{9,13},{10,18},{13,17},{14,22},{15,3},{1... | collective-permute-start | bytes 9224 | tf_op jit(solution)/shard_map/ppermute | solution.py:79

commit v5 on v4

--- a/solution.py
+++ b/solution.py
@@ -31,6 +31,18 @@
     return summed + lax.ppermute(summed.astype(jnp.bfloat16), "samp", pairs_chip).astype(jnp.float32)
 
 
+def standardize(values, present, axis):
+    seen_count, first_sum, second_sum = lax.psum(
+        (jnp.sum(present, -2), jnp.sum(present * values, -2), jnp.sum(present * values * values, -2)),
+        axis,
+    )
+    seen_count = jnp.maximum(seen_count, 1.0)
+    column_mean = first_sum / seen_count
+    spread = second_sum / seen_count - column_mean * column_mean
+    scale = lax.rsqrt(spread + 1e-05)
+    return ((values - column_mean[..., None, :]) * scale[..., None, :] * present).astype(jnp.bfloat16)
+
+
 def local(dosages, observed):
     coded = jnp.where(observed != 0, dosages, jnp.asarray(-1, dosages.dtype))
     raw = {offset: from_behind(coded, "var", -PARTNER_STEP[offset]) for offset in range(1, BAND + 1)}
@@ -40,28 +52,17 @@
     n_var = lax.axis_size("var")
     position = lax.axis_index("var")
     me = lax.axis_index("samp")
-    partial = jnp.stack([jnp.sum(present, 0), jnp.sum(present * values, 0), jnp.sum(present * values * values, 0)])
-    stats = lax.all_gather(lax.psum(partial, "samp"), "var")
-    seen_count = jnp.maximum(stats[:, 0], 1.0)
-    column_mean = stats[:, 1] / seen_count
-    spread = stats[:, 2] / seen_count - column_mean * column_mean
-    inverse_sd = lax.rsqrt(spread + 1e-05)
-    own_mean = lax.dynamic_index_in_dim(column_mean, position, 0, keepdims=False)
-    own_sd = lax.dynamic_index_in_dim(inverse_sd, position, 0, keepdims=False)
-    standard = ((values - own_mean) * own_sd * present).astype(jnp.bfloat16)
+    standard = standardize(values, present, "samp")
     samples = standard.shape[0] * n_samp
     block_width = standard.shape[1]
 
     owned = {0: reduce_to_owner(gram_of(standard, standard), 0, n_samp)}
     arrived, owned[0] = lax.optimization_barrier(([raw[d] for d in PROCESS_ORDER], owned[0]))
-    for offset, coded_partner in zip(PROCESS_ORDER, arrived):
-        source = jnp.clip(position + PARTNER_STEP[offset], 0, n_var - 1)
-        partner_mean = lax.dynamic_index_in_dim(column_mean, source, 0, keepdims=False)
-        partner_sd = lax.dynamic_index_in_dim(inverse_sd, source, 0, keepdims=False)
-        partner_values = coded_partner.astype(jnp.float32)
-        partner_present = (partner_values >= 0).astype(jnp.float32)
-        partner = ((partner_values - partner_mean) * partner_sd * partner_present).astype(jnp.bfloat16)
-        owned[offset] = reduce_to_owner(gram_of(standard, partner), offset, n_samp)
+    partner_values = jnp.stack([coded_partner.astype(jnp.float32) for coded_partner in arrived])
+    partner_present = (partner_values >= 0).astype(jnp.float32)
+    partners = standardize(partner_values, partner_present, "samp")
+    for index, offset in enumerate(PROCESS_ORDER):
+        owned[offset] = reduce_to_owner(gram_of(standard, partners[index]), offset, n_samp)
     gram = lax.dynamic_index_in_dim(jnp.stack([owned[d] for d in range(BAND + 1)]), me, 0, keepdims=False)
 
     steps = jnp.array([0] + [PARTNER_STEP[d] for d in range(1, BAND + 1)], jnp.int32)

time: 278 us -> 242 us (0.87)
  blocking collectives: 161 us -> 29.9 us
  waiting for transfers between devices: 36.2 us -> 126 us
  other arithmetic: 25.6 us -> 41.2 us
  matrix products: 17.1 us -> 10.9 us
    all_gather x1 -> x0, blocking collectives: 138 us -> none  [local(): stats = lax.all_gather(lax.psum(partial, 'samp'), 'var')]
    ppermute x3, waiting for transfers between devices: 0.01 us -> 88 us  [from_behind(): lax.ppermute(value, axis, [(source, source + steps) for source in range(l...]
    psum x1 -> x2, blocking collectives: 10.9 us -> 21.6 us  [standardize(): lax.psum((jnp.sum(present, -2), jnp.sum(present * values, -2), jnp.sum(pr...]
    convert_element_type x1 -> x2, other arithmetic: 3.93 us -> 11.9 us  [standardize(): ((values - column_mean[..., None, :]) * scale[..., None, :] * present).as...]
    reduce_sum x1 -> x2, other arithmetic: 2.06 us -> 9.71 us  [standardize(): jnp.sum(present * values, -2)]
    dot_general x4, matrix products: 17.1 us -> 10.9 us  [gram_of(): lax.dot_general(left, right, (((0,), (0,)), ((), ())), preferred_element_...]
    unnamed x1, blocking collectives: 12.9 us -> 8.27 us
  transfers between devices with their start and end apart: 12 -> 12, of which waited for: 4 -> 7; matrix products, arithmetic and copies ran while one was open for 11% -> 11% of each run, Pallas kernels for 0% -> 0%
where the time goes in v5:
time: 242 us; the launch traced here: 240 us
  waiting for transfers between devices  126 us (52%)
  other arithmetic  41.2 us (17%)
  blocking collectives  29.9 us (12%)
  starting transfers between devices  29.1 us (12%)
  matrix products  10.9 us (5%)
    ppermute x3, waiting for transfers between devices, from_behind(): lax.ppermute(value, axis, [(source, source + steps) for source in range(l...  88 us
    ppermute x4, waiting for transfers between devices, reduce_to_owner(): lax.ppermute(summed.astype(jnp.bfloat16), 'samp', pairs_chip)  33.4 us
    psum x2, blocking collectives, standardize(): lax.psum((jnp.sum(present, -2), jnp.sum(present * values, -2), jnp.sum(pr...  21.6 us
    convert_element_type x2, other arithmetic, standardize(): ((values - column_mean[..., None, :]) * scale[..., None, :] * present).as...  11.9 us
    ppermute x3, starting transfers between devices, from_behind(): lax.ppermute(value, axis, [(source, source + steps) for source in range(l...  11 us
    dot_general x4, matrix products, gram_of(): lax.dot_general(left, right, (((0,), (0,)), ((), ())), preferred_element_...  10.9 us
    reduce_sum x2, other arithmetic, standardize(): jnp.sum(present * values, -2)  9.71 us
    unnamed x1, blocking collectives  8.27 us
  transfers between devices with their start and end apart: 12, of which 7 were waited for; matrix products, arithmetic and copies ran while one was open for 11% of the time, Pallas kernels for 0%

profile of v5, /device:TPU:14, one launch (start us, length us, event | category | flops | bytes accessed | tf_op | source)
XLA Modules:
  0.0 239.8 jit_solution(3107022374201188229)
XLA Ops:
  0.0 6.3 %compare_select_fusion = bf16[2048,768]{1,0:T(8,128)(2,1)} fusion(bf16[2048,768]{1,0:T(8,128)(2,1)} %param.3, s32[2048,768]{1,0:T(8,128)} %param.4), kind=kLoop, calls=%fused_computation.23 | loop fusion | flops 3145728 | bytes 12582912 | tf_op jit(solution)/shard_map/jit(_where)/select_n | solution.py:47
  6.3 2.5 %collective-permute-start = (bf16[2048,768]{1,0:T(8,128)(2,1)}, bf16[2048,768]{1,0:T(8,128)(2,1)}, u32[]{:S(2)}, u32[]{:S(2)}) collective-permute-start(bf16[2048,768]{1,0:T(8,128)(2,1)} %compare_select_fusion), channel_id=1, source_target_pairs={{8,0},{12,4},{16,8},{20,12},{24,16},{28,20},{9,1},{13,5},{17,9},{2... | collective-permute-start | bytes 9437192 | tf_op jit(solution)/shard_map/ppermute | solution.py:14
  8.8 6.2 %collective-permute-start.1 = (bf16[2048,768]{1,0:T(8,128)(2,1)}, bf16[2048,768]{1,0:T(8,128)(2,1)}, u32[]{:S(2)}, u32[]{:S(2)}) collective-permute-start(bf16[2048,768]{1,0:T(8,128)(2,1)} %compare_select_fusion), channel_id=1, source_target_pairs={{0,12},{4,16},{8,20},{12,24},{16,28},{1,13},{5,17},{9,21},{13,25},... | collective-permute-start | bytes 9437192 | tf_op jit(solution)/shard_map/ppermute | solution.py:14
  15.0 2.4 collective-permute-start.2
  17.4 2.1 fusion.9
  19.5 10.9 %all-reduce.2 = (f32[768]{0:T(1024)S(1)}, f32[768]{0:T(1024)S(1)}, f32[768]{0:T(1024)S(1)}) all-reduce(f32[768]{0:T(1024)S(1)} %get-tuple-element.17, f32[768]{0:T(1024)S(1)} %get-tuple-element.18, f32[768]{0:T(1024)S(1)} %get-tuple-element.16), channel_id=1, replica_groups=mesh['var'=8,'samp'=4] {'samp'}, use_global_device_ids=true, to_apply=%region_5.6 | all-reduce | flops 2304 | bytes 18432 | tf_op jit(solution)/shard_map/psum | solution.py:35
  30.4 4.9 %fusion.7 = bf16[2048,768]{1,0:T(8,128)(2,1)S(1)} fusion(bf16[2048,768]{1,0:T(8,128)(2,1)} %param.3, s32[2048,768]{1,0:T(8,128)} %param.4, f32[768]{0:T(1024)S(1)} %get-tuple-element.30, f32[768]{0:T(1024)S(1)} %get-tuple-element.29), kind=kLoop, calls=%fused_computation.20 | loop fusion | flops 9437184 | bytes 12589056 | tf_op jit(solution)/shard_map/convert_element_type | solution.py:43
  35.3 2.7 %fusion.24 = (bf16[768,768]{1,0:T(8,128)(2,1)S(1)}, f32[768,768]{1,0:T(8,128)S(1)}) fusion(bf16[2048,768]{1,0:T(8,128)(2,1)S(1)} %fusion.7), kind=kOutput, calls=%fused_computation.57 | convolution fusion | flops 2416508928 | bytes 6684672 | tf_op jit(solution)/shard_map/dot_general | solution.py:24
  38.0 1.3 collective-permute-start.3
  39.3 3.4 %collective-permute-done.3 = bf16[768,768]{1,0:T(8,128)(2,1)S(1)} collective-permute-done((bf16[768,768]{1,0:T(8,128)(2,1)S(1)}, bf16[768,768]{1,0:T(8,128)(2,1)S(1)}, u32[]{:S(2)}, u32[]{:S(2)}) %collective-permute-start.3) | collective-permute-done | bytes 1179680 | tf_op jit(solution)/shard_map/ppermute | solution.py:29
  42.7 0.3 fusion.19
  43.0 2.5 %collective-permute-start.4 = (bf16[768,768]{1,0:T(8,128)(2,1)S(1)}, bf16[768,768]{1,0:T(8,128)(2,1)S(1)}, u32[]{:S(2)}, u32[]{:S(2)}) collective-permute-start(bf16[768,768]{1,0:T(8,128)(2,1)S(1)} %fusion.19), channel_id=1, source_target_pairs={{2,0},{6,4},{10,8},{14,12},{18,16},{22,20},{26,24},{30,28}} | collective-permute-start | bytes 3538952 | tf_op jit(solution)/shard_map/ppermute | solution.py:31
  45.5 13.6 %collective-permute-done.4 = bf16[768,768]{1,0:T(8,128)(2,1)S(1)} collective-permute-done((bf16[768,768]{1,0:T(8,128)(2,1)S(1)}, bf16[768,768]{1,0:T(8,128)(2,1)S(1)}, u32[]{:S(2)}, u32[]{:S(2)}) %collective-permute-start.4) | collective-permute-done | bytes 1179680 | tf_op jit(solution)/shard_map/ppermute | solution.py:31
  59.2 1.7 convert_add_fusion.3
  60.9 17.6 %collective-permute-done = bf16[2048,768]{1,0:T(8,128)(2,1)} collective-permute-done((bf16[2048,768]{1,0:T(8,128)(2,1)}, bf16[2048,768]{1,0:T(8,128)(2,1)}, u32[]{:S(2)}, u32[]{:S(2)}) %collective-permute-start) | collective-permute-done | bytes 3145760 | tf_op jit(solution)/shard_map/ppermute | solution.py:14
  78.5 69.4 %collective-permute-done.1 = bf16[2048,768]{1,0:T(8,128)(2,1)} collective-permute-done((bf16[2048,768]{1,0:T(8,128)(2,1)}, bf16[2048,768]{1,0:T(8,128)(2,1)}, u32[]{:S(2)}, u32[]{:S(2)}) %collective-permute-start.1) | collective-permute-done | bytes 3145760 | tf_op jit(solution)/shard_map/ppermute | solution.py:14
  147.9 1.0 collective-permute-done.2
  148.9 7.7 %fusion = (f32[3,768]{1,0:T(4,128)S(1)}, f32[3,768]{1,0:T(4,128)S(1)}, f32[3,768]{1,0:T(4,128)S(1)}) fusion(bf16[1,2048,768]{2,1,0:T(8,128)(2,1)} %bitcast.3, bf16[1,2048,768]{2,1,0:T(8,128)(2,1)} %bitcast.2, bf16[1,2048,768]{2,1,0:T(8,128)(2,1)} %bitcast.1), kind=kLoop, calls=%fused_computation.4 | loop fusion | flops 47179008 | bytes 9464832 | tf_op jit(solution)/shard_map/reduce_sum | solution.py:36
  156.6 10.7 %all-reduce.1 = (f32[3,768]{1,0:T(4,128)S(1)}, f32[3,768]{1,0:T(4,128)S(1)}, f32[3,768]{1,0:T(4,128)S(1)}) all-reduce(f32[3,768]{1,0:T(4,128)S(1)} %get-tuple-element.14, f32[3,768]{1,0:T(4,128)S(1)} %get-tuple-element.15, f32[3,768]{1,0:T(4,128)S(1)} %get-tuple-element.13), channel_id=1, replica_groups=mesh['var'=8,'samp'=4] {'samp'}, use_global_device_ids=true, to_apply=%region_11.12 | all-reduce | flops 6912 | bytes 55296 | tf_op jit(solution)/shard_map/psum | solution.py:35
  167.3 7.0 %fusion.3 = bf16[3,2048,768]{2,1,0:T(8,128)(2,1)S(1)} fusion(f32[3,768]{1,0:T(4,128)S(1)} %get-tuple-element.28, f32[3,768]{1,0:T(4,128)S(1)} %get-tuple-element.27, bf16[1,2048,768]{2,1,0:T(8,128)(2,1)} %bitcast.3, bf16[1,2048,768]{2,1,0:T(8,128)(2,1)} %bitcast.2, bf16[1,2048,768]{2,1,0:T(8,128)(2,1)} %bitcast.1), kind=kLoop, calls=%fused_computation.7 | loop fusion | flops 37748736 | bytes 18892800 | tf_op jit(solution)/shard_map/convert_element_type | solution.py:43
  174.3 2.7 %fusion.27 = (bf16[768,768]{1,0:T(8,128)(2,1)S(1)}, f32[768,768]{1,0:T(8,128)S(1)}) fusion(bf16[2048,768]{1,0:T(8,128)(2,1)S(1)} %fusion.7, bf16[3,2048,768]{2,1,0:T(8,128)(2,1)S(1)} %fusion.3), kind=kOutput, calls=%fused_computation.60 | convolution fusion | flops 2416508928 | bytes 9830400 | tf_op jit(solution)/shard_map/dot_general | solution.py:24
  177.1 1.5 collective-permute-start.5
  178.5 2.7 %fusion.26 = (bf16[768,768]{1,0:T(8,128)(2,1)S(1)}, f32[768,768]{1,0:T(8,128)S(1)}) fusion(bf16[2048,768]{1,0:T(8,128)(2,1)S(1)} %fusion.7, bf16[3,2048,768]{2,1,0:T(8,128)(2,1)S(1)} %fusion.3), kind=kOutput, calls=%fused_computation.59 | convolution fusion | flops 2416508928 | bytes 9830400 | tf_op jit(solution)/shard_map/dot_general | solution.py:24
  181.3 1.3 collective-permute-start.7
  182.6 2.7 %fusion.25 = (bf16[768,768]{1,0:T(8,128)(2,1)S(1)}, f32[768,768]{1,0:T(8,128)S(1)}) fusion(bf16[2048,768]{1,0:T(8,128)(2,1)S(1)} %fusion.7, bf16[3,2048,768]{2,1,0:T(8,128)(2,1)S(1)} %fusion.3), kind=kOutput, calls=%fused_computation.58 | convolution fusion | flops 2416508928 | bytes 9830400 | tf_op jit(solution)/shard_map/dot_general | solution.py:24
  185.3 3.2 %collective-permute-start.9 = (bf16[768,768]{1,0:T(8,128)(2,1)S(1)}, bf16[768,768]{1,0:T(8,128)(2,1)S(1)}, u32[]{:S(2)}, u32[]{:S(2)}) collective-permute-start(bf16[768,768]{1,0:T(8,128)(2,1)S(1)} %get-tuple-element.33), channel_id=1, source_target_pairs={{0,1},{2,3},{4,5},{6,7},{8,9},{10,11},{12,13},{14,15},{16,17},{18,... | collective-permute-start | bytes 3538952 | tf_op jit(solution)/shard_map/ppermute | solution.py:29
  188.5 0.0 collective-permute-done.5
  188.5 1.4 fusion.20
  189.9 1.7 collective-permute-start.6
  191.6 0.0 collective-permute-done.7
  191.6 1.4 fusion.21
  193.1 1.3 collective-permute-start.8
  194.3 0.0 collective-permute-done.9
  194.4 0.0 copy-start.16
  194.4 1.4 fusion.22
  195.8 1.8 collective-permute-start.10
  197.6 0.6 dynamic_slice.8
  198.9 1.7 add_bitcast_fusion.2
  200.7 19.8 %collective-permute-done.8 = bf16[768,768]{1,0:T(8,128)(2,1)} collective-permute-done((bf16[768,768]{1,0:T(8,128)(2,1)}, bf16[768,768]{1,0:T(8,128)(2,1)}, u32[]{:S(2)}, u32[]{:S(2)}) %collective-permute-start.8) | collective-permute-done | bytes 1179680 | tf_op jit(solution)/shard_map/ppermute | solution.py:31
  220.4 1.7 add_bitcast_fusion.1
  222.1 1.8 add_bitcast_fusion
  223.9 0.2 copy-done.8
  224.1 1.2 fusion.23
  225.3 3.5 %collective-permute-start.11 = (f32[768]{0:T(1024)S(1)}, f32[768]{0:T(1024)S(1)}, u32[]{:S(2)}, u32[]{:S(2)}) collective-permute-start(f32[768]{0:T(1024)S(1)} %broadcast_multiply_fusion), channel_id=1, source_target_pairs={{1,5},{2,10},{5,9},{6,14},{9,13},{10,18},{13,17},{14,22},{15,3},{1... | collective-permute-start | bytes 9224 | tf_op jit(solution)/shard_map/ppermute | solution.py:80
  228.8 0.6 dynamic-slice
  230.1 0.8 collective-permute-done.11
  230.8 8.3 %all-reduce = f32[768]{0:T(1024)S(1)} all-reduce(f32[768]{0:T(1024)S(1)} %add.75), channel_id=2, replica_groups=mesh['var'=8,'samp'=4] {'samp'}, use_global_device_ids=true, to_apply=%region_14.15.clone | all-reduce | flops 768 | bytes 6144
  239.1 0.6 dynamic-slice_multiply_fusion
  (38 shorter events, 0.1 us)
Async XLA Ops:
  0.0 17.4 %copy-start.1 = (bf16[2048,768]{1,0:T(8,128)(2,1)S(1)}, bf16[2048,768]{1,0:T(8,128)(2,1)}, u32[]{:S(2)}) copy-start(bf16[2048,768]{1,0:T(8,128)(2,1)} %param.3) | copy-start | bytes 9437188
  0.0 17.4 %copy-start = (s32[2048,768]{1,0:T(8,128)S(1)}, s32[2048,768]{1,0:T(8,128)}, u32[]{:S(2)}) copy-start(s32[2048,768]{1,0:T(8,128)} %param.4) | copy-start | bytes 18874372
  6.3 72.2 %collective-permute-start = (bf16[2048,768]{1,0:T(8,128)(2,1)}, bf16[2048,768]{1,0:T(8,128)(2,1)}, u32[]{:S(2)}, u32[]{:S(2)}) collective-permute-start(bf16[2048,768]{1,0:T(8,128)(2,1)} %compare_select_fusion), channel_id=1, source_target_pairs={{8,0},{12,4},{16,8},{20,12},{24,16},{28,20},{9,1},{13,5},{17,9},{2... | collective-permute-start | bytes 9437192 | tf_op jit(solution)/shard_map/ppermute | solution.py:14
  8.8 139.1 %collective-permute-start.1 = (bf16[2048,768]{1,0:T(8,128)(2,1)}, bf16[2048,768]{1,0:T(8,128)(2,1)}, u32[]{:S(2)}, u32[]{:S(2)}) collective-permute-start(bf16[2048,768]{1,0:T(8,128)(2,1)} %compare_select_fusion), channel_id=1, source_target_pairs={{0,12},{4,16},{8,20},{12,24},{16,28},{1,13},{5,17},{9,21},{13,25},... | collective-permute-start | bytes 9437192 | tf_op jit(solution)/shard_map/ppermute | solution.py:14
  15.0 133.9 %collective-permute-start.2 = (bf16[2048,768]{1,0:T(8,128)(2,1)}, bf16[2048,768]{1,0:T(8,128)(2,1)}, u32[]{:S(2)}, u32[]{:S(2)}) collective-permute-start(bf16[2048,768]{1,0:T(8,128)(2,1)} %compare_select_fusion), channel_id=1, source_target_pairs={{4,0},{8,4},{12,8},{16,12},{20,16},{24,20},{28,24},{5,1},{9,5},{13... | collective-permute-start | bytes 9437192 | tf_op jit(solution)/shard_map/ppermute | solution.py:14
  38.0 4.7 %collective-permute-start.3 = (bf16[768,768]{1,0:T(8,128)(2,1)S(1)}, bf16[768,768]{1,0:T(8,128)(2,1)S(1)}, u32[]{:S(2)}, u32[]{:S(2)}) collective-permute-start(bf16[768,768]{1,0:T(8,128)(2,1)S(1)} %get-tuple-element.31), channel_id=1, source_target_pairs={{1,0},{3,2},{5,4},{7,6},{9,8},{11,10},{13,12},{15,14},{17,16},{19,... | collective-permute-start | bytes 3538952 | tf_op jit(solution)/shard_map/ppermute | solution.py:29
  43.0 16.2 %collective-permute-start.4 = (bf16[768,768]{1,0:T(8,128)(2,1)S(1)}, bf16[768,768]{1,0:T(8,128)(2,1)S(1)}, u32[]{:S(2)}, u32[]{:S(2)}) collective-permute-start(bf16[768,768]{1,0:T(8,128)(2,1)S(1)} %fusion.19), channel_id=1, source_target_pairs={{2,0},{6,4},{10,8},{14,12},{18,16},{22,20},{26,24},{30,28}} | collective-permute-start | bytes 3538952 | tf_op jit(solution)/shard_map/ppermute | solution.py:31
  177.0 11.5 %copy-start.6 = (f32[768,768]{1,0:T(8,128)}, f32[768,768]{1,0:T(8,128)S(1)}, u32[]{:S(2)}) copy-start(f32[768,768]{1,0:T(8,128)S(1)} %get-tuple-element.38) | copy-start | bytes 7077892
  177.1 11.4 %collective-permute-start.5 = (bf16[768,768]{1,0:T(8,128)(2,1)S(1)}, bf16[768,768]{1,0:T(8,128)(2,1)S(1)}, u32[]{:S(2)}, u32[]{:S(2)}) collective-permute-start(bf16[768,768]{1,0:T(8,128)(2,1)S(1)} %get-tuple-element.37), channel_id=1, source_target_pairs={{0,1},{2,3},{4,5},{6,7},{8,9},{10,11},{12,13},{14,15},{16,17},{18,... | collective-permute-start | bytes 3538952 | tf_op jit(solution)/shard_map/ppermute | solution.py:29
  181.3 10.4 %copy-start.4 = (f32[768,768]{1,0:T(8,128)}, f32[768,768]{1,0:T(8,128)S(1)}, u32[]{:S(2)}) copy-start(f32[768,768]{1,0:T(8,128)S(1)} %get-tuple-element.36) | copy-start | bytes 7077892
  181.3 10.3 %collective-permute-start.7 = (bf16[768,768]{1,0:T(8,128)(2,1)S(1)}, bf16[768,768]{1,0:T(8,128)(2,1)S(1)}, u32[]{:S(2)}, u32[]{:S(2)}) collective-permute-start(bf16[768,768]{1,0:T(8,128)(2,1)S(1)} %get-tuple-element.35), channel_id=1, source_target_pairs={{1,0},{3,2},{5,4},{7,6},{9,8},{11,10},{13,12},{15,14},{17,16},{19,... | collective-permute-start | bytes 3538952 | tf_op jit(solution)/shard_map/ppermute | solution.py:29
  185.3 9.1 %copy-start.2 = (f32[768,768]{1,0:T(8,128)}, f32[768,768]{1,0:T(8,128)S(1)}, u32[]{:S(2)}) copy-start(f32[768,768]{1,0:T(8,128)S(1)} %get-tuple-element.34) | copy-start | bytes 7077892
  185.3 9.0 %collective-permute-start.9 = (bf16[768,768]{1,0:T(8,128)(2,1)S(1)}, bf16[768,768]{1,0:T(8,128)(2,1)S(1)}, u32[]{:S(2)}, u32[]{:S(2)}) collective-permute-start(bf16[768,768]{1,0:T(8,128)(2,1)S(1)} %get-tuple-element.33), channel_id=1, source_target_pairs={{0,1},{2,3},{4,5},{6,7},{8,9},{10,11},{12,13},{14,15},{16,17},{18,... | collective-permute-start | bytes 3538952 | tf_op jit(solution)/shard_map/ppermute | solution.py:29
  188.5 1.4 copy-start.11
  189.9 9.0 %collective-permute-start.6 = (bf16[768,768]{1,0:T(8,128)(2,1)}, bf16[768,768]{1,0:T(8,128)(2,1)}, u32[]{:S(2)}, u32[]{:S(2)}) collective-permute-start(bf16[768,768]{1,0:T(8,128)(2,1)} %fusion.20), channel_id=1, source_target_pairs={{3,1},{7,5},{11,9},{15,13},{19,17},{23,21},{27,25},{31,29}} | collective-permute-start | bytes 3538952 | tf_op jit(solution)/shard_map/ppermute | solution.py:31
  191.6 1.4 copy-start.9
  193.1 27.4 %collective-permute-start.8 = (bf16[768,768]{1,0:T(8,128)(2,1)}, bf16[768,768]{1,0:T(8,128)(2,1)}, u32[]{:S(2)}, u32[]{:S(2)}) collective-permute-start(bf16[768,768]{1,0:T(8,128)(2,1)} %fusion.21), channel_id=1, source_target_pairs={{0,2},{4,6},{8,10},{12,14},{16,18},{20,22},{24,26},{28,30}} | collective-permute-start | bytes 3538952 | tf_op jit(solution)/shard_map/ppermute | solution.py:31
  194.4 1.4 copy-start.13
  194.4 3.2 %copy-start.16 = (s32[4]{0:T(128)S(1)}, s32[4]{0:T(128)}, u32[]{:S(2)}) copy-start(s32[4]{0:T(128)} %constant.45.clone) | copy-start | bytes 52
  194.4 4.5 %copy-start.7 = (f32[768,768]{1,0:T(8,128)S(1)}, f32[768,768]{1,0:T(8,128)}, u32[]{:S(2)}) copy-start(f32[768,768]{1,0:T(8,128)} %copy-done.6) | copy-start | bytes 7077892
  194.4 4.5 %copy-start.12 = (bf16[768,768]{1,0:T(8,128)(2,1)S(1)}, bf16[768,768]{1,0:T(8,128)(2,1)}, u32[]{:S(2)}) copy-start(bf16[768,768]{1,0:T(8,128)(2,1)} %copy-done.11) | copy-start | bytes 3538948
  195.8 26.3 %collective-permute-start.10 = (bf16[768,768]{1,0:T(8,128)(2,1)}, bf16[768,768]{1,0:T(8,128)(2,1)}, u32[]{:S(2)}, u32[]{:S(2)}) collective-permute-start(bf16[768,768]{1,0:T(8,128)(2,1)} %fusion.22), channel_id=1, source_target_pairs={{1,3},{5,7},{9,11},{13,15},{17,19},{21,23},{25,27},{29,31}} | collective-permute-start | bytes 3538952 | tf_op jit(solution)/shard_map/ppermute | solution.py:31
  198.9 21.6 %copy-start.5 = (f32[768,768]{1,0:T(8,128)S(1)}, f32[768,768]{1,0:T(8,128)}, u32[]{:S(2)}) copy-start(f32[768,768]{1,0:T(8,128)} %copy-done.4) | copy-start | bytes 7077892
  198.9 21.6 %copy-start.10 = (bf16[768,768]{1,0:T(8,128)(2,1)S(1)}, bf16[768,768]{1,0:T(8,128)(2,1)}, u32[]{:S(2)}) copy-start(bf16[768,768]{1,0:T(8,128)(2,1)} %copy-done.9) | copy-start | bytes 3538948
  200.7 21.5 %copy-start.3 = (f32[768,768]{1,0:T(8,128)S(1)}, f32[768,768]{1,0:T(8,128)}, u32[]{:S(2)}) copy-start(f32[768,768]{1,0:T(8,128)} %copy-done.2) | copy-start | bytes 7077892
  200.7 21.5 %copy-start.14 = (bf16[768,768]{1,0:T(8,128)(2,1)S(1)}, bf16[768,768]{1,0:T(8,128)(2,1)}, u32[]{:S(2)}) copy-start(bf16[768,768]{1,0:T(8,128)(2,1)} %copy-done.13) | copy-start | bytes 3538948
  222.1 2.0 copy-start.8
  224.1 4.7 %copy-start.15 = (u32[32]{0:T(128)S(1)}, u32[32]{0:T(128)}, u32[]{:S(2)}) copy-start(u32[32]{0:T(128)} %constant.48) | copy-start | bytes 388
  225.3 5.5 %collective-permute-start.11 = (f32[768]{0:T(1024)S(1)}, f32[768]{0:T(1024)S(1)}, u32[]{:S(2)}, u32[]{:S(2)}) collective-permute-start(f32[768]{0:T(1024)S(1)} %broadcast_multiply_fusion), channel_id=1, source_target_pairs={{1,5},{2,10},{5,9},{6,14},{9,13},{10,18},{13,17},{14,22},{15,3},{1... | collective-permute-start | bytes 9224 | tf_op jit(solution)/shard_map/ppermute | solution.py:80

commit v6 on v1

v6 whole, which is shorter than its diff:
```python
import jax
import jax.numpy as jnp
from jax import lax
from jax.sharding import PartitionSpec as P

BAND = 3
PARTNER_STEP = {1: 1, 2: 2, 3: -3}
PROCESS_ORDER = (2, 3, 1)


def from_behind(value, axis, steps):
    count = lax.axis_size(axis)
    leading, last = (max(0, -steps), min(count, count - steps))
    return lax.ppermute(value, axis, [(source, source + steps) for source in range(leading, last)])


def adjusted_r2(gram_part, samples):
    correl = gram_part / samples
    squared = correl * correl
    return squared - (1.0 - squared) / (samples - 2)


def gram_of(left, right):
    return lax.dot_general(left, right, (((0,), (0,)), ((), ())), preferred_element_type=jnp.float32)


def reduce_quarters(part, n_samp):
    me = lax.axis_index("samp")
    core, chip = me % 2, me // 2
    quarters = part.reshape(2, 2, part.shape[0] // 4, part.shape[1])
    keep = lax.dynamic_index_in_dim(quarters, core, 1, keepdims=False)
    send = lax.dynamic_index_in_dim(quarters, 1 - core, 1, keepdims=False)
    pairs_core = [(s, s ^ 1) for s in range(n_samp)]
    summed = keep + lax.ppermute(send.astype(jnp.bfloat16), "samp", pairs_core).astype(jnp.float32)
    keep = lax.dynamic_index_in_dim(summed, chip, 0, keepdims=False)
    send = lax.dynamic_index_in_dim(summed, 1 - chip, 0, keepdims=False)
    pairs_chip = [(s, s ^ 2) for s in range(n_samp)]
    return keep + lax.ppermute(send.astype(jnp.bfloat16), "samp", pairs_chip).astype(jnp.float32)


def local(dosages, observed):
    values = dosages.astype(jnp.float32)
    present = observed.astype(jnp.float32)
    seen_count, first_sum, second_sum = lax.psum(
        (jnp.sum(present, 0), jnp.sum(present * values, 0), jnp.sum(present * values * values, 0)),
        "samp",
    )
    seen_count = jnp.maximum(seen_count, 1.0)
    column_mean = first_sum / seen_count
    spread = second_sum / seen_count - column_mean * column_mean
    standard = ((values - column_mean) * lax.rsqrt(spread + 1e-05) * present).astype(jnp.bfloat16)
    n_samp = lax.axis_size("samp")
    n_var = lax.axis_size("var")
    samples = standard.shape[0] * n_samp
    block_width = standard.shape[1]
    position = lax.axis_index("var")
    raw = {offset: from_behind(standard, "var", -PARTNER_STEP[offset]) for offset in range(1, BAND + 1)}

    owned = {0: reduce_quarters(gram_of(standard, standard), n_samp)}
    arrived, owned[0] = lax.optimization_barrier(([raw[d] for d in PROCESS_ORDER], owned[0]))
    for offset, partner in zip(PROCESS_ORDER, arrived):
        owned[offset] = reduce_quarters(gram_of(standard, partner), n_samp)

    row_total = jnp.sum(adjusted_r2(owned[0], samples), 1)
    incoming = jnp.zeros((block_width,), jnp.float32)
    for offset in range(1, BAND + 1):
        step = PARTNER_STEP[offset]
        in_range = ((position + step >= 0) & (position + step < n_var)).astype(jnp.float32)
        adjusted = adjusted_r2(owned[offset], samples) * in_range
        row_total = row_total + jnp.sum(adjusted, 1)
        incoming = incoming + from_behind(jnp.sum(adjusted, 0), "var", step)
    total = row_total + lax.psum_scatter(incoming, "samp", scatter_dimension=0, tiled=True)
    return total / block_width


def solution(mesh):
    placed = (P("samp", "var"), P("samp", "var"))
    return jax.shard_map(
        local, mesh=mesh, in_specs=placed, out_specs=P(("var", "samp")), check_vma=False
    )
```

time: 228 us -> 277 us (1.21); the launches traced: 226 us -> 272 us
  starting transfers between devices: 27.5 us -> 89.5 us
  waiting for transfers between devices: 142 us -> 128 us
  other arithmetic: 25.1 us -> 14.3 us
  matrix products: 12.7 us -> 22.2 us
    ppermute x3 -> x6, starting transfers between devices: 9.41 us -> 84.4 us  [from_behind(): lax.ppermute(value, axis, [(source, source + steps) for source in range(l...]
    ppermute x9 -> x8, starting transfers between devices: 18.1 us -> 5.11 us  [the longest x4 4.32 us: reduce_quarters(): lax.ppermute(send.astype(jnp.bfloat16), 'samp', pairs_chip)]
    ppermute x3 -> x6, waiting for transfers between devices: 125 us -> 113 us  [from_behind(): lax.ppermute(value, axis, [(source, source + steps) for source in range(l...]
    dot_general x4, matrix products: 12.7 us -> 22.2 us  [gram_of(): lax.dot_general(left, right, (((0,), (0,)), ((), ())), preferred_element_...]
    another operation x4 -> x0, other arithmetic: 6.69 us -> none  [local(): gram = lax.dynamic_index_in_dim(jnp.stack(owned), me, 0, keepdims=False)]
    convert_element_type x4 -> x0, other arithmetic: 6.38 us -> none  [reduce_to_owner(): summed.astype(jnp.bfloat16)]
    ppermute x9 -> x8, waiting for transfers between devices: 16.8 us -> 15.3 us  [the longest x4 13.2 us: reduce_quarters(): lax.ppermute(send.astype(jnp.bfloat16), 'samp', pairs_chip)]
  transfers between devices with their start and end apart: 12 -> 14, of which waited for: 4 -> 6; matrix products, arithmetic and copies ran while one was open for 11% -> 7% of each run, Pallas kernels for 0% -> 0%
where the time goes in v6:
time: 277 us; the launch traced here: 272 us
  waiting for transfers between devices  128 us (46%)
  starting transfers between devices  89.5 us (32%)
  matrix products  22.2 us (8%)
  blocking collectives  15.9 us (6%)
  other arithmetic  14.3 us (5%)
    ppermute x6, waiting for transfers between devices, from_behind(): lax.ppermute(value, axis, [(source, source + steps) for source in range(l...  113 us
    ppermute x6, starting transfers between devices, from_behind(): lax.ppermute(value, axis, [(source, source + steps) for source in range(l...  84.4 us
    dot_general x4, matrix products, gram_of(): lax.dot_general(left, right, (((0,), (0,)), ((), ())), preferred_element_...  22.2 us
    ppermute x4, waiting for transfers between devices, reduce_quarters(): lax.ppermute(send.astype(jnp.bfloat16), 'samp', pairs_chip)  13.2 us
    psum x1, blocking collectives, local(): lax.psum((jnp.sum(present, 0), jnp.sum(present * values, 0), jnp.sum(pres...  10.2 us
    unnamed x1, blocking collectives  5.74 us
    convert_element_type x1, other arithmetic, local(): ((values - column_mean) * lax.rsqrt(spread + 1e-05) * present).astype(jnp...  5.6 us
  transfers between devices with their start and end apart: 14, of which 6 were waited for; matrix products, arithmetic and copies ran while one was open for 7% of the time, Pallas kernels for 0%

profile of v6, /device:TPU:14, one launch (start us, length us, event | category | flops | bytes accessed | tf_op | source)
XLA Modules:
  0.0 272.0 jit_solution(9257426257315046869)
XLA Ops:
  0.0 5.4 %fusion.4 = (f32[768]{0:T(1024)S(1)}, f32[768]{0:T(1024)S(1)}, f32[768]{0:T(1024)S(1)}) fusion(bf16[2048,768]{1,0:T(8,128)(2,1)} %param.2, s32[2048,768]{1,0:T(8,128)} %param.3), kind=kLoop, calls=%fused_computation.8 | loop fusion | flops 11007744 | bytes 9446400 | tf_op jit(solution)/shard_map/reduce_sum | solution.py:45
  5.4 10.2 %all-reduce.1 = (f32[768]{0:T(1024)S(1)}, f32[768]{0:T(1024)S(1)}, f32[768]{0:T(1024)S(1)}) all-reduce(f32[768]{0:T(1024)S(1)} %get-tuple-element.14, f32[768]{0:T(1024)S(1)} %get-tuple-element.15, f32[768]{0:T(1024)S(1)} %get-tuple-element.13), channel_id=1, replica_groups=mesh['var'=8,'samp'=4] {'samp'}, use_global_device_ids=true, to_apply=%region_5.0 | all-reduce | flops 2304 | bytes 18432 | tf_op jit(solution)/shard_map/psum | solution.py:44
  15.6 5.6 %fusion.2 = bf16[2048,768]{1,0:T(8,128)(2,1)} fusion(bf16[2048,768]{1,0:T(8,128)(2,1)S(1)} %copy-done, s32[2048,768]{1,0:T(8,128)} %param.3, f32[768]{0:T(1024)S(1)} %get-tuple-element.26, f32[768]{0:T(1024)S(1)} %get-tuple-element.25), kind=kLoop, calls=%fused_computation.5 | loop fusion | flops 9437184 | bytes 12589056 | tf_op jit(solution)/shard_map/convert_element_type | solution.py:51
  21.2 2.4 collective-permute-start.2
  23.6 5.3 %collective-permute-start.1 = (bf16[2048,768]{1,0:T(8,128)(2,1)}, bf16[2048,768]{1,0:T(8,128)(2,1)}, u32[]{:S(2)}, u32[]{:S(2)}) collective-permute-start(bf16[2048,768]{1,0:T(8,128)(2,1)} %fusion.2), channel_id=1, source_target_pairs={{0,12},{4,16},{8,20},{12,24},{16,28},{1,13},{5,17},{9,21},{13,25},... | collective-permute-start | bytes 9437192 | tf_op jit(solution)/shard_map/ppermute | solution.py:14
  29.0 4.2 %collective-permute-start = (bf16[2048,768]{1,0:T(8,128)(2,1)}, bf16[2048,768]{1,0:T(8,128)(2,1)}, u32[]{:S(2)}, u32[]{:S(2)}) collective-permute-start(bf16[2048,768]{1,0:T(8,128)(2,1)} %fusion.2), channel_id=1, source_target_pairs={{8,0},{12,4},{16,8},{20,12},{24,16},{28,20},{9,1},{13,5},{17,9},{2... | collective-permute-start | bytes 9437192 | tf_op jit(solution)/shard_map/ppermute | solution.py:14
  33.2 5.5 %fusion.26 = f32[768,768]{1,0:T(8,128)S(1)} fusion(bf16[2048,768]{1,0:T(8,128)(2,1)} %fusion.2), kind=kOutput, calls=%fused_computation.54 | convolution fusion | flops 2415919104 | bytes 5505024 | tf_op jit(solution)/shard_map/dot_general | solution.py:24
  38.7 0.0 copy-start.1
  38.8 0.1 fusion.5
  38.8 0.1 collective-permute-start.3
  38.9 2.1 collective-permute-done.3
  41.0 1.2 bitcast_add_fusion.3
  42.3 1.6 collective-permute-start.4
  43.8 0.6 dynamic-slice
  45.1 6.3 %collective-permute-done.4 = bf16[192,768]{1,0:T(8,128)(2,1)S(1)} collective-permute-done((bf16[192,768]{1,0:T(8,128)(2,1)S(1)}, bf16[192,768]{1,0:T(8,128)(2,1)S(1)}, u32[]{:S(2)}, u32[]{:S(2)}) %collective-permute-start.4) | collective-permute-done | bytes 294944 | tf_op jit(solution)/shard_map/ppermute | solution.py:38
  51.4 0.1 bitcast_add_fusion.7
  51.4 107.5 %collective-permute-done.2 = bf16[2048,768]{1,0:T(8,128)(2,1)} collective-permute-done((bf16[2048,768]{1,0:T(8,128)(2,1)}, bf16[2048,768]{1,0:T(8,128)(2,1)}, u32[]{:S(2)}, u32[]{:S(2)}) %collective-permute-start.2) | collective-permute-done | bytes 3145760 | tf_op jit(solution)/shard_map/ppermute | solution.py:14
  159.0 4.2 %collective-permute-done.1 = bf16[2048,768]{1,0:T(8,128)(2,1)} collective-permute-done((bf16[2048,768]{1,0:T(8,128)(2,1)}, bf16[2048,768]{1,0:T(8,128)(2,1)}, u32[]{:S(2)}, u32[]{:S(2)}) %collective-permute-start.1) | collective-permute-done | bytes 3145760 | tf_op jit(solution)/shard_map/ppermute | solution.py:14
  163.2 5.6 %fusion.27 = f32[768,768]{1,0:T(8,128)S(1)} fusion(bf16[2048,768]{1,0:T(8,128)(2,1)} %fusion.2, bf16[2048,768]{1,0:T(8,128)(2,1)} %collective-permute-done.2), kind=kOutput, calls=%fused_computation.55 | convolution fusion | flops 2415919104 | bytes 8650752 | tf_op jit(solution)/shard_map/dot_general | solution.py:24
  168.8 0.1 fusion.6
  168.8 0.1 collective-permute-start.5
  168.9 5.6 %fusion.29 = f32[768,768]{1,0:T(8,128)S(1)} fusion(bf16[2048,768]{1,0:T(8,128)(2,1)} %fusion.2, bf16[2048,768]{1,0:T(8,128)(2,1)} %collective-permute-done.1), kind=kOutput, calls=%fused_computation.57 | convolution fusion | flops 2415919104 | bytes 8650752 | tf_op jit(solution)/shard_map/dot_general | solution.py:24
  174.5 0.1 fusion.8
  174.6 0.6 collective-permute-start.9
  175.1 5.6 %fusion.28 = f32[768,768]{1,0:T(8,128)S(1)} fusion(bf16[2048,768]{1,0:T(8,128)(2,1)} %fusion.2, bf16[2048,768]{1,0:T(8,128)(2,1)} %collective-permute-done), kind=kOutput, calls=%fused_computation.56 | convolution fusion | flops 2415919104 | bytes 8650752 | tf_op jit(solution)/shard_map/dot_general | solution.py:24
  180.7 0.1 fusion.7
  180.8 0.1 collective-permute-start.7
  180.8 0.0 collective-permute-done.5
  180.9 0.1 bitcast_add_fusion.2
  181.0 0.6 collective-permute-start.6
  181.6 0.0 collective-permute-done.9
  181.6 0.1 bitcast_add_fusion
  181.7 1.6 collective-permute-start.10
  183.3 0.0 collective-permute-done.7
  183.3 0.1 bitcast_add_fusion.1
  183.5 0.6 collective-permute-start.8
  184.1 6.9 %collective-permute-done.6 = bf16[192,768]{1,0:T(8,128)(2,1)S(1)} collective-permute-done((bf16[192,768]{1,0:T(8,128)(2,1)S(1)}, bf16[192,768]{1,0:T(8,128)(2,1)S(1)}, u32[]{:S(2)}, u32[]{:S(2)}) %collective-permute-start.6) | collective-permute-done | bytes 294944 | tf_op jit(solution)/shard_map/ppermute | solution.py:38
  191.0 0.3 fusion.20
  191.2 64.1 %collective-permute-start.11 = (f32[768]{0:T(1024)S(1)}, f32[768]{0:T(1024)S(1)}, u32[]{:S(2)}, u32[]{:S(2)}) collective-permute-start(f32[768]{0:T(1024)S(1)} %get-tuple-element.17), channel_id=1, source_target_pairs={{0,4},{4,8},{8,12},{12,16},{16,20},{20,24},{24,28},{1,5},{5,9},{9,... | collective-permute-start | bytes 9224 | tf_op jit(solution)/shard_map/ppermute | solution.py:14
  255.3 0.0 collective-permute-done.10
  255.3 0.3 fusion.24
  255.6 1.9 collective-permute-start.13
  257.5 0.3 fusion.22
  257.8 6.4 %collective-permute-start.12 = (f32[768]{0:T(1024)S(1)}, f32[768]{0:T(1024)S(1)}, u32[]{:S(2)}, u32[]{:S(2)}) collective-permute-start(f32[768]{0:T(1024)S(1)} %get-tuple-element.19), channel_id=1, source_target_pairs={{0,8},{4,12},{8,16},{12,20},{16,24},{20,28},{1,9},{5,13},{9,17},{1... | collective-permute-start | bytes 9224 | tf_op jit(solution)/shard_map/ppermute | solution.py:14
  264.3 0.2 subtract_reduce_fusion
  264.5 1.1 collective-permute-done.12
  265.6 5.7 %all-reduce = f32[768]{0:T(1024)S(1)} all-reduce(f32[768]{0:T(1024)S(1)} %add_add_fusion), channel_id=2, replica_groups=mesh['var'=8,'samp'=4] {'samp'}, use_global_device_ids=true, to_apply=%region_13.14.clone | all-reduce | flops 768 | bytes 6144
  271.3 0.6 fusion.25
  (13 shorter events, 0.2 us)
Async XLA Ops:
  0.0 15.6 %copy-start = (bf16[2048,768]{1,0:T(8,128)(2,1)S(1)}, bf16[2048,768]{1,0:T(8,128)(2,1)}, u32[]{:S(2)}) copy-start(bf16[2048,768]{1,0:T(8,128)(2,1)} %param.2) | copy-start | bytes 9437188
  21.2 137.7 %collective-permute-start.2 = (bf16[2048,768]{1,0:T(8,128)(2,1)}, bf16[2048,768]{1,0:T(8,128)(2,1)}, u32[]{:S(2)}, u32[]{:S(2)}) collective-permute-start(bf16[2048,768]{1,0:T(8,128)(2,1)} %fusion.2), channel_id=1, source_target_pairs={{4,0},{8,4},{12,8},{16,12},{20,16},{24,20},{28,24},{5,1},{9,5},{13... | collective-permute-start | bytes 9437192 | tf_op jit(solution)/shard_map/ppermute | solution.py:14
  23.6 139.5 %collective-permute-start.1 = (bf16[2048,768]{1,0:T(8,128)(2,1)}, bf16[2048,768]{1,0:T(8,128)(2,1)}, u32[]{:S(2)}, u32[]{:S(2)}) collective-permute-start(bf16[2048,768]{1,0:T(8,128)(2,1)} %fusion.2), channel_id=1, source_target_pairs={{0,12},{4,16},{8,20},{12,24},{16,28},{1,13},{5,17},{9,21},{13,25},... | collective-permute-start | bytes 9437192 | tf_op jit(solution)/shard_map/ppermute | solution.py:14
  29.0 134.2 %collective-permute-start = (bf16[2048,768]{1,0:T(8,128)(2,1)}, bf16[2048,768]{1,0:T(8,128)(2,1)}, u32[]{:S(2)}, u32[]{:S(2)}) collective-permute-start(bf16[2048,768]{1,0:T(8,128)(2,1)} %fusion.2), channel_id=1, source_target_pairs={{8,0},{12,4},{16,8},{20,12},{24,16},{28,20},{9,1},{13,5},{17,9},{2... | collective-permute-start | bytes 9437192 | tf_op jit(solution)/shard_map/ppermute | solution.py:14
  38.7 5.1 %copy-start.1 = (u32[32]{0:T(128)S(1)}, u32[32]{0:T(128)}, u32[]{:S(2)}) copy-start(u32[32]{0:T(128)} %constant.114) | copy-start | bytes 388
  38.8 2.2 collective-permute-start.3
  42.3 9.1 %collective-permute-start.4 = (bf16[192,768]{1,0:T(8,128)(2,1)S(1)}, bf16[192,768]{1,0:T(8,128)(2,1)S(1)}, u32[]{:S(2)}, u32[]{:S(2)}) collective-permute-start(bf16[192,768]{1,0:T(8,128)(2,1)S(1)} %fusion.15), channel_id=1, source_target_pairs={{0,2},{1,3},{2,0},{3,1},{4,6},{5,7},{6,4},{7,5},{8,10},{9,11},{10,... | collective-permute-start | bytes 884744 | tf_op jit(solution)/shard_map/ppermute | solution.py:38
  168.8 12.0 %collective-permute-start.5 = (bf16[2,192,768]{2,1,0:T(8,128)(2,1)S(1)}, bf16[2,192,768]{2,1,0:T(8,128)(2,1)S(1)}, u32[]{:S(2)}, u32[]{:S(2)}) collective-permute-start(bf16[2,192,768]{2,1,0:T(8,128)(2,1)S(1)} %fusion.6), channel_id=1, source_target_pairs={{0,1},{1,0},{2,3},{3,2},{4,5},{5,4},{6,7},{7,6},{8,9},{9,8},{10,11... | collective-permute-start | bytes 1769480 | tf_op jit(solution)/shard_map/ppermute | solution.py:34
  174.6 7.0 %collective-permute-start.9 = (bf16[2,192,768]{2,1,0:T(8,128)(2,1)S(1)}, bf16[2,192,768]{2,1,0:T(8,128)(2,1)S(1)}, u32[]{:S(2)}, u32[]{:S(2)}) collective-permute-start(bf16[2,192,768]{2,1,0:T(8,128)(2,1)S(1)} %fusion.8), channel_id=1, source_target_pairs={{0,1},{1,0},{2,3},{3,2},{4,5},{5,4},{6,7},{7,6},{8,9},{9,8},{10,11... | collective-permute-start | bytes 1769480 | tf_op jit(solution)/shard_map/ppermute | solution.py:34
  180.8 2.6 collective-permute-start.7
  181.0 9.9 %collective-permute-start.6 = (bf16[192,768]{1,0:T(8,128)(2,1)S(1)}, bf16[192,768]{1,0:T(8,128)(2,1)S(1)}, u32[]{:S(2)}, u32[]{:S(2)}) collective-permute-start(bf16[192,768]{1,0:T(8,128)(2,1)S(1)} %fusion.16), channel_id=1, source_target_pairs={{0,2},{1,3},{2,0},{3,1},{4,6},{5,7},{6,4},{7,5},{8,10},{9,11},{10,... | collective-permute-start | bytes 884744 | tf_op jit(solution)/shard_map/ppermute | solution.py:38
  181.7 73.6 %collective-permute-start.10 = (bf16[192,768]{1,0:T(8,128)(2,1)S(1)}, bf16[192,768]{1,0:T(8,128)(2,1)S(1)}, u32[]{:S(2)}, u32[]{:S(2)}) collective-permute-start(bf16[192,768]{1,0:T(8,128)(2,1)S(1)} %fusion.18), channel_id=1, source_target_pairs={{0,2},{1,3},{2,0},{3,1},{4,6},{5,7},{6,4},{7,5},{8,10},{9,11},{10,... | collective-permute-start | bytes 884744 | tf_op jit(solution)/shard_map/ppermute | solution.py:38
  183.5 74.0 %collective-permute-start.8 = (bf16[192,768]{1,0:T(8,128)(2,1)S(1)}, bf16[192,768]{1,0:T(8,128)(2,1)S(1)}, u32[]{:S(2)}, u32[]{:S(2)}) collective-permute-start(bf16[192,768]{1,0:T(8,128)(2,1)S(1)} %fusion.17), channel_id=1, source_target_pairs={{0,2},{1,3},{2,0},{3,1},{4,6},{5,7},{6,4},{7,5},{8,10},{9,11},{10,... | collective-permute-start | bytes 884744 | tf_op jit(solution)/shard_map/ppermute | solution.py:38
  191.2 73.2 %collective-permute-start.11 = (f32[768]{0:T(1024)S(1)}, f32[768]{0:T(1024)S(1)}, u32[]{:S(2)}, u32[]{:S(2)}) collective-permute-start(f32[768]{0:T(1024)S(1)} %get-tuple-element.17), channel_id=1, source_target_pairs={{0,4},{4,8},{8,12},{12,16},{16,20},{20,24},{24,28},{1,5},{5,9},{9,... | collective-permute-start | bytes 9224 | tf_op jit(solution)/shard_map/ppermute | solution.py:14
  255.6 8.9 %collective-permute-start.13 = (f32[768]{0:T(1024)S(1)}, f32[768]{0:T(1024)S(1)}, u32[]{:S(2)}, u32[]{:S(2)}) collective-permute-start(f32[768]{0:T(1024)S(1)} %get-tuple-element.21), channel_id=1, source_target_pairs={{12,0},{16,4},{20,8},{24,12},{28,16},{13,1},{17,5},{21,9},{25,13},... | collective-permute-start | bytes 9224 | tf_op jit(solution)/shard_map/ppermute | solution.py:14
  257.8 7.8 %collective-permute-start.12 = (f32[768]{0:T(1024)S(1)}, f32[768]{0:T(1024)S(1)}, u32[]{:S(2)}, u32[]{:S(2)}) collective-permute-start(f32[768]{0:T(1024)S(1)} %get-tuple-element.19), channel_id=1, source_target_pairs={{0,8},{4,12},{8,16},{12,20},{16,24},{20,28},{1,9},{5,13},{9,17},{1... | collective-permute-start | bytes 9224 | tf_op jit(solution)/shard_map/ppermute | solution.py:14

commit v7 on v6

--- a/solution.py
+++ b/solution.py
@@ -56,10 +56,10 @@
     position = lax.axis_index("var")
     raw = {offset: from_behind(standard, "var", -PARTNER_STEP[offset]) for offset in range(1, BAND + 1)}
 
-    owned = {0: reduce_quarters(gram_of(standard, standard), n_samp)}
-    arrived, owned[0] = lax.optimization_barrier(([raw[d] for d in PROCESS_ORDER], owned[0]))
+    arrived, standard_late = lax.optimization_barrier(([raw[d] for d in PROCESS_ORDER], standard))
+    owned = {0: reduce_quarters(gram_of(standard_late, standard_late), n_samp)}
     for offset, partner in zip(PROCESS_ORDER, arrived):
-        owned[offset] = reduce_quarters(gram_of(standard, partner), n_samp)
+        owned[offset] = reduce_quarters(gram_of(standard_late, partner), n_samp)
 
     row_total = jnp.sum(adjusted_r2(owned[0], samples), 1)
     incoming = jnp.zeros((block_width,), jnp.float32)

time: 277 us -> 222 us (0.80); the launches traced: 272 us -> 221 us
  starting transfers between devices: 89.5 us -> 26.5 us
  waiting for transfers between devices: 128 us -> 142 us
    ppermute x6, starting transfers between devices: 84.4 us -> 20.9 us  [from_behind(): lax.ppermute(value, axis, [(source, source + steps) for source in range(l...]
    ppermute x6, waiting for transfers between devices: 113 us -> 130 us  [from_behind(): lax.ppermute(value, axis, [(source, source + steps) for source in range(l...]
  transfers between devices with their start and end apart: 14 -> 14, of which waited for: 6 -> 8; matrix products, arithmetic and copies ran while one was open for 7% -> 6% of each run, Pallas kernels for 0% -> 0%
where the time goes in v7:
time: 222 us; the launch traced here: 221 us
  waiting for transfers between devices  142 us (64%)
  starting transfers between devices  26.5 us (12%)
  matrix products  21.3 us (10%)
  blocking collectives  16 us (7%)
  other arithmetic  13.2 us (6%)
    ppermute x6, waiting for transfers between devices, from_behind(): lax.ppermute(value, axis, [(source, source + steps) for source in range(l...  130 us
    dot_general x4, matrix products, gram_of(): lax.dot_general(left, right, (((0,), (0,)), ((), ())), preferred_element_...  21.3 us
    ppermute x6, starting transfers between devices, from_behind(): lax.ppermute(value, axis, [(source, source + steps) for source in range(l...  20.9 us
    ppermute x4, waiting for transfers between devices, reduce_quarters(): lax.ppermute(send.astype(jnp.bfloat16), 'samp', pairs_chip)  12.5 us
    psum x1, blocking collectives, local(): lax.psum((jnp.sum(present, 0), jnp.sum(present * values, 0), jnp.sum(pres...  10.2 us
    unnamed x1, blocking collectives  5.85 us
    convert_element_type x1, other arithmetic, local(): ((values - column_mean) * lax.rsqrt(spread + 1e-05) * present).astype(jnp...  5.6 us
    reduce_sum x1, other arithmetic, local(): jnp.sum(present * values, 0)  5.42 us
  transfers between devices with their start and end apart: 14, of which 8 were waited for; matrix products, arithmetic and copies ran while one was open for 6% of the time, Pallas kernels for 0%

profile of v7, /device:TPU:14, one launch (start us, length us, event | category | flops | bytes accessed | tf_op | source)
XLA Modules:
  0.0 221.1 jit_solution(15621392096819268040)
XLA Ops:
  0.0 5.4 %fusion.4 = (f32[768]{0:T(1024)S(1)}, f32[768]{0:T(1024)S(1)}, f32[768]{0:T(1024)S(1)}) fusion(bf16[2048,768]{1,0:T(8,128)(2,1)} %param.2, s32[2048,768]{1,0:T(8,128)} %param.3), kind=kLoop, calls=%fused_computation.8 | loop fusion | flops 11007744 | bytes 9446400 | tf_op jit(solution)/shard_map/reduce_sum | solution.py:45
  5.4 10.2 %all-reduce.1 = (f32[768]{0:T(1024)S(1)}, f32[768]{0:T(1024)S(1)}, f32[768]{0:T(1024)S(1)}) all-reduce(f32[768]{0:T(1024)S(1)} %get-tuple-element.14, f32[768]{0:T(1024)S(1)} %get-tuple-element.15, f32[768]{0:T(1024)S(1)} %get-tuple-element.13), channel_id=1, replica_groups=mesh['var'=8,'samp'=4] {'samp'}, use_global_device_ids=true, to_apply=%region_5.0 | all-reduce | flops 2304 | bytes 18432 | tf_op jit(solution)/shard_map/psum | solution.py:44
  15.6 0.0 copy-start.1
  15.6 5.6 %fusion.2 = bf16[2048,768]{1,0:T(8,128)(2,1)} fusion(bf16[2048,768]{1,0:T(8,128)(2,1)S(1)} %copy-done, s32[2048,768]{1,0:T(8,128)} %param.3, f32[768]{0:T(1024)S(1)} %get-tuple-element.26, f32[768]{0:T(1024)S(1)} %get-tuple-element.25), kind=kLoop, calls=%fused_computation.5 | loop fusion | flops 9437184 | bytes 12589056 | tf_op jit(solution)/shard_map/convert_element_type | solution.py:51
  21.2 2.3 %collective-permute-start = (bf16[2048,768]{1,0:T(8,128)(2,1)}, bf16[2048,768]{1,0:T(8,128)(2,1)S(1)}, u32[]{:S(2)}, u32[]{:S(2)}) collective-permute-start(bf16[2048,768]{1,0:T(8,128)(2,1)} %fusion.2), channel_id=1, source_target_pairs={{8,0},{12,4},{16,8},{20,12},{24,16},{28,20},{9,1},{13,5},{17,9},{2... | collective-permute-start | bytes 9437192 | tf_op jit(solution)/shard_map/ppermute | solution.py:14
  23.6 4.6 %collective-permute-start.1 = (bf16[2048,768]{1,0:T(8,128)(2,1)}, bf16[2048,768]{1,0:T(8,128)(2,1)}, u32[]{:S(2)}, u32[]{:S(2)}) collective-permute-start(bf16[2048,768]{1,0:T(8,128)(2,1)} %fusion.2), channel_id=1, source_target_pairs={{0,12},{4,16},{8,20},{12,24},{16,28},{1,13},{5,17},{9,21},{13,25},... | collective-permute-start | bytes 9437192 | tf_op jit(solution)/shard_map/ppermute | solution.py:14
  28.2 4.1 %collective-permute-start.2 = (bf16[2048,768]{1,0:T(8,128)(2,1)}, bf16[2048,768]{1,0:T(8,128)(2,1)}, u32[]{:S(2)}, u32[]{:S(2)}) collective-permute-start(bf16[2048,768]{1,0:T(8,128)(2,1)} %fusion.2), channel_id=1, source_target_pairs={{4,0},{8,4},{12,8},{16,12},{20,16},{24,20},{28,24},{5,1},{9,5},{13... | collective-permute-start | bytes 9437192 | tf_op jit(solution)/shard_map/ppermute | solution.py:14
  32.4 0.6 dynamic-slice
  33.6 59.1 %collective-permute-done = bf16[2048,768]{1,0:T(8,128)(2,1)S(1)} collective-permute-done((bf16[2048,768]{1,0:T(8,128)(2,1)}, bf16[2048,768]{1,0:T(8,128)(2,1)S(1)}, u32[]{:S(2)}, u32[]{:S(2)}) %collective-permute-start) | collective-permute-done | bytes 3145760 | tf_op jit(solution)/shard_map/ppermute | solution.py:14
  92.7 69.5 %collective-permute-done.1 = bf16[2048,768]{1,0:T(8,128)(2,1)} collective-permute-done((bf16[2048,768]{1,0:T(8,128)(2,1)}, bf16[2048,768]{1,0:T(8,128)(2,1)}, u32[]{:S(2)}, u32[]{:S(2)}) %collective-permute-start.1) | collective-permute-done | bytes 3145760 | tf_op jit(solution)/shard_map/ppermute | solution.py:14
  162.2 1.0 collective-permute-done.2
  163.2 5.6 %fusion.28 = f32[768,768]{1,0:T(8,128)S(1)} fusion(bf16[2048,768]{1,0:T(8,128)(2,1)} %fusion.2), kind=kOutput, calls=%fused_computation.56 | convolution fusion | flops 2415919104 | bytes 5505024 | tf_op jit(solution)/shard_map/dot_general | solution.py:24
  168.8 5.6 %fusion.31 = f32[768,768]{1,0:T(8,128)S(1)} fusion(bf16[2048,768]{1,0:T(8,128)(2,1)} %fusion.2, bf16[2048,768]{1,0:T(8,128)(2,1)} %collective-permute-done.1), kind=kOutput, calls=%fused_computation.59 | convolution fusion | flops 2415919104 | bytes 8650752 | tf_op jit(solution)/shard_map/dot_general | solution.py:24
  174.3 0.1 fusion.8
  174.4 0.1 collective-permute-start.9
  174.5 5.6 %fusion.29 = f32[768,768]{1,0:T(8,128)S(1)} fusion(bf16[2048,768]{1,0:T(8,128)(2,1)} %fusion.2, bf16[2048,768]{1,0:T(8,128)(2,1)} %collective-permute-done.2), kind=kOutput, calls=%fused_computation.57 | convolution fusion | flops 2415919104 | bytes 8650752 | tf_op jit(solution)/shard_map/dot_general | solution.py:24
  180.1 0.1 fusion.6
  180.2 0.6 collective-permute-start.5
  180.7 4.6 %fusion.30 = f32[768,768]{1,0:T(8,128)S(1)} fusion(bf16[2048,768]{1,0:T(8,128)(2,1)} %fusion.2, bf16[2048,768]{1,0:T(8,128)(2,1)S(1)} %collective-permute-done), kind=kOutput, calls=%fused_computation.58 | convolution fusion | flops 2415919104 | bytes 8650752 | tf_op jit(solution)/shard_map/dot_general | solution.py:24
  185.3 0.1 fusion.7
  185.4 0.1 collective-permute-start.7
  185.5 0.1 fusion.5
  185.6 0.5 collective-permute-start.3
  186.1 0.1 bitcast_add_fusion
  186.3 0.6 collective-permute-start.10
  186.8 0.0 collective-permute-done.5
  186.8 0.1 bitcast_add_fusion.2
  187.0 1.6 collective-permute-start.6
  188.6 0.1 bitcast_add_fusion.1
  188.7 0.6 collective-permute-start.8
  189.3 0.0 collective-permute-done.3
  189.3 0.1 bitcast_add_fusion.3
  189.5 1.6 collective-permute-start.4
  191.1 5.2 %collective-permute-done.10 = bf16[192,768]{1,0:T(8,128)(2,1)S(1)} collective-permute-done((bf16[192,768]{1,0:T(8,128)(2,1)S(1)}, bf16[192,768]{1,0:T(8,128)(2,1)S(1)}, u32[]{:S(2)}, u32[]{:S(2)}) %collective-permute-start.10) | collective-permute-done | bytes 294944 | tf_op jit(solution)/shard_map/ppermute | solution.py:38
  196.2 0.3 fusion.26
  196.5 1.9 collective-permute-start.13
  198.4 4.1 %collective-permute-done.6 = bf16[192,768]{1,0:T(8,128)(2,1)S(1)} collective-permute-done((bf16[192,768]{1,0:T(8,128)(2,1)S(1)}, bf16[192,768]{1,0:T(8,128)(2,1)S(1)}, u32[]{:S(2)}, u32[]{:S(2)}) %collective-permute-start.6) | collective-permute-done | bytes 294944 | tf_op jit(solution)/shard_map/ppermute | solution.py:38
  202.5 0.3 fusion.22
  202.8 4.4 %collective-permute-start.11 = (f32[768]{0:T(1024)S(1)}, f32[768]{0:T(1024)S(1)}, u32[]{:S(2)}, u32[]{:S(2)}) collective-permute-start(f32[768]{0:T(1024)S(1)} %get-tuple-element.17), channel_id=1, source_target_pairs={{0,4},{4,8},{8,12},{12,16},{16,20},{20,24},{24,28},{1,5},{5,9},{9,... | collective-permute-start | bytes 9224 | tf_op jit(solution)/shard_map/ppermute | solution.py:14
  207.3 1.6 collective-permute-done.8
  208.9 0.3 fusion.24
  209.1 3.5 %collective-permute-start.12 = (f32[768]{0:T(1024)S(1)}, f32[768]{0:T(1024)S(1)}, u32[]{:S(2)}, u32[]{:S(2)}) collective-permute-start(f32[768]{0:T(1024)S(1)} %get-tuple-element.19), channel_id=1, source_target_pairs={{0,8},{4,12},{8,16},{12,20},{16,24},{20,28},{1,9},{5,13},{9,17},{1... | collective-permute-start | bytes 9224 | tf_op jit(solution)/shard_map/ppermute | solution.py:14
  212.6 1.6 collective-permute-done.4
  214.2 0.2 subtract_reduce_fusion
  214.5 0.0 collective-permute-done.13
  214.5 0.2 collective-permute-done.12
  214.6 5.8 %all-reduce = f32[768]{0:T(1024)S(1)} all-reduce(f32[768]{0:T(1024)S(1)} %add_add_fusion), channel_id=2, replica_groups=mesh['var'=8,'samp'=4] {'samp'}, use_global_device_ids=true, to_apply=%region_13.14.clone | all-reduce | flops 768 | bytes 6144
  220.5 0.6 fusion.27
  (12 shorter events, 0.2 us)
Async XLA Ops:
  0.0 15.6 %copy-start = (bf16[2048,768]{1,0:T(8,128)(2,1)S(1)}, bf16[2048,768]{1,0:T(8,128)(2,1)}, u32[]{:S(2)}) copy-start(bf16[2048,768]{1,0:T(8,128)(2,1)} %param.2) | copy-start | bytes 9437188
  15.6 16.8 %copy-start.1 = (u32[32]{0:T(128)S(1)}, u32[32]{0:T(128)}, u32[]{:S(2)}) copy-start(u32[32]{0:T(128)} %constant.114) | copy-start | bytes 388
  21.2 71.5 %collective-permute-start = (bf16[2048,768]{1,0:T(8,128)(2,1)}, bf16[2048,768]{1,0:T(8,128)(2,1)S(1)}, u32[]{:S(2)}, u32[]{:S(2)}) collective-permute-start(bf16[2048,768]{1,0:T(8,128)(2,1)} %fusion.2), channel_id=1, source_target_pairs={{8,0},{12,4},{16,8},{20,12},{24,16},{28,20},{9,1},{13,5},{17,9},{2... | collective-permute-start | bytes 9437192 | tf_op jit(solution)/shard_map/ppermute | solution.py:14
  23.6 138.6 %collective-permute-start.1 = (bf16[2048,768]{1,0:T(8,128)(2,1)}, bf16[2048,768]{1,0:T(8,128)(2,1)}, u32[]{:S(2)}, u32[]{:S(2)}) collective-permute-start(bf16[2048,768]{1,0:T(8,128)(2,1)} %fusion.2), channel_id=1, source_target_pairs={{0,12},{4,16},{8,20},{12,24},{16,28},{1,13},{5,17},{9,21},{13,25},... | collective-permute-start | bytes 9437192 | tf_op jit(solution)/shard_map/ppermute | solution.py:14
  28.2 135.0 %collective-permute-start.2 = (bf16[2048,768]{1,0:T(8,128)(2,1)}, bf16[2048,768]{1,0:T(8,128)(2,1)}, u32[]{:S(2)}, u32[]{:S(2)}) collective-permute-start(bf16[2048,768]{1,0:T(8,128)(2,1)} %fusion.2), channel_id=1, source_target_pairs={{4,0},{8,4},{12,8},{16,12},{20,16},{24,20},{28,24},{5,1},{9,5},{13... | collective-permute-start | bytes 9437192 | tf_op jit(solution)/shard_map/ppermute | solution.py:14
  174.4 11.7 %collective-permute-start.9 = (bf16[2,192,768]{2,1,0:T(8,128)(2,1)S(1)}, bf16[2,192,768]{2,1,0:T(8,128)(2,1)S(1)}, u32[]{:S(2)}, u32[]{:S(2)}) collective-permute-start(bf16[2,192,768]{2,1,0:T(8,128)(2,1)S(1)} %fusion.8), channel_id=1, source_target_pairs={{0,1},{1,0},{2,3},{3,2},{4,5},{5,4},{6,7},{7,6},{8,9},{9,8},{10,11... | collective-permute-start | bytes 1769480 | tf_op jit(solution)/shard_map/ppermute | solution.py:34
  180.2 6.7 %collective-permute-start.5 = (bf16[2,192,768]{2,1,0:T(8,128)(2,1)S(1)}, bf16[2,192,768]{2,1,0:T(8,128)(2,1)S(1)}, u32[]{:S(2)}, u32[]{:S(2)}) collective-permute-start(bf16[2,192,768]{2,1,0:T(8,128)(2,1)S(1)} %fusion.6), channel_id=1, source_target_pairs={{0,1},{1,0},{2,3},{3,2},{4,5},{5,4},{6,7},{7,6},{8,9},{9,8},{10,11... | collective-permute-start | bytes 1769480 | tf_op jit(solution)/shard_map/ppermute | solution.py:34
  185.4 3.2 %collective-permute-start.7 = (bf16[2,192,768]{2,1,0:T(8,128)(2,1)S(1)}, bf16[2,192,768]{2,1,0:T(8,128)(2,1)S(1)}, u32[]{:S(2)}, u32[]{:S(2)}) collective-permute-start(bf16[2,192,768]{2,1,0:T(8,128)(2,1)S(1)} %fusion.7), channel_id=1, source_target_pairs={{0,1},{1,0},{2,3},{3,2},{4,5},{5,4},{6,7},{7,6},{8,9},{9,8},{10,11... | collective-permute-start | bytes 1769480 | tf_op jit(solution)/shard_map/ppermute | solution.py:34
  185.6 3.8 %collective-permute-start.3 = (bf16[2,192,768]{2,1,0:T(8,128)(2,1)S(1)}, bf16[2,192,768]{2,1,0:T(8,128)(2,1)S(1)}, u32[]{:S(2)}, u32[]{:S(2)}) collective-permute-start(bf16[2,192,768]{2,1,0:T(8,128)(2,1)S(1)} %fusion.5), channel_id=1, source_target_pairs={{0,1},{1,0},{2,3},{3,2},{4,5},{5,4},{6,7},{7,6},{8,9},{9,8},{10,11... | collective-permute-start | bytes 1769480 | tf_op jit(solution)/shard_map/ppermute | solution.py:34
  186.3 9.9 %collective-permute-start.10 = (bf16[192,768]{1,0:T(8,128)(2,1)S(1)}, bf16[192,768]{1,0:T(8,128)(2,1)S(1)}, u32[]{:S(2)}, u32[]{:S(2)}) collective-permute-start(bf16[192,768]{1,0:T(8,128)(2,1)S(1)} %fusion.20), channel_id=1, source_target_pairs={{0,2},{1,3},{2,0},{3,1},{4,6},{5,7},{6,4},{7,5},{8,10},{9,11},{10,... | collective-permute-start | bytes 884744 | tf_op jit(solution)/shard_map/ppermute | solution.py:38
  187.0 15.5 %collective-permute-start.6 = (bf16[192,768]{1,0:T(8,128)(2,1)S(1)}, bf16[192,768]{1,0:T(8,128)(2,1)S(1)}, u32[]{:S(2)}, u32[]{:S(2)}) collective-permute-start(bf16[192,768]{1,0:T(8,128)(2,1)S(1)} %fusion.18), channel_id=1, source_target_pairs={{0,2},{1,3},{2,0},{3,1},{4,6},{5,7},{6,4},{7,5},{8,10},{9,11},{10,... | collective-permute-start | bytes 884744 | tf_op jit(solution)/shard_map/ppermute | solution.py:38
  188.7 20.1 %collective-permute-start.8 = (bf16[192,768]{1,0:T(8,128)(2,1)S(1)}, bf16[192,768]{1,0:T(8,128)(2,1)S(1)}, u32[]{:S(2)}, u32[]{:S(2)}) collective-permute-start(bf16[192,768]{1,0:T(8,128)(2,1)S(1)} %fusion.19), channel_id=1, source_target_pairs={{0,2},{1,3},{2,0},{3,1},{4,6},{5,7},{6,4},{7,5},{8,10},{9,11},{10,... | collective-permute-start | bytes 884744 | tf_op jit(solution)/shard_map/ppermute | solution.py:38
  189.5 24.8 %collective-permute-start.4 = (bf16[192,768]{1,0:T(8,128)(2,1)S(1)}, bf16[192,768]{1,0:T(8,128)(2,1)S(1)}, u32[]{:S(2)}, u32[]{:S(2)}) collective-permute-start(bf16[192,768]{1,0:T(8,128)(2,1)S(1)} %fusion.17), channel_id=1, source_target_pairs={{0,2},{1,3},{2,0},{3,1},{4,6},{5,7},{6,4},{7,5},{8,10},{9,11},{10,... | collective-permute-start | bytes 884744 | tf_op jit(solution)/shard_map/ppermute | solution.py:38
  196.5 18.0 %collective-permute-start.13 = (f32[768]{0:T(1024)S(1)}, f32[768]{0:T(1024)S(1)}, u32[]{:S(2)}, u32[]{:S(2)}) collective-permute-start(f32[768]{0:T(1024)S(1)} %get-tuple-element.21), channel_id=1, source_target_pairs={{12,0},{16,4},{20,8},{24,12},{28,16},{13,1},{17,5},{21,9},{25,13},... | collective-permute-start | bytes 9224 | tf_op jit(solution)/shard_map/ppermute | solution.py:14
  202.8 11.7 %collective-permute-start.11 = (f32[768]{0:T(1024)S(1)}, f32[768]{0:T(1024)S(1)}, u32[]{:S(2)}, u32[]{:S(2)}) collective-permute-start(f32[768]{0:T(1024)S(1)} %get-tuple-element.17), channel_id=1, source_target_pairs={{0,4},{4,8},{8,12},{12,16},{16,20},{20,24},{24,28},{1,5},{5,9},{9,... | collective-permute-start | bytes 9224 | tf_op jit(solution)/shard_map/ppermute | solution.py:14
  209.1 5.5 %collective-permute-start.12 = (f32[768]{0:T(1024)S(1)}, f32[768]{0:T(1024)S(1)}, u32[]{:S(2)}, u32[]{:S(2)}) collective-permute-start(f32[768]{0:T(1024)S(1)} %get-tuple-element.19), channel_id=1, source_target_pairs={{0,8},{4,12},{8,16},{12,20},{16,24},{20,28},{1,9},{5,13},{9,17},{1... | collective-permute-start | bytes 9224 | tf_op jit(solution)/shard_map/ppermute | solution.py:14

commit v8 on v7

--- a/solution.py
+++ b/solution.py
@@ -56,8 +56,10 @@
     position = lax.axis_index("var")
     raw = {offset: from_behind(standard, "var", -PARTNER_STEP[offset]) for offset in range(1, BAND + 1)}
 
-    arrived, standard_late = lax.optimization_barrier(([raw[d] for d in PROCESS_ORDER], standard))
-    owned = {0: reduce_quarters(gram_of(standard_late, standard_late), n_samp)}
+    arrived, gram_same, standard_late = lax.optimization_barrier(
+        ([raw[d] for d in PROCESS_ORDER], gram_of(standard, standard), standard)
+    )
+    owned = {0: reduce_quarters(gram_same, n_samp)}
     for offset, partner in zip(PROCESS_ORDER, arrived):
         owned[offset] = reduce_quarters(gram_of(standard_late, partner), n_samp)
 

time: 222 us -> 223 us (level)
  transfers between devices with their start and end apart: 14 -> 14, of which waited for: 8 -> 7; matrix products, arithmetic and copies ran while one was open for 6% -> 11% of each run, Pallas kernels for 0% -> 0%
where the time goes in v8:
time: 223 us
  waiting for transfers between devices  144 us (65%)
  starting transfers between devices  26 us (12%)
  matrix products  21.3 us (10%)
  blocking collectives  16 us (7%)
  other arithmetic  13.2 us (6%)
    ppermute x6, waiting for transfers between devices, from_behind(): lax.ppermute(value, axis, [(source, source + steps) for source in range(l...  130 us
    dot_general x4, matrix products, gram_of(): lax.dot_general(left, right, (((0,), (0,)), ((), ())), preferred_element_...  21.3 us
    ppermute x6, starting transfers between devices, from_behind(): lax.ppermute(value, axis, [(source, source + steps) for source in range(l...  20.4 us
    ppermute x4, waiting for transfers between devices, reduce_quarters(): lax.ppermute(send.astype(jnp.bfloat16), 'samp', pairs_chip)  14.7 us
    psum x1, blocking collectives, local(): lax.psum((jnp.sum(present, 0), jnp.sum(present * values, 0), jnp.sum(pres...  10.2 us
    unnamed x1, blocking collectives  5.85 us
    convert_element_type x1, other arithmetic, local(): ((values - column_mean) * lax.rsqrt(spread + 1e-05) * present).astype(jnp...  5.6 us
    reduce_sum x1, other arithmetic, local(): jnp.sum(present * values, 0)  5.42 us
  transfers between devices with their start and end apart: 14, of which 7 were waited for; matrix products, arithmetic and copies ran while one was open for 11% of the time, Pallas kernels for 0%

profile of v8, /device:TPU:14, one launch (start us, length us, event | category | flops | bytes accessed | tf_op | source)
XLA Modules:
  0.0 222.9 jit_solution(6317566232214882421)
XLA Ops:
  0.0 5.4 %fusion.4 = (f32[768]{0:T(1024)S(1)}, f32[768]{0:T(1024)S(1)}, f32[768]{0:T(1024)S(1)}) fusion(bf16[2048,768]{1,0:T(8,128)(2,1)} %param.2, s32[2048,768]{1,0:T(8,128)} %param.3), kind=kLoop, calls=%fused_computation.8 | loop fusion | flops 11007744 | bytes 9446400 | tf_op jit(solution)/shard_map/reduce_sum | solution.py:45
  5.4 10.2 %all-reduce.1 = (f32[768]{0:T(1024)S(1)}, f32[768]{0:T(1024)S(1)}, f32[768]{0:T(1024)S(1)}) all-reduce(f32[768]{0:T(1024)S(1)} %get-tuple-element.16, f32[768]{0:T(1024)S(1)} %get-tuple-element.17, f32[768]{0:T(1024)S(1)} %get-tuple-element.15), channel_id=1, replica_groups=mesh['var'=8,'samp'=4] {'samp'}, use_global_device_ids=true, to_apply=%region_5.0 | all-reduce | flops 2304 | bytes 18432 | tf_op jit(solution)/shard_map/psum | solution.py:44
  15.6 0.0 copy-start.1
  15.6 5.6 %fusion.2 = bf16[2048,768]{1,0:T(8,128)(2,1)} fusion(bf16[2048,768]{1,0:T(8,128)(2,1)S(1)} %copy-done, s32[2048,768]{1,0:T(8,128)} %param.3, f32[768]{0:T(1024)S(1)} %get-tuple-element.28, f32[768]{0:T(1024)S(1)} %get-tuple-element.27), kind=kLoop, calls=%fused_computation.5 | loop fusion | flops 9437184 | bytes 12589056 | tf_op jit(solution)/shard_map/convert_element_type | solution.py:51
  21.2 2.3 %collective-permute-start = (bf16[2048,768]{1,0:T(8,128)(2,1)}, bf16[2048,768]{1,0:T(8,128)(2,1)}, u32[]{:S(2)}, u32[]{:S(2)}) collective-permute-start(bf16[2048,768]{1,0:T(8,128)(2,1)} %fusion.2), channel_id=1, source_target_pairs={{8,0},{12,4},{16,8},{20,12},{24,16},{28,20},{9,1},{13,5},{17,9},{2... | collective-permute-start | bytes 9437192 | tf_op jit(solution)/shard_map/ppermute | solution.py:14
  23.6 6.1 %collective-permute-start.1 = (bf16[2048,768]{1,0:T(8,128)(2,1)}, bf16[2048,768]{1,0:T(8,128)(2,1)S(1)}, u32[]{:S(2)}, u32[]{:S(2)}) collective-permute-start(bf16[2048,768]{1,0:T(8,128)(2,1)} %fusion.2), channel_id=1, source_target_pairs={{0,12},{4,16},{8,20},{12,24},{16,28},{1,13},{5,17},{9,21},{13,25},... | collective-permute-start | bytes 9437192 | tf_op jit(solution)/shard_map/ppermute | solution.py:14
  29.7 2.1 collective-permute-start.2
  31.9 0.6 dynamic-slice
  33.1 5.6 %fusion.28 = f32[768,768]{1,0:T(8,128)S(1)} fusion(bf16[2048,768]{1,0:T(8,128)(2,1)} %fusion.2), kind=kOutput, calls=%fused_computation.56 | convolution fusion | flops 2415919104 | bytes 5505024 | tf_op jit(solution)/shard_map/dot_general | solution.py:24
  38.7 54.1 %collective-permute-done = bf16[2048,768]{1,0:T(8,128)(2,1)} collective-permute-done((bf16[2048,768]{1,0:T(8,128)(2,1)}, bf16[2048,768]{1,0:T(8,128)(2,1)}, u32[]{:S(2)}, u32[]{:S(2)}) %collective-permute-start) | collective-permute-done | bytes 3145760 | tf_op jit(solution)/shard_map/ppermute | solution.py:14
  92.8 69.4 %collective-permute-done.1 = bf16[2048,768]{1,0:T(8,128)(2,1)S(1)} collective-permute-done((bf16[2048,768]{1,0:T(8,128)(2,1)}, bf16[2048,768]{1,0:T(8,128)(2,1)S(1)}, u32[]{:S(2)}, u32[]{:S(2)}) %collective-permute-start.1) | collective-permute-done | bytes 3145760 | tf_op jit(solution)/shard_map/ppermute | solution.py:14
  162.2 1.0 collective-permute-done.2
  163.2 0.1 fusion.5
  163.3 0.1 collective-permute-start.3
  163.3 5.6 %fusion.30 = f32[768,768]{1,0:T(8,128)S(1)} fusion(bf16[2048,768]{1,0:T(8,128)(2,1)} %fusion.2, bf16[2048,768]{1,0:T(8,128)(2,1)} %collective-permute-done), kind=kOutput, calls=%fused_computation.58 | convolution fusion | flops 2415919104 | bytes 8650752 | tf_op jit(solution)/shard_map/dot_general | solution.py:24
  168.9 0.1 fusion.7
  169.0 0.6 collective-permute-start.7
  169.6 5.6 %fusion.29 = f32[768,768]{1,0:T(8,128)S(1)} fusion(bf16[2048,768]{1,0:T(8,128)(2,1)} %fusion.2, bf16[2048,768]{1,0:T(8,128)(2,1)} %collective-permute-done.2), kind=kOutput, calls=%fused_computation.57 | convolution fusion | flops 2415919104 | bytes 8650752 | tf_op jit(solution)/shard_map/dot_general | solution.py:24
  175.1 0.1 fusion.6
  175.2 0.1 collective-permute-start.5
  175.3 4.6 %fusion.31 = f32[768,768]{1,0:T(8,128)S(1)} fusion(bf16[2048,768]{1,0:T(8,128)(2,1)} %fusion.2, bf16[2048,768]{1,0:T(8,128)(2,1)S(1)} %collective-permute-done.1), kind=kOutput, calls=%fused_computation.59 | convolution fusion | flops 2415919104 | bytes 8650752 | tf_op jit(solution)/shard_map/dot_general | solution.py:24
  179.9 0.1 fusion.8
  180.0 0.6 collective-permute-start.9
  180.5 0.0 collective-permute-done.3
  180.5 0.1 bitcast_add_fusion.3
  180.7 0.6 collective-permute-start.4
  181.3 0.1 bitcast_add_fusion.1
  181.4 1.6 collective-permute-start.8
  183.0 0.1 bitcast_add_fusion.2
  183.2 0.6 collective-permute-start.6
  183.7 0.1 bitcast_add_fusion
  183.9 1.6 collective-permute-start.10
  185.5 11.5 %collective-permute-done.8 = bf16[192,768]{1,0:T(8,128)(2,1)S(1)} collective-permute-done((bf16[192,768]{1,0:T(8,128)(2,1)S(1)}, bf16[192,768]{1,0:T(8,128)(2,1)S(1)}, u32[]{:S(2)}, u32[]{:S(2)}) %collective-permute-start.8) | collective-permute-done | bytes 294944 | tf_op jit(solution)/shard_map/ppermute | solution.py:38
  197.0 0.3 fusion.24
  197.3 3.5 %collective-permute-start.12 = (f32[768]{0:T(1024)S(1)}, f32[768]{0:T(1024)S(1)}, u32[]{:S(2)}, u32[]{:S(2)}) collective-permute-start(f32[768]{0:T(1024)S(1)} %get-tuple-element.21), channel_id=1, source_target_pairs={{0,8},{4,12},{8,16},{12,20},{16,24},{20,28},{1,9},{5,13},{9,17},{1... | collective-permute-start | bytes 9224 | tf_op jit(solution)/shard_map/ppermute | solution.py:14
  200.7 2.5 %collective-permute-done.6 = bf16[192,768]{1,0:T(8,128)(2,1)S(1)} collective-permute-done((bf16[192,768]{1,0:T(8,128)(2,1)S(1)}, bf16[192,768]{1,0:T(8,128)(2,1)S(1)}, u32[]{:S(2)}, u32[]{:S(2)}) %collective-permute-start.6) | collective-permute-done | bytes 294944 | tf_op jit(solution)/shard_map/ppermute | solution.py:38
  203.3 0.3 fusion.22
  203.6 4.4 %collective-permute-start.11 = (f32[768]{0:T(1024)S(1)}, f32[768]{0:T(1024)S(1)}, u32[]{:S(2)}, u32[]{:S(2)}) collective-permute-start(f32[768]{0:T(1024)S(1)} %get-tuple-element.19), channel_id=1, source_target_pairs={{0,4},{4,8},{8,12},{12,16},{16,20},{20,24},{24,28},{1,5},{5,9},{9,... | collective-permute-start | bytes 9224 | tf_op jit(solution)/shard_map/ppermute | solution.py:14
  208.0 0.7 collective-permute-done.10
  208.7 0.3 fusion.26
  208.9 1.9 collective-permute-start.13
  210.9 0.0 collective-permute-done.4
  210.9 0.2 subtract_reduce_fusion
  211.1 0.0 collective-permute-done.12
  211.1 0.0 collective-permute-done.11
  211.1 5.3 %collective-permute-done.13 = f32[768]{0:T(1024)S(1)} collective-permute-done((f32[768]{0:T(1024)S(1)}, f32[768]{0:T(1024)S(1)}, u32[]{:S(2)}, u32[]{:S(2)}) %collective-permute-start.13) | collective-permute-done | bytes 3104 | tf_op jit(solution)/shard_map/ppermute | solution.py:14
  216.4 5.8 %all-reduce = f32[768]{0:T(1024)S(1)} all-reduce(f32[768]{0:T(1024)S(1)} %add_add_fusion), channel_id=2, replica_groups=mesh['var'=8,'samp'=4] {'samp'}, use_global_device_ids=true, to_apply=%region_13.14.clone | all-reduce | flops 768 | bytes 6144
  222.3 0.6 fusion.27
  (12 shorter events, 0.2 us)
Async XLA Ops:
  0.0 15.6 %copy-start = (bf16[2048,768]{1,0:T(8,128)(2,1)S(1)}, bf16[2048,768]{1,0:T(8,128)(2,1)}, u32[]{:S(2)}) copy-start(bf16[2048,768]{1,0:T(8,128)(2,1)} %param.2) | copy-start | bytes 9437188
  15.6 16.3 %copy-start.1 = (u32[32]{0:T(128)S(1)}, u32[32]{0:T(128)}, u32[]{:S(2)}) copy-start(u32[32]{0:T(128)} %constant.114) | copy-start | bytes 388
  21.2 71.6 %collective-permute-start = (bf16[2048,768]{1,0:T(8,128)(2,1)}, bf16[2048,768]{1,0:T(8,128)(2,1)}, u32[]{:S(2)}, u32[]{:S(2)}) collective-permute-start(bf16[2048,768]{1,0:T(8,128)(2,1)} %fusion.2), channel_id=1, source_target_pairs={{8,0},{12,4},{16,8},{20,12},{24,16},{28,20},{9,1},{13,5},{17,9},{2... | collective-permute-start | bytes 9437192 | tf_op jit(solution)/shard_map/ppermute | solution.py:14
  23.6 138.6 %collective-permute-start.1 = (bf16[2048,768]{1,0:T(8,128)(2,1)}, bf16[2048,768]{1,0:T(8,128)(2,1)S(1)}, u32[]{:S(2)}, u32[]{:S(2)}) collective-permute-start(bf16[2048,768]{1,0:T(8,128)(2,1)} %fusion.2), channel_id=1, source_target_pairs={{0,12},{4,16},{8,20},{12,24},{16,28},{1,13},{5,17},{9,21},{13,25},... | collective-permute-start | bytes 9437192 | tf_op jit(solution)/shard_map/ppermute | solution.py:14
  29.7 133.5 %collective-permute-start.2 = (bf16[2048,768]{1,0:T(8,128)(2,1)}, bf16[2048,768]{1,0:T(8,128)(2,1)}, u32[]{:S(2)}, u32[]{:S(2)}) collective-permute-start(bf16[2048,768]{1,0:T(8,128)(2,1)} %fusion.2), channel_id=1, source_target_pairs={{4,0},{8,4},{12,8},{16,12},{20,16},{24,20},{28,24},{5,1},{9,5},{13... | collective-permute-start | bytes 9437192 | tf_op jit(solution)/shard_map/ppermute | solution.py:14
  163.3 17.3 %collective-permute-start.3 = (bf16[2,192,768]{2,1,0:T(8,128)(2,1)S(1)}, bf16[2,192,768]{2,1,0:T(8,128)(2,1)S(1)}, u32[]{:S(2)}, u32[]{:S(2)}) collective-permute-start(bf16[2,192,768]{2,1,0:T(8,128)(2,1)S(1)} %fusion.5), channel_id=1, source_target_pairs={{0,1},{1,0},{2,3},{3,2},{4,5},{5,4},{6,7},{7,6},{8,9},{9,8},{10,11... | collective-permute-start | bytes 1769480 | tf_op jit(solution)/shard_map/ppermute | solution.py:34
  169.0 12.3 %collective-permute-start.7 = (bf16[2,192,768]{2,1,0:T(8,128)(2,1)S(1)}, bf16[2,192,768]{2,1,0:T(8,128)(2,1)S(1)}, u32[]{:S(2)}, u32[]{:S(2)}) collective-permute-start(bf16[2,192,768]{2,1,0:T(8,128)(2,1)S(1)} %fusion.7), channel_id=1, source_target_pairs={{0,1},{1,0},{2,3},{3,2},{4,5},{5,4},{6,7},{7,6},{8,9},{9,8},{10,11... | collective-permute-start | bytes 1769480 | tf_op jit(solution)/shard_map/ppermute | solution.py:34
  175.2 7.8 %collective-permute-start.5 = (bf16[2,192,768]{2,1,0:T(8,128)(2,1)S(1)}, bf16[2,192,768]{2,1,0:T(8,128)(2,1)S(1)}, u32[]{:S(2)}, u32[]{:S(2)}) collective-permute-start(bf16[2,192,768]{2,1,0:T(8,128)(2,1)S(1)} %fusion.6), channel_id=1, source_target_pairs={{0,1},{1,0},{2,3},{3,2},{4,5},{5,4},{6,7},{7,6},{8,9},{9,8},{10,11... | collective-permute-start | bytes 1769480 | tf_op jit(solution)/shard_map/ppermute | solution.py:34
  180.0 3.8 %collective-permute-start.9 = (bf16[2,192,768]{2,1,0:T(8,128)(2,1)S(1)}, bf16[2,192,768]{2,1,0:T(8,128)(2,1)S(1)}, u32[]{:S(2)}, u32[]{:S(2)}) collective-permute-start(bf16[2,192,768]{2,1,0:T(8,128)(2,1)S(1)} %fusion.8), channel_id=1, source_target_pairs={{0,1},{1,0},{2,3},{3,2},{4,5},{5,4},{6,7},{7,6},{8,9},{9,8},{10,11... | collective-permute-start | bytes 1769480 | tf_op jit(solution)/shard_map/ppermute | solution.py:34
  180.7 30.2 %collective-permute-start.4 = (bf16[192,768]{1,0:T(8,128)(2,1)S(1)}, bf16[192,768]{1,0:T(8,128)(2,1)S(1)}, u32[]{:S(2)}, u32[]{:S(2)}) collective-permute-start(bf16[192,768]{1,0:T(8,128)(2,1)S(1)} %fusion.17), channel_id=1, source_target_pairs={{0,2},{1,3},{2,0},{3,1},{4,6},{5,7},{6,4},{7,5},{8,10},{9,11},{10,... | collective-permute-start | bytes 884744 | tf_op jit(solution)/shard_map/ppermute | solution.py:38
  181.4 15.5 %collective-permute-start.8 = (bf16[192,768]{1,0:T(8,128)(2,1)S(1)}, bf16[192,768]{1,0:T(8,128)(2,1)S(1)}, u32[]{:S(2)}, u32[]{:S(2)}) collective-permute-start(bf16[192,768]{1,0:T(8,128)(2,1)S(1)} %fusion.19), channel_id=1, source_target_pairs={{0,2},{1,3},{2,0},{3,1},{4,6},{5,7},{6,4},{7,5},{8,10},{9,11},{10,... | collective-permute-start | bytes 884744 | tf_op jit(solution)/shard_map/ppermute | solution.py:38
  183.2 20.1 %collective-permute-start.6 = (bf16[192,768]{1,0:T(8,128)(2,1)S(1)}, bf16[192,768]{1,0:T(8,128)(2,1)S(1)}, u32[]{:S(2)}, u32[]{:S(2)}) collective-permute-start(bf16[192,768]{1,0:T(8,128)(2,1)S(1)} %fusion.18), channel_id=1, source_target_pairs={{0,2},{1,3},{2,0},{3,1},{4,6},{5,7},{6,4},{7,5},{8,10},{9,11},{10,... | collective-permute-start | bytes 884744 | tf_op jit(solution)/shard_map/ppermute | solution.py:38
  183.9 24.8 %collective-permute-start.10 = (bf16[192,768]{1,0:T(8,128)(2,1)S(1)}, bf16[192,768]{1,0:T(8,128)(2,1)S(1)}, u32[]{:S(2)}, u32[]{:S(2)}) collective-permute-start(bf16[192,768]{1,0:T(8,128)(2,1)S(1)} %fusion.20), channel_id=1, source_target_pairs={{0,2},{1,3},{2,0},{3,1},{4,6},{5,7},{6,4},{7,5},{8,10},{9,11},{10,... | collective-permute-start | bytes 884744 | tf_op jit(solution)/shard_map/ppermute | solution.py:38
  197.3 13.9 %collective-permute-start.12 = (f32[768]{0:T(1024)S(1)}, f32[768]{0:T(1024)S(1)}, u32[]{:S(2)}, u32[]{:S(2)}) collective-permute-start(f32[768]{0:T(1024)S(1)} %get-tuple-element.21), channel_id=1, source_target_pairs={{0,8},{4,12},{8,16},{12,20},{16,24},{20,28},{1,9},{5,13},{9,17},{1... | collective-permute-start | bytes 9224 | tf_op jit(solution)/shard_map/ppermute | solution.py:14
  203.6 7.6 %collective-permute-start.11 = (f32[768]{0:T(1024)S(1)}, f32[768]{0:T(1024)S(1)}, u32[]{:S(2)}, u32[]{:S(2)}) collective-permute-start(f32[768]{0:T(1024)S(1)} %get-tuple-element.19), channel_id=1, source_target_pairs={{0,4},{4,8},{8,12},{12,16},{16,20},{20,24},{24,28},{1,5},{5,9},{9,... | collective-permute-start | bytes 9224 | tf_op jit(solution)/shard_map/ppermute | solution.py:14
  208.9 7.5 %collective-permute-start.13 = (f32[768]{0:T(1024)S(1)}, f32[768]{0:T(1024)S(1)}, u32[]{:S(2)}, u32[]{:S(2)}) collective-permute-start(f32[768]{0:T(1024)S(1)} %get-tuple-element.23), channel_id=1, source_target_pairs={{12,0},{16,4},{20,8},{24,12},{28,16},{13,1},{17,5},{21,9},{25,13},... | collective-permute-start | bytes 9224 | tf_op jit(solution)/shard_map/ppermute | solution.py:14

commit v9 on v8

--- a/solution.py
+++ b/solution.py
@@ -38,6 +38,13 @@
     return keep + lax.ppermute(send.astype(jnp.bfloat16), "samp", pairs_chip).astype(jnp.float32)
 
 
+def reduce_to_owner(part, owner, n_samp):
+    pairs_core = [(s, s ^ 1) for s in range(n_samp) if (s & 1) != (owner & 1)]
+    summed = part + lax.ppermute(part.astype(jnp.bfloat16), "samp", pairs_core).astype(jnp.float32)
+    pairs_chip = [(owner ^ 2, owner)]
+    return summed + lax.ppermute(summed.astype(jnp.bfloat16), "samp", pairs_chip).astype(jnp.float32)
+
+
 def local(dosages, observed):
     values = dosages.astype(jnp.float32)
     present = observed.astype(jnp.float32)
@@ -56,15 +63,17 @@
     position = lax.axis_index("var")
     raw = {offset: from_behind(standard, "var", -PARTNER_STEP[offset]) for offset in range(1, BAND + 1)}
 
-    arrived, gram_same, standard_late = lax.optimization_barrier(
-        ([raw[d] for d in PROCESS_ORDER], gram_of(standard, standard), standard)
+    same_total = reduce_to_owner(gram_of(standard, standard), 0, n_samp)
+    arrived, same_total, standard_late = lax.optimization_barrier(
+        ([raw[d] for d in PROCESS_ORDER], same_total, standard)
     )
-    owned = {0: reduce_quarters(gram_same, n_samp)}
+    owned = {}
     for offset, partner in zip(PROCESS_ORDER, arrived):
         owned[offset] = reduce_quarters(gram_of(standard_late, partner), n_samp)
 
-    row_total = jnp.sum(adjusted_r2(owned[0], samples), 1)
-    incoming = jnp.zeros((block_width,), jnp.float32)
+    me = lax.axis_index("samp")
+    incoming = jnp.sum(adjusted_r2(same_total, samples), 1) * (me == 0).astype(jnp.float32)
+    row_total = jnp.zeros((block_width // n_samp,), jnp.float32)
     for offset in range(1, BAND + 1):
         step = PARTNER_STEP[offset]
         in_range = ((position + step >= 0) & (position + step < n_var)).astype(jnp.float32)

time: 223 us -> 214 us (0.960)
  waiting for transfers between devices: 144 us -> 133 us
  matrix products: 21.3 us -> 16.5 us
  starting transfers between devices: 26 us -> 29.9 us
  other arithmetic: 13.2 us -> 16.6 us
    ppermute x6, waiting for transfers between devices: 130 us -> 107 us  [from_behind(): lax.ppermute(value, axis, [(source, source + steps) for source in range(l...]
    ppermute x0 -> x2, waiting for transfers between devices: none -> 15.2 us  [the longest x1 11.7 us: reduce_to_owner(): lax.ppermute(summed.astype(jnp.bfloat16), 'samp', pairs_chip)]
    ppermute x0 -> x2, starting transfers between devices: none -> 5.76 us  [the longest x1 4.47 us: reduce_to_owner(): lax.ppermute(summed.astype(jnp.bfloat16), 'samp', pairs_chip)]
    dot_general x4, matrix products: 21.3 us -> 16.5 us  [gram_of(): lax.dot_general(left, right, (((0,), (0,)), ((), ())), preferred_element_...]
    ppermute x4 -> x3, waiting for transfers between devices: 14.7 us -> 10.5 us  [reduce_quarters(): lax.ppermute(send.astype(jnp.bfloat16), 'samp', pairs_chip)]
    add x0 -> x1, other arithmetic: none -> 2.64 us  [reduce_to_owner(): summed + lax.ppermute(summed.astype(jnp.bfloat16), 'samp', pairs_chip).as...]
  transfers between devices with their start and end apart: 14 -> 14, of which waited for: 7 -> 9; matrix products, arithmetic and copies ran while one was open for 11% -> 9% of each run, Pallas kernels for 0% -> 0%
where the time goes in v9:
time: 214 us; the launch traced here: 213 us
  waiting for transfers between devices  133 us (62%)
  starting transfers between devices  29.9 us (14%)
  other arithmetic  16.6 us (8%)
  matrix products  16.5 us (8%)
  blocking collectives  16 us (7%)
    ppermute x6, waiting for transfers between devices, from_behind(): lax.ppermute(value, axis, [(source, source + steps) for source in range(l...  107 us
    ppermute x6, starting transfers between devices, from_behind(): lax.ppermute(value, axis, [(source, source + steps) for source in range(l...  20.7 us
    dot_general x4, matrix products, gram_of(): lax.dot_general(left, right, (((0,), (0,)), ((), ())), preferred_element_...  16.5 us
    ppermute x1, waiting for transfers between devices, reduce_to_owner(): lax.ppermute(summed.astype(jnp.bfloat16), 'samp', pairs_chip)  11.7 us
    ppermute x3, waiting for transfers between devices, reduce_quarters(): lax.ppermute(send.astype(jnp.bfloat16), 'samp', pairs_chip)  10.5 us
    psum x1, blocking collectives, local(): lax.psum((jnp.sum(present, 0), jnp.sum(present * values, 0), jnp.sum(pres...  10.2 us
    unnamed x1, blocking collectives  5.85 us
    reduce_sum x1, other arithmetic, local(): jnp.sum(present * values, 0)  5.28 us
  transfers between devices with their start and end apart: 14, of which 9 were waited for; matrix products, arithmetic and copies ran while one was open for 9% of the time, Pallas kernels for 0%

profile of v9, /device:TPU:14, one launch (start us, length us, event | category | flops | bytes accessed | tf_op | source)
XLA Modules:
  0.0 213.4 jit_solution(5224228898900562021)
XLA Ops:
  0.0 5.3 %fusion.4 = (f32[768]{0:T(1024)S(1)}, f32[768]{0:T(1024)S(1)}, f32[768]{0:T(1024)S(1)}) fusion(bf16[2048,768]{1,0:T(8,128)(2,1)} %param.2, s32[2048,768]{1,0:T(8,128)} %param.3), kind=kLoop, calls=%fused_computation.8 | loop fusion | flops 11007744 | bytes 9446400 | tf_op jit(solution)/shard_map/reduce_sum | solution.py:52
  5.3 10.2 %all-reduce.1 = (f32[768]{0:T(1024)S(1)}, f32[768]{0:T(1024)S(1)}, f32[768]{0:T(1024)S(1)}) all-reduce(f32[768]{0:T(1024)S(1)} %get-tuple-element.16, f32[768]{0:T(1024)S(1)} %get-tuple-element.17, f32[768]{0:T(1024)S(1)} %get-tuple-element.15), channel_id=1, replica_groups=mesh['var'=8,'samp'=4] {'samp'}, use_global_device_ids=true, to_apply=%region_5.0 | all-reduce | flops 2304 | bytes 18432 | tf_op jit(solution)/shard_map/psum | solution.py:51
  15.5 4.9 %fusion.2 = bf16[2048,768]{1,0:T(8,128)(2,1)S(1)} fusion(bf16[2048,768]{1,0:T(8,128)(2,1)} %param.2, s32[2048,768]{1,0:T(8,128)} %param.3, f32[768]{0:T(1024)S(1)} %get-tuple-element.28, f32[768]{0:T(1024)S(1)} %get-tuple-element.27), kind=kLoop, calls=%fused_computation.5 | loop fusion | flops 9437184 | bytes 12589056 | tf_op jit(solution)/shard_map/convert_element_type | solution.py:58
  20.4 2.4 %collective-permute-start = (bf16[2048,768]{1,0:T(8,128)(2,1)S(1)}, bf16[2048,768]{1,0:T(8,128)(2,1)}, u32[]{:S(2)}, u32[]{:S(2)}) collective-permute-start(bf16[2048,768]{1,0:T(8,128)(2,1)S(1)} %fusion.2), channel_id=1, source_target_pairs={{8,0},{12,4},{16,8},{20,12},{24,16},{28,20},{9,1},{13,5},{17,9},{2... | collective-permute-start | bytes 9437192 | tf_op jit(solution)/shard_map/ppermute | solution.py:14
  22.7 6.1 %collective-permute-start.1 = (bf16[2048,768]{1,0:T(8,128)(2,1)S(1)}, bf16[2048,768]{1,0:T(8,128)(2,1)}, u32[]{:S(2)}, u32[]{:S(2)}) collective-permute-start(bf16[2048,768]{1,0:T(8,128)(2,1)S(1)} %fusion.2), channel_id=1, source_target_pairs={{0,12},{4,16},{8,20},{12,24},{16,28},{1,13},{5,17},{9,21},{13,25},... | collective-permute-start | bytes 9437192 | tf_op jit(solution)/shard_map/ppermute | solution.py:14
  28.9 2.4 %collective-permute-start.2 = (bf16[2048,768]{1,0:T(8,128)(2,1)S(1)}, bf16[2048,768]{1,0:T(8,128)(2,1)}, u32[]{:S(2)}, u32[]{:S(2)}) collective-permute-start(bf16[2048,768]{1,0:T(8,128)(2,1)S(1)} %fusion.2), channel_id=1, source_target_pairs={{4,0},{8,4},{12,8},{16,12},{20,16},{24,20},{28,24},{5,1},{9,5},{13... | collective-permute-start | bytes 9437192 | tf_op jit(solution)/shard_map/ppermute | solution.py:14
  31.3 2.7 %fusion.25 = (bf16[768,768]{1,0:T(8,128)(2,1)S(1)}, f32[768,768]{1,0:T(8,128)S(1)}) fusion(bf16[2048,768]{1,0:T(8,128)(2,1)S(1)} %fusion.2), kind=kOutput, calls=%fused_computation.51 | convolution fusion | flops 2416508928 | bytes 6684672 | tf_op jit(solution)/shard_map/dot_general | solution.py:24
  34.0 1.3 collective-permute-start.3
  35.3 3.4 %collective-permute-done.3 = bf16[768,768]{1,0:T(8,128)(2,1)S(1)} collective-permute-done((bf16[768,768]{1,0:T(8,128)(2,1)S(1)}, bf16[768,768]{1,0:T(8,128)(2,1)S(1)}, u32[]{:S(2)}, u32[]{:S(2)}) %collective-permute-start.3) | collective-permute-done | bytes 1179680 | tf_op jit(solution)/shard_map/ppermute | solution.py:43
  38.7 1.4 fusion.5
  40.2 4.5 %collective-permute-start.4 = (bf16[768,768]{1,0:T(8,128)(2,1)}, bf16[768,768]{1,0:T(8,128)(2,1)}, u32[]{:S(2)}, u32[]{:S(2)}) collective-permute-start(bf16[768,768]{1,0:T(8,128)(2,1)} %fusion.5), channel_id=1, source_target_pairs={{2,0},{6,4},{10,8},{14,12},{18,16},{22,20},{26,24},{30,28}} | collective-permute-start | bytes 3538952 | tf_op jit(solution)/shard_map/ppermute | solution.py:45
  44.7 0.6 dynamic-slice
  45.9 11.7 %collective-permute-done.4 = bf16[768,768]{1,0:T(8,128)(2,1)} collective-permute-done((bf16[768,768]{1,0:T(8,128)(2,1)}, bf16[768,768]{1,0:T(8,128)(2,1)}, u32[]{:S(2)}, u32[]{:S(2)}) %collective-permute-start.4) | collective-permute-done | bytes 1179680 | tf_op jit(solution)/shard_map/ppermute | solution.py:45
  57.6 2.6 %convert_add_fusion = f32[768,768]{1,0:T(8,128)S(1)} fusion(bf16[768,768]{1,0:T(8,128)(2,1)} %collective-permute-done.4, f32[768,768]{1,0:T(8,128)} %copy-done, bf16[768,768]{1,0:T(8,128)(2,1)} %copy-done.1), kind=kLoop, calls=%fused_computation.10 | loop fusion | flops 2359296 | bytes 7077888 | tf_op jit(solution)/shard_map/add | solution.py:45
  60.3 31.5 %collective-permute-done = bf16[2048,768]{1,0:T(8,128)(2,1)} collective-permute-done((bf16[2048,768]{1,0:T(8,128)(2,1)S(1)}, bf16[2048,768]{1,0:T(8,128)(2,1)}, u32[]{:S(2)}, u32[]{:S(2)}) %collective-permute-start) | collective-permute-done | bytes 3145760 | tf_op jit(solution)/shard_map/ppermute | solution.py:14
  91.7 69.3 %collective-permute-done.1 = bf16[2048,768]{1,0:T(8,128)(2,1)} collective-permute-done((bf16[2048,768]{1,0:T(8,128)(2,1)S(1)}, bf16[2048,768]{1,0:T(8,128)(2,1)}, u32[]{:S(2)}, u32[]{:S(2)}) %collective-permute-start.1) | collective-permute-done | bytes 3145760 | tf_op jit(solution)/shard_map/ppermute | solution.py:14
  161.1 1.1 collective-permute-done.2
  162.1 4.6 %fusion.26 = f32[768,768]{1,0:T(8,128)S(1)} fusion(bf16[2048,768]{1,0:T(8,128)(2,1)S(1)} %fusion.2, bf16[2048,768]{1,0:T(8,128)(2,1)} %collective-permute-done.2), kind=kOutput, calls=%fused_computation.52 | convolution fusion | flops 2415919104 | bytes 8650752 | tf_op jit(solution)/shard_map/dot_general | solution.py:24
  166.7 0.1 fusion.6
  166.8 0.1 collective-permute-start.5
  166.9 4.6 %fusion.27 = f32[768,768]{1,0:T(8,128)S(1)} fusion(bf16[2048,768]{1,0:T(8,128)(2,1)S(1)} %fusion.2, bf16[2048,768]{1,0:T(8,128)(2,1)} %collective-permute-done), kind=kOutput, calls=%fused_computation.53 | convolution fusion | flops 2415919104 | bytes 8650752 | tf_op jit(solution)/shard_map/dot_general | solution.py:24
  171.5 0.1 fusion.7
  171.6 0.6 collective-permute-start.7
  172.1 4.6 %fusion.28 = f32[768,768]{1,0:T(8,128)S(1)} fusion(bf16[2048,768]{1,0:T(8,128)(2,1)S(1)} %fusion.2, bf16[2048,768]{1,0:T(8,128)(2,1)} %collective-permute-done.1), kind=kOutput, calls=%fused_computation.54 | convolution fusion | flops 2415919104 | bytes 8650752 | tf_op jit(solution)/shard_map/dot_general | solution.py:24
  176.8 0.1 fusion.8
  176.8 0.1 collective-permute-start.9
  176.9 0.0 collective-permute-done.5
  176.9 0.1 bitcast_add_fusion.2
  177.1 0.6 collective-permute-start.6
  177.7 0.1 bitcast_add_fusion.1
  177.8 1.6 collective-permute-start.8
  179.4 0.0 collective-permute-done.9
  179.4 0.1 bitcast_add_fusion
  179.6 0.6 collective-permute-start.10
  180.1 6.9 %collective-permute-done.6 = bf16[192,768]{1,0:T(8,128)(2,1)S(1)} collective-permute-done((bf16[192,768]{1,0:T(8,128)(2,1)S(1)}, bf16[192,768]{1,0:T(8,128)(2,1)S(1)}, u32[]{:S(2)}, u32[]{:S(2)}) %collective-permute-start.6) | collective-permute-done | bytes 294944 | tf_op jit(solution)/shard_map/ppermute | solution.py:38
  187.0 0.3 fusion.19
  187.3 4.4 %collective-permute-start.11 = (f32[768]{0:T(1024)S(1)}, f32[768]{0:T(1024)S(1)}, u32[]{:S(2)}, u32[]{:S(2)}) collective-permute-start(f32[768]{0:T(1024)S(1)} %get-tuple-element.21), channel_id=1, source_target_pairs={{0,4},{4,8},{8,12},{12,16},{16,20},{20,24},{24,28},{1,5},{5,9},{9,... | collective-permute-start | bytes 9224 | tf_op jit(solution)/shard_map/ppermute | solution.py:14
  191.7 1.6 collective-permute-done.8
  193.3 0.3 fusion.21
  193.6 3.5 %collective-permute-start.12 = (f32[768]{0:T(1024)S(1)}, f32[768]{0:T(1024)S(1)}, u32[]{:S(2)}, u32[]{:S(2)}) collective-permute-start(f32[768]{0:T(1024)S(1)} %get-tuple-element.19), channel_id=1, source_target_pairs={{0,8},{4,12},{8,16},{12,20},{16,24},{20,28},{1,9},{5,13},{9,17},{1... | collective-permute-start | bytes 9224 | tf_op jit(solution)/shard_map/ppermute | solution.py:14
  197.1 2.1 collective-permute-done.10
  199.2 0.3 fusion.23
  199.5 1.9 collective-permute-start.13
  201.4 0.5 subtract_reduce_fusion
  201.9 0.0 collective-permute-done.11
  201.9 5.0 %collective-permute-done.13 = f32[768]{0:T(1024)S(1)} collective-permute-done((f32[768]{0:T(1024)S(1)}, f32[768]{0:T(1024)S(1)}, u32[]{:S(2)}, u32[]{:S(2)}) %collective-permute-start.13) | collective-permute-done | bytes 3104 | tf_op jit(solution)/shard_map/ppermute | solution.py:14
  206.9 5.9 %all-reduce = f32[768]{0:T(1024)S(1)} all-reduce(f32[768]{0:T(1024)S(1)} %add_add_fusion), channel_id=2, replica_groups=mesh['var'=8,'samp'=4] {'samp'}, use_global_device_ids=true, to_apply=%region_13.14.clone | all-reduce | flops 768 | bytes 6144
  212.8 0.6 fusion.24
  (13 shorter events, 0.2 us)
Async XLA Ops:
  20.4 71.4 %collective-permute-start = (bf16[2048,768]{1,0:T(8,128)(2,1)S(1)}, bf16[2048,768]{1,0:T(8,128)(2,1)}, u32[]{:S(2)}, u32[]{:S(2)}) collective-permute-start(bf16[2048,768]{1,0:T(8,128)(2,1)S(1)} %fusion.2), channel_id=1, source_target_pairs={{8,0},{12,4},{16,8},{20,12},{24,16},{28,20},{9,1},{13,5},{17,9},{2... | collective-permute-start | bytes 9437192 | tf_op jit(solution)/shard_map/ppermute | solution.py:14
  22.7 138.3 %collective-permute-start.1 = (bf16[2048,768]{1,0:T(8,128)(2,1)S(1)}, bf16[2048,768]{1,0:T(8,128)(2,1)}, u32[]{:S(2)}, u32[]{:S(2)}) collective-permute-start(bf16[2048,768]{1,0:T(8,128)(2,1)S(1)} %fusion.2), channel_id=1, source_target_pairs={{0,12},{4,16},{8,20},{12,24},{16,28},{1,13},{5,17},{9,21},{13,25},... | collective-permute-start | bytes 9437192 | tf_op jit(solution)/shard_map/ppermute | solution.py:14
  28.9 133.3 %collective-permute-start.2 = (bf16[2048,768]{1,0:T(8,128)(2,1)S(1)}, bf16[2048,768]{1,0:T(8,128)(2,1)}, u32[]{:S(2)}, u32[]{:S(2)}) collective-permute-start(bf16[2048,768]{1,0:T(8,128)(2,1)S(1)} %fusion.2), channel_id=1, source_target_pairs={{4,0},{8,4},{12,8},{16,12},{20,16},{24,20},{28,24},{5,1},{9,5},{13... | collective-permute-start | bytes 9437192 | tf_op jit(solution)/shard_map/ppermute | solution.py:14
  34.0 6.2 %copy-start = (f32[768,768]{1,0:T(8,128)}, f32[768,768]{1,0:T(8,128)S(1)}, u32[]{:S(2)}) copy-start(f32[768,768]{1,0:T(8,128)S(1)} %get-tuple-element.30) | copy-start | bytes 7077892
  34.0 4.7 %collective-permute-start.3 = (bf16[768,768]{1,0:T(8,128)(2,1)S(1)}, bf16[768,768]{1,0:T(8,128)(2,1)S(1)}, u32[]{:S(2)}, u32[]{:S(2)}) collective-permute-start(bf16[768,768]{1,0:T(8,128)(2,1)S(1)} %get-tuple-element.29), channel_id=1, source_target_pairs={{1,0},{3,2},{5,4},{7,6},{9,8},{11,10},{13,12},{15,14},{17,16},{19,... | collective-permute-start | bytes 3538952 | tf_op jit(solution)/shard_map/ppermute | solution.py:43
  38.7 1.5 copy-start.1
  38.7 5.9 %copy-start.2 = (u32[32]{0:T(128)S(1)}, u32[32]{0:T(128)}, u32[]{:S(2)}) copy-start(u32[32]{0:T(128)} %constant.105) | copy-start | bytes 388
  40.2 17.4 %collective-permute-start.4 = (bf16[768,768]{1,0:T(8,128)(2,1)}, bf16[768,768]{1,0:T(8,128)(2,1)}, u32[]{:S(2)}, u32[]{:S(2)}) collective-permute-start(bf16[768,768]{1,0:T(8,128)(2,1)} %fusion.5), channel_id=1, source_target_pairs={{2,0},{6,4},{10,8},{14,12},{18,16},{22,20},{26,24},{30,28}} | collective-permute-start | bytes 3538952 | tf_op jit(solution)/shard_map/ppermute | solution.py:45
  166.8 10.1 %collective-permute-start.5 = (bf16[2,192,768]{2,1,0:T(8,128)(2,1)S(1)}, bf16[2,192,768]{2,1,0:T(8,128)(2,1)S(1)}, u32[]{:S(2)}, u32[]{:S(2)}) collective-permute-start(bf16[2,192,768]{2,1,0:T(8,128)(2,1)S(1)} %fusion.6), channel_id=1, source_target_pairs={{0,1},{1,0},{2,3},{3,2},{4,5},{5,4},{6,7},{7,6},{8,9},{9,8},{10,11... | collective-permute-start | bytes 1769480 | tf_op jit(solution)/shard_map/ppermute | solution.py:34
  171.6 6.1 %collective-permute-start.7 = (bf16[2,192,768]{2,1,0:T(8,128)(2,1)S(1)}, bf16[2,192,768]{2,1,0:T(8,128)(2,1)S(1)}, u32[]{:S(2)}, u32[]{:S(2)}) collective-permute-start(bf16[2,192,768]{2,1,0:T(8,128)(2,1)S(1)} %fusion.7), channel_id=1, source_target_pairs={{0,1},{1,0},{2,3},{3,2},{4,5},{5,4},{6,7},{7,6},{8,9},{9,8},{10,11... | collective-permute-start | bytes 1769480 | tf_op jit(solution)/shard_map/ppermute | solution.py:34
  176.8 2.6 %collective-permute-start.9 = (bf16[2,192,768]{2,1,0:T(8,128)(2,1)S(1)}, bf16[2,192,768]{2,1,0:T(8,128)(2,1)S(1)}, u32[]{:S(2)}, u32[]{:S(2)}) collective-permute-start(bf16[2,192,768]{2,1,0:T(8,128)(2,1)S(1)} %fusion.8), channel_id=1, source_target_pairs={{0,1},{1,0},{2,3},{3,2},{4,5},{5,4},{6,7},{7,6},{8,9},{9,8},{10,11... | collective-permute-start | bytes 1769480 | tf_op jit(solution)/shard_map/ppermute | solution.py:34
  177.1 9.9 %collective-permute-start.6 = (bf16[192,768]{1,0:T(8,128)(2,1)S(1)}, bf16[192,768]{1,0:T(8,128)(2,1)S(1)}, u32[]{:S(2)}, u32[]{:S(2)}) collective-permute-start(bf16[192,768]{1,0:T(8,128)(2,1)S(1)} %fusion.15), channel_id=1, source_target_pairs={{0,2},{1,3},{2,0},{3,1},{4,6},{5,7},{6,4},{7,5},{8,10},{9,11},{10,... | collective-permute-start | bytes 884744 | tf_op jit(solution)/shard_map/ppermute | solution.py:38
  177.8 15.5 %collective-permute-start.8 = (bf16[192,768]{1,0:T(8,128)(2,1)S(1)}, bf16[192,768]{1,0:T(8,128)(2,1)S(1)}, u32[]{:S(2)}, u32[]{:S(2)}) collective-permute-start(bf16[192,768]{1,0:T(8,128)(2,1)S(1)} %fusion.16), channel_id=1, source_target_pairs={{0,2},{1,3},{2,0},{3,1},{4,6},{5,7},{6,4},{7,5},{8,10},{9,11},{10,... | collective-permute-start | bytes 884744 | tf_op jit(solution)/shard_map/ppermute | solution.py:38
  179.6 19.6 %collective-permute-start.10 = (bf16[192,768]{1,0:T(8,128)(2,1)S(1)}, bf16[192,768]{1,0:T(8,128)(2,1)S(1)}, u32[]{:S(2)}, u32[]{:S(2)}) collective-permute-start(bf16[192,768]{1,0:T(8,128)(2,1)S(1)} %fusion.17), channel_id=1, source_target_pairs={{0,2},{1,3},{2,0},{3,1},{4,6},{5,7},{6,4},{7,5},{8,10},{9,11},{10,... | collective-permute-start | bytes 884744 | tf_op jit(solution)/shard_map/ppermute | solution.py:38
  187.3 14.6 %collective-permute-start.11 = (f32[768]{0:T(1024)S(1)}, f32[768]{0:T(1024)S(1)}, u32[]{:S(2)}, u32[]{:S(2)}) collective-permute-start(f32[768]{0:T(1024)S(1)} %get-tuple-element.21), channel_id=1, source_target_pairs={{0,4},{4,8},{8,12},{12,16},{16,20},{20,24},{24,28},{1,5},{5,9},{9,... | collective-permute-start | bytes 9224 | tf_op jit(solution)/shard_map/ppermute | solution.py:14
  193.6 8.3 %collective-permute-start.12 = (f32[768]{0:T(1024)S(1)}, f32[768]{0:T(1024)S(1)}, u32[]{:S(2)}, u32[]{:S(2)}) collective-permute-start(f32[768]{0:T(1024)S(1)} %get-tuple-element.19), channel_id=1, source_target_pairs={{0,8},{4,12},{8,16},{12,20},{16,24},{20,28},{1,9},{5,13},{9,17},{1... | collective-permute-start | bytes 9224 | tf_op jit(solution)/shard_map/ppermute | solution.py:14
  199.5 7.5 %collective-permute-start.13 = (f32[768]{0:T(1024)S(1)}, f32[768]{0:T(1024)S(1)}, u32[]{:S(2)}, u32[]{:S(2)}) collective-permute-start(f32[768]{0:T(1024)S(1)} %get-tuple-element.23), channel_id=1, source_target_pairs={{12,0},{16,4},{20,8},{24,12},{28,16},{13,1},{17,5},{21,9},{25,13},... | collective-permute-start | bytes 9224 | tf_op jit(solution)/shard_map/ppermute | solution.py:14

commit v10 on v9

--- a/solution.py
+++ b/solution.py
@@ -5,7 +5,7 @@
 
 BAND = 3
 PARTNER_STEP = {1: 1, 2: 2, 3: -3}
-PROCESS_ORDER = (2, 3, 1)
+LATE_OFFSETS = (2, 3)
 
 
 def from_behind(value, axis, steps):
@@ -64,17 +64,22 @@
     raw = {offset: from_behind(standard, "var", -PARTNER_STEP[offset]) for offset in range(1, BAND + 1)}
 
     same_total = reduce_to_owner(gram_of(standard, standard), 0, n_samp)
-    arrived, same_total, standard_late = lax.optimization_barrier(
-        ([raw[d] for d in PROCESS_ORDER], same_total, standard)
+    next_total = reduce_to_owner(gram_of(standard, raw[1]), 1, n_samp)
+    arrived, same_total, next_total, standard_late = lax.optimization_barrier(
+        ([raw[d] for d in LATE_OFFSETS], same_total, next_total, standard)
     )
     owned = {}
-    for offset, partner in zip(PROCESS_ORDER, arrived):
+    for offset, partner in zip(LATE_OFFSETS, arrived):
         owned[offset] = reduce_quarters(gram_of(standard_late, partner), n_samp)
 
     me = lax.axis_index("samp")
     incoming = jnp.sum(adjusted_r2(same_total, samples), 1) * (me == 0).astype(jnp.float32)
+    next_in_range = (position + PARTNER_STEP[1] < n_var).astype(jnp.float32)
+    next_adjusted = adjusted_r2(next_total, samples) * (next_in_range * (me == 1).astype(jnp.float32))
+    incoming = incoming + jnp.sum(next_adjusted, 1)
+    incoming = incoming + from_behind(jnp.sum(next_adjusted, 0), "var", PARTNER_STEP[1])
     row_total = jnp.zeros((block_width // n_samp,), jnp.float32)
-    for offset in range(1, BAND + 1):
+    for offset in LATE_OFFSETS:
         step = PARTNER_STEP[offset]
         in_range = ((position + step >= 0) & (position + step < n_var)).astype(jnp.float32)
         adjusted = adjusted_r2(owned[offset], samples) * in_range

time: 214 us -> 265 us (1.24)
  starting transfers between devices: 29.9 us -> 59.9 us
  waiting for transfers between devices: 133 us -> 142 us
  other arithmetic: 16.6 us -> 24.3 us
  local copies, waits for them, and re-layouts: 0.92 us -> 3.8 us
    ppermute x6, starting transfers between devices: 20.7 us -> 48.9 us  [from_behind(): lax.ppermute(value, axis, [(source, source + steps) for source in range(l...]
    ppermute x6, waiting for transfers between devices: 107 us -> 122 us  [from_behind(): lax.ppermute(value, axis, [(source, source + steps) for source in range(l...]
    ppermute x3 -> x2, waiting for transfers between devices: 10.5 us -> 0.01 us  [reduce_quarters(): lax.ppermute(send.astype(jnp.bfloat16), 'samp', pairs_chip)]
    ppermute x1 -> x2, waiting for transfers between devices: 11.7 us -> 20.7 us  [reduce_to_owner(): lax.ppermute(summed.astype(jnp.bfloat16), 'samp', pairs_chip)]
    add x1 -> x2, other arithmetic: 2.64 us -> 7.19 us  [reduce_to_owner(): summed + lax.ppermute(summed.astype(jnp.bfloat16), 'samp', pairs_chip).as...]
    ppermute x1 -> x2, waiting for transfers between devices: 3.44 us -> 0.01 us  [reduce_to_owner(): lax.ppermute(part.astype(jnp.bfloat16), 'samp', pairs_core)]
  transfers between devices with their start and end apart: 14 -> 14, of which waited for: 9 -> 3; matrix products, arithmetic and copies ran while one was open for 9% -> 9% of each run, Pallas kernels for 0% -> 0%
where the time goes in v10:
time: 265 us; the launch traced here: 262 us
  waiting for transfers between devices  142 us (54%)
  starting transfers between devices  59.9 us (23%)
  other arithmetic  24.3 us (9%)
  blocking collectives  15.9 us (6%)
  matrix products  14.7 us (6%)
  local copies, waits for them, and re-layouts  3.8 us (1%)
    ppermute x6, waiting for transfers between devices, from_behind(): lax.ppermute(value, axis, [(source, source + steps) for source in range(l...  122 us
    ppermute x6, starting transfers between devices, from_behind(): lax.ppermute(value, axis, [(source, source + steps) for source in range(l...  48.9 us
    ppermute x2, waiting for transfers between devices, reduce_to_owner(): lax.ppermute(summed.astype(jnp.bfloat16), 'samp', pairs_chip)  20.7 us
    dot_general x4, matrix products, gram_of(): lax.dot_general(left, right, (((0,), (0,)), ((), ())), preferred_element_...  14.7 us
    psum x1, blocking collectives, local(): lax.psum((jnp.sum(present, 0), jnp.sum(present * values, 0), jnp.sum(pres...  10.2 us
    add x2, other arithmetic, reduce_to_owner(): summed + lax.ppermute(summed.astype(jnp.bfloat16), 'samp', pairs_chip).as...  7.19 us
    unnamed x1, blocking collectives  5.75 us
  transfers between devices with their start and end apart: 14, of which 3 were waited for; matrix products, arithmetic and copies ran while one was open for 9% of the time, Pallas kernels for 0%

profile of v10, /device:TPU:14, one launch (start us, length us, event | category | flops | bytes accessed | tf_op | source)
XLA Modules:
  0.0 261.8 jit_solution(15114990850732055090)
XLA Ops:
  0.0 5.3 %fusion.4 = (f32[768]{0:T(1024)S(1)}, f32[768]{0:T(1024)S(1)}, f32[768]{0:T(1024)S(1)}) fusion(bf16[2048,768]{1,0:T(8,128)(2,1)} %param.2, s32[2048,768]{1,0:T(8,128)} %param.3), kind=kLoop, calls=%fused_computation.8 | loop fusion | flops 11007744 | bytes 9446400 | tf_op jit(solution)/shard_map/reduce_sum | solution.py:52
  5.3 10.2 %all-reduce.1 = (f32[768]{0:T(1024)S(1)}, f32[768]{0:T(1024)S(1)}, f32[768]{0:T(1024)S(1)}) all-reduce(f32[768]{0:T(1024)S(1)} %get-tuple-element.16, f32[768]{0:T(1024)S(1)} %get-tuple-element.17, f32[768]{0:T(1024)S(1)} %get-tuple-element.15), channel_id=1, replica_groups=mesh['var'=8,'samp'=4] {'samp'}, use_global_device_ids=true, to_apply=%region_5.0 | all-reduce | flops 2304 | bytes 18432 | tf_op jit(solution)/shard_map/psum | solution.py:51
  15.5 4.9 %fusion.2 = bf16[2048,768]{1,0:T(8,128)(2,1)S(1)} fusion(bf16[2048,768]{1,0:T(8,128)(2,1)} %param.2, s32[2048,768]{1,0:T(8,128)} %param.3, f32[768]{0:T(1024)S(1)} %get-tuple-element.28, f32[768]{0:T(1024)S(1)} %get-tuple-element.27), kind=kLoop, calls=%fused_computation.5 | loop fusion | flops 9437184 | bytes 12589056 | tf_op jit(solution)/shard_map/convert_element_type | solution.py:58
  20.4 2.4 collective-permute-start.4
  22.8 2.3 collective-permute-start
  25.1 7.1 %collective-permute-start.1 = (bf16[2048,768]{1,0:T(8,128)(2,1)S(1)}, bf16[2048,768]{1,0:T(8,128)(2,1)}, u32[]{:S(2)}, u32[]{:S(2)}) collective-permute-start(bf16[2048,768]{1,0:T(8,128)(2,1)S(1)} %fusion.2), channel_id=1, source_target_pairs={{0,12},{4,16},{8,20},{12,24},{16,28},{1,13},{5,17},{9,21},{13,25},... | collective-permute-start | bytes 9437192 | tf_op jit(solution)/shard_map/ppermute | solution.py:14
  32.2 2.7 %fusion.22 = (bf16[768,768]{1,0:T(8,128)(2,1)S(1)}, f32[768,768]{1,0:T(8,128)S(1)}) fusion(bf16[2048,768]{1,0:T(8,128)(2,1)S(1)} %fusion.2), kind=kOutput, calls=%fused_computation.46 | convolution fusion | flops 2416508928 | bytes 6684672 | tf_op jit(solution)/shard_map/dot_general | solution.py:24
  34.9 1.3 collective-permute-start.2
  36.2 119.5 %collective-permute-done.4 = bf16[2048,768]{1,0:T(8,128)(2,1)S(1)} collective-permute-done((bf16[2048,768]{1,0:T(8,128)(2,1)S(1)}, bf16[2048,768]{1,0:T(8,128)(2,1)S(1)}, u32[]{:S(2)}, u32[]{:S(2)}) %collective-permute-start.4) | collective-permute-done | bytes 3145760 | tf_op jit(solution)/shard_map/ppermute | solution.py:14
  155.7 2.7 %fusion.23 = (bf16[768,768]{1,0:T(8,128)(2,1)S(1)}, f32[768,768]{1,0:T(8,128)S(1)}) fusion(bf16[2048,768]{1,0:T(8,128)(2,1)S(1)} %fusion.2, bf16[2048,768]{1,0:T(8,128)(2,1)S(1)} %collective-permute-done.4), kind=kOutput, calls=%fused_computation.47 | convolution fusion | flops 2416508928 | bytes 9830400 | tf_op jit(solution)/shard_map/dot_general | solution.py:24
  158.5 1.4 collective-permute-start.5
  159.8 0.0 collective-permute-done.2
  159.9 1.4 fusion.5
  161.3 3.5 %collective-permute-start.3 = (bf16[768,768]{1,0:T(8,128)(2,1)}, bf16[768,768]{1,0:T(8,128)(2,1)}, u32[]{:S(2)}, u32[]{:S(2)}) collective-permute-start(bf16[768,768]{1,0:T(8,128)(2,1)} %fusion.5), channel_id=1, source_target_pairs={{2,0},{6,4},{10,8},{14,12},{18,16},{22,20},{26,24},{30,28}} | collective-permute-start | bytes 3538952 | tf_op jit(solution)/shard_map/ppermute | solution.py:45
  164.8 0.0 collective-permute-done.5
  164.8 1.4 fusion.6
  166.2 1.7 collective-permute-start.6
  167.9 20.7 %collective-permute-done.3 = bf16[768,768]{1,0:T(8,128)(2,1)} collective-permute-done((bf16[768,768]{1,0:T(8,128)(2,1)}, bf16[768,768]{1,0:T(8,128)(2,1)}, u32[]{:S(2)}, u32[]{:S(2)}) %collective-permute-start.3) | collective-permute-done | bytes 1179680 | tf_op jit(solution)/shard_map/ppermute | solution.py:45
  188.6 4.1 %convert_add_fusion.2 = f32[768,768]{1,0:T(8,128)} fusion(bf16[768,768]{1,0:T(8,128)(2,1)} %collective-permute-done.3, f32[768,768]{1,0:T(8,128)} %copy-done, bf16[768,768]{1,0:T(8,128)(2,1)} %copy-done.5), kind=kLoop, calls=%fused_computation.13 | loop fusion | flops 2359296 | bytes 7077888 | tf_op jit(solution)/shard_map/add | solution.py:45
  192.7 0.0 collective-permute-done.6
  192.7 3.1 %convert_add_fusion = f32[768,768]{1,0:T(8,128)} fusion(bf16[768,768]{1,0:T(8,128)(2,1)} %collective-permute-done.6, f32[768,768]{1,0:T(8,128)S(1)} %copy-done.2, bf16[768,768]{1,0:T(8,128)(2,1)S(1)} %copy-done.7), kind=kLoop, calls=%fused_computation.11 | loop fusion | flops 2359296 | bytes 7077888 | tf_op jit(solution)/shard_map/add | solution.py:45
  195.8 0.0 collective-permute-done
  195.8 0.0 collective-permute-done.1
  195.8 4.6 %fusion.24 = f32[768,768]{1,0:T(8,128)S(1)} fusion(bf16[2048,768]{1,0:T(8,128)(2,1)S(1)} %fusion.2, bf16[2048,768]{1,0:T(8,128)(2,1)} %collective-permute-done), kind=kOutput, calls=%fused_computation.48 | convolution fusion | flops 2415919104 | bytes 8650752 | tf_op jit(solution)/shard_map/dot_general | solution.py:24
  200.4 1.0 fusion.9
  201.4 0.7 copy-done.10
  202.1 4.6 %fusion.25 = f32[768,768]{1,0:T(8,128)S(1)} fusion(bf16[2048,768]{1,0:T(8,128)(2,1)S(1)} %fusion.2, bf16[2048,768]{1,0:T(8,128)(2,1)} %collective-permute-done.1), kind=kOutput, calls=%fused_computation.49 | convolution fusion | flops 2415919104 | bytes 8650752 | tf_op jit(solution)/shard_map/dot_general | solution.py:24
  206.7 1.4 copy-done.8
  208.1 0.1 fusion.10
  208.2 0.6 collective-permute-start.9
  208.8 0.6 dynamic-slice
  210.0 0.0 collective-permute-done.7
  210.0 1.6 bitcast_add_fusion.1
  211.6 2.5 collective-permute-start.8
  214.2 0.1 bitcast_add_fusion
  214.3 0.1 collective-permute-start.10
  214.5 0.7 fusion.8
  215.1 27.8 %collective-permute-start.11 = (f32[768]{0:T(1024)S(1)}, f32[768]{0:T(1024)S(1)}, u32[]{:S(2)}, u32[]{:S(2)}) collective-permute-start(f32[768]{0:T(1024)S(1)} %get-tuple-element.19), channel_id=1, source_target_pairs={{0,4},{4,8},{8,12},{12,16},{16,20},{20,24},{24,28},{1,5},{5,9},{9,... | collective-permute-start | bytes 9224 | tf_op jit(solution)/shard_map/ppermute | solution.py:14
  242.9 0.0 collective-permute-done.8
  243.0 0.3 fusion.18
  243.2 1.9 collective-permute-start.12
  245.2 0.0 collective-permute-done.10
  245.2 0.3 fusion.20
  245.5 7.3 %collective-permute-start.13 = (f32[768]{0:T(1024)S(1)}, f32[768]{0:T(1024)S(1)}, u32[]{:S(2)}, u32[]{:S(2)}) collective-permute-start(f32[768]{0:T(1024)S(1)} %get-tuple-element.21), channel_id=1, source_target_pairs={{12,0},{16,4},{20,8},{24,12},{28,16},{13,1},{17,5},{21,9},{25,13},... | collective-permute-start | bytes 9224 | tf_op jit(solution)/shard_map/ppermute | solution.py:14
  252.8 0.5 subtract_reduce_fusion
  253.4 2.0 collective-permute-done.13
  255.4 5.8 %all-reduce = f32[768]{0:T(1024)S(1)} all-reduce(f32[768]{0:T(1024)S(1)} %add_add_fusion), channel_id=2, replica_groups=mesh['var'=8,'samp'=4] {'samp'}, use_global_device_ids=true, to_apply=%region_13.14.clone | all-reduce | flops 768 | bytes 6144
  261.2 0.6 fusion.21
  (30 shorter events, 0.2 us)
Async XLA Ops:
  20.4 135.3 %collective-permute-start.4 = (bf16[2048,768]{1,0:T(8,128)(2,1)S(1)}, bf16[2048,768]{1,0:T(8,128)(2,1)S(1)}, u32[]{:S(2)}, u32[]{:S(2)}) collective-permute-start(bf16[2048,768]{1,0:T(8,128)(2,1)S(1)} %fusion.2), channel_id=1, source_target_pairs={{4,0},{8,4},{12,8},{16,12},{20,16},{24,20},{28,24},{5,1},{9,5},{13... | collective-permute-start | bytes 9437192 | tf_op jit(solution)/shard_map/ppermute | solution.py:14
  22.8 173.0 %collective-permute-start = (bf16[2048,768]{1,0:T(8,128)(2,1)S(1)}, bf16[2048,768]{1,0:T(8,128)(2,1)}, u32[]{:S(2)}, u32[]{:S(2)}) collective-permute-start(bf16[2048,768]{1,0:T(8,128)(2,1)S(1)} %fusion.2), channel_id=1, source_target_pairs={{8,0},{12,4},{16,8},{20,12},{24,16},{28,20},{9,1},{13,5},{17,9},{2... | collective-permute-start | bytes 9437192 | tf_op jit(solution)/shard_map/ppermute | solution.py:14
  25.1 170.7 %collective-permute-start.1 = (bf16[2048,768]{1,0:T(8,128)(2,1)S(1)}, bf16[2048,768]{1,0:T(8,128)(2,1)}, u32[]{:S(2)}, u32[]{:S(2)}) collective-permute-start(bf16[2048,768]{1,0:T(8,128)(2,1)S(1)} %fusion.2), channel_id=1, source_target_pairs={{0,12},{4,16},{8,20},{12,24},{16,28},{1,13},{5,17},{9,21},{13,25},... | collective-permute-start | bytes 9437192 | tf_op jit(solution)/shard_map/ppermute | solution.py:14
  34.9 124.9 %copy-start = (f32[768,768]{1,0:T(8,128)}, f32[768,768]{1,0:T(8,128)S(1)}, u32[]{:S(2)}) copy-start(f32[768,768]{1,0:T(8,128)S(1)} %get-tuple-element.30) | copy-start | bytes 7077892
  34.9 124.9 %collective-permute-start.2 = (bf16[768,768]{1,0:T(8,128)(2,1)S(1)}, bf16[768,768]{1,0:T(8,128)(2,1)S(1)}, u32[]{:S(2)}, u32[]{:S(2)}) collective-permute-start(bf16[768,768]{1,0:T(8,128)(2,1)S(1)} %get-tuple-element.29), channel_id=1, source_target_pairs={{1,0},{3,2},{5,4},{7,6},{9,8},{11,10},{13,12},{15,14},{17,16},{19,... | collective-permute-start | bytes 3538952 | tf_op jit(solution)/shard_map/ppermute | solution.py:43
  158.5 6.3 %copy-start.1 = (f32[768,768]{1,0:T(8,128)}, f32[768,768]{1,0:T(8,128)S(1)}, u32[]{:S(2)}) copy-start(f32[768,768]{1,0:T(8,128)S(1)} %get-tuple-element.32) | copy-start | bytes 7077892
  158.5 6.3 %collective-permute-start.5 = (bf16[768,768]{1,0:T(8,128)(2,1)S(1)}, bf16[768,768]{1,0:T(8,128)(2,1)S(1)}, u32[]{:S(2)}, u32[]{:S(2)}) collective-permute-start(bf16[768,768]{1,0:T(8,128)(2,1)S(1)} %get-tuple-element.31), channel_id=1, source_target_pairs={{0,1},{2,3},{4,5},{6,7},{8,9},{10,11},{12,13},{14,15},{16,17},{18,... | collective-permute-start | bytes 3538952 | tf_op jit(solution)/shard_map/ppermute | solution.py:43
  159.9 1.4 copy-start.5
  161.3 27.3 %collective-permute-start.3 = (bf16[768,768]{1,0:T(8,128)(2,1)}, bf16[768,768]{1,0:T(8,128)(2,1)}, u32[]{:S(2)}, u32[]{:S(2)}) collective-permute-start(bf16[768,768]{1,0:T(8,128)(2,1)} %fusion.5), channel_id=1, source_target_pairs={{2,0},{6,4},{10,8},{14,12},{18,16},{22,20},{26,24},{30,28}} | collective-permute-start | bytes 3538952 | tf_op jit(solution)/shard_map/ppermute | solution.py:45
  164.8 1.4 copy-start.6
  166.2 26.5 %collective-permute-start.6 = (bf16[768,768]{1,0:T(8,128)(2,1)}, bf16[768,768]{1,0:T(8,128)(2,1)}, u32[]{:S(2)}, u32[]{:S(2)}) collective-permute-start(bf16[768,768]{1,0:T(8,128)(2,1)} %fusion.6), channel_id=1, source_target_pairs={{3,1},{7,5},{11,9},{15,13},{19,17},{23,21},{27,25},{31,29}} | collective-permute-start | bytes 3538952 | tf_op jit(solution)/shard_map/ppermute | solution.py:45
  167.9 24.8 %copy-start.2 = (f32[768,768]{1,0:T(8,128)S(1)}, f32[768,768]{1,0:T(8,128)}, u32[]{:S(2)}) copy-start(f32[768,768]{1,0:T(8,128)} %copy-done.1) | copy-start | bytes 7077892
  167.9 24.8 %copy-start.7 = (bf16[768,768]{1,0:T(8,128)(2,1)S(1)}, bf16[768,768]{1,0:T(8,128)(2,1)}, u32[]{:S(2)}) copy-start(bf16[768,768]{1,0:T(8,128)(2,1)} %copy-done.6) | copy-start | bytes 3538948
  200.4 1.6 copy-start.10
  202.1 6.7 %copy-start.11 = (u32[32]{0:T(128)S(1)}, u32[32]{0:T(128)}, u32[]{:S(2)}) copy-start(u32[32]{0:T(128)} %constant.94) | copy-start | bytes 388
  202.1 7.9 %collective-permute-start.7 = (bf16[2,192,768]{2,1,0:T(8,128)(2,1)}, bf16[2,192,768]{2,1,0:T(8,128)(2,1)}, u32[]{:S(2)}, u32[]{:S(2)}) collective-permute-start(bf16[2,192,768]{2,1,0:T(8,128)(2,1)} %fusion.9), channel_id=1, source_target_pairs={{0,1},{1,0},{2,3},{3,2},{4,5},{5,4},{6,7},{7,6},{8,9},{9,8},{10,11... | collective-permute-start | bytes 1769480 | tf_op jit(solution)/shard_map/ppermute | solution.py:34
  206.7 1.4 copy-start.8
  208.2 6.0 %copy-start.9 = (f32[768,768]{1,0:T(8,128)S(1)}, f32[768,768]{1,0:T(8,128)}, u32[]{:S(2)}) copy-start(f32[768,768]{1,0:T(8,128)} %copy-done.8) | copy-start | bytes 7077892
  208.2 6.0 %collective-permute-start.9 = (bf16[2,192,768]{2,1,0:T(8,128)(2,1)S(1)}, bf16[2,192,768]{2,1,0:T(8,128)(2,1)S(1)}, u32[]{:S(2)}, u32[]{:S(2)}) collective-permute-start(bf16[2,192,768]{2,1,0:T(8,128)(2,1)S(1)} %fusion.10), channel_id=1, source_target_pairs={{0,1},{1,0},{2,3},{3,2},{4,5},{5,4},{6,7},{7,6},{8,9},{9,8},{10,11... | collective-permute-start | bytes 1769480 | tf_op jit(solution)/shard_map/ppermute | solution.py:34
  211.6 2.9 %copy-start.4 = (f32[768,768]{1,0:T(8,128)S(1)}, f32[768,768]{1,0:T(8,128)}, u32[]{:S(2)}) copy-start(f32[768,768]{1,0:T(8,128)} %convert_add_fusion) | copy-start | bytes 7077892
  211.6 31.3 %collective-permute-start.8 = (bf16[192,768]{1,0:T(8,128)(2,1)S(1)}, bf16[192,768]{1,0:T(8,128)(2,1)S(1)}, u32[]{:S(2)}, u32[]{:S(2)}) collective-permute-start(bf16[192,768]{1,0:T(8,128)(2,1)S(1)} %fusion.15), channel_id=1, source_target_pairs={{0,2},{1,3},{2,0},{3,1},{4,6},{5,7},{6,4},{7,5},{8,10},{9,11},{10,... | collective-permute-start | bytes 884744 | tf_op jit(solution)/shard_map/ppermute | solution.py:38
  214.3 38.5 %copy-start.3 = (f32[768,768]{1,0:T(8,128)S(1)}, f32[768,768]{1,0:T(8,128)}, u32[]{:S(2)}) copy-start(f32[768,768]{1,0:T(8,128)} %convert_add_fusion.2) | copy-start | bytes 7077892
  214.3 30.8 %collective-permute-start.10 = (bf16[192,768]{1,0:T(8,128)(2,1)S(1)}, bf16[192,768]{1,0:T(8,128)(2,1)S(1)}, u32[]{:S(2)}, u32[]{:S(2)}) collective-permute-start(bf16[192,768]{1,0:T(8,128)(2,1)S(1)} %fusion.16), channel_id=1, source_target_pairs={{0,2},{1,3},{2,0},{3,1},{4,6},{5,7},{6,4},{7,5},{8,10},{9,11},{10,... | collective-permute-start | bytes 884744 | tf_op jit(solution)/shard_map/ppermute | solution.py:38
  215.1 38.2 %collective-permute-start.11 = (f32[768]{0:T(1024)S(1)}, f32[768]{0:T(1024)S(1)}, u32[]{:S(2)}, u32[]{:S(2)}) collective-permute-start(f32[768]{0:T(1024)S(1)} %get-tuple-element.19), channel_id=1, source_target_pairs={{0,4},{4,8},{8,12},{12,16},{16,20},{20,24},{24,28},{1,5},{5,9},{9,... | collective-permute-start | bytes 9224 | tf_op jit(solution)/shard_map/ppermute | solution.py:14
  243.2 10.1 %collective-permute-start.12 = (f32[768]{0:T(1024)S(1)}, f32[768]{0:T(1024)S(1)}, u32[]{:S(2)}, u32[]{:S(2)}) collective-permute-start(f32[768]{0:T(1024)S(1)} %get-tuple-element.23), channel_id=1, source_target_pairs={{0,8},{4,12},{8,16},{12,20},{16,24},{20,28},{1,9},{5,13},{9,17},{1... | collective-permute-start | bytes 9224 | tf_op jit(solution)/shard_map/ppermute | solution.py:14
  245.5 9.9 %collective-permute-start.13 = (f32[768]{0:T(1024)S(1)}, f32[768]{0:T(1024)S(1)}, u32[]{:S(2)}, u32[]{:S(2)}) collective-permute-start(f32[768]{0:T(1024)S(1)} %get-tuple-element.21), channel_id=1, source_target_pairs={{12,0},{16,4},{20,8},{24,12},{28,16},{13,1},{17,5},{21,9},{25,13},... | collective-permute-start | bytes 9224 | tf_op jit(solution)/shard_map/ppermute | solution.py:14

commit v11 on v9

--- a/solution.py
+++ b/solution.py
@@ -5,7 +5,7 @@
 
 BAND = 3
 PARTNER_STEP = {1: 1, 2: 2, 3: -3}
-PROCESS_ORDER = (2, 3, 1)
+LATE_OFFSETS = (2, 3)
 
 
 def from_behind(value, axis, steps):
@@ -64,11 +64,12 @@
     raw = {offset: from_behind(standard, "var", -PARTNER_STEP[offset]) for offset in range(1, BAND + 1)}
 
     same_total = reduce_to_owner(gram_of(standard, standard), 0, n_samp)
-    arrived, same_total, standard_late = lax.optimization_barrier(
-        ([raw[d] for d in PROCESS_ORDER], same_total, standard)
+    next_gram = gram_of(standard, raw[1])
+    arrived, same_total, next_gram, standard_late = lax.optimization_barrier(
+        ([raw[d] for d in LATE_OFFSETS], same_total, next_gram, standard)
     )
-    owned = {}
-    for offset, partner in zip(PROCESS_ORDER, arrived):
+    owned = {1: reduce_quarters(next_gram, n_samp)}
+    for offset, partner in zip(LATE_OFFSETS, arrived):
         owned[offset] = reduce_quarters(gram_of(standard_late, partner), n_samp)
 
     me = lax.axis_index("samp")

time: 214 us -> 261 us (1.22); the launches traced: 213 us -> 257 us
  starting transfers between devices: 29.9 us -> 78.1 us
  waiting for transfers between devices: 133 us -> 128 us
    ppermute x6, starting transfers between devices: 20.7 us -> 67.8 us  [from_behind(): lax.ppermute(value, axis, [(source, source + steps) for source in range(l...]
    ppermute x3, waiting for transfers between devices: 10.5 us -> 5.87 us  [reduce_quarters(): lax.ppermute(send.astype(jnp.bfloat16), 'samp', pairs_chip)]
    ppermute x6, waiting for transfers between devices: 107 us -> 110 us  [from_behind(): lax.ppermute(value, axis, [(source, source + steps) for source in range(l...]
    ppermute x1, waiting for transfers between devices: 3.44 us -> 0.01 us  [reduce_to_owner(): lax.ppermute(part.astype(jnp.bfloat16), 'samp', pairs_core)]
  transfers between devices with their start and end apart: 14 -> 14, of which waited for: 9 -> 5; matrix products, arithmetic and copies ran while one was open for 9% -> 9% of each run, Pallas kernels for 0% -> 0%
where the time goes in v11:
time: 261 us; the launch traced here: 257 us
  waiting for transfers between devices  128 us (49%)
  starting transfers between devices  78.1 us (30%)
  other arithmetic  16.6 us (6%)
  matrix products  16.5 us (6%)
  blocking collectives  15.9 us (6%)
    ppermute x6, waiting for transfers between devices, from_behind(): lax.ppermute(value, axis, [(source, source + steps) for source in range(l...  110 us
    ppermute x6, starting transfers between devices, from_behind(): lax.ppermute(value, axis, [(source, source + steps) for source in range(l...  67.8 us
    dot_general x4, matrix products, gram_of(): lax.dot_general(left, right, (((0,), (0,)), ((), ())), preferred_element_...  16.5 us
    ppermute x1, waiting for transfers between devices, reduce_to_owner(): lax.ppermute(summed.astype(jnp.bfloat16), 'samp', pairs_chip)  11.7 us
    psum x1, blocking collectives, local(): lax.psum((jnp.sum(present, 0), jnp.sum(present * values, 0), jnp.sum(pres...  10.2 us
    ppermute x3, waiting for transfers between devices, reduce_quarters(): lax.ppermute(send.astype(jnp.bfloat16), 'samp', pairs_chip)  5.87 us
    unnamed x1, blocking collectives  5.75 us
    reduce_sum x1, other arithmetic, local(): jnp.sum(present * values, 0)  5.28 us
  transfers between devices with their start and end apart: 14, of which 5 were waited for; matrix products, arithmetic and copies ran while one was open for 9% of the time, Pallas kernels for 0%

profile of v11, /device:TPU:14, one launch (start us, length us, event | category | flops | bytes accessed | tf_op | source)
XLA Modules:
  0.0 256.9 jit_solution(8981482100284043309)
XLA Ops:
  0.0 5.3 %fusion.4 = (f32[768]{0:T(1024)S(1)}, f32[768]{0:T(1024)S(1)}, f32[768]{0:T(1024)S(1)}) fusion(bf16[2048,768]{1,0:T(8,128)(2,1)} %param.2, s32[2048,768]{1,0:T(8,128)} %param.3), kind=kLoop, calls=%fused_computation.8 | loop fusion | flops 11007744 | bytes 9446400 | tf_op jit(solution)/shard_map/reduce_sum | solution.py:52
  5.3 10.2 %all-reduce.1 = (f32[768]{0:T(1024)S(1)}, f32[768]{0:T(1024)S(1)}, f32[768]{0:T(1024)S(1)}) all-reduce(f32[768]{0:T(1024)S(1)} %get-tuple-element.16, f32[768]{0:T(1024)S(1)} %get-tuple-element.17, f32[768]{0:T(1024)S(1)} %get-tuple-element.15), channel_id=1, replica_groups=mesh['var'=8,'samp'=4] {'samp'}, use_global_device_ids=true, to_apply=%region_5.0 | all-reduce | flops 2304 | bytes 18432 | tf_op jit(solution)/shard_map/psum | solution.py:51
  15.5 4.9 %fusion.2 = bf16[2048,768]{1,0:T(8,128)(2,1)S(1)} fusion(bf16[2048,768]{1,0:T(8,128)(2,1)} %param.2, s32[2048,768]{1,0:T(8,128)} %param.3, f32[768]{0:T(1024)S(1)} %get-tuple-element.28, f32[768]{0:T(1024)S(1)} %get-tuple-element.27), kind=kLoop, calls=%fused_computation.5 | loop fusion | flops 9437184 | bytes 12589056 | tf_op jit(solution)/shard_map/convert_element_type | solution.py:58
  20.4 2.4 collective-permute-start.4
  22.8 2.7 %fusion.25 = (bf16[768,768]{1,0:T(8,128)(2,1)S(1)}, f32[768,768]{1,0:T(8,128)S(1)}) fusion(bf16[2048,768]{1,0:T(8,128)(2,1)S(1)} %fusion.2), kind=kOutput, calls=%fused_computation.51 | convolution fusion | flops 2416508928 | bytes 6684672 | tf_op jit(solution)/shard_map/dot_general | solution.py:24
  25.5 1.3 collective-permute-start.2
  26.8 2.3 collective-permute-start
  29.1 7.1 %collective-permute-start.1 = (bf16[2048,768]{1,0:T(8,128)(2,1)S(1)}, bf16[2048,768]{1,0:T(8,128)(2,1)}, u32[]{:S(2)}, u32[]{:S(2)}) collective-permute-start(bf16[2048,768]{1,0:T(8,128)(2,1)S(1)} %fusion.2), channel_id=1, source_target_pairs={{0,12},{4,16},{8,20},{12,24},{16,28},{1,13},{5,17},{9,21},{13,25},... | collective-permute-start | bytes 9437192 | tf_op jit(solution)/shard_map/ppermute | solution.py:14
  36.2 0.0 collective-permute-done.2
  36.3 0.0 copy-start.2
  36.3 1.4 fusion.5
  37.7 4.5 %collective-permute-start.3 = (bf16[768,768]{1,0:T(8,128)(2,1)}, bf16[768,768]{1,0:T(8,128)(2,1)}, u32[]{:S(2)}, u32[]{:S(2)}) collective-permute-start(bf16[768,768]{1,0:T(8,128)(2,1)} %fusion.5), channel_id=1, source_target_pairs={{2,0},{6,4},{10,8},{14,12},{18,16},{22,20},{26,24},{30,28}} | collective-permute-start | bytes 3538952 | tf_op jit(solution)/shard_map/ppermute | solution.py:45
  42.2 0.6 dynamic-slice
  43.4 11.7 %collective-permute-done.3 = bf16[768,768]{1,0:T(8,128)(2,1)} collective-permute-done((bf16[768,768]{1,0:T(8,128)(2,1)}, bf16[768,768]{1,0:T(8,128)(2,1)}, u32[]{:S(2)}, u32[]{:S(2)}) %collective-permute-start.3) | collective-permute-done | bytes 1179680 | tf_op jit(solution)/shard_map/ppermute | solution.py:45
  55.1 2.6 %convert_add_fusion = f32[768,768]{1,0:T(8,128)S(1)} fusion(bf16[768,768]{1,0:T(8,128)(2,1)} %collective-permute-done.3, f32[768,768]{1,0:T(8,128)} %copy-done, bf16[768,768]{1,0:T(8,128)(2,1)} %copy-done.1), kind=kLoop, calls=%fused_computation.10 | loop fusion | flops 2359296 | bytes 7077888 | tf_op jit(solution)/shard_map/add | solution.py:45
  57.8 91.9 %collective-permute-done.4 = bf16[2048,768]{1,0:T(8,128)(2,1)} collective-permute-done((bf16[2048,768]{1,0:T(8,128)(2,1)S(1)}, bf16[2048,768]{1,0:T(8,128)(2,1)}, u32[]{:S(2)}, u32[]{:S(2)}) %collective-permute-start.4) | collective-permute-done | bytes 3145760 | tf_op jit(solution)/shard_map/ppermute | solution.py:14
  149.7 4.6 %fusion.26 = f32[768,768]{1,0:T(8,128)S(1)} fusion(bf16[2048,768]{1,0:T(8,128)(2,1)S(1)} %fusion.2, bf16[2048,768]{1,0:T(8,128)(2,1)} %collective-permute-done.4), kind=kOutput, calls=%fused_computation.52 | convolution fusion | flops 2415919104 | bytes 8650752 | tf_op jit(solution)/shard_map/dot_general | solution.py:24
  154.3 16.0 %collective-permute-done.1 = bf16[2048,768]{1,0:T(8,128)(2,1)} collective-permute-done((bf16[2048,768]{1,0:T(8,128)(2,1)S(1)}, bf16[2048,768]{1,0:T(8,128)(2,1)}, u32[]{:S(2)}, u32[]{:S(2)}) %collective-permute-start.1) | collective-permute-done | bytes 3145760 | tf_op jit(solution)/shard_map/ppermute | solution.py:14
  170.3 0.1 fusion.6
  170.4 0.2 collective-permute-start.5
  170.6 4.6 %fusion.27 = f32[768,768]{1,0:T(8,128)S(1)} fusion(bf16[2048,768]{1,0:T(8,128)(2,1)S(1)} %fusion.2, bf16[2048,768]{1,0:T(8,128)(2,1)} %collective-permute-done), kind=kOutput, calls=%fused_computation.53 | convolution fusion | flops 2415919104 | bytes 8650752 | tf_op jit(solution)/shard_map/dot_general | solution.py:24
  175.2 0.1 fusion.7
  175.2 0.5 collective-permute-start.7
  175.7 4.6 %fusion.28 = f32[768,768]{1,0:T(8,128)S(1)} fusion(bf16[2048,768]{1,0:T(8,128)(2,1)S(1)} %fusion.2, bf16[2048,768]{1,0:T(8,128)(2,1)} %collective-permute-done.1), kind=kOutput, calls=%fused_computation.54 | convolution fusion | flops 2415919104 | bytes 8650752 | tf_op jit(solution)/shard_map/dot_general | solution.py:24
  180.3 0.1 fusion.8
  180.4 0.2 collective-permute-start.9
  180.6 0.0 collective-permute-done.5
  180.6 0.1 bitcast_add_fusion.2
  180.7 1.6 collective-permute-start.6
  182.3 0.1 bitcast_add_fusion.1
  182.5 0.6 collective-permute-start.8
  183.0 0.0 collective-permute-done.9
  183.0 0.1 bitcast_add_fusion
  183.2 1.6 collective-permute-start.10
  184.8 5.9 %collective-permute-done.6 = bf16[192,768]{1,0:T(8,128)(2,1)S(1)} collective-permute-done((bf16[192,768]{1,0:T(8,128)(2,1)S(1)}, bf16[192,768]{1,0:T(8,128)(2,1)S(1)}, u32[]{:S(2)}, u32[]{:S(2)}) %collective-permute-start.6) | collective-permute-done | bytes 294944 | tf_op jit(solution)/shard_map/ppermute | solution.py:38
  190.7 0.3 fusion.19
  191.0 47.5 %collective-permute-start.11 = (f32[768]{0:T(1024)S(1)}, f32[768]{0:T(1024)S(1)}, u32[]{:S(2)}, u32[]{:S(2)}) collective-permute-start(f32[768]{0:T(1024)S(1)} %get-tuple-element.21), channel_id=1, source_target_pairs={{0,4},{4,8},{8,12},{12,16},{16,20},{20,24},{24,28},{1,5},{5,9},{9,... | collective-permute-start | bytes 9224 | tf_op jit(solution)/shard_map/ppermute | solution.py:14
  238.5 0.3 fusion.21
  238.8 1.9 collective-permute-start.12
  240.7 0.0 collective-permute-done.10
  240.8 0.3 fusion.23
  241.0 6.5 %collective-permute-start.13 = (f32[768]{0:T(1024)S(1)}, f32[768]{0:T(1024)S(1)}, u32[]{:S(2)}, u32[]{:S(2)}) collective-permute-start(f32[768]{0:T(1024)S(1)} %get-tuple-element.23), channel_id=1, source_target_pairs={{12,0},{16,4},{20,8},{24,12},{28,16},{13,1},{17,5},{21,9},{25,13},... | collective-permute-start | bytes 9224 | tf_op jit(solution)/shard_map/ppermute | solution.py:14
  247.6 0.5 subtract_reduce_fusion
  248.1 0.0 collective-permute-done.11
  248.1 0.0 collective-permute-done.12
  248.1 2.4 collective-permute-done.13
  250.5 5.7 %all-reduce = f32[768]{0:T(1024)S(1)} all-reduce(f32[768]{0:T(1024)S(1)} %add_add_fusion), channel_id=2, replica_groups=mesh['var'=8,'samp'=4] {'samp'}, use_global_device_ids=true, to_apply=%region_13.14.clone | all-reduce | flops 768 | bytes 6144
  256.2 0.6 fusion.24
  (13 shorter events, 0.2 us)
Async XLA Ops:
  20.4 129.4 %collective-permute-start.4 = (bf16[2048,768]{1,0:T(8,128)(2,1)S(1)}, bf16[2048,768]{1,0:T(8,128)(2,1)}, u32[]{:S(2)}, u32[]{:S(2)}) collective-permute-start(bf16[2048,768]{1,0:T(8,128)(2,1)S(1)} %fusion.2), channel_id=1, source_target_pairs={{4,0},{8,4},{12,8},{16,12},{20,16},{24,20},{28,24},{5,1},{9,5},{13... | collective-permute-start | bytes 9437192 | tf_op jit(solution)/shard_map/ppermute | solution.py:14
  25.5 12.2 %copy-start = (f32[768,768]{1,0:T(8,128)}, f32[768,768]{1,0:T(8,128)S(1)}, u32[]{:S(2)}) copy-start(f32[768,768]{1,0:T(8,128)S(1)} %get-tuple-element.30) | copy-start | bytes 7077892
  25.5 10.7 %collective-permute-start.2 = (bf16[768,768]{1,0:T(8,128)(2,1)S(1)}, bf16[768,768]{1,0:T(8,128)(2,1)S(1)}, u32[]{:S(2)}, u32[]{:S(2)}) collective-permute-start(bf16[768,768]{1,0:T(8,128)(2,1)S(1)} %get-tuple-element.29), channel_id=1, source_target_pairs={{1,0},{3,2},{5,4},{7,6},{9,8},{11,10},{13,12},{15,14},{17,16},{19,... | collective-permute-start | bytes 3538952 | tf_op jit(solution)/shard_map/ppermute | solution.py:43
  26.8 127.5 %collective-permute-start = (bf16[2048,768]{1,0:T(8,128)(2,1)S(1)}, bf16[2048,768]{1,0:T(8,128)(2,1)}, u32[]{:S(2)}, u32[]{:S(2)}) collective-permute-start(bf16[2048,768]{1,0:T(8,128)(2,1)S(1)} %fusion.2), channel_id=1, source_target_pairs={{8,0},{12,4},{16,8},{20,12},{24,16},{28,20},{9,1},{13,5},{17,9},{2... | collective-permute-start | bytes 9437192 | tf_op jit(solution)/shard_map/ppermute | solution.py:14
  29.1 141.2 %collective-permute-start.1 = (bf16[2048,768]{1,0:T(8,128)(2,1)S(1)}, bf16[2048,768]{1,0:T(8,128)(2,1)}, u32[]{:S(2)}, u32[]{:S(2)}) collective-permute-start(bf16[2048,768]{1,0:T(8,128)(2,1)S(1)} %fusion.2), channel_id=1, source_target_pairs={{0,12},{4,16},{8,20},{12,24},{16,28},{1,13},{5,17},{9,21},{13,25},... | collective-permute-start | bytes 9437192 | tf_op jit(solution)/shard_map/ppermute | solution.py:14
  36.2 1.5 copy-start.1
  36.3 5.9 %copy-start.2 = (u32[32]{0:T(128)S(1)}, u32[32]{0:T(128)}, u32[]{:S(2)}) copy-start(u32[32]{0:T(128)} %constant.105) | copy-start | bytes 388
  37.7 17.4 %collective-permute-start.3 = (bf16[768,768]{1,0:T(8,128)(2,1)}, bf16[768,768]{1,0:T(8,128)(2,1)}, u32[]{:S(2)}, u32[]{:S(2)}) collective-permute-start(bf16[768,768]{1,0:T(8,128)(2,1)} %fusion.5), channel_id=1, source_target_pairs={{2,0},{6,4},{10,8},{14,12},{18,16},{22,20},{26,24},{30,28}} | collective-permute-start | bytes 3538952 | tf_op jit(solution)/shard_map/ppermute | solution.py:45
  170.4 10.2 %collective-permute-start.5 = (bf16[2,192,768]{2,1,0:T(8,128)(2,1)S(1)}, bf16[2,192,768]{2,1,0:T(8,128)(2,1)S(1)}, u32[]{:S(2)}, u32[]{:S(2)}) collective-permute-start(bf16[2,192,768]{2,1,0:T(8,128)(2,1)S(1)} %fusion.6), channel_id=1, source_target_pairs={{0,1},{1,0},{2,3},{3,2},{4,5},{5,4},{6,7},{7,6},{8,9},{9,8},{10,11... | collective-permute-start | bytes 1769480 | tf_op jit(solution)/shard_map/ppermute | solution.py:34
  175.2 7.1 %collective-permute-start.7 = (bf16[2,192,768]{2,1,0:T(8,128)(2,1)S(1)}, bf16[2,192,768]{2,1,0:T(8,128)(2,1)S(1)}, u32[]{:S(2)}, u32[]{:S(2)}) collective-permute-start(bf16[2,192,768]{2,1,0:T(8,128)(2,1)S(1)} %fusion.7), channel_id=1, source_target_pairs={{0,1},{1,0},{2,3},{3,2},{4,5},{5,4},{6,7},{7,6},{8,9},{9,8},{10,11... | collective-permute-start | bytes 1769480 | tf_op jit(solution)/shard_map/ppermute | solution.py:34
  180.4 2.7 %collective-permute-start.9 = (bf16[2,192,768]{2,1,0:T(8,128)(2,1)S(1)}, bf16[2,192,768]{2,1,0:T(8,128)(2,1)S(1)}, u32[]{:S(2)}, u32[]{:S(2)}) collective-permute-start(bf16[2,192,768]{2,1,0:T(8,128)(2,1)S(1)} %fusion.8), channel_id=1, source_target_pairs={{0,1},{1,0},{2,3},{3,2},{4,5},{5,4},{6,7},{7,6},{8,9},{9,8},{10,11... | collective-permute-start | bytes 1769480 | tf_op jit(solution)/shard_map/ppermute | solution.py:34
  180.7 9.9 %collective-permute-start.6 = (bf16[192,768]{1,0:T(8,128)(2,1)S(1)}, bf16[192,768]{1,0:T(8,128)(2,1)S(1)}, u32[]{:S(2)}, u32[]{:S(2)}) collective-permute-start(bf16[192,768]{1,0:T(8,128)(2,1)S(1)} %fusion.15), channel_id=1, source_target_pairs={{0,2},{1,3},{2,0},{3,1},{4,6},{5,7},{6,4},{7,5},{8,10},{9,11},{10,... | collective-permute-start | bytes 884744 | tf_op jit(solution)/shard_map/ppermute | solution.py:38
  182.5 56.0 %collective-permute-start.8 = (bf16[192,768]{1,0:T(8,128)(2,1)S(1)}, bf16[192,768]{1,0:T(8,128)(2,1)S(1)}, u32[]{:S(2)}, u32[]{:S(2)}) collective-permute-start(bf16[192,768]{1,0:T(8,128)(2,1)S(1)} %fusion.16), channel_id=1, source_target_pairs={{0,2},{1,3},{2,0},{3,1},{4,6},{5,7},{6,4},{7,5},{8,10},{9,11},{10,... | collective-permute-start | bytes 884744 | tf_op jit(solution)/shard_map/ppermute | solution.py:38
  183.2 57.5 %collective-permute-start.10 = (bf16[192,768]{1,0:T(8,128)(2,1)S(1)}, bf16[192,768]{1,0:T(8,128)(2,1)S(1)}, u32[]{:S(2)}, u32[]{:S(2)}) collective-permute-start(bf16[192,768]{1,0:T(8,128)(2,1)S(1)} %fusion.17), channel_id=1, source_target_pairs={{0,2},{1,3},{2,0},{3,1},{4,6},{5,7},{6,4},{7,5},{8,10},{9,11},{10,... | collective-permute-start | bytes 884744 | tf_op jit(solution)/shard_map/ppermute | solution.py:38
  191.0 57.1 %collective-permute-start.11 = (f32[768]{0:T(1024)S(1)}, f32[768]{0:T(1024)S(1)}, u32[]{:S(2)}, u32[]{:S(2)}) collective-permute-start(f32[768]{0:T(1024)S(1)} %get-tuple-element.21), channel_id=1, source_target_pairs={{0,4},{4,8},{8,12},{12,16},{16,20},{20,24},{24,28},{1,5},{5,9},{9,... | collective-permute-start | bytes 9224 | tf_op jit(solution)/shard_map/ppermute | solution.py:14
  238.8 9.3 %collective-permute-start.12 = (f32[768]{0:T(1024)S(1)}, f32[768]{0:T(1024)S(1)}, u32[]{:S(2)}, u32[]{:S(2)}) collective-permute-start(f32[768]{0:T(1024)S(1)} %get-tuple-element.19), channel_id=1, source_target_pairs={{0,8},{4,12},{8,16},{12,20},{16,24},{20,28},{1,9},{5,13},{9,17},{1... | collective-permute-start | bytes 9224 | tf_op jit(solution)/shard_map/ppermute | solution.py:14
  241.0 9.4 %collective-permute-start.13 = (f32[768]{0:T(1024)S(1)}, f32[768]{0:T(1024)S(1)}, u32[]{:S(2)}, u32[]{:S(2)}) collective-permute-start(f32[768]{0:T(1024)S(1)} %get-tuple-element.23), channel_id=1, source_target_pairs={{12,0},{16,4},{20,8},{24,12},{28,16},{13,1},{17,5},{21,9},{25,13},... | collective-permute-start | bytes 9224 | tf_op jit(solution)/shard_map/ppermute | solution.py:14

commit v12 on v9

--- a/solution.py
+++ b/solution.py
@@ -4,7 +4,7 @@
 from jax.sharding import PartitionSpec as P
 
 BAND = 3
-PARTNER_STEP = {1: 1, 2: 2, 3: -3}
+PARTNER_STEP = {1: 1, 2: 2, 3: 3}
 PROCESS_ORDER = (2, 3, 1)
 
 

time: 214 us -> 345 us (1.61)
  waiting for transfers between devices: 133 us -> 272 us
  starting transfers between devices: 29.9 us -> 21.2 us
    ppermute x6, waiting for transfers between devices: 107 us -> 242 us  [from_behind(): lax.ppermute(value, axis, [(source, source + steps) for source in range(l...]
    ppermute x6, starting transfers between devices: 20.7 us -> 12 us  [from_behind(): lax.ppermute(value, axis, [(source, source + steps) for source in range(l...]
    ppermute x3, waiting for transfers between devices: 10.5 us -> 14.6 us  [reduce_quarters(): lax.ppermute(send.astype(jnp.bfloat16), 'samp', pairs_chip)]
  transfers between devices with their start and end apart: 14 -> 14, of which waited for: 9 -> 9; matrix products, arithmetic and copies ran while one was open for 9% -> 5% of each run, Pallas kernels for 0% -> 0%
where the time goes in v12:
time: 345 us; the launch traced here: 344 us
  waiting for transfers between devices  272 us (79%)
  starting transfers between devices  21.2 us (6%)
  other arithmetic  16.6 us (5%)
  matrix products  16.5 us (5%)
  blocking collectives  16 us (5%)
    ppermute x6, waiting for transfers between devices, from_behind(): lax.ppermute(value, axis, [(source, source + steps) for source in range(l...  242 us
    dot_general x4, matrix products, gram_of(): lax.dot_general(left, right, (((0,), (0,)), ((), ())), preferred_element_...  16.5 us
    ppermute x3, waiting for transfers between devices, reduce_quarters(): lax.ppermute(send.astype(jnp.bfloat16), 'samp', pairs_chip)  14.6 us
    ppermute x6, starting transfers between devices, from_behind(): lax.ppermute(value, axis, [(source, source + steps) for source in range(l...  12 us
    ppermute x1, waiting for transfers between devices, reduce_to_owner(): lax.ppermute(summed.astype(jnp.bfloat16), 'samp', pairs_chip)  11.7 us
    psum x1, blocking collectives, local(): lax.psum((jnp.sum(present, 0), jnp.sum(present * values, 0), jnp.sum(pres...  10.2 us
  transfers between devices with their start and end apart: 14, of which 9 were waited for; matrix products, arithmetic and copies ran while one was open for 5% of the time, Pallas kernels for 0%

profile of v12, /device:TPU:14, one launch (start us, length us, event | category | flops | bytes accessed | tf_op | source)
XLA Modules:
  0.0 344.1 jit_solution(6855252447732292065)
XLA Ops:
  0.0 5.3 %fusion.4 = (f32[768]{0:T(1024)S(1)}, f32[768]{0:T(1024)S(1)}, f32[768]{0:T(1024)S(1)}) fusion(bf16[2048,768]{1,0:T(8,128)(2,1)} %param.2, s32[2048,768]{1,0:T(8,128)} %param.3), kind=kLoop, calls=%fused_computation.8 | loop fusion | flops 11007744 | bytes 9446400 | tf_op jit(solution)/shard_map/reduce_sum | solution.py:52
  5.3 10.2 %all-reduce.1 = (f32[768]{0:T(1024)S(1)}, f32[768]{0:T(1024)S(1)}, f32[768]{0:T(1024)S(1)}) all-reduce(f32[768]{0:T(1024)S(1)} %get-tuple-element.16, f32[768]{0:T(1024)S(1)} %get-tuple-element.17, f32[768]{0:T(1024)S(1)} %get-tuple-element.15), channel_id=1, replica_groups=mesh['var'=8,'samp'=4] {'samp'}, use_global_device_ids=true, to_apply=%region_5.0 | all-reduce | flops 2304 | bytes 18432 | tf_op jit(solution)/shard_map/psum | solution.py:51
  15.5 4.9 %fusion.2 = bf16[2048,768]{1,0:T(8,128)(2,1)S(1)} fusion(bf16[2048,768]{1,0:T(8,128)(2,1)} %param.2, s32[2048,768]{1,0:T(8,128)} %param.3, f32[768]{0:T(1024)S(1)} %get-tuple-element.28, f32[768]{0:T(1024)S(1)} %get-tuple-element.27), kind=kLoop, calls=%fused_computation.5 | loop fusion | flops 9437184 | bytes 12589056 | tf_op jit(solution)/shard_map/convert_element_type | solution.py:58
  20.4 2.4 collective-permute-start
  22.7 1.9 collective-permute-start.1
  24.7 1.9 collective-permute-start.2
  26.6 2.7 fusion.25
  29.3 1.3 collective-permute-start.3
  30.6 3.4 %collective-permute-done.3 = bf16[768,768]{1,0:T(8,128)(2,1)S(1)} collective-permute-done((bf16[768,768]{1,0:T(8,128)(2,1)S(1)}, bf16[768,768]{1,0:T(8,128)(2,1)S(1)}, u32[]{:S(2)}, u32[]{:S(2)}) %collective-permute-start.3) | collective-permute-done | bytes 1179680 | tf_op jit(solution)/shard_map/ppermute | solution.py:43
  34.1 1.4 fusion.5
  35.5 4.5 %collective-permute-start.4 = (bf16[768,768]{1,0:T(8,128)(2,1)}, bf16[768,768]{1,0:T(8,128)(2,1)}, u32[]{:S(2)}, u32[]{:S(2)}) collective-permute-start(bf16[768,768]{1,0:T(8,128)(2,1)} %fusion.5), channel_id=1, source_target_pairs={{2,0},{6,4},{10,8},{14,12},{18,16},{22,20},{26,24},{30,28}} | collective-permute-start | bytes 3538952 | tf_op jit(solution)/shard_map/ppermute | solution.py:45
  40.0 0.6 dynamic-slice
  41.2 11.7 %collective-permute-done.4 = bf16[768,768]{1,0:T(8,128)(2,1)} collective-permute-done((bf16[768,768]{1,0:T(8,128)(2,1)}, bf16[768,768]{1,0:T(8,128)(2,1)}, u32[]{:S(2)}, u32[]{:S(2)}) %collective-permute-start.4) | collective-permute-done | bytes 1179680 | tf_op jit(solution)/shard_map/ppermute | solution.py:45
  53.0 2.6 convert_add_fusion
  55.6 37.7 %collective-permute-done = bf16[2048,768]{1,0:T(8,128)(2,1)} collective-permute-done((bf16[2048,768]{1,0:T(8,128)(2,1)S(1)}, bf16[2048,768]{1,0:T(8,128)(2,1)}, u32[]{:S(2)}, u32[]{:S(2)}) %collective-permute-start) | collective-permute-done | bytes 3145760 | tf_op jit(solution)/shard_map/ppermute | solution.py:14
  93.3 68.4 %collective-permute-done.1 = bf16[2048,768]{1,0:T(8,128)(2,1)} collective-permute-done((bf16[2048,768]{1,0:T(8,128)(2,1)S(1)}, bf16[2048,768]{1,0:T(8,128)(2,1)}, u32[]{:S(2)}, u32[]{:S(2)}) %collective-permute-start.1) | collective-permute-done | bytes 3145760 | tf_op jit(solution)/shard_map/ppermute | solution.py:14
  161.8 132.2 %collective-permute-done.2 = bf16[2048,768]{1,0:T(8,128)(2,1)} collective-permute-done((bf16[2048,768]{1,0:T(8,128)(2,1)S(1)}, bf16[2048,768]{1,0:T(8,128)(2,1)}, u32[]{:S(2)}, u32[]{:S(2)}) %collective-permute-start.2) | collective-permute-done | bytes 3145760 | tf_op jit(solution)/shard_map/ppermute | solution.py:14
  293.9 4.6 %fusion.26 = f32[768,768]{1,0:T(8,128)S(1)} fusion(bf16[2048,768]{1,0:T(8,128)(2,1)S(1)} %fusion.2, bf16[2048,768]{1,0:T(8,128)(2,1)} %collective-permute-done.2), kind=kOutput, calls=%fused_computation.52 | convolution fusion | flops 2415919104 | bytes 8650752 | tf_op jit(solution)/shard_map/dot_general | solution.py:24
  298.5 0.1 fusion.6
  298.6 0.1 collective-permute-start.5
  298.7 4.6 %fusion.27 = f32[768,768]{1,0:T(8,128)S(1)} fusion(bf16[2048,768]{1,0:T(8,128)(2,1)S(1)} %fusion.2, bf16[2048,768]{1,0:T(8,128)(2,1)} %collective-permute-done), kind=kOutput, calls=%fused_computation.53 | convolution fusion | flops 2415919104 | bytes 8650752 | tf_op jit(solution)/shard_map/dot_general | solution.py:24
  303.3 0.1 fusion.7
  303.4 0.6 collective-permute-start.7
  303.9 4.6 %fusion.28 = f32[768,768]{1,0:T(8,128)S(1)} fusion(bf16[2048,768]{1,0:T(8,128)(2,1)S(1)} %fusion.2, bf16[2048,768]{1,0:T(8,128)(2,1)} %collective-permute-done.1), kind=kOutput, calls=%fused_computation.54 | convolution fusion | flops 2415919104 | bytes 8650752 | tf_op jit(solution)/shard_map/dot_general | solution.py:24
  308.5 0.1 fusion.8
  308.6 0.1 collective-permute-start.9
  308.7 0.0 collective-permute-done.5
  308.7 0.1 bitcast_add_fusion.2
  308.9 0.6 collective-permute-start.6
  309.4 0.0 collective-permute-done.7
  309.4 0.1 bitcast_add_fusion.1
  309.6 1.6 collective-permute-start.8
  311.2 0.0 collective-permute-done.9
  311.2 0.1 bitcast_add_fusion
  311.4 0.6 collective-permute-start.10
  311.9 6.9 %collective-permute-done.6 = bf16[192,768]{1,0:T(8,128)(2,1)S(1)} collective-permute-done((bf16[192,768]{1,0:T(8,128)(2,1)S(1)}, bf16[192,768]{1,0:T(8,128)(2,1)S(1)}, u32[]{:S(2)}, u32[]{:S(2)}) %collective-permute-start.6) | collective-permute-done | bytes 294944 | tf_op jit(solution)/shard_map/ppermute | solution.py:38
  318.8 0.3 fusion.19
  319.1 1.9 collective-permute-start.11
  321.0 4.1 %collective-permute-done.8 = bf16[192,768]{1,0:T(8,128)(2,1)S(1)} collective-permute-done((bf16[192,768]{1,0:T(8,128)(2,1)S(1)}, bf16[192,768]{1,0:T(8,128)(2,1)S(1)}, u32[]{:S(2)}, u32[]{:S(2)}) %collective-permute-start.8) | collective-permute-done | bytes 294944 | tf_op jit(solution)/shard_map/ppermute | solution.py:38
  325.1 0.3 fusion.21
  325.4 1.9 collective-permute-start.12
  327.3 3.6 %collective-permute-done.10 = bf16[192,768]{1,0:T(8,128)(2,1)S(1)} collective-permute-done((bf16[192,768]{1,0:T(8,128)(2,1)S(1)}, bf16[192,768]{1,0:T(8,128)(2,1)S(1)}, u32[]{:S(2)}, u32[]{:S(2)}) %collective-permute-start.10) | collective-permute-done | bytes 294944 | tf_op jit(solution)/shard_map/ppermute | solution.py:38
  331.0 0.3 fusion.23
  331.2 1.9 collective-permute-start.13
  333.2 0.5 subtract_reduce_fusion
  333.7 3.9 %collective-permute-done.13 = f32[768]{0:T(1024)S(1)} collective-permute-done((f32[768]{0:T(1024)S(1)}, f32[768]{0:T(1024)S(1)}, u32[]{:S(2)}, u32[]{:S(2)}) %collective-permute-start.13) | collective-permute-done | bytes 3104 | tf_op jit(solution)/shard_map/ppermute | solution.py:14
  337.7 5.8 %all-reduce = f32[768]{0:T(1024)S(1)} all-reduce(f32[768]{0:T(1024)S(1)} %add_add_fusion), channel_id=2, replica_groups=mesh['var'=8,'samp'=4] {'samp'}, use_global_device_ids=true, to_apply=%region_13.14.clone | all-reduce | flops 768 | bytes 6144
  343.5 0.6 fusion.24
  (13 shorter events, 0.2 us)
Async XLA Ops:
  20.4 73.0 %collective-permute-start = (bf16[2048,768]{1,0:T(8,128)(2,1)S(1)}, bf16[2048,768]{1,0:T(8,128)(2,1)}, u32[]{:S(2)}, u32[]{:S(2)}) collective-permute-start(bf16[2048,768]{1,0:T(8,128)(2,1)S(1)} %fusion.2), channel_id=1, source_target_pairs={{8,0},{12,4},{16,8},{20,12},{24,16},{28,20},{9,1},{13,5},{17,9},{2... | collective-permute-start | bytes 9437192 | tf_op jit(solution)/shard_map/ppermute | solution.py:14
  22.7 139.0 %collective-permute-start.1 = (bf16[2048,768]{1,0:T(8,128)(2,1)S(1)}, bf16[2048,768]{1,0:T(8,128)(2,1)}, u32[]{:S(2)}, u32[]{:S(2)}) collective-permute-start(bf16[2048,768]{1,0:T(8,128)(2,1)S(1)} %fusion.2), channel_id=1, source_target_pairs={{12,0},{16,4},{20,8},{24,12},{28,16},{13,1},{17,5},{21,9},{25,13},... | collective-permute-start | bytes 9437192 | tf_op jit(solution)/shard_map/ppermute | solution.py:14
  24.7 269.3 %collective-permute-start.2 = (bf16[2048,768]{1,0:T(8,128)(2,1)S(1)}, bf16[2048,768]{1,0:T(8,128)(2,1)}, u32[]{:S(2)}, u32[]{:S(2)}) collective-permute-start(bf16[2048,768]{1,0:T(8,128)(2,1)S(1)} %fusion.2), channel_id=1, source_target_pairs={{4,0},{8,4},{12,8},{16,12},{20,16},{24,20},{28,24},{5,1},{9,5},{13... | collective-permute-start | bytes 9437192 | tf_op jit(solution)/shard_map/ppermute | solution.py:14
  29.3 6.2 %copy-start = (f32[768,768]{1,0:T(8,128)}, f32[768,768]{1,0:T(8,128)S(1)}, u32[]{:S(2)}) copy-start(f32[768,768]{1,0:T(8,128)S(1)} %get-tuple-element.30) | copy-start | bytes 7077892
  29.3 4.7 %collective-permute-start.3 = (bf16[768,768]{1,0:T(8,128)(2,1)S(1)}, bf16[768,768]{1,0:T(8,128)(2,1)S(1)}, u32[]{:S(2)}, u32[]{:S(2)}) collective-permute-start(bf16[768,768]{1,0:T(8,128)(2,1)S(1)} %get-tuple-element.29), channel_id=1, source_target_pairs={{1,0},{3,2},{5,4},{7,6},{9,8},{11,10},{13,12},{15,14},{17,16},{19,... | collective-permute-start | bytes 3538952 | tf_op jit(solution)/shard_map/ppermute | solution.py:43
  34.1 1.5 copy-start.1
  34.1 5.9 %copy-start.2 = (u32[32]{0:T(128)S(1)}, u32[32]{0:T(128)}, u32[]{:S(2)}) copy-start(u32[32]{0:T(128)} %constant.104) | copy-start | bytes 388
  35.5 17.4 %collective-permute-start.4 = (bf16[768,768]{1,0:T(8,128)(2,1)}, bf16[768,768]{1,0:T(8,128)(2,1)}, u32[]{:S(2)}, u32[]{:S(2)}) collective-permute-start(bf16[768,768]{1,0:T(8,128)(2,1)} %fusion.5), channel_id=1, source_target_pairs={{2,0},{6,4},{10,8},{14,12},{18,16},{22,20},{26,24},{30,28}} | collective-permute-start | bytes 3538952 | tf_op jit(solution)/shard_map/ppermute | solution.py:45
  298.6 10.1 %collective-permute-start.5 = (bf16[2,192,768]{2,1,0:T(8,128)(2,1)S(1)}, bf16[2,192,768]{2,1,0:T(8,128)(2,1)S(1)}, u32[]{:S(2)}, u32[]{:S(2)}) collective-permute-start(bf16[2,192,768]{2,1,0:T(8,128)(2,1)S(1)} %fusion.6), channel_id=1, source_target_pairs={{0,1},{1,0},{2,3},{3,2},{4,5},{5,4},{6,7},{7,6},{8,9},{9,8},{10,11... | collective-permute-start | bytes 1769480 | tf_op jit(solution)/shard_map/ppermute | solution.py:34
  303.4 6.1 %collective-permute-start.7 = (bf16[2,192,768]{2,1,0:T(8,128)(2,1)S(1)}, bf16[2,192,768]{2,1,0:T(8,128)(2,1)S(1)}, u32[]{:S(2)}, u32[]{:S(2)}) collective-permute-start(bf16[2,192,768]{2,1,0:T(8,128)(2,1)S(1)} %fusion.7), channel_id=1, source_target_pairs={{0,1},{1,0},{2,3},{3,2},{4,5},{5,4},{6,7},{7,6},{8,9},{9,8},{10,11... | collective-permute-start | bytes 1769480 | tf_op jit(solution)/shard_map/ppermute | solution.py:34
  308.6 2.6 collective-permute-start.9
  308.9 9.9 %collective-permute-start.6 = (bf16[192,768]{1,0:T(8,128)(2,1)S(1)}, bf16[192,768]{1,0:T(8,128)(2,1)S(1)}, u32[]{:S(2)}, u32[]{:S(2)}) collective-permute-start(bf16[192,768]{1,0:T(8,128)(2,1)S(1)} %fusion.15), channel_id=1, source_target_pairs={{0,2},{1,3},{2,0},{3,1},{4,6},{5,7},{6,4},{7,5},{8,10},{9,11},{10,... | collective-permute-start | bytes 884744 | tf_op jit(solution)/shard_map/ppermute | solution.py:38
  309.6 15.5 %collective-permute-start.8 = (bf16[192,768]{1,0:T(8,128)(2,1)S(1)}, bf16[192,768]{1,0:T(8,128)(2,1)S(1)}, u32[]{:S(2)}, u32[]{:S(2)}) collective-permute-start(bf16[192,768]{1,0:T(8,128)(2,1)S(1)} %fusion.16), channel_id=1, source_target_pairs={{0,2},{1,3},{2,0},{3,1},{4,6},{5,7},{6,4},{7,5},{8,10},{9,11},{10,... | collective-permute-start | bytes 884744 | tf_op jit(solution)/shard_map/ppermute | solution.py:38
  311.4 19.6 %collective-permute-start.10 = (bf16[192,768]{1,0:T(8,128)(2,1)S(1)}, bf16[192,768]{1,0:T(8,128)(2,1)S(1)}, u32[]{:S(2)}, u32[]{:S(2)}) collective-permute-start(bf16[192,768]{1,0:T(8,128)(2,1)S(1)} %fusion.17), channel_id=1, source_target_pairs={{0,2},{1,3},{2,0},{3,1},{4,6},{5,7},{6,4},{7,5},{8,10},{9,11},{10,... | collective-permute-start | bytes 884744 | tf_op jit(solution)/shard_map/ppermute | solution.py:38
  319.1 14.6 %collective-permute-start.11 = (f32[768]{0:T(1024)S(1)}, f32[768]{0:T(1024)S(1)}, u32[]{:S(2)}, u32[]{:S(2)}) collective-permute-start(f32[768]{0:T(1024)S(1)} %get-tuple-element.21), channel_id=1, source_target_pairs={{0,4},{4,8},{8,12},{12,16},{16,20},{20,24},{24,28},{1,5},{5,9},{9,... | collective-permute-start | bytes 9224 | tf_op jit(solution)/shard_map/ppermute | solution.py:14
  325.4 8.3 %collective-permute-start.12 = (f32[768]{0:T(1024)S(1)}, f32[768]{0:T(1024)S(1)}, u32[]{:S(2)}, u32[]{:S(2)}) collective-permute-start(f32[768]{0:T(1024)S(1)} %get-tuple-element.19), channel_id=1, source_target_pairs={{0,8},{4,12},{8,16},{12,20},{16,24},{20,28},{1,9},{5,13},{9,17},{1... | collective-permute-start | bytes 9224 | tf_op jit(solution)/shard_map/ppermute | solution.py:14
  331.2 6.4 %collective-permute-start.13 = (f32[768]{0:T(1024)S(1)}, f32[768]{0:T(1024)S(1)}, u32[]{:S(2)}, u32[]{:S(2)}) collective-permute-start(f32[768]{0:T(1024)S(1)} %get-tuple-element.23), channel_id=1, source_target_pairs={{0,12},{4,16},{8,20},{12,24},{16,28},{1,13},{5,17},{9,21},{13,25},... | collective-permute-start | bytes 9224 | tf_op jit(solution)/shard_map/ppermute | solution.py:14

commit v13 on v9

--- a/solution.py
+++ b/solution.py
@@ -48,27 +48,34 @@
 def local(dosages, observed):
     values = dosages.astype(jnp.float32)
     present = observed.astype(jnp.float32)
-    seen_count, first_sum, second_sum = lax.psum(
-        (jnp.sum(present, 0), jnp.sum(present * values, 0), jnp.sum(present * values * values, 0)),
-        "samp",
-    )
-    seen_count = jnp.maximum(seen_count, 1.0)
-    column_mean = first_sum / seen_count
-    spread = second_sum / seen_count - column_mean * column_mean
-    standard = ((values - column_mean) * lax.rsqrt(spread + 1e-05) * present).astype(jnp.bfloat16)
     n_samp = lax.axis_size("samp")
     n_var = lax.axis_size("var")
+    position = lax.axis_index("var")
+    partial = jnp.stack([jnp.sum(present, 0), jnp.sum(present * values, 0), jnp.sum(present * values * values, 0)])
+    partner_partials = [from_behind(partial, "var", -PARTNER_STEP[d]) for d in PROCESS_ORDER]
+    coded = jnp.where(observed != 0, dosages, jnp.asarray(-1, dosages.dtype))
+    coded, partner_partials = lax.optimization_barrier((coded, partner_partials))
+    raw = {offset: from_behind(coded, "var", -PARTNER_STEP[offset]) for offset in range(1, BAND + 1)}
+    stats = lax.psum(jnp.stack([partial] + partner_partials), "samp")
+    seen_count = jnp.maximum(stats[:, 0], 1.0)
+    column_mean = stats[:, 1] / seen_count
+    spread = stats[:, 2] / seen_count - column_mean * column_mean
+    scale = lax.rsqrt(spread + 1e-05)
+    standard = ((values - column_mean[0]) * scale[0] * present).astype(jnp.bfloat16)
     samples = standard.shape[0] * n_samp
     block_width = standard.shape[1]
-    position = lax.axis_index("var")
-    raw = {offset: from_behind(standard, "var", -PARTNER_STEP[offset]) for offset in range(1, BAND + 1)}
 
     same_total = reduce_to_owner(gram_of(standard, standard), 0, n_samp)
     arrived, same_total, standard_late = lax.optimization_barrier(
         ([raw[d] for d in PROCESS_ORDER], same_total, standard)
     )
     owned = {}
-    for offset, partner in zip(PROCESS_ORDER, arrived):
+    for index, (offset, coded_partner) in enumerate(zip(PROCESS_ORDER, arrived)):
+        partner_values = coded_partner.astype(jnp.float32)
+        partner_present = (partner_values >= 0).astype(jnp.float32)
+        partner = (
+            (partner_values - column_mean[index + 1]) * scale[index + 1] * partner_present
+        ).astype(jnp.bfloat16)
         owned[offset] = reduce_quarters(gram_of(standard_late, partner), n_samp)
 
     me = lax.axis_index("samp")

time: 214 us -> 212 us (level)
  waiting for transfers between devices: 133 us -> 119 us
  starting transfers between devices: 29.9 us -> 38.3 us
    ppermute x6 -> x9, waiting for transfers between devices: 107 us -> 93.9 us  [from_behind(): lax.ppermute(value, axis, [(source, source + steps) for source in range(l...]
    ppermute x6 -> x9, starting transfers between devices: 20.7 us -> 30.1 us  [from_behind(): lax.ppermute(value, axis, [(source, source + steps) for source in range(l...]
    select_n x0 -> x1, other arithmetic: none -> 2.51 us  [local(): coded = jnp.where(observed != 0, dosages, jnp.asarray(-1, dosages.dtype))]
  transfers between devices with their start and end apart: 14 -> 17, of which waited for: 9 -> 10; matrix products, arithmetic and copies ran while one was open for 9% -> 12% of each run, Pallas kernels for 0% -> 0%
where the time goes in v13:
time: 212 us
  waiting for transfers between devices  119 us (56%)
  starting transfers between devices  38.3 us (18%)
  matrix products  17.3 us (8%)
  blocking collectives  17.2 us (8%)
  other arithmetic  17.1 us (8%)
  local copies, waits for them, and re-layouts  2.25 us (1%)
    ppermute x9, waiting for transfers between devices, from_behind(): lax.ppermute(value, axis, [(source, source + steps) for source in range(l...  93.9 us
    ppermute x9, starting transfers between devices, from_behind(): lax.ppermute(value, axis, [(source, source + steps) for source in range(l...  30.1 us
    dot_general x4, matrix products, gram_of(): lax.dot_general(left, right, (((0,), (0,)), ((), ())), preferred_element_...  17.3 us
    psum x1, blocking collectives, local(): stats = lax.psum(jnp.stack([partial] + partner_partials), 'samp')  11.3 us
    ppermute x1, waiting for transfers between devices, reduce_to_owner(): lax.ppermute(summed.astype(jnp.bfloat16), 'samp', pairs_chip)  11.1 us
    ppermute x3, waiting for transfers between devices, reduce_quarters(): lax.ppermute(send.astype(jnp.bfloat16), 'samp', pairs_chip)  10.3 us
    unnamed x1, blocking collectives  5.88 us
    reduce_sum x1, other arithmetic, local(): jnp.sum(present * values, 0)  5.42 us
  transfers between devices with their start and end apart: 17, of which 10 were waited for; matrix products, arithmetic and copies ran while one was open for 12% of the time, Pallas kernels for 0%

profile of v13, /device:TPU:14, one launch (start us, length us, event | category | flops | bytes accessed | tf_op | source)
XLA Modules:
  0.0 211.9 jit_solution(14062730401039141935)
XLA Ops:
  0.0 5.4 %fusion.13 = (f32[768]{0:T(1024)S(1)}, f32[768]{0:T(1024)S(1)}, f32[768]{0:T(1024)S(1)}) fusion(bf16[2048,768]{1,0:T(8,128)(2,1)} %param.2, s32[2048,768]{1,0:T(8,128)} %param.3), kind=kLoop, calls=%fused_computation.24 | loop fusion | flops 11007744 | bytes 9446400 | tf_op jit(solution)/shard_map/reduce_sum | solution.py:54
  5.5 2.4 %collective-permute-start = (f32[3,768]{1,0:T(4,128)S(1)}, f32[3,768]{1,0:T(4,128)S(1)}, u32[]{:S(2)}, u32[]{:S(2)}) collective-permute-start(f32[3,768]{1,0:T(4,128)S(1)} %get-tuple-element.43), channel_id=1, source_target_pairs={{8,0},{12,4},{16,8},{20,12},{24,16},{28,20},{9,1},{13,5},{17,9},{2... | collective-permute-start | bytes 27656 | tf_op jit(solution)/shard_map/ppermute | solution.py:14
  7.8 4.4 %collective-permute-start.1 = (f32[3,768]{1,0:T(4,128)S(1)}, f32[3,768]{1,0:T(4,128)S(1)}, u32[]{:S(2)}, u32[]{:S(2)}) collective-permute-start(f32[3,768]{1,0:T(4,128)S(1)} %get-tuple-element.43), channel_id=1, source_target_pairs={{0,12},{4,16},{8,20},{12,24},{16,28},{1,13},{5,17},{9,21},{13,25},... | collective-permute-start | bytes 27656 | tf_op jit(solution)/shard_map/ppermute | solution.py:14
  12.3 2.4 %collective-permute-start.2 = (f32[3,768]{1,0:T(4,128)S(1)}, f32[3,768]{1,0:T(4,128)S(1)}, u32[]{:S(2)}, u32[]{:S(2)}) collective-permute-start(f32[3,768]{1,0:T(4,128)S(1)} %get-tuple-element.43), channel_id=1, source_target_pairs={{4,0},{8,4},{12,8},{16,12},{20,16},{24,20},{28,24},{5,1},{9,5},{13... | collective-permute-start | bytes 27656 | tf_op jit(solution)/shard_map/ppermute | solution.py:14
  14.7 2.5 %compare_select_fusion = bf16[2048,768]{1,0:T(8,128)(2,1)} fusion(bf16[2048,768]{1,0:T(8,128)(2,1)S(1)} %copy-done.1, s32[2048,768]{1,0:T(8,128)S(1)} %copy-done), kind=kLoop, calls=%fused_computation.23 | loop fusion | flops 3145728 | bytes 12582912 | tf_op jit(solution)/shard_map/jit(_where)/select_n | solution.py:56
  17.2 1.5 collective-permute-done.2
  18.8 2.3 %collective-permute-start.3 = (bf16[2048,768]{1,0:T(8,128)(2,1)}, bf16[2048,768]{1,0:T(8,128)(2,1)}, u32[]{:S(2)}, u32[]{:S(2)}) collective-permute-start(bf16[2048,768]{1,0:T(8,128)(2,1)} %compare_select_fusion), channel_id=1, source_target_pairs={{8,0},{12,4},{16,8},{20,12},{24,16},{28,20},{9,1},{13,5},{17,9},{2... | collective-permute-start | bytes 9437192 | tf_op jit(solution)/shard_map/ppermute | solution.py:14
  21.1 5.5 %collective-permute-start.4 = (bf16[2048,768]{1,0:T(8,128)(2,1)}, bf16[2048,768]{1,0:T(8,128)(2,1)}, u32[]{:S(2)}, u32[]{:S(2)}) collective-permute-start(bf16[2048,768]{1,0:T(8,128)(2,1)} %compare_select_fusion), channel_id=1, source_target_pairs={{0,12},{4,16},{8,20},{12,24},{16,28},{1,13},{5,17},{9,21},{13,25},... | collective-permute-start | bytes 9437192 | tf_op jit(solution)/shard_map/ppermute | solution.py:14
  26.7 3.0 %collective-permute-start.5 = (bf16[2048,768]{1,0:T(8,128)(2,1)}, bf16[2048,768]{1,0:T(8,128)(2,1)}, u32[]{:S(2)}, u32[]{:S(2)}) collective-permute-start(bf16[2048,768]{1,0:T(8,128)(2,1)} %compare_select_fusion), channel_id=1, source_target_pairs={{4,0},{8,4},{12,8},{16,12},{20,16},{24,20},{28,24},{5,1},{9,5},{13... | collective-permute-start | bytes 9437192 | tf_op jit(solution)/shard_map/ppermute | solution.py:14
  29.7 11.3 %psum.7 = f32[4,3,768]{2,1,0:T(4,128)S(1)} all-reduce(f32[4,3,768]{2,1,0:T(4,128)S(1)} %pad_maximum_fusion), channel_id=1, replica_groups=mesh['var'=8,'samp'=4] {'samp'}, use_global_device_ids=true, to_apply=%region_3.4 | all-reduce | flops 9216 | bytes 73728 | tf_op jit(solution)/shard_map/psum | solution.py:59
  41.1 0.7 slice_reduce_fusion.4
  41.7 3.9 %fusion.12 = bf16[2048,768]{1,0:T(8,128)(2,1)S(1)} fusion(bf16[2048,768]{1,0:T(8,128)(2,1)S(1)} %copy-done.1, s32[2048,768]{1,0:T(8,128)} %param.3, f32[768]{0:T(1024)S(1)} %get-tuple-element.38, f32[768]{0:T(1024)S(1)} %get-tuple-element.46), kind=kLoop, calls=%fused_computation.21 | loop fusion | flops 9437184 | bytes 12589056 | tf_op jit(solution)/shard_map/convert_element_type | solution.py:64
  45.7 2.7 %fusion.54 = (bf16[768,768]{1,0:T(8,128)(2,1)S(1)}, f32[768,768]{1,0:T(8,128)S(1)}) fusion(bf16[2048,768]{1,0:T(8,128)(2,1)S(1)} %fusion.12), kind=kOutput, calls=%fused_computation.96 | convolution fusion | flops 2416508928 | bytes 6684672 | tf_op jit(solution)/shard_map/dot_general | solution.py:24
  48.4 1.3 collective-permute-start.6
  49.7 3.4 %collective-permute-done.6 = bf16[768,768]{1,0:T(8,128)(2,1)S(1)} collective-permute-done((bf16[768,768]{1,0:T(8,128)(2,1)S(1)}, bf16[768,768]{1,0:T(8,128)(2,1)S(1)}, u32[]{:S(2)}, u32[]{:S(2)}) %collective-permute-start.6) | collective-permute-done | bytes 1179680 | tf_op jit(solution)/shard_map/ppermute | solution.py:43
  53.2 1.3 fusion.29
  54.4 3.4 %collective-permute-start.7 = (bf16[768,768]{1,0:T(8,128)(2,1)}, bf16[768,768]{1,0:T(8,128)(2,1)}, u32[]{:S(2)}, u32[]{:S(2)}) collective-permute-start(bf16[768,768]{1,0:T(8,128)(2,1)} %fusion.29), channel_id=1, source_target_pairs={{2,0},{6,4},{10,8},{14,12},{18,16},{22,20},{26,24},{30,28}} | collective-permute-start | bytes 3538952 | tf_op jit(solution)/shard_map/ppermute | solution.py:45
  57.9 1.2 dynamic-slice
  59.8 11.1 %collective-permute-done.7 = bf16[768,768]{1,0:T(8,128)(2,1)} collective-permute-done((bf16[768,768]{1,0:T(8,128)(2,1)}, bf16[768,768]{1,0:T(8,128)(2,1)}, u32[]{:S(2)}, u32[]{:S(2)}) %collective-permute-start.7) | collective-permute-done | bytes 1179680 | tf_op jit(solution)/shard_map/ppermute | solution.py:45
  70.9 1.6 convert_add_fusion
  72.5 16.7 %collective-permute-done.3 = bf16[2048,768]{1,0:T(8,128)(2,1)} collective-permute-done((bf16[2048,768]{1,0:T(8,128)(2,1)}, bf16[2048,768]{1,0:T(8,128)(2,1)}, u32[]{:S(2)}, u32[]{:S(2)}) %collective-permute-start.3) | collective-permute-done | bytes 3145760 | tf_op jit(solution)/shard_map/ppermute | solution.py:14
  89.1 69.7 %collective-permute-done.4 = bf16[2048,768]{1,0:T(8,128)(2,1)} collective-permute-done((bf16[2048,768]{1,0:T(8,128)(2,1)}, bf16[2048,768]{1,0:T(8,128)(2,1)}, u32[]{:S(2)}, u32[]{:S(2)}) %collective-permute-start.4) | collective-permute-done | bytes 3145760 | tf_op jit(solution)/shard_map/ppermute | solution.py:14
  158.8 0.7 collective-permute-done.5
  159.5 4.9 %fusion.18 = f32[768,768]{1,0:T(8,128)S(1)} fusion(bf16[2048,768]{1,0:T(8,128)(2,1)S(1)} %copy-done.3, bf16[2048,768]{1,0:T(8,128)(2,1)} %collective-permute-done.5, f32[768]{0:T(1024)S(1)} %copy-done.4, f32[768]{0:T(1024)S(1)} %copy-done.5), kind=kOutput, calls=%fused_computation.27 | convolution fusion | flops 2425356288 | bytes 8656896 | tf_op jit(solution)/shard_map/dot_general | solution.py:24
  164.5 0.1 collective-permute-start.8
  164.5 4.9 %fusion.16 = f32[768,768]{1,0:T(8,128)S(1)} fusion(bf16[2048,768]{1,0:T(8,128)(2,1)S(1)} %copy-done.3, bf16[2048,768]{1,0:T(8,128)(2,1)} %collective-permute-done.3, f32[768]{0:T(1024)S(1)} %get-tuple-element.37, f32[768]{0:T(1024)S(1)} %get-tuple-element.47), kind=kOutput, calls=%fused_computation.26 | convolution fusion | flops 2425356288 | bytes 8656896 | tf_op jit(solution)/shard_map/dot_general | solution.py:24
  169.5 0.6 collective-permute-start.10
  170.1 4.9 %fusion.14 = f32[768,768]{1,0:T(8,128)S(1)} fusion(bf16[2048,768]{1,0:T(8,128)(2,1)S(1)} %copy-done.3, bf16[2048,768]{1,0:T(8,128)(2,1)} %collective-permute-done.4, f32[768]{0:T(1024)S(1)} %get-tuple-element.39, f32[768]{0:T(1024)S(1)} %get-tuple-element.48), kind=kOutput, calls=%fused_computation.25 | convolution fusion | flops 2425356288 | bytes 8656896 | tf_op jit(solution)/shard_map/dot_general | solution.py:24
  175.0 0.1 collective-permute-start.12
  175.1 0.1 bitcast_add_fusion.2
  175.3 0.6 collective-permute-start.9
  175.9 0.1 bitcast_add_fusion.1
  176.0 1.6 collective-permute-start.11
  177.6 0.1 bitcast_add_fusion
  177.8 0.6 collective-permute-start.13
  178.4 6.9 %collective-permute-done.9 = bf16[192,768]{1,0:T(8,128)(2,1)S(1)} collective-permute-done((bf16[192,768]{1,0:T(8,128)(2,1)S(1)}, bf16[192,768]{1,0:T(8,128)(2,1)S(1)}, u32[]{:S(2)}, u32[]{:S(2)}) %collective-permute-start.9) | collective-permute-done | bytes 294944 | tf_op jit(solution)/shard_map/ppermute | solution.py:38
  185.2 0.3 fusion.43
  185.5 4.7 %collective-permute-start.14 = (f32[768]{0:T(1024)S(1)}, f32[768]{0:T(1024)S(1)}, u32[]{:S(2)}, u32[]{:S(2)}) collective-permute-start(f32[768]{0:T(1024)S(1)} %get-tuple-element.29), channel_id=1, source_target_pairs={{0,4},{4,8},{8,12},{12,16},{16,20},{20,24},{24,28},{1,5},{5,9},{9,... | collective-permute-start | bytes 9224 | tf_op jit(solution)/shard_map/ppermute | solution.py:14
  190.2 1.4 collective-permute-done.11
  191.5 0.3 fusion.45
  191.8 3.5 %collective-permute-start.15 = (f32[768]{0:T(1024)S(1)}, f32[768]{0:T(1024)S(1)}, u32[]{:S(2)}, u32[]{:S(2)}) collective-permute-start(f32[768]{0:T(1024)S(1)} %get-tuple-element.27), channel_id=1, source_target_pairs={{0,8},{4,12},{8,16},{12,20},{16,24},{20,28},{1,9},{5,13},{9,17},{1... | collective-permute-start | bytes 9224 | tf_op jit(solution)/shard_map/ppermute | solution.py:14
  195.3 2.1 collective-permute-done.13
  197.4 0.3 fusion.47
  197.7 1.9 collective-permute-start.16
  199.6 0.5 subtract_reduce_fusion
  200.1 5.3 %collective-permute-done.16 = f32[768]{0:T(1024)S(1)} collective-permute-done((f32[768]{0:T(1024)S(1)}, f32[768]{0:T(1024)S(1)}, u32[]{:S(2)}, u32[]{:S(2)}) %collective-permute-start.16) | collective-permute-done | bytes 3104 | tf_op jit(solution)/shard_map/ppermute | solution.py:14
  205.4 5.9 %all-reduce = f32[768]{0:T(1024)S(1)} all-reduce(f32[768]{0:T(1024)S(1)} %add_add_fusion), channel_id=2, replica_groups=mesh['var'=8,'samp'=4] {'samp'}, use_global_device_ids=true, to_apply=%region_11.12.clone | all-reduce | flops 768 | bytes 6144
  211.3 0.6 fusion.49
  (32 shorter events, 0.5 us)
Async XLA Ops:
  0.0 14.7 %copy-start.1 = (bf16[2048,768]{1,0:T(8,128)(2,1)S(1)}, bf16[2048,768]{1,0:T(8,128)(2,1)}, u32[]{:S(2)}) copy-start(bf16[2048,768]{1,0:T(8,128)(2,1)} %param.2) | copy-start | bytes 9437188
  0.0 14.7 %copy-start = (s32[2048,768]{1,0:T(8,128)S(1)}, s32[2048,768]{1,0:T(8,128)}, u32[]{:S(2)}) copy-start(s32[2048,768]{1,0:T(8,128)} %param.3) | copy-start | bytes 18874372
  5.5 11.8 %collective-permute-start = (f32[3,768]{1,0:T(4,128)S(1)}, f32[3,768]{1,0:T(4,128)S(1)}, u32[]{:S(2)}, u32[]{:S(2)}) collective-permute-start(f32[3,768]{1,0:T(4,128)S(1)} %get-tuple-element.43), channel_id=1, source_target_pairs={{8,0},{12,4},{16,8},{20,12},{24,16},{28,20},{9,1},{13,5},{17,9},{2... | collective-permute-start | bytes 27656 | tf_op jit(solution)/shard_map/ppermute | solution.py:14
  7.8 9.4 %collective-permute-start.1 = (f32[3,768]{1,0:T(4,128)S(1)}, f32[3,768]{1,0:T(4,128)S(1)}, u32[]{:S(2)}, u32[]{:S(2)}) collective-permute-start(f32[3,768]{1,0:T(4,128)S(1)} %get-tuple-element.43), channel_id=1, source_target_pairs={{0,12},{4,16},{8,20},{12,24},{16,28},{1,13},{5,17},{9,21},{13,25},... | collective-permute-start | bytes 27656 | tf_op jit(solution)/shard_map/ppermute | solution.py:14
  12.3 6.5 %collective-permute-start.2 = (f32[3,768]{1,0:T(4,128)S(1)}, f32[3,768]{1,0:T(4,128)S(1)}, u32[]{:S(2)}, u32[]{:S(2)}) collective-permute-start(f32[3,768]{1,0:T(4,128)S(1)} %get-tuple-element.43), channel_id=1, source_target_pairs={{4,0},{8,4},{12,8},{16,12},{20,16},{24,20},{28,24},{5,1},{9,5},{13... | collective-permute-start | bytes 27656 | tf_op jit(solution)/shard_map/ppermute | solution.py:14
  18.8 70.3 %collective-permute-start.3 = (bf16[2048,768]{1,0:T(8,128)(2,1)}, bf16[2048,768]{1,0:T(8,128)(2,1)}, u32[]{:S(2)}, u32[]{:S(2)}) collective-permute-start(bf16[2048,768]{1,0:T(8,128)(2,1)} %compare_select_fusion), channel_id=1, source_target_pairs={{8,0},{12,4},{16,8},{20,12},{24,16},{28,20},{9,1},{13,5},{17,9},{2... | collective-permute-start | bytes 9437192 | tf_op jit(solution)/shard_map/ppermute | solution.py:14
  21.1 137.7 %collective-permute-start.4 = (bf16[2048,768]{1,0:T(8,128)(2,1)}, bf16[2048,768]{1,0:T(8,128)(2,1)}, u32[]{:S(2)}, u32[]{:S(2)}) collective-permute-start(bf16[2048,768]{1,0:T(8,128)(2,1)} %compare_select_fusion), channel_id=1, source_target_pairs={{0,12},{4,16},{8,20},{12,24},{16,28},{1,13},{5,17},{9,21},{13,25},... | collective-permute-start | bytes 9437192 | tf_op jit(solution)/shard_map/ppermute | solution.py:14
  26.7 132.9 %collective-permute-start.5 = (bf16[2048,768]{1,0:T(8,128)(2,1)}, bf16[2048,768]{1,0:T(8,128)(2,1)}, u32[]{:S(2)}, u32[]{:S(2)}) collective-permute-start(bf16[2048,768]{1,0:T(8,128)(2,1)} %compare_select_fusion), channel_id=1, source_target_pairs={{4,0},{8,4},{12,8},{16,12},{20,16},{24,20},{28,24},{5,1},{9,5},{13... | collective-permute-start | bytes 9437192 | tf_op jit(solution)/shard_map/ppermute | solution.py:14
  45.7 2.8 %copy-start.2 = (bf16[2048,768]{1,0:T(8,128)(2,1)}, bf16[2048,768]{1,0:T(8,128)(2,1)S(1)}, u32[]{:S(2)}) copy-start(bf16[2048,768]{1,0:T(8,128)(2,1)S(1)} %fusion.12) | copy-start | bytes 9437188
  48.4 4.7 %collective-permute-start.6 = (bf16[768,768]{1,0:T(8,128)(2,1)S(1)}, bf16[768,768]{1,0:T(8,128)(2,1)S(1)}, u32[]{:S(2)}, u32[]{:S(2)}) collective-permute-start(bf16[768,768]{1,0:T(8,128)(2,1)S(1)} %get-tuple-element.44), channel_id=1, source_target_pairs={{1,0},{3,2},{5,4},{7,6},{9,8},{11,10},{13,12},{15,14},{17,16},{19,... | collective-permute-start | bytes 3538952 | tf_op jit(solution)/shard_map/ppermute | solution.py:43
  54.4 16.4 %collective-permute-start.7 = (bf16[768,768]{1,0:T(8,128)(2,1)}, bf16[768,768]{1,0:T(8,128)(2,1)}, u32[]{:S(2)}, u32[]{:S(2)}) collective-permute-start(bf16[768,768]{1,0:T(8,128)(2,1)} %fusion.29), channel_id=1, source_target_pairs={{2,0},{6,4},{10,8},{14,12},{18,16},{22,20},{26,24},{30,28}} | collective-permute-start | bytes 3538952 | tf_op jit(solution)/shard_map/ppermute | solution.py:45
  59.8 99.7 %copy-start.3 = (bf16[2048,768]{1,0:T(8,128)(2,1)S(1)}, bf16[2048,768]{1,0:T(8,128)(2,1)}, u32[]{:S(2)}) copy-start(bf16[2048,768]{1,0:T(8,128)(2,1)} %copy-done.2) | copy-start | bytes 9437188
  59.8 99.7 %copy-start.4 = (f32[768]{0:T(1024)S(1)}, f32[768]{0:T(1024)}, u32[]{:S(2)}) copy-start(f32[768]{0:T(1024)} %get-tuple-element.36) | copy-start | bytes 9220
  59.8 99.7 %copy-start.5 = (f32[768]{0:T(1024)S(1)}, f32[768]{0:T(1024)}, u32[]{:S(2)}) copy-start(f32[768]{0:T(1024)} %get-tuple-element.49) | copy-start | bytes 9220
  164.5 10.6 %collective-permute-start.8 = (bf16[2,192,768]{2,1,0:T(8,128)(2,1)S(1)}, bf16[2,192,768]{2,1,0:T(8,128)(2,1)S(1)}, u32[]{:S(2)}, u32[]{:S(2)}) collective-permute-start(bf16[2,192,768]{2,1,0:T(8,128)(2,1)S(1)} %fusion.30), channel_id=1, source_target_pairs={{0,1},{1,0},{2,3},{3,2},{4,5},{5,4},{6,7},{7,6},{8,9},{9,8},{10,11... | collective-permute-start | bytes 1769480 | tf_op jit(solution)/shard_map/ppermute | solution.py:34
  169.5 6.4 %collective-permute-start.10 = (bf16[2,192,768]{2,1,0:T(8,128)(2,1)S(1)}, bf16[2,192,768]{2,1,0:T(8,128)(2,1)S(1)}, u32[]{:S(2)}, u32[]{:S(2)}) collective-permute-start(bf16[2,192,768]{2,1,0:T(8,128)(2,1)S(1)} %fusion.31), channel_id=1, source_target_pairs={{0,1},{1,0},{2,3},{3,2},{4,5},{5,4},{6,7},{7,6},{8,9},{9,8},{10,11... | collective-permute-start | bytes 1769480 | tf_op jit(solution)/shard_map/ppermute | solution.py:34
  175.0 2.6 %collective-permute-start.12 = (bf16[2,192,768]{2,1,0:T(8,128)(2,1)S(1)}, bf16[2,192,768]{2,1,0:T(8,128)(2,1)S(1)}, u32[]{:S(2)}, u32[]{:S(2)}) collective-permute-start(bf16[2,192,768]{2,1,0:T(8,128)(2,1)S(1)} %fusion.32), channel_id=1, source_target_pairs={{0,1},{1,0},{2,3},{3,2},{4,5},{5,4},{6,7},{7,6},{8,9},{9,8},{10,11... | collective-permute-start | bytes 1769480 | tf_op jit(solution)/shard_map/ppermute | solution.py:34
  175.3 9.9 %collective-permute-start.9 = (bf16[192,768]{1,0:T(8,128)(2,1)S(1)}, bf16[192,768]{1,0:T(8,128)(2,1)S(1)}, u32[]{:S(2)}, u32[]{:S(2)}) collective-permute-start(bf16[192,768]{1,0:T(8,128)(2,1)S(1)} %fusion.39), channel_id=1, source_target_pairs={{0,2},{1,3},{2,0},{3,1},{4,6},{5,7},{6,4},{7,5},{8,10},{9,11},{10,... | collective-permute-start | bytes 884744 | tf_op jit(solution)/shard_map/ppermute | solution.py:38
  176.0 15.5 %collective-permute-start.11 = (bf16[192,768]{1,0:T(8,128)(2,1)S(1)}, bf16[192,768]{1,0:T(8,128)(2,1)S(1)}, u32[]{:S(2)}, u32[]{:S(2)}) collective-permute-start(bf16[192,768]{1,0:T(8,128)(2,1)S(1)} %fusion.40), channel_id=1, source_target_pairs={{0,2},{1,3},{2,0},{3,1},{4,6},{5,7},{6,4},{7,5},{8,10},{9,11},{10,... | collective-permute-start | bytes 884744 | tf_op jit(solution)/shard_map/ppermute | solution.py:38
  177.8 19.6 %collective-permute-start.13 = (bf16[192,768]{1,0:T(8,128)(2,1)S(1)}, bf16[192,768]{1,0:T(8,128)(2,1)S(1)}, u32[]{:S(2)}, u32[]{:S(2)}) collective-permute-start(bf16[192,768]{1,0:T(8,128)(2,1)S(1)} %fusion.41), channel_id=1, source_target_pairs={{0,2},{1,3},{2,0},{3,1},{4,6},{5,7},{6,4},{7,5},{8,10},{9,11},{10,... | collective-permute-start | bytes 884744 | tf_op jit(solution)/shard_map/ppermute | solution.py:38
  185.5 14.6 %collective-permute-start.14 = (f32[768]{0:T(1024)S(1)}, f32[768]{0:T(1024)S(1)}, u32[]{:S(2)}, u32[]{:S(2)}) collective-permute-start(f32[768]{0:T(1024)S(1)} %get-tuple-element.29), channel_id=1, source_target_pairs={{0,4},{4,8},{8,12},{12,16},{16,20},{20,24},{24,28},{1,5},{5,9},{9,... | collective-permute-start | bytes 9224 | tf_op jit(solution)/shard_map/ppermute | solution.py:14
  191.8 8.3 %collective-permute-start.15 = (f32[768]{0:T(1024)S(1)}, f32[768]{0:T(1024)S(1)}, u32[]{:S(2)}, u32[]{:S(2)}) collective-permute-start(f32[768]{0:T(1024)S(1)} %get-tuple-element.27), channel_id=1, source_target_pairs={{0,8},{4,12},{8,16},{12,20},{16,24},{20,28},{1,9},{5,13},{9,17},{1... | collective-permute-start | bytes 9224 | tf_op jit(solution)/shard_map/ppermute | solution.py:14
  197.7 7.7 %collective-permute-start.16 = (f32[768]{0:T(1024)S(1)}, f32[768]{0:T(1024)S(1)}, u32[]{:S(2)}, u32[]{:S(2)}) collective-permute-start(f32[768]{0:T(1024)S(1)} %get-tuple-element.31), channel_id=1, source_target_pairs={{12,0},{16,4},{20,8},{24,12},{28,16},{13,1},{17,5},{21,9},{25,13},... | collective-permute-start | bytes 9224 | tf_op jit(solution)/shard_map/ppermute | solution.py:14

commit v14 on v13

--- a/solution.py
+++ b/solution.py
@@ -87,7 +87,14 @@
         adjusted = adjusted_r2(owned[offset], samples) * in_range
         row_total = row_total + jnp.sum(adjusted, 1)
         incoming = incoming + from_behind(jnp.sum(adjusted, 0), "var", step)
-    total = row_total + lax.psum_scatter(incoming, "samp", scatter_dimension=0, tiled=True)
+    core, chip = me % 2, me // 2
+    halves = incoming.reshape(2, 2, block_width // n_samp)
+    keep = lax.dynamic_index_in_dim(halves, core, 1, keepdims=False)
+    send = lax.dynamic_index_in_dim(halves, 1 - core, 1, keepdims=False)
+    summed = keep + lax.ppermute(send, "samp", [(s, s ^ 1) for s in range(n_samp)])
+    keep = lax.dynamic_index_in_dim(summed, chip, 0, keepdims=False)
+    send = lax.dynamic_index_in_dim(summed, 1 - chip, 0, keepdims=False)
+    total = row_total + keep + lax.ppermute(send, "samp", [(s, s ^ 2) for s in range(n_samp)])
     return total / block_width
 
 

time: 212 us -> 211 us (level)
  waiting for transfers between devices: 119 us -> 125 us
  blocking collectives: 17.2 us -> 11.3 us
    unnamed x1 -> x0, blocking collectives: 5.88 us -> none
    ppermute x0 -> x2, waiting for transfers between devices: none -> 4.2 us  [the longest x1 3.05 us: local(): lax.ppermute(send, 'samp', [(s, s ^ 2) for s in range(n_samp)])]
  transfers between devices with their start and end apart: 17 -> 19, of which waited for: 10 -> 12; matrix products, arithmetic and copies ran while one was open for 12% -> 11% of each run, Pallas kernels for 0% -> 0%
where the time goes in v14:
time: 211 us
  waiting for transfers between devices  125 us (59%)
  starting transfers between devices  38.9 us (18%)
  matrix products  17.3 us (8%)
  other arithmetic  16.9 us (8%)
  blocking collectives  11.3 us (5%)
    ppermute x9, waiting for transfers between devices, from_behind(): lax.ppermute(value, axis, [(source, source + steps) for source in range(l...  93.9 us
    ppermute x9, starting transfers between devices, from_behind(): lax.ppermute(value, axis, [(source, source + steps) for source in range(l...  30 us
    dot_general x4, matrix products, gram_of(): lax.dot_general(left, right, (((0,), (0,)), ((), ())), preferred_element_...  17.3 us
    ppermute x1, waiting for transfers between devices, reduce_to_owner(): lax.ppermute(summed.astype(jnp.bfloat16), 'samp', pairs_chip)  13 us
    psum x1, blocking collectives, local(): stats = lax.psum(jnp.stack([partial] + partner_partials), 'samp')  11.3 us
    ppermute x3, waiting for transfers between devices, reduce_quarters(): lax.ppermute(send.astype(jnp.bfloat16), 'samp', pairs_chip)  10.4 us
    reduce_sum x1, other arithmetic, local(): jnp.sum(present * values, 0)  5.42 us
  transfers between devices with their start and end apart: 19, of which 12 were waited for; matrix products, arithmetic and copies ran while one was open for 11% of the time, Pallas kernels for 0%

profile of v14, /device:TPU:14, one launch (start us, length us, event | category | flops | bytes accessed | tf_op | source)
XLA Modules:
  0.0 210.8 jit_solution(10030485542058574591)
XLA Ops:
  0.0 5.4 %fusion.13 = (f32[768]{0:T(1024)S(1)}, f32[768]{0:T(1024)S(1)}, f32[768]{0:T(1024)S(1)}) fusion(bf16[2048,768]{1,0:T(8,128)(2,1)} %param.2, s32[2048,768]{1,0:T(8,128)} %param.3), kind=kLoop, calls=%fused_computation.24 | loop fusion | flops 11007744 | bytes 9446400 | tf_op jit(solution)/shard_map/reduce_sum | solution.py:54
  5.5 2.4 %collective-permute-start = (f32[3,768]{1,0:T(4,128)S(1)}, f32[3,768]{1,0:T(4,128)S(1)}, u32[]{:S(2)}, u32[]{:S(2)}) collective-permute-start(f32[3,768]{1,0:T(4,128)S(1)} %get-tuple-element.43), channel_id=1, source_target_pairs={{8,0},{12,4},{16,8},{20,12},{24,16},{28,20},{9,1},{13,5},{17,9},{2... | collective-permute-start | bytes 27656 | tf_op jit(solution)/shard_map/ppermute | solution.py:14
  7.8 4.4 %collective-permute-start.1 = (f32[3,768]{1,0:T(4,128)S(1)}, f32[3,768]{1,0:T(4,128)S(1)}, u32[]{:S(2)}, u32[]{:S(2)}) collective-permute-start(f32[3,768]{1,0:T(4,128)S(1)} %get-tuple-element.43), channel_id=1, source_target_pairs={{0,12},{4,16},{8,20},{12,24},{16,28},{1,13},{5,17},{9,21},{13,25},... | collective-permute-start | bytes 27656 | tf_op jit(solution)/shard_map/ppermute | solution.py:14
  12.3 2.4 %collective-permute-start.2 = (f32[3,768]{1,0:T(4,128)S(1)}, f32[3,768]{1,0:T(4,128)S(1)}, u32[]{:S(2)}, u32[]{:S(2)}) collective-permute-start(f32[3,768]{1,0:T(4,128)S(1)} %get-tuple-element.43), channel_id=1, source_target_pairs={{4,0},{8,4},{12,8},{16,12},{20,16},{24,20},{28,24},{5,1},{9,5},{13... | collective-permute-start | bytes 27656 | tf_op jit(solution)/shard_map/ppermute | solution.py:14
  14.7 2.4 %compare_select_fusion = bf16[2048,768]{1,0:T(8,128)(2,1)} fusion(bf16[2048,768]{1,0:T(8,128)(2,1)S(1)} %copy-done.1, s32[2048,768]{1,0:T(8,128)S(1)} %copy-done), kind=kLoop, calls=%fused_computation.23 | loop fusion | flops 3145728 | bytes 12582912 | tf_op jit(solution)/shard_map/jit(_where)/select_n | solution.py:56
  17.1 1.7 collective-permute-done.2
  18.8 2.3 %collective-permute-start.3 = (bf16[2048,768]{1,0:T(8,128)(2,1)}, bf16[2048,768]{1,0:T(8,128)(2,1)}, u32[]{:S(2)}, u32[]{:S(2)}) collective-permute-start(bf16[2048,768]{1,0:T(8,128)(2,1)} %compare_select_fusion), channel_id=1, source_target_pairs={{8,0},{12,4},{16,8},{20,12},{24,16},{28,20},{9,1},{13,5},{17,9},{2... | collective-permute-start | bytes 9437192 | tf_op jit(solution)/shard_map/ppermute | solution.py:14
  21.1 5.4 %collective-permute-start.4 = (bf16[2048,768]{1,0:T(8,128)(2,1)}, bf16[2048,768]{1,0:T(8,128)(2,1)}, u32[]{:S(2)}, u32[]{:S(2)}) collective-permute-start(bf16[2048,768]{1,0:T(8,128)(2,1)} %compare_select_fusion), channel_id=1, source_target_pairs={{0,12},{4,16},{8,20},{12,24},{16,28},{1,13},{5,17},{9,21},{13,25},... | collective-permute-start | bytes 9437192 | tf_op jit(solution)/shard_map/ppermute | solution.py:14
  26.5 3.1 %collective-permute-start.5 = (bf16[2048,768]{1,0:T(8,128)(2,1)}, bf16[2048,768]{1,0:T(8,128)(2,1)}, u32[]{:S(2)}, u32[]{:S(2)}) collective-permute-start(bf16[2048,768]{1,0:T(8,128)(2,1)} %compare_select_fusion), channel_id=1, source_target_pairs={{4,0},{8,4},{12,8},{16,12},{20,16},{24,20},{28,24},{5,1},{9,5},{13... | collective-permute-start | bytes 9437192 | tf_op jit(solution)/shard_map/ppermute | solution.py:14
  29.7 11.3 %psum.7 = f32[4,3,768]{2,1,0:T(4,128)S(1)} all-reduce(f32[4,3,768]{2,1,0:T(4,128)S(1)} %pad_maximum_fusion), channel_id=1, replica_groups=mesh['var'=8,'samp'=4] {'samp'}, use_global_device_ids=true, to_apply=%region_3.4 | all-reduce | flops 9216 | bytes 73728 | tf_op jit(solution)/shard_map/psum | solution.py:59
  41.1 0.7 slice_reduce_fusion.4
  41.7 3.9 %fusion.12 = bf16[2048,768]{1,0:T(8,128)(2,1)S(1)} fusion(bf16[2048,768]{1,0:T(8,128)(2,1)S(1)} %copy-done.1, s32[2048,768]{1,0:T(8,128)} %param.3, f32[768]{0:T(1024)S(1)} %get-tuple-element.38, f32[768]{0:T(1024)S(1)} %get-tuple-element.50), kind=kLoop, calls=%fused_computation.21 | loop fusion | flops 9437184 | bytes 12589056 | tf_op jit(solution)/shard_map/convert_element_type | solution.py:64
  45.7 2.7 %fusion.53 = (bf16[768,768]{1,0:T(8,128)(2,1)S(1)}, f32[768,768]{1,0:T(8,128)S(1)}) fusion(bf16[2048,768]{1,0:T(8,128)(2,1)S(1)} %fusion.12), kind=kOutput, calls=%fused_computation.101 | convolution fusion | flops 2416508928 | bytes 6684672 | tf_op jit(solution)/shard_map/dot_general | solution.py:24
  48.4 1.3 collective-permute-start.6
  49.7 3.4 %collective-permute-done.6 = bf16[768,768]{1,0:T(8,128)(2,1)S(1)} collective-permute-done((bf16[768,768]{1,0:T(8,128)(2,1)S(1)}, bf16[768,768]{1,0:T(8,128)(2,1)S(1)}, u32[]{:S(2)}, u32[]{:S(2)}) %collective-permute-start.6) | collective-permute-done | bytes 1179680 | tf_op jit(solution)/shard_map/ppermute | solution.py:43
  53.1 1.3 fusion.29
  54.4 3.4 %collective-permute-start.7 = (bf16[768,768]{1,0:T(8,128)(2,1)}, bf16[768,768]{1,0:T(8,128)(2,1)}, u32[]{:S(2)}, u32[]{:S(2)}) collective-permute-start(bf16[768,768]{1,0:T(8,128)(2,1)} %fusion.29), channel_id=1, source_target_pairs={{2,0},{6,4},{10,8},{14,12},{18,16},{22,20},{26,24},{30,28}} | collective-permute-start | bytes 3538952 | tf_op jit(solution)/shard_map/ppermute | solution.py:45
  57.8 13.0 %collective-permute-done.7 = bf16[768,768]{1,0:T(8,128)(2,1)} collective-permute-done((bf16[768,768]{1,0:T(8,128)(2,1)}, bf16[768,768]{1,0:T(8,128)(2,1)}, u32[]{:S(2)}, u32[]{:S(2)}) %collective-permute-start.7) | collective-permute-done | bytes 1179680 | tf_op jit(solution)/shard_map/ppermute | solution.py:45
  70.8 1.6 convert_add_fusion
  72.4 16.7 %collective-permute-done.3 = bf16[2048,768]{1,0:T(8,128)(2,1)} collective-permute-done((bf16[2048,768]{1,0:T(8,128)(2,1)}, bf16[2048,768]{1,0:T(8,128)(2,1)}, u32[]{:S(2)}, u32[]{:S(2)}) %collective-permute-start.3) | collective-permute-done | bytes 3145760 | tf_op jit(solution)/shard_map/ppermute | solution.py:14
  89.1 69.6 %collective-permute-done.4 = bf16[2048,768]{1,0:T(8,128)(2,1)} collective-permute-done((bf16[2048,768]{1,0:T(8,128)(2,1)}, bf16[2048,768]{1,0:T(8,128)(2,1)}, u32[]{:S(2)}, u32[]{:S(2)}) %collective-permute-start.4) | collective-permute-done | bytes 3145760 | tf_op jit(solution)/shard_map/ppermute | solution.py:14
  158.7 0.8 collective-permute-done.5
  159.5 4.9 %fusion.18 = f32[768,768]{1,0:T(8,128)S(1)} fusion(bf16[2048,768]{1,0:T(8,128)(2,1)S(1)} %copy-done.3, bf16[2048,768]{1,0:T(8,128)(2,1)} %collective-permute-done.5, f32[768]{0:T(1024)S(1)} %copy-done.4, f32[768]{0:T(1024)S(1)} %copy-done.5), kind=kOutput, calls=%fused_computation.27 | convolution fusion | flops 2425356288 | bytes 8656896 | tf_op jit(solution)/shard_map/dot_general | solution.py:24
  164.5 4.9 %fusion.16 = f32[768,768]{1,0:T(8,128)S(1)} fusion(bf16[2048,768]{1,0:T(8,128)(2,1)S(1)} %copy-done.3, bf16[2048,768]{1,0:T(8,128)(2,1)} %collective-permute-done.3, f32[768]{0:T(1024)S(1)} %get-tuple-element.37, f32[768]{0:T(1024)S(1)} %get-tuple-element.51), kind=kOutput, calls=%fused_computation.26 | convolution fusion | flops 2425356288 | bytes 8656896 | tf_op jit(solution)/shard_map/dot_general | solution.py:24
  169.5 0.6 collective-permute-start.10
  170.1 4.9 %fusion.14 = f32[768,768]{1,0:T(8,128)S(1)} fusion(bf16[2048,768]{1,0:T(8,128)(2,1)S(1)} %copy-done.3, bf16[2048,768]{1,0:T(8,128)(2,1)} %collective-permute-done.4, f32[768]{0:T(1024)S(1)} %get-tuple-element.39, f32[768]{0:T(1024)S(1)} %get-tuple-element.52), kind=kOutput, calls=%fused_computation.25 | convolution fusion | flops 2425356288 | bytes 8656896 | tf_op jit(solution)/shard_map/dot_general | solution.py:24
  175.0 0.1 collective-permute-start.12
  175.1 0.1 bitcast_add_fusion.2
  175.3 0.6 collective-permute-start.9
  175.9 0.1 bitcast_add_fusion.1
  176.0 1.6 collective-permute-start.11
  177.6 0.1 bitcast_add_fusion
  177.8 0.6 collective-permute-start.13
  178.4 6.9 %collective-permute-done.9 = bf16[192,768]{1,0:T(8,128)(2,1)S(1)} collective-permute-done((bf16[192,768]{1,0:T(8,128)(2,1)S(1)}, bf16[192,768]{1,0:T(8,128)(2,1)S(1)}, u32[]{:S(2)}, u32[]{:S(2)}) %collective-permute-start.9) | collective-permute-done | bytes 294944 | tf_op jit(solution)/shard_map/ppermute | solution.py:38
  185.2 0.3 fusion.43
  185.5 4.5 %collective-permute-start.14 = (f32[768]{0:T(1024)S(1)}, f32[768]{0:T(1024)S(1)}, u32[]{:S(2)}, u32[]{:S(2)}) collective-permute-start(f32[768]{0:T(1024)S(1)} %get-tuple-element.29), channel_id=1, source_target_pairs={{0,4},{4,8},{8,12},{12,16},{16,20},{20,24},{24,28},{1,5},{5,9},{9,... | collective-permute-start | bytes 9224 | tf_op jit(solution)/shard_map/ppermute | solution.py:14
  190.0 1.5 collective-permute-done.11
  191.5 0.3 fusion.45
  191.8 3.5 %collective-permute-start.15 = (f32[768]{0:T(1024)S(1)}, f32[768]{0:T(1024)S(1)}, u32[]{:S(2)}, u32[]{:S(2)}) collective-permute-start(f32[768]{0:T(1024)S(1)} %get-tuple-element.27), channel_id=1, source_target_pairs={{0,8},{4,12},{8,16},{12,20},{16,24},{20,28},{1,9},{5,13},{9,17},{1... | collective-permute-start | bytes 9224 | tf_op jit(solution)/shard_map/ppermute | solution.py:14
  195.3 2.1 collective-permute-done.13
  197.4 0.3 fusion.47
  197.7 1.9 collective-permute-start.16
  199.6 0.5 subtract_reduce_fusion
  200.1 5.1 %collective-permute-done.16 = f32[768]{0:T(1024)S(1)} collective-permute-done((f32[768]{0:T(1024)S(1)}, f32[768]{0:T(1024)S(1)}, u32[]{:S(2)}, u32[]{:S(2)}) %collective-permute-start.16) | collective-permute-done | bytes 3104 | tf_op jit(solution)/shard_map/ppermute | solution.py:14
  205.4 1.1 collective-permute-done.17
  206.6 0.6 collective-permute-start.18
  207.2 3.0 %collective-permute-done.18 = f32[192]{0:T(256)S(1)} collective-permute-done((f32[192]{0:T(256)S(1)}, f32[192]{0:T(256)S(1)}, u32[]{:S(2)}, u32[]{:S(2)}) %collective-permute-start.18) | collective-permute-done | bytes 800 | tf_op jit(solution)/shard_map/ppermute | solution.py:97
  210.2 0.6 add_multiply_fusion
  (39 shorter events, 0.7 us)
Async XLA Ops:
  0.0 14.7 %copy-start.1 = (bf16[2048,768]{1,0:T(8,128)(2,1)S(1)}, bf16[2048,768]{1,0:T(8,128)(2,1)}, u32[]{:S(2)}) copy-start(bf16[2048,768]{1,0:T(8,128)(2,1)} %param.2) | copy-start | bytes 9437188
  0.0 14.7 %copy-start = (s32[2048,768]{1,0:T(8,128)S(1)}, s32[2048,768]{1,0:T(8,128)}, u32[]{:S(2)}) copy-start(s32[2048,768]{1,0:T(8,128)} %param.3) | copy-start | bytes 18874372
  5.5 11.6 %collective-permute-start = (f32[3,768]{1,0:T(4,128)S(1)}, f32[3,768]{1,0:T(4,128)S(1)}, u32[]{:S(2)}, u32[]{:S(2)}) collective-permute-start(f32[3,768]{1,0:T(4,128)S(1)} %get-tuple-element.43), channel_id=1, source_target_pairs={{8,0},{12,4},{16,8},{20,12},{24,16},{28,20},{9,1},{13,5},{17,9},{2... | collective-permute-start | bytes 27656 | tf_op jit(solution)/shard_map/ppermute | solution.py:14
  7.8 9.3 %collective-permute-start.1 = (f32[3,768]{1,0:T(4,128)S(1)}, f32[3,768]{1,0:T(4,128)S(1)}, u32[]{:S(2)}, u32[]{:S(2)}) collective-permute-start(f32[3,768]{1,0:T(4,128)S(1)} %get-tuple-element.43), channel_id=1, source_target_pairs={{0,12},{4,16},{8,20},{12,24},{16,28},{1,13},{5,17},{9,21},{13,25},... | collective-permute-start | bytes 27656 | tf_op jit(solution)/shard_map/ppermute | solution.py:14
  12.3 6.5 %collective-permute-start.2 = (f32[3,768]{1,0:T(4,128)S(1)}, f32[3,768]{1,0:T(4,128)S(1)}, u32[]{:S(2)}, u32[]{:S(2)}) collective-permute-start(f32[3,768]{1,0:T(4,128)S(1)} %get-tuple-element.43), channel_id=1, source_target_pairs={{4,0},{8,4},{12,8},{16,12},{20,16},{24,20},{28,24},{5,1},{9,5},{13... | collective-permute-start | bytes 27656 | tf_op jit(solution)/shard_map/ppermute | solution.py:14
  18.8 70.3 %collective-permute-start.3 = (bf16[2048,768]{1,0:T(8,128)(2,1)}, bf16[2048,768]{1,0:T(8,128)(2,1)}, u32[]{:S(2)}, u32[]{:S(2)}) collective-permute-start(bf16[2048,768]{1,0:T(8,128)(2,1)} %compare_select_fusion), channel_id=1, source_target_pairs={{8,0},{12,4},{16,8},{20,12},{24,16},{28,20},{9,1},{13,5},{17,9},{2... | collective-permute-start | bytes 9437192 | tf_op jit(solution)/shard_map/ppermute | solution.py:14
  21.1 137.5 %collective-permute-start.4 = (bf16[2048,768]{1,0:T(8,128)(2,1)}, bf16[2048,768]{1,0:T(8,128)(2,1)}, u32[]{:S(2)}, u32[]{:S(2)}) collective-permute-start(bf16[2048,768]{1,0:T(8,128)(2,1)} %compare_select_fusion), channel_id=1, source_target_pairs={{0,12},{4,16},{8,20},{12,24},{16,28},{1,13},{5,17},{9,21},{13,25},... | collective-permute-start | bytes 9437192 | tf_op jit(solution)/shard_map/ppermute | solution.py:14
  26.5 133.0 %collective-permute-start.5 = (bf16[2048,768]{1,0:T(8,128)(2,1)}, bf16[2048,768]{1,0:T(8,128)(2,1)}, u32[]{:S(2)}, u32[]{:S(2)}) collective-permute-start(bf16[2048,768]{1,0:T(8,128)(2,1)} %compare_select_fusion), channel_id=1, source_target_pairs={{4,0},{8,4},{12,8},{16,12},{20,16},{24,20},{28,24},{5,1},{9,5},{13... | collective-permute-start | bytes 9437192 | tf_op jit(solution)/shard_map/ppermute | solution.py:14
  45.7 2.7 %copy-start.2 = (bf16[2048,768]{1,0:T(8,128)(2,1)}, bf16[2048,768]{1,0:T(8,128)(2,1)S(1)}, u32[]{:S(2)}) copy-start(bf16[2048,768]{1,0:T(8,128)(2,1)S(1)} %fusion.12) | copy-start | bytes 9437188
  48.4 4.7 %collective-permute-start.6 = (bf16[768,768]{1,0:T(8,128)(2,1)S(1)}, bf16[768,768]{1,0:T(8,128)(2,1)S(1)}, u32[]{:S(2)}, u32[]{:S(2)}) collective-permute-start(bf16[768,768]{1,0:T(8,128)(2,1)S(1)} %get-tuple-element.48), channel_id=1, source_target_pairs={{1,0},{3,2},{5,4},{7,6},{9,8},{11,10},{13,12},{15,14},{17,16},{19,... | collective-permute-start | bytes 3538952 | tf_op jit(solution)/shard_map/ppermute | solution.py:43
  54.4 16.4 %collective-permute-start.7 = (bf16[768,768]{1,0:T(8,128)(2,1)}, bf16[768,768]{1,0:T(8,128)(2,1)}, u32[]{:S(2)}, u32[]{:S(2)}) collective-permute-start(bf16[768,768]{1,0:T(8,128)(2,1)} %fusion.29), channel_id=1, source_target_pairs={{2,0},{6,4},{10,8},{14,12},{18,16},{22,20},{26,24},{30,28}} | collective-permute-start | bytes 3538952 | tf_op jit(solution)/shard_map/ppermute | solution.py:45
  57.8 101.7 %copy-start.3 = (bf16[2048,768]{1,0:T(8,128)(2,1)S(1)}, bf16[2048,768]{1,0:T(8,128)(2,1)}, u32[]{:S(2)}) copy-start(bf16[2048,768]{1,0:T(8,128)(2,1)} %copy-done.2) | copy-start | bytes 9437188
  57.8 101.7 %copy-start.4 = (f32[768]{0:T(1024)S(1)}, f32[768]{0:T(1024)}, u32[]{:S(2)}) copy-start(f32[768]{0:T(1024)} %get-tuple-element.36) | copy-start | bytes 9220
  57.8 101.7 %copy-start.5 = (f32[768]{0:T(1024)S(1)}, f32[768]{0:T(1024)}, u32[]{:S(2)}) copy-start(f32[768]{0:T(1024)} %get-tuple-element.53) | copy-start | bytes 9220
  164.5 10.6 %collective-permute-start.8 = (bf16[2,192,768]{2,1,0:T(8,128)(2,1)S(1)}, bf16[2,192,768]{2,1,0:T(8,128)(2,1)S(1)}, u32[]{:S(2)}, u32[]{:S(2)}) collective-permute-start(bf16[2,192,768]{2,1,0:T(8,128)(2,1)S(1)} %fusion.30), channel_id=1, source_target_pairs={{0,1},{1,0},{2,3},{3,2},{4,5},{5,4},{6,7},{7,6},{8,9},{9,8},{10,11... | collective-permute-start | bytes 1769480 | tf_op jit(solution)/shard_map/ppermute | solution.py:34
  169.5 6.4 %collective-permute-start.10 = (bf16[2,192,768]{2,1,0:T(8,128)(2,1)S(1)}, bf16[2,192,768]{2,1,0:T(8,128)(2,1)S(1)}, u32[]{:S(2)}, u32[]{:S(2)}) collective-permute-start(bf16[2,192,768]{2,1,0:T(8,128)(2,1)S(1)} %fusion.31), channel_id=1, source_target_pairs={{0,1},{1,0},{2,3},{3,2},{4,5},{5,4},{6,7},{7,6},{8,9},{9,8},{10,11... | collective-permute-start | bytes 1769480 | tf_op jit(solution)/shard_map/ppermute | solution.py:34
  175.0 2.6 %collective-permute-start.12 = (bf16[2,192,768]{2,1,0:T(8,128)(2,1)S(1)}, bf16[2,192,768]{2,1,0:T(8,128)(2,1)S(1)}, u32[]{:S(2)}, u32[]{:S(2)}) collective-permute-start(bf16[2,192,768]{2,1,0:T(8,128)(2,1)S(1)} %fusion.32), channel_id=1, source_target_pairs={{0,1},{1,0},{2,3},{3,2},{4,5},{5,4},{6,7},{7,6},{8,9},{9,8},{10,11... | collective-permute-start | bytes 1769480 | tf_op jit(solution)/shard_map/ppermute | solution.py:34
  175.3 9.9 %collective-permute-start.9 = (bf16[192,768]{1,0:T(8,128)(2,1)S(1)}, bf16[192,768]{1,0:T(8,128)(2,1)S(1)}, u32[]{:S(2)}, u32[]{:S(2)}) collective-permute-start(bf16[192,768]{1,0:T(8,128)(2,1)S(1)} %fusion.39), channel_id=1, source_target_pairs={{0,2},{1,3},{2,0},{3,1},{4,6},{5,7},{6,4},{7,5},{8,10},{9,11},{10,... | collective-permute-start | bytes 884744 | tf_op jit(solution)/shard_map/ppermute | solution.py:38
  176.0 15.5 %collective-permute-start.11 = (bf16[192,768]{1,0:T(8,128)(2,1)S(1)}, bf16[192,768]{1,0:T(8,128)(2,1)S(1)}, u32[]{:S(2)}, u32[]{:S(2)}) collective-permute-start(bf16[192,768]{1,0:T(8,128)(2,1)S(1)} %fusion.40), channel_id=1, source_target_pairs={{0,2},{1,3},{2,0},{3,1},{4,6},{5,7},{6,4},{7,5},{8,10},{9,11},{10,... | collective-permute-start | bytes 884744 | tf_op jit(solution)/shard_map/ppermute | solution.py:38
  177.8 19.6 %collective-permute-start.13 = (bf16[192,768]{1,0:T(8,128)(2,1)S(1)}, bf16[192,768]{1,0:T(8,128)(2,1)S(1)}, u32[]{:S(2)}, u32[]{:S(2)}) collective-permute-start(bf16[192,768]{1,0:T(8,128)(2,1)S(1)} %fusion.41), channel_id=1, source_target_pairs={{0,2},{1,3},{2,0},{3,1},{4,6},{5,7},{6,4},{7,5},{8,10},{9,11},{10,... | collective-permute-start | bytes 884744 | tf_op jit(solution)/shard_map/ppermute | solution.py:38
  185.5 14.6 %collective-permute-start.14 = (f32[768]{0:T(1024)S(1)}, f32[768]{0:T(1024)S(1)}, u32[]{:S(2)}, u32[]{:S(2)}) collective-permute-start(f32[768]{0:T(1024)S(1)} %get-tuple-element.29), channel_id=1, source_target_pairs={{0,4},{4,8},{8,12},{12,16},{16,20},{20,24},{24,28},{1,5},{5,9},{9,... | collective-permute-start | bytes 9224 | tf_op jit(solution)/shard_map/ppermute | solution.py:14
  191.8 8.3 %collective-permute-start.15 = (f32[768]{0:T(1024)S(1)}, f32[768]{0:T(1024)S(1)}, u32[]{:S(2)}, u32[]{:S(2)}) collective-permute-start(f32[768]{0:T(1024)S(1)} %get-tuple-element.27), channel_id=1, source_target_pairs={{0,8},{4,12},{8,16},{12,20},{16,24},{20,28},{1,9},{5,13},{9,17},{1... | collective-permute-start | bytes 9224 | tf_op jit(solution)/shard_map/ppermute | solution.py:14
  197.7 7.6 %collective-permute-start.16 = (f32[768]{0:T(1024)S(1)}, f32[768]{0:T(1024)S(1)}, u32[]{:S(2)}, u32[]{:S(2)}) collective-permute-start(f32[768]{0:T(1024)S(1)} %get-tuple-element.31), channel_id=1, source_target_pairs={{12,0},{16,4},{20,8},{24,12},{28,16},{13,1},{17,5},{21,9},{25,13},... | collective-permute-start | bytes 9224 | tf_op jit(solution)/shard_map/ppermute | solution.py:14
  205.4 1.2 collective-permute-start.17
  206.6 3.6 %collective-permute-start.18 = (f32[192]{0:T(256)S(1)}, f32[192]{0:T(256)S(1)}, u32[]{:S(2)}, u32[]{:S(2)}) collective-permute-start(f32[192]{0:T(256)S(1)} %bitcast.93), channel_id=1, source_target_pairs={{0,2},{1,3},{2,0},{3,1},{4,6},{5,7},{6,4},{7,5},{8,10},{9,11},{10,... | collective-permute-start | bytes 2312 | tf_op jit(solution)/shard_map/ppermute | solution.py:97

commit v15 on v14

--- a/solution.py
+++ b/solution.py
@@ -70,13 +70,17 @@
         ([raw[d] for d in PROCESS_ORDER], same_total, standard)
     )
     owned = {}
-    for index, (offset, coded_partner) in enumerate(zip(PROCESS_ORDER, arrived)):
+    for index, offset in enumerate(PROCESS_ORDER):
+        coded_partner = arrived[index]
         partner_values = coded_partner.astype(jnp.float32)
         partner_present = (partner_values >= 0).astype(jnp.float32)
         partner = (
             (partner_values - column_mean[index + 1]) * scale[index + 1] * partner_present
         ).astype(jnp.bfloat16)
         owned[offset] = reduce_quarters(gram_of(standard_late, partner), n_samp)
+        if index == 0:
+            rest, owned[offset] = lax.optimization_barrier((arrived[1:], owned[offset]))
+            arrived = arrived[:1] + list(rest)
 
     me = lax.axis_index("samp")
     incoming = jnp.sum(adjusted_r2(same_total, samples), 1) * (me == 0).astype(jnp.float32)

time: 211 us -> 227 us (1.076)
  other arithmetic: 16.9 us -> 24.5 us
  local copies, waits for them, and re-layouts: 1.12 us -> 6.73 us
  waiting for transfers between devices: 125 us -> 128 us
    unnamed x13 -> x27, local copies, waits for them, and re-layouts: 0.03 us -> 4.52 us
    add x3, other arithmetic: 0.33 us -> 3.36 us  [reduce_quarters(): keep + lax.ppermute(send.astype(jnp.bfloat16), 'samp', pairs_core).astype...]
    ppermute x3, waiting for transfers between devices: 10.4 us -> 13.4 us  [reduce_quarters(): lax.ppermute(send.astype(jnp.bfloat16), 'samp', pairs_chip)]
    add x1, other arithmetic: 1.58 us -> 4.02 us  [reduce_to_owner(): summed + lax.ppermute(summed.astype(jnp.bfloat16), 'samp', pairs_chip).as...]
    ppermute x3, waiting for transfers between devices: 0.01 us -> 2.35 us  [reduce_quarters(): lax.ppermute(send.astype(jnp.bfloat16), 'samp', pairs_core)]
  transfers between devices with their start and end apart: 19 -> 19, of which waited for: 12 -> 13; matrix products, arithmetic and copies ran while one was open for 11% -> 10% of each run, Pallas kernels for 0% -> 0%
where the time goes in v15:
time: 227 us
  waiting for transfers between devices  128 us (56%)
  starting transfers between devices  38.3 us (17%)
  other arithmetic  24.5 us (11%)
  matrix products  17.2 us (8%)
  blocking collectives  11.3 us (5%)
  local copies, waits for them, and re-layouts  6.73 us (3%)
    ppermute x9, waiting for transfers between devices, from_behind(): lax.ppermute(value, axis, [(source, source + steps) for source in range(l...  91.8 us
    ppermute x9, starting transfers between devices, from_behind(): lax.ppermute(value, axis, [(source, source + steps) for source in range(l...  30 us
    dot_general x4, matrix products, gram_of(): lax.dot_general(left, right, (((0,), (0,)), ((), ())), preferred_element_...  17.2 us
    ppermute x3, waiting for transfers between devices, reduce_quarters(): lax.ppermute(send.astype(jnp.bfloat16), 'samp', pairs_chip)  13.4 us
    ppermute x1, waiting for transfers between devices, reduce_to_owner(): lax.ppermute(summed.astype(jnp.bfloat16), 'samp', pairs_chip)  12.9 us
    psum x1, blocking collectives, local(): stats = lax.psum(jnp.stack([partial] + partner_partials), 'samp')  11.3 us
    reduce_sum x1, other arithmetic, local(): jnp.sum(present * values, 0)  5.42 us
  transfers between devices with their start and end apart: 19, of which 13 were waited for; matrix products, arithmetic and copies ran while one was open for 10% of the time, Pallas kernels for 0%

profile of v15, /device:TPU:14, one launch (start us, length us, event | category | flops | bytes accessed | tf_op | source)
XLA Modules:
  0.0 226.7 jit_solution(4203499349292119710)
XLA Ops:
  0.0 5.4 %fusion.13 = (f32[768]{0:T(1024)S(1)}, f32[768]{0:T(1024)S(1)}, f32[768]{0:T(1024)S(1)}) fusion(bf16[2048,768]{1,0:T(8,128)(2,1)} %param.2, s32[2048,768]{1,0:T(8,128)} %param.3), kind=kLoop, calls=%fused_computation.24 | loop fusion | flops 11007744 | bytes 9446400 | tf_op jit(solution)/shard_map/reduce_sum | solution.py:54
  5.5 2.4 %collective-permute-start = (f32[3,768]{1,0:T(4,128)S(1)}, f32[3,768]{1,0:T(4,128)S(1)}, u32[]{:S(2)}, u32[]{:S(2)}) collective-permute-start(f32[3,768]{1,0:T(4,128)S(1)} %get-tuple-element.49), channel_id=1, source_target_pairs={{8,0},{12,4},{16,8},{20,12},{24,16},{28,20},{9,1},{13,5},{17,9},{2... | collective-permute-start | bytes 27656 | tf_op jit(solution)/shard_map/ppermute | solution.py:14
  7.8 4.4 %collective-permute-start.1 = (f32[3,768]{1,0:T(4,128)S(1)}, f32[3,768]{1,0:T(4,128)S(1)}, u32[]{:S(2)}, u32[]{:S(2)}) collective-permute-start(f32[3,768]{1,0:T(4,128)S(1)} %get-tuple-element.49), channel_id=1, source_target_pairs={{0,12},{4,16},{8,20},{12,24},{16,28},{1,13},{5,17},{9,21},{13,25},... | collective-permute-start | bytes 27656 | tf_op jit(solution)/shard_map/ppermute | solution.py:14
  12.3 2.4 %collective-permute-start.2 = (f32[3,768]{1,0:T(4,128)S(1)}, f32[3,768]{1,0:T(4,128)S(1)}, u32[]{:S(2)}, u32[]{:S(2)}) collective-permute-start(f32[3,768]{1,0:T(4,128)S(1)} %get-tuple-element.49), channel_id=1, source_target_pairs={{4,0},{8,4},{12,8},{16,12},{20,16},{24,20},{28,24},{5,1},{9,5},{13... | collective-permute-start | bytes 27656 | tf_op jit(solution)/shard_map/ppermute | solution.py:14
  14.7 2.4 %compare_select_fusion = bf16[2048,768]{1,0:T(8,128)(2,1)} fusion(bf16[2048,768]{1,0:T(8,128)(2,1)S(1)} %copy-done.1, s32[2048,768]{1,0:T(8,128)S(1)} %copy-done), kind=kLoop, calls=%fused_computation.23 | loop fusion | flops 3145728 | bytes 12582912 | tf_op jit(solution)/shard_map/jit(_where)/select_n | solution.py:56
  17.1 1.7 collective-permute-done.2
  18.8 2.3 %collective-permute-start.3 = (bf16[2048,768]{1,0:T(8,128)(2,1)}, bf16[2048,768]{1,0:T(8,128)(2,1)}, u32[]{:S(2)}, u32[]{:S(2)}) collective-permute-start(bf16[2048,768]{1,0:T(8,128)(2,1)} %compare_select_fusion), channel_id=1, source_target_pairs={{8,0},{12,4},{16,8},{20,12},{24,16},{28,20},{9,1},{13,5},{17,9},{2... | collective-permute-start | bytes 9437192 | tf_op jit(solution)/shard_map/ppermute | solution.py:14
  21.1 5.4 %collective-permute-start.4 = (bf16[2048,768]{1,0:T(8,128)(2,1)}, bf16[2048,768]{1,0:T(8,128)(2,1)}, u32[]{:S(2)}, u32[]{:S(2)}) collective-permute-start(bf16[2048,768]{1,0:T(8,128)(2,1)} %compare_select_fusion), channel_id=1, source_target_pairs={{0,12},{4,16},{8,20},{12,24},{16,28},{1,13},{5,17},{9,21},{13,25},... | collective-permute-start | bytes 9437192 | tf_op jit(solution)/shard_map/ppermute | solution.py:14
  26.5 3.1 %collective-permute-start.5 = (bf16[2048,768]{1,0:T(8,128)(2,1)}, bf16[2048,768]{1,0:T(8,128)(2,1)}, u32[]{:S(2)}, u32[]{:S(2)}) collective-permute-start(bf16[2048,768]{1,0:T(8,128)(2,1)} %compare_select_fusion), channel_id=1, source_target_pairs={{4,0},{8,4},{12,8},{16,12},{20,16},{24,20},{28,24},{5,1},{9,5},{13... | collective-permute-start | bytes 9437192 | tf_op jit(solution)/shard_map/ppermute | solution.py:14
  29.7 11.3 %psum.7 = f32[4,3,768]{2,1,0:T(4,128)S(1)} all-reduce(f32[4,3,768]{2,1,0:T(4,128)S(1)} %pad_maximum_fusion), channel_id=1, replica_groups=mesh['var'=8,'samp'=4] {'samp'}, use_global_device_ids=true, to_apply=%region_3.4 | all-reduce | flops 9216 | bytes 73728 | tf_op jit(solution)/shard_map/psum | solution.py:59
  41.2 3.9 %fusion.12 = bf16[2048,768]{1,0:T(8,128)(2,1)S(1)} fusion(bf16[2048,768]{1,0:T(8,128)(2,1)S(1)} %copy-done.1, s32[2048,768]{1,0:T(8,128)} %param.3, f32[768]{0:T(1024)S(1)} %get-tuple-element.44, f32[768]{0:T(1024)S(1)} %get-tuple-element.56), kind=kLoop, calls=%fused_computation.21 | loop fusion | flops 9437184 | bytes 12589056 | tf_op jit(solution)/shard_map/convert_element_type | solution.py:64
  45.1 2.7 %fusion.51 = (bf16[768,768]{1,0:T(8,128)(2,1)S(1)}, f32[768,768]{1,0:T(8,128)S(1)}) fusion(bf16[2048,768]{1,0:T(8,128)(2,1)S(1)} %fusion.12), kind=kOutput, calls=%fused_computation.99 | convolution fusion | flops 2416508928 | bytes 6684672 | tf_op jit(solution)/shard_map/dot_general | solution.py:24
  47.8 1.3 collective-permute-start.6
  49.1 3.4 %collective-permute-done.6 = bf16[768,768]{1,0:T(8,128)(2,1)S(1)} collective-permute-done((bf16[768,768]{1,0:T(8,128)(2,1)S(1)}, bf16[768,768]{1,0:T(8,128)(2,1)S(1)}, u32[]{:S(2)}, u32[]{:S(2)}) %collective-permute-start.6) | collective-permute-done | bytes 1179680 | tf_op jit(solution)/shard_map/ppermute | solution.py:43
  52.6 1.4 fusion.29
  54.0 3.5 %collective-permute-start.7 = (bf16[768,768]{1,0:T(8,128)(2,1)}, bf16[768,768]{1,0:T(8,128)(2,1)}, u32[]{:S(2)}, u32[]{:S(2)}) collective-permute-start(bf16[768,768]{1,0:T(8,128)(2,1)} %fusion.29), channel_id=1, source_target_pairs={{2,0},{6,4},{10,8},{14,12},{18,16},{22,20},{26,24},{30,28}} | collective-permute-start | bytes 3538952 | tf_op jit(solution)/shard_map/ppermute | solution.py:45
  57.5 12.9 %collective-permute-done.7 = bf16[768,768]{1,0:T(8,128)(2,1)} collective-permute-done((bf16[768,768]{1,0:T(8,128)(2,1)}, bf16[768,768]{1,0:T(8,128)(2,1)}, u32[]{:S(2)}, u32[]{:S(2)}) %collective-permute-start.7) | collective-permute-done | bytes 1179680 | tf_op jit(solution)/shard_map/ppermute | solution.py:45
  70.4 4.0 %convert_add_fusion = f32[768,768]{1,0:T(8,128)} fusion(bf16[768,768]{1,0:T(8,128)(2,1)} %collective-permute-done.7, f32[768,768]{1,0:T(8,128)} %copy-done.4, bf16[768,768]{1,0:T(8,128)(2,1)} %copy-done.6), kind=kLoop, calls=%fused_computation.38 | loop fusion | flops 2359296 | bytes 7077888 | tf_op jit(solution)/shard_map/add | solution.py:45
  74.5 14.6 %collective-permute-done.3 = bf16[2048,768]{1,0:T(8,128)(2,1)} collective-permute-done((bf16[2048,768]{1,0:T(8,128)(2,1)}, bf16[2048,768]{1,0:T(8,128)(2,1)}, u32[]{:S(2)}, u32[]{:S(2)}) %collective-permute-start.3) | collective-permute-done | bytes 3145760 | tf_op jit(solution)/shard_map/ppermute | solution.py:14
  89.1 69.6 %collective-permute-done.4 = bf16[2048,768]{1,0:T(8,128)(2,1)} collective-permute-done((bf16[2048,768]{1,0:T(8,128)(2,1)}, bf16[2048,768]{1,0:T(8,128)(2,1)}, u32[]{:S(2)}, u32[]{:S(2)}) %collective-permute-start.4) | collective-permute-done | bytes 3145760 | tf_op jit(solution)/shard_map/ppermute | solution.py:14
  158.7 0.8 collective-permute-done.5
  159.5 4.8 %fusion.18 = f32[768,768]{1,0:T(8,128)S(1)} fusion(bf16[2048,768]{1,0:T(8,128)(2,1)S(1)} %copy-done.3, bf16[2048,768]{1,0:T(8,128)(2,1)} %collective-permute-done.3, f32[768]{0:T(1024)S(1)} %get-tuple-element.43, f32[768]{0:T(1024)S(1)} %get-tuple-element.57), kind=kOutput, calls=%fused_computation.27 | convolution fusion | flops 2425356288 | bytes 8656896 | tf_op jit(solution)/shard_map/dot_general | solution.py:24
  164.4 1.4 copy-done.12
  165.8 0.9 fusion.30
  166.7 2.3 %collective-permute-done.8 = bf16[2,192,768]{2,1,0:T(8,128)(2,1)} collective-permute-done((bf16[2,192,768]{2,1,0:T(8,128)(2,1)}, bf16[2,192,768]{2,1,0:T(8,128)(2,1)}, u32[]{:S(2)}, u32[]{:S(2)}) %collective-permute-start.8) | collective-permute-done | bytes 589856 | tf_op jit(solution)/shard_map/ppermute | solution.py:34
  169.0 1.6 bitcast_add_fusion.2
  170.6 1.0 copy-done.7
  171.6 0.6 collective-permute-start.9
  172.2 8.6 %collective-permute-done.9 = bf16[192,768]{1,0:T(8,128)(2,1)} collective-permute-done((bf16[192,768]{1,0:T(8,128)(2,1)S(1)}, bf16[192,768]{1,0:T(8,128)(2,1)}, u32[]{:S(2)}, u32[]{:S(2)}) %collective-permute-start.9) | collective-permute-done | bytes 294944 | tf_op jit(solution)/shard_map/ppermute | solution.py:38
  180.9 2.0 bitcast_add_fusion.5
  182.9 4.8 %fusion.16 = f32[768,768]{1,0:T(8,128)S(1)} fusion(bf16[2048,768]{1,0:T(8,128)(2,1)S(1)} %copy-done.3, bf16[2048,768]{1,0:T(8,128)(2,1)} %collective-permute-done.5, f32[768]{0:T(1024)S(1)} %get-tuple-element.42, f32[768]{0:T(1024)S(1)} %get-tuple-element.59), kind=kOutput, calls=%fused_computation.26 | convolution fusion | flops 2425356288 | bytes 8656896 | tf_op jit(solution)/shard_map/dot_general | solution.py:24
  187.8 1.0 fusion.31
  188.7 0.6 copy-done.11
  189.4 4.8 %fusion.14 = f32[768,768]{1,0:T(8,128)S(1)} fusion(bf16[2048,768]{1,0:T(8,128)(2,1)S(1)} %copy-done.3, bf16[2048,768]{1,0:T(8,128)(2,1)} %collective-permute-done.4, f32[768]{0:T(1024)S(1)} %get-tuple-element.45, f32[768]{0:T(1024)S(1)} %get-tuple-element.58), kind=kOutput, calls=%fused_computation.25 | convolution fusion | flops 2425356288 | bytes 8656896 | tf_op jit(solution)/shard_map/dot_general | solution.py:24
  194.2 1.4 copy-done.9
  195.8 1.7 bitcast_add_fusion.1
  197.6 0.6 collective-permute-start.11
  198.3 1.6 collective-permute-start.13
  200.1 3.5 %collective-permute-start.15 = (f32[768]{0:T(1024)S(1)}, f32[768]{0:T(1024)S(1)}, u32[]{:S(2)}, u32[]{:S(2)}) collective-permute-start(f32[768]{0:T(1024)S(1)} %get-tuple-element.37), channel_id=1, source_target_pairs={{0,8},{4,12},{8,16},{12,20},{16,24},{20,28},{1,9},{5,13},{9,17},{1... | collective-permute-start | bytes 9224 | tf_op jit(solution)/shard_map/ppermute | solution.py:14
  203.6 3.9 %collective-permute-done.11 = bf16[192,768]{1,0:T(8,128)(2,1)S(1)} collective-permute-done((bf16[192,768]{1,0:T(8,128)(2,1)S(1)}, bf16[192,768]{1,0:T(8,128)(2,1)S(1)}, u32[]{:S(2)}, u32[]{:S(2)}) %collective-permute-start.11) | collective-permute-done | bytes 294944 | tf_op jit(solution)/shard_map/ppermute | solution.py:38
  207.8 4.5 %collective-permute-start.14 = (f32[768]{0:T(1024)S(1)}, f32[768]{0:T(1024)S(1)}, u32[]{:S(2)}, u32[]{:S(2)}) collective-permute-start(f32[768]{0:T(1024)S(1)} %get-tuple-element.33), channel_id=1, source_target_pairs={{0,4},{4,8},{8,12},{12,16},{16,20},{20,24},{24,28},{1,5},{5,9},{9,... | collective-permute-start | bytes 9224 | tf_op jit(solution)/shard_map/ppermute | solution.py:14
  212.4 0.9 collective-permute-done.13
  213.5 1.9 collective-permute-start.16
  216.0 5.1 %collective-permute-done.16 = f32[768]{0:T(1024)S(1)} collective-permute-done((f32[768]{0:T(1024)S(1)}, f32[768]{0:T(1024)S(1)}, u32[]{:S(2)}, u32[]{:S(2)}) %collective-permute-start.16) | collective-permute-done | bytes 3104 | tf_op jit(solution)/shard_map/ppermute | solution.py:14
  221.3 1.1 collective-permute-done.17
  222.5 0.6 collective-permute-start.18
  223.1 3.0 %collective-permute-done.18 = f32[192]{0:T(256)S(1)} collective-permute-done((f32[192]{0:T(256)S(1)}, f32[192]{0:T(256)S(1)}, u32[]{:S(2)}, u32[]{:S(2)}) %collective-permute-start.18) | collective-permute-done | bytes 800 | tf_op jit(solution)/shard_map/ppermute | solution.py:101
  226.1 0.6 add_multiply_fusion
  (54 shorter events, 2.1 us)
Async XLA Ops:
  0.0 14.7 %copy-start.1 = (bf16[2048,768]{1,0:T(8,128)(2,1)S(1)}, bf16[2048,768]{1,0:T(8,128)(2,1)}, u32[]{:S(2)}) copy-start(bf16[2048,768]{1,0:T(8,128)(2,1)} %param.2) | copy-start | bytes 9437188
  0.0 14.7 %copy-start = (s32[2048,768]{1,0:T(8,128)S(1)}, s32[2048,768]{1,0:T(8,128)}, u32[]{:S(2)}) copy-start(s32[2048,768]{1,0:T(8,128)} %param.3) | copy-start | bytes 18874372
  5.5 11.6 %collective-permute-start = (f32[3,768]{1,0:T(4,128)S(1)}, f32[3,768]{1,0:T(4,128)S(1)}, u32[]{:S(2)}, u32[]{:S(2)}) collective-permute-start(f32[3,768]{1,0:T(4,128)S(1)} %get-tuple-element.49), channel_id=1, source_target_pairs={{8,0},{12,4},{16,8},{20,12},{24,16},{28,20},{9,1},{13,5},{17,9},{2... | collective-permute-start | bytes 27656 | tf_op jit(solution)/shard_map/ppermute | solution.py:14
  7.8 9.3 %collective-permute-start.1 = (f32[3,768]{1,0:T(4,128)S(1)}, f32[3,768]{1,0:T(4,128)S(1)}, u32[]{:S(2)}, u32[]{:S(2)}) collective-permute-start(f32[3,768]{1,0:T(4,128)S(1)} %get-tuple-element.49), channel_id=1, source_target_pairs={{0,12},{4,16},{8,20},{12,24},{16,28},{1,13},{5,17},{9,21},{13,25},... | collective-permute-start | bytes 27656 | tf_op jit(solution)/shard_map/ppermute | solution.py:14
  12.3 6.5 %collective-permute-start.2 = (f32[3,768]{1,0:T(4,128)S(1)}, f32[3,768]{1,0:T(4,128)S(1)}, u32[]{:S(2)}, u32[]{:S(2)}) collective-permute-start(f32[3,768]{1,0:T(4,128)S(1)} %get-tuple-element.49), channel_id=1, source_target_pairs={{4,0},{8,4},{12,8},{16,12},{20,16},{24,20},{28,24},{5,1},{9,5},{13... | collective-permute-start | bytes 27656 | tf_op jit(solution)/shard_map/ppermute | solution.py:14
  18.8 70.3 %collective-permute-start.3 = (bf16[2048,768]{1,0:T(8,128)(2,1)}, bf16[2048,768]{1,0:T(8,128)(2,1)}, u32[]{:S(2)}, u32[]{:S(2)}) collective-permute-start(bf16[2048,768]{1,0:T(8,128)(2,1)} %compare_select_fusion), channel_id=1, source_target_pairs={{8,0},{12,4},{16,8},{20,12},{24,16},{28,20},{9,1},{13,5},{17,9},{2... | collective-permute-start | bytes 9437192 | tf_op jit(solution)/shard_map/ppermute | solution.py:14
  21.1 137.5 %collective-permute-start.4 = (bf16[2048,768]{1,0:T(8,128)(2,1)}, bf16[2048,768]{1,0:T(8,128)(2,1)}, u32[]{:S(2)}, u32[]{:S(2)}) collective-permute-start(bf16[2048,768]{1,0:T(8,128)(2,1)} %compare_select_fusion), channel_id=1, source_target_pairs={{0,12},{4,16},{8,20},{12,24},{16,28},{1,13},{5,17},{9,21},{13,25},... | collective-permute-start | bytes 9437192 | tf_op jit(solution)/shard_map/ppermute | solution.py:14
  26.5 133.0 %collective-permute-start.5 = (bf16[2048,768]{1,0:T(8,128)(2,1)}, bf16[2048,768]{1,0:T(8,128)(2,1)}, u32[]{:S(2)}, u32[]{:S(2)}) collective-permute-start(bf16[2048,768]{1,0:T(8,128)(2,1)} %compare_select_fusion), channel_id=1, source_target_pairs={{4,0},{8,4},{12,8},{16,12},{20,16},{24,20},{28,24},{5,1},{9,5},{13... | collective-permute-start | bytes 9437192 | tf_op jit(solution)/shard_map/ppermute | solution.py:14
  45.1 2.7 %copy-start.2 = (bf16[2048,768]{1,0:T(8,128)(2,1)}, bf16[2048,768]{1,0:T(8,128)(2,1)S(1)}, u32[]{:S(2)}) copy-start(bf16[2048,768]{1,0:T(8,128)(2,1)S(1)} %fusion.12) | copy-start | bytes 9437188
  47.8 4.8 %copy-start.4 = (f32[768,768]{1,0:T(8,128)}, f32[768,768]{1,0:T(8,128)S(1)}, u32[]{:S(2)}) copy-start(f32[768,768]{1,0:T(8,128)S(1)} %get-tuple-element.55) | copy-start | bytes 7077892
  47.8 4.7 %collective-permute-start.6 = (bf16[768,768]{1,0:T(8,128)(2,1)S(1)}, bf16[768,768]{1,0:T(8,128)(2,1)S(1)}, u32[]{:S(2)}, u32[]{:S(2)}) collective-permute-start(bf16[768,768]{1,0:T(8,128)(2,1)S(1)} %get-tuple-element.54), channel_id=1, source_target_pairs={{1,0},{3,2},{5,4},{7,6},{9,8},{11,10},{13,12},{15,14},{17,16},{19,... | collective-permute-start | bytes 3538952 | tf_op jit(solution)/shard_map/ppermute | solution.py:43
  52.6 1.4 copy-start.6
  54.0 16.4 %collective-permute-start.7 = (bf16[768,768]{1,0:T(8,128)(2,1)}, bf16[768,768]{1,0:T(8,128)(2,1)}, u32[]{:S(2)}, u32[]{:S(2)}) collective-permute-start(bf16[768,768]{1,0:T(8,128)(2,1)} %fusion.29), channel_id=1, source_target_pairs={{2,0},{6,4},{10,8},{14,12},{18,16},{22,20},{26,24},{30,28}} | collective-permute-start | bytes 3538952 | tf_op jit(solution)/shard_map/ppermute | solution.py:45
  57.5 102.0 %copy-start.3 = (bf16[2048,768]{1,0:T(8,128)(2,1)S(1)}, bf16[2048,768]{1,0:T(8,128)(2,1)}, u32[]{:S(2)}) copy-start(bf16[2048,768]{1,0:T(8,128)(2,1)} %copy-done.2) | copy-start | bytes 9437188
  164.4 1.4 copy-start.12
  166.7 2.3 %collective-permute-start.8 = (bf16[2,192,768]{2,1,0:T(8,128)(2,1)}, bf16[2,192,768]{2,1,0:T(8,128)(2,1)}, u32[]{:S(2)}, u32[]{:S(2)}) collective-permute-start(bf16[2,192,768]{2,1,0:T(8,128)(2,1)} %fusion.30), channel_id=1, source_target_pairs={{0,1},{1,0},{2,3},{3,2},{4,5},{5,4},{6,7},{7,6},{8,9},{9,8},{10,11... | collective-permute-start | bytes 1769480 | tf_op jit(solution)/shard_map/ppermute | solution.py:34
  170.6 1.0 copy-start.7
  171.6 9.2 %collective-permute-start.9 = (bf16[192,768]{1,0:T(8,128)(2,1)S(1)}, bf16[192,768]{1,0:T(8,128)(2,1)}, u32[]{:S(2)}, u32[]{:S(2)}) collective-permute-start(bf16[192,768]{1,0:T(8,128)(2,1)S(1)} %fusion.39), channel_id=1, source_target_pairs={{0,2},{1,3},{2,0},{3,1},{4,6},{5,7},{6,4},{7,5},{8,10},{9,11},{10,... | collective-permute-start | bytes 884744 | tf_op jit(solution)/shard_map/ppermute | solution.py:38
  187.7 1.6 copy-start.11
  188.7 7.1 %collective-permute-start.10 = (bf16[2,192,768]{2,1,0:T(8,128)(2,1)}, bf16[2,192,768]{2,1,0:T(8,128)(2,1)}, u32[]{:S(2)}, u32[]{:S(2)}) collective-permute-start(bf16[2,192,768]{2,1,0:T(8,128)(2,1)} %fusion.31), channel_id=1, source_target_pairs={{0,1},{1,0},{2,3},{3,2},{4,5},{5,4},{6,7},{7,6},{8,9},{9,8},{10,11... | collective-permute-start | bytes 1769480 | tf_op jit(solution)/shard_map/ppermute | solution.py:34
  194.2 1.4 copy-start.9
  195.7 2.5 %copy-start.10 = (f32[768,768]{1,0:T(8,128)S(1)}, f32[768,768]{1,0:T(8,128)}, u32[]{:S(2)}) copy-start(f32[768,768]{1,0:T(8,128)} %copy-done.9) | copy-start | bytes 7077892
  195.7 2.5 %collective-permute-start.12 = (bf16[2,192,768]{2,1,0:T(8,128)(2,1)S(1)}, bf16[2,192,768]{2,1,0:T(8,128)(2,1)S(1)}, u32[]{:S(2)}, u32[]{:S(2)}) collective-permute-start(bf16[2,192,768]{2,1,0:T(8,128)(2,1)S(1)} %fusion.32), channel_id=1, source_target_pairs={{0,1},{1,0},{2,3},{3,2},{4,5},{5,4},{6,7},{7,6},{8,9},{9,8},{10,11... | collective-permute-start | bytes 1769480 | tf_op jit(solution)/shard_map/ppermute | solution.py:34
  195.8 4.1 %copy-start.8 = (f32[192,768]{1,0:T(8,128)S(1)}, f32[192,768]{1,0:T(8,128)}, u32[]{:S(2)}) copy-start(f32[192,768]{1,0:T(8,128)} %bitcast_add_fusion.5) | copy-start | bytes 1769476
  197.5 17.9 %copy-start.5 = (f32[768,768]{1,0:T(8,128)S(1)}, f32[768,768]{1,0:T(8,128)}, u32[]{:S(2)}) copy-start(f32[768,768]{1,0:T(8,128)} %convert_add_fusion) | copy-start | bytes 7077892
  197.6 9.9 %collective-permute-start.11 = (bf16[192,768]{1,0:T(8,128)(2,1)S(1)}, bf16[192,768]{1,0:T(8,128)(2,1)S(1)}, u32[]{:S(2)}, u32[]{:S(2)}) collective-permute-start(bf16[192,768]{1,0:T(8,128)(2,1)S(1)} %fusion.40), channel_id=1, source_target_pairs={{0,2},{1,3},{2,0},{3,1},{4,6},{5,7},{6,4},{7,5},{8,10},{9,11},{10,... | collective-permute-start | bytes 884744 | tf_op jit(solution)/shard_map/ppermute | solution.py:38
  198.3 14.9 %collective-permute-start.13 = (bf16[192,768]{1,0:T(8,128)(2,1)S(1)}, bf16[192,768]{1,0:T(8,128)(2,1)S(1)}, u32[]{:S(2)}, u32[]{:S(2)}) collective-permute-start(bf16[192,768]{1,0:T(8,128)(2,1)S(1)} %fusion.41), channel_id=1, source_target_pairs={{0,2},{1,3},{2,0},{3,1},{4,6},{5,7},{6,4},{7,5},{8,10},{9,11},{10,... | collective-permute-start | bytes 884744 | tf_op jit(solution)/shard_map/ppermute | solution.py:38
  200.1 15.8 %collective-permute-start.15 = (f32[768]{0:T(1024)S(1)}, f32[768]{0:T(1024)S(1)}, u32[]{:S(2)}, u32[]{:S(2)}) collective-permute-start(f32[768]{0:T(1024)S(1)} %get-tuple-element.37), channel_id=1, source_target_pairs={{0,8},{4,12},{8,16},{12,20},{16,24},{20,28},{1,9},{5,13},{9,17},{1... | collective-permute-start | bytes 9224 | tf_op jit(solution)/shard_map/ppermute | solution.py:14
  207.8 8.2 %collective-permute-start.14 = (f32[768]{0:T(1024)S(1)}, f32[768]{0:T(1024)S(1)}, u32[]{:S(2)}, u32[]{:S(2)}) collective-permute-start(f32[768]{0:T(1024)S(1)} %get-tuple-element.33), channel_id=1, source_target_pairs={{0,4},{4,8},{8,12},{12,16},{16,20},{20,24},{24,28},{1,5},{5,9},{9,... | collective-permute-start | bytes 9224 | tf_op jit(solution)/shard_map/ppermute | solution.py:14
  213.5 7.6 %collective-permute-start.16 = (f32[768]{0:T(1024)S(1)}, f32[768]{0:T(1024)S(1)}, u32[]{:S(2)}, u32[]{:S(2)}) collective-permute-start(f32[768]{0:T(1024)S(1)} %get-tuple-element.35), channel_id=1, source_target_pairs={{12,0},{16,4},{20,8},{24,12},{28,16},{13,1},{17,5},{21,9},{25,13},... | collective-permute-start | bytes 9224 | tf_op jit(solution)/shard_map/ppermute | solution.py:14
  221.2 1.2 collective-permute-start.17
  222.5 3.6 %collective-permute-start.18 = (f32[192]{0:T(256)S(1)}, f32[192]{0:T(256)S(1)}, u32[]{:S(2)}, u32[]{:S(2)}) collective-permute-start(f32[192]{0:T(256)S(1)} %bitcast.83), channel_id=1, source_target_pairs={{0,2},{1,3},{2,0},{3,1},{4,6},{5,7},{6,4},{7,5},{8,10},{9,11},{10,... | collective-permute-start | bytes 2312 | tf_op jit(solution)/shard_map/ppermute | solution.py:101
